TPU v7x, 128 devices: a whole 4x4x4 slice. The times are simulated.
128 devices in a mesh: grp: 2 (over y_hi), row: 64 (over z, y_lo, x, core).
Axes of the slice: x: 4, y: 4 (y_hi: 2, y_lo: 2; y = y_hi * 2 + y_lo), z: 4, core: 2. Of those that a mesh axis runs over, the one named last changes fastest.
Arguments:
- features: bfloat16 [65536, 256], P(('grp', 'row')), may hold values from -6 to 6
- weight: bfloat16 [256, 256], replicated, may hold values from -0.375 to 0.375
- block_vals: bfloat16 [2, 512, 16, 128, 128], P('grp', 'row'), may hold values from -0.125 to 0.125
- block_cols: int32 [2, 512, 16], P('grp', 'row'), may hold values from 0 to 255, as said below
- block_count: int32 [2, 512], P('grp', 'row'), may hold values from 1 to 16, as said below
- cotangent: bfloat16 [65536, 256], P(('grp', 'row')), may hold values from -6 to 6
Outputs:
- activated: bfloat16 [65536, 256], P(('grp', 'row'))
- weight_grad: float32 [256, 256], replicated
- input_grad: bfloat16 [65536, 256], P(('grp', 'row'))
Inputs may be any that keep to these rules, and one draw needn't show every extreme that they name: `block_cols`: within one destination row block the 16 column blocks are distinct and ascending. `block_count`: in every draw some device holds 16 live slots in each of its row blocks.
All inputs are finite; a program needn't handle non-finite values.
Results may differ from a plain program's by a relative error of at most 0.0062.
Values may be sent and summed in bfloat16 or wider, within the bound.
No kernel may reach another device: no remote copies, remote signals or barrier semaphores. Data moves between devices by JAX's collectives and lax.ppermute only.
A program may use at most 128 MiB of HBM per device.

v0:
```python
import math

import jax
import jax.numpy as jnp
from jax import lax
from jax.sharding import PartitionSpec as P


def silu_slope(pre):
    sigma = jax.nn.sigmoid(pre)
    return sigma * (1.0 + pre * (1.0 - sigma))


def body(features, weight, block_vals, block_cols, block_count, cotangent):
    rows_dev, width = features.shape
    block = block_vals.shape[-1]
    slot_total = block_vals.shape[2]
    groups = lax.axis_size("grp")
    members = lax.axis_size("row")
    verts = rows_dev * groups * members
    slots = jnp.arange(slot_total)
    gathered = lax.all_gather(features, "row", axis=0, tiled=True)
    col_blocks = gathered.shape[0] // block
    panel_blocks = gathered.reshape(col_blocks, block, width)

    def aggregate(items):
        values, columns, count = items
        masked = jnp.where((slots < count)[:, None, None], values, jnp.zeros_like(values))
        picked = panel_blocks[columns]
        return jnp.einsum("kij,kjf->if", masked, picked, preferred_element_type=jnp.float32)

    partial_value = lax.map(aggregate, (block_vals[0], block_cols[0], block_count[0])).reshape(
        -1, width
    )
    summed = lax.psum_scatter(partial_value, "grp", scatter_dimension=0, tiled=True)
    aggregated = summed.astype(jnp.bfloat16)
    pre = jnp.dot(aggregated, weight, preferred_element_type=jnp.float32)
    activated = jax.nn.silu(pre).astype(jnp.bfloat16)
    pre_grad = (cotangent.astype(jnp.float32) * silu_slope(pre)).astype(jnp.bfloat16)
    local_grad = jnp.dot(aggregated.T, pre_grad, preferred_element_type=jnp.float32)
    own_grad = jnp.dot(pre_grad, weight.T, preferred_element_type=jnp.float32).astype(jnp.bfloat16)
    rows_grad = lax.all_gather(own_grad, "grp", axis=0, tiled=True)
    weight_grad = lax.psum(local_grad, ("grp", "row")) * (1.0 / math.sqrt(verts))
    by_block = rows_grad.reshape(-1, block, width)

    def spread(carry, items):
        values, columns, count, grad_block = items
        masked = jnp.where((slots < count)[:, None, None], values, jnp.zeros_like(values))
        contrib = jnp.einsum("kij,if->kjf", masked, grad_block, preferred_element_type=jnp.float32)
        return (carry.at[columns].add(contrib), None)

    total, unused = lax.scan(
        spread,
        jnp.zeros((col_blocks, block, width), jnp.float32),
        (block_vals[0], block_cols[0], block_count[0], by_block),
    )
    term = total.reshape(-1, width)
    input_grad = lax.psum_scatter(term, "row", scatter_dimension=0, tiled=True).astype(jnp.bfloat16)
    return (activated, weight_grad, input_grad)


def solution(mesh):
    placed = (
        P(("grp", "row"), None),
        P(),
        P("grp", "row", None, None, None),
        P("grp", "row", None),
        P("grp", "row"),
        P(("grp", "row"), None),
    )
    return jax.shard_map(
        body,
        mesh=mesh,
        in_specs=placed,
        out_specs=(P(("grp", "row"), None), P(), P(("grp", "row"), None)),
        check_vma=False,
    )
```

profile of v0, /device:TPU:0, one launch (start us, length us, event | category | flops | bytes accessed | tf_op | source)
XLA Modules:
  0.0 743.4 jit_solution(15940612499893916046)
XLA Ops:
  8.0 127.3 %all-gather.2.cloned.1.call-done = bf16[32768,256]{1,0:T(8,128)(2,1)} async-done(((bf16[512,256]{1,0:T(8,128)(2,1)}), bf16[32768,256]{1,0:T(8,128)(2,1)}) %all-gather.2.cloned.1.call-update) | async-done | bytes 16777232 | tf_op jit(solution)/shard_map/all_gather | solution.py:22
  135.3 88.4 %while.22 = (s32[]{:T(128)}, f32[8,128,256]{2,1,0:T(8,128)}, s32[8]{0:T(128)}, bf16[8,16,128,128]{3,2,1,0:T(8,128)(2,1)}, s32[8,16]{1,0:T(8,128)}, /*index=5*/bf16[256,128,256]{2,1,0:T(8,128)(2,1)}, s32[]{:T(128)}) while((s32[]{:T(128)}, f32[8,128,256]{2,1,0:T(8,128)}, s32[8]{0:T(128)}, bf16[8,16,128,128]{3,2,1,0:T(8,128)(2,1)}, ...), condition=%wide.region_1.2_spmd.clone, body=%wide.region_0.1_spmd.clone.sunk | while | flops 134480960 | bytes 3806601 | solution.py:32
  135.3 1.2 dynamic_slice.67
  137.9 6.4 gather_fusion
  144.3 2.1 fusion.42
  146.3 1.2 dynamic_slice.67
  148.9 6.4 gather_fusion
  155.3 2.1 fusion.42
  157.4 1.2 dynamic_slice.67
  160.0 6.4 gather_fusion
  166.4 2.1 fusion.42
  168.4 1.2 dynamic_slice.67
  171.0 6.4 gather_fusion
  177.4 2.1 fusion.42
  182.1 6.4 gather_fusion
  188.5 2.0 fusion.42
  193.1 6.4 gather_fusion
  199.5 2.1 fusion.42
  204.1 6.4 gather_fusion
  210.5 2.1 fusion.42
  215.2 6.4 gather_fusion
  221.6 2.1 fusion.42
  223.7 6.5 copy.9
  230.2 17.2 %reduce-scatter.3.cloned.1.call-done = f32[512,256]{1,0:T(8,128)} async-done(((f32[1024,256]{1,0:T(8,128)}), f32[512,256]{1,0:T(8,128)}) %reduce-scatter.3.cloned.1.call-update) | async-done | bytes 524304 | tf_op jit(solution)/shard_map/reduce_scatter | solution.py:35
  247.4 2.2 multiply_convert_fusion
  250.9 10.2 %all_gather.7 = bf16[1024,256]{1,0:T(8,128)(2,1)S(1)} all-gather(bf16[512,256]{1,0:T(8,128)(2,1)S(1)} %convolution_convert_fusion), channel_id=1, replica_groups=mesh['grp'=2,'row'=64] {'grp'}, dimensions={0}, use_global_device_ids=true | all-gather | bytes 786432 | tf_op jit(solution)/shard_map/all_gather | solution.py:42
  261.1 11.2 %broadcast_in_dim.28 = f32[256,128,256]{2,1,0:T(8,128)} broadcast(f32[]{:T(128)} %constant.27.clone.1), dimensions={} | broadcast | bytes 33554436 | tf_op jit(solution)/shard_map/broadcast_in_dim | solution.py:54
  272.4 63.9 %while.23 = (s32[]{:T(128)}, f32[256,128,256]{2,1,0:T(8,128)}, s32[8,16]{1,0:T(8,128)}, s32[8]{0:T(128)S(1)}, bf16[8,16,128,128]{2,3,1,0:T(8,128)(2,1)}, /*index=5*/bf16[8,128,256]{2,1,0:T(8,128)(2,1)S(1)}, s32[]{:T(128)}) while((s32[]{:T(128)}, f32[256,128,256]{2,1,0:T(8,128)}, s32[8,16]{1,0:T(8,128)}, s32[8]{0:T(128)S(1)}, ...), condition=%wide.region_6.7_spmd.clone, body=%wide.region_4.6_spmd.clone.sunk | while | flops 135004224 | bytes 8980281 | solution.py:52
  274.2 1.5 fusion.46
  275.7 4.7 scatter_fusion
  282.3 1.5 fusion.46
  283.8 4.7 scatter_fusion
  290.3 1.5 fusion.46
  291.8 4.6 scatter_fusion
  298.3 1.5 fusion.46
  299.8 4.6 scatter_fusion
  306.3 1.5 fusion.46
  307.8 4.6 scatter_fusion
  314.2 1.5 fusion.46
  315.8 4.6 scatter_fusion
  322.2 1.5 fusion.46
  323.7 4.6 scatter_fusion
  330.2 1.5 fusion.46
  331.7 4.6 scatter_fusion
  336.3 58.5 %all-reduce.2.cloned.1.call-done = f32[256,256]{1,0:T(8,128)} async-done(((f32[256,256]{1,0:T(8,128)}), f32[256,256]{1,0:T(8,128)}) %all-reduce.2.cloned.1.call-update) | async-done | bytes 262160 | tf_op jit(solution)/shard_map/psum | solution.py:43
  394.8 1.7 broadcast_multiply_fusion
  396.5 338.6 %reduce-scatter.5.cloned.1.call-done = f32[512,256]{1,0:T(8,128)} async-done(((f32[32768,256]{1,0:T(8,128)}), f32[512,256]{1,0:T(8,128)}) %reduce-scatter.5.cloned.1.call-update) | async-done | bytes 524304 | tf_op jit(solution)/shard_map/reduce_scatter | solution.py:58
  735.1 1.8 convert_element_type.23
  (71 shorter events, 32.6 us)
Async XLA Ops:
  7.2 240.2 %copy-start = (bf16[256,256]{1,0:T(8,128)(2,1)S(1)}, bf16[256,256]{1,0:T(8,128)(2,1)}, u32[]{:S(2)}) copy-start(bf16[256,256]{1,0:T(8,128)(2,1)} %param.11) | copy-start | bytes 393220
  7.2 128.1 %all-gather.2.cloned.1.call-start = ((), (), s32[]{:S(2)}) async-start(), calls=%async_computation.2 | async-start | bytes 17039360 | tf_op jit(solution)/shard_map/all_gather | solution.py:22
  7.9 239.5 %reduce-scatter.3.cloned.1.call-start = ((), (), s32[]{:S(2)}) async-start(), calls=%async_computation.3 | async-start | bytes 1572864 | tf_op jit(solution)/shard_map/reduce_scatter | solution.py:35
  223.7 23.7 %copy-start.2 = (bf16[512,256]{1,0:T(8,128)(2,1)S(1)}, bf16[512,256]{1,0:T(8,128)(2,1)}, u32[]{:S(2)}) copy-start(bf16[512,256]{1,0:T(8,128)(2,1)} %param.15) | copy-start | bytes 786436
  223.7 171.1 %all-reduce.2.cloned.1.call-start = ((), (), s32[]{:S(2)}) async-start(), calls=%async_computation.4 | async-start | bytes 524288 | tf_op jit(solution)/shard_map/psum | solution.py:43
  247.4 2.5 copy-start.1
  250.9 484.2 %reduce-scatter.5.cloned.1.call-start = ((), (), s32[]{:S(2)}) async-start(), calls=%async_computation.5 | async-start | bytes 34078720 | tf_op jit(solution)/shard_map/reduce_scatter | solution.py:58
  261.1 11.2 %copy-start.3 = (s32[8]{0:T(128)S(1)}, s32[8]{0:T(128)}, u32[]{:S(2)}) copy-start(s32[8]{0:T(128)} %get-tuple-element.273) | copy-start | bytes 100
Sparse Core Ops, SparseCore 0:
  9.7 125.4 all-gather.1
  223.8 23.5 reduce-scatter.2
  253.4 141.3 all-reduce.1
  397.2 337.8 reduce-scatter.4
where the time goes:
time: 746 us; the launch traced here: 743 us
  waiting for transfers between devices  542 us (73%)
  local copies, waits for them, and re-layouts  83.3 us (11%)
  other arithmetic  61.4 us (8%)
  matrix products  32 us (4%)
  between operations  13.8 us (2%)
  blocking collectives  10.2 us (1%)
    reduce_scatter x1, waiting for transfers between devices, body(): lax.psum_scatter(term, 'row', scatter_dimension=0, tiled=True)  339 us
    all_gather x1, waiting for transfers between devices, body(): gathered = lax.all_gather(features, 'row', axis=0, tiled=True)  127 us
    psum x1, waiting for transfers between devices, body(): lax.psum(local_grad, ('grp', 'row')) * (1.0 / math.sqrt(verts))  58.5 us
    gather x8, local copies, waits for them, and re-layouts, aggregate(): picked = panel_blocks[columns]  51.1 us
    scatter-add x8, other arithmetic, spread(): return (carry.at[columns].add(contrib), None)  37 us
    reduce_scatter x1, waiting for transfers between devices, body(): lax.psum_scatter(partial_value, 'grp', scatter_dimension=0, tiled=True)  17.2 us
    dot_general x8, matrix products, aggregate(): jnp.einsum('kij,kjf->if', masked, picked, preferred_element_type=jnp.floa...  16.4 us
  transfers between devices with their start and end apart: 4, of which 4 were waited for; matrix products, arithmetic and copies ran while one was open for 11% of the time, Pallas kernels for 0%

commit v1 on v0

v1 whole, which is shorter than its diff:
```python
import functools
import math

import jax
import jax.numpy as jnp
from jax import lax
from jax.experimental import pallas as pl
from jax.experimental.pallas import tpu as pltpu
from jax.sharding import PartitionSpec as P

VMEM_LIMIT = 60 * 1024 * 1024


def silu_slope(pre):
    sigma = jax.nn.sigmoid(pre)
    return sigma * (1.0 + pre * (1.0 - sigma))


def aggregate_kernel(cols_ref, count_ref, vals_hbm, panel_hbm, out_ref, vals, panel, sems):
    row_blocks, slot_total, block, _ = vals.shape
    col_blocks = panel.shape[0] // block
    load_vals = pltpu.make_async_copy(vals_hbm, vals, sems.at[0])
    load_panel = pltpu.make_async_copy(panel_hbm, panel, sems.at[1])
    load_vals.start()
    load_panel.start()
    load_vals.wait()
    load_panel.wait()
    for t in range(row_blocks):
        live = jnp.clip(count_ref[t], 0, slot_total)

        def body(k, acc):
            col = jnp.clip(cols_ref[t, k], 0, col_blocks - 1)
            start = pl.multiple_of(col * block, block)
            return acc + jnp.dot(
                vals[t, k], panel[pl.ds(start, block), :], preferred_element_type=jnp.float32
            )

        out_ref[t] = lax.fori_loop(0, live, body, jnp.zeros(out_ref.shape[1:], jnp.float32))


def spread_kernel(cols_ref, count_ref, vals_hbm, grad_ref, out_hbm, vals, total, sems):
    row_blocks, slot_total, block, _ = vals.shape
    col_blocks = total.shape[0]
    load_vals = pltpu.make_async_copy(vals_hbm, vals, sems.at[0])
    load_vals.start()

    def clear(c, carry):
        total[c] = jnp.zeros(total.shape[1:], total.dtype)
        return carry

    lax.fori_loop(0, col_blocks, clear, 0)
    load_vals.wait()
    for t in range(row_blocks):
        live = jnp.clip(count_ref[t], 0, slot_total)
        grad = grad_ref[t]

        def body(k, carry):
            col = jnp.clip(cols_ref[t, k], 0, col_blocks - 1)
            contrib = lax.dot_general(
                vals[t, k], grad, (((0,), (0,)), ((), ())), preferred_element_type=jnp.float32
            )
            total[col] += contrib
            return carry

        lax.fori_loop(0, live, body, 0)
    store = pltpu.make_async_copy(total, out_hbm, sems.at[1])
    store.start()
    store.wait()


def aggregate(cols, count, vals, panel):
    row_blocks, slot_total, block, _ = vals.shape
    width = panel.shape[1]
    return pl.pallas_call(
        aggregate_kernel,
        out_shape=jax.ShapeDtypeStruct((row_blocks, block, width), jnp.float32),
        in_specs=[
            pl.BlockSpec(memory_space=pltpu.SMEM),
            pl.BlockSpec(memory_space=pltpu.SMEM),
            pl.BlockSpec(memory_space=pl.ANY),
            pl.BlockSpec(memory_space=pl.ANY),
        ],
        out_specs=pl.BlockSpec(memory_space=pltpu.VMEM),
        scratch_shapes=[
            pltpu.VMEM(vals.shape, vals.dtype),
            pltpu.VMEM(panel.shape, panel.dtype),
            pltpu.SemaphoreType.DMA((2,)),
        ],
        compiler_params=pltpu.CompilerParams(vmem_limit_bytes=VMEM_LIMIT),
        cost_estimate=pl.CostEstimate(
            flops=2 * row_blocks * slot_total * block * block * width,
            bytes_accessed=vals.size * 2 + panel.size * 2 + row_blocks * block * width * 4,
            transcendentals=0,
        ),
    )(cols, count, vals, panel)


def spread(cols, count, vals, grad, col_blocks):
    row_blocks, slot_total, block, _ = vals.shape
    width = grad.shape[-1]
    return pl.pallas_call(
        spread_kernel,
        out_shape=jax.ShapeDtypeStruct((col_blocks, block, width), jnp.float32),
        in_specs=[
            pl.BlockSpec(memory_space=pltpu.SMEM),
            pl.BlockSpec(memory_space=pltpu.SMEM),
            pl.BlockSpec(memory_space=pl.ANY),
            pl.BlockSpec(memory_space=pltpu.VMEM),
        ],
        out_specs=pl.BlockSpec(memory_space=pl.ANY),
        scratch_shapes=[
            pltpu.VMEM(vals.shape, vals.dtype),
            pltpu.VMEM((col_blocks, block, width), jnp.float32),
            pltpu.SemaphoreType.DMA((2,)),
        ],
        compiler_params=pltpu.CompilerParams(vmem_limit_bytes=VMEM_LIMIT),
        cost_estimate=pl.CostEstimate(
            flops=2 * row_blocks * slot_total * block * block * width,
            bytes_accessed=vals.size * 2 + grad.size * 2 + col_blocks * block * width * 4,
            transcendentals=0,
        ),
    )(cols, count, vals, grad)


def body(features, weight, block_vals, block_cols, block_count, cotangent):
    rows_dev, width = features.shape
    block = block_vals.shape[-1]
    groups = lax.axis_size("grp")
    members = lax.axis_size("row")
    verts = rows_dev * groups * members
    gathered = lax.all_gather(features, "row", axis=0, tiled=True)
    col_blocks = gathered.shape[0] // block
    cols = block_cols[0]
    count = block_count[0]
    vals = block_vals[0]

    partial_value = aggregate(cols, count, vals, gathered).reshape(-1, width)
    summed = lax.psum_scatter(partial_value, "grp", scatter_dimension=0, tiled=True)
    aggregated = summed.astype(jnp.bfloat16)
    pre = jnp.dot(aggregated, weight, preferred_element_type=jnp.float32)
    activated = jax.nn.silu(pre).astype(jnp.bfloat16)
    pre_grad = (cotangent.astype(jnp.float32) * silu_slope(pre)).astype(jnp.bfloat16)
    local_grad = jnp.dot(aggregated.T, pre_grad, preferred_element_type=jnp.float32)
    own_grad = jnp.dot(pre_grad, weight.T, preferred_element_type=jnp.float32).astype(jnp.bfloat16)
    rows_grad = lax.all_gather(own_grad, "grp", axis=0, tiled=True)
    weight_grad = lax.psum(local_grad, ("grp", "row")) * (1.0 / math.sqrt(verts))
    by_block = rows_grad.reshape(-1, block, width)

    term = spread(cols, count, vals, by_block, col_blocks).reshape(-1, width)
    input_grad = lax.psum_scatter(term, "row", scatter_dimension=0, tiled=True).astype(jnp.bfloat16)
    return (activated, weight_grad, input_grad)


def solution(mesh):
    placed = (
        P(("grp", "row"), None),
        P(),
        P("grp", "row", None, None, None),
        P("grp", "row", None),
        P("grp", "row"),
        P(("grp", "row"), None),
    )
    return jax.shard_map(
        body,
        mesh=mesh,
        in_specs=placed,
        out_specs=(P(("grp", "row"), None), P(), P(("grp", "row"), None)),
        check_vma=False,
    )
```

time: 746 us -> 683 us (0.916)
  local copies, waits for them, and re-layouts: 83.3 us -> 0.01 us
  waiting for transfers between devices: 542 us -> 618 us
  other arithmetic: 61.4 us -> 3.44 us
  Pallas kernels: 0 us -> 32.6 us
  matrix products: 32 us -> 4.42 us
    psum x1, waiting for transfers between devices: 58.5 us -> 113 us  [body(): lax.psum(local_grad, ('grp', 'row')) * (1.0 / math.sqrt(verts))]
    gather x8 -> x0, local copies, waits for them, and re-layouts: 51.1 us -> none  [aggregate(): picked = panel_blocks[columns]]
    scatter-add x8 -> x0, other arithmetic: 37 us -> none  [spread(): return (carry.at[columns].add(contrib), None)]
    pallas_call x0 -> x2, Pallas kernels: none -> 32.6 us  [the longest x1 19.7 us: spread(): pl.pallas_call(spread_kernel, out_shape=jax.ShapeDtypeStruct((col_blocks,...]
    dot_general x16 -> x0, matrix products: 28.5 us -> none  [the longest x8 16.4 us: aggregate(): jnp.einsum('kij,kjf->if', masked, picked, preferred_element_type=jnp.floa...]
    reduce_scatter x1, waiting for transfers between devices: 17.2 us -> 38.5 us  [body(): lax.psum_scatter(partial_value, 'grp', scatter_dimension=0, tiled=True)]
    dynamic_slice x16 -> x0, local copies, waits for them, and re-layouts: 14.5 us -> none  [body(): lax.map(aggregate, (block_vals[0], block_cols[0], block_count[0]))]
    broadcast_in_dim x1 -> x0, local copies, waits for them, and re-layouts: 11.2 us -> none  [body(): jnp.zeros((col_blocks, block, width), jnp.float32)]
  transfers between devices with their start and end apart: 4 -> 4, of which waited for: 4 -> 4; matrix products, arithmetic and copies ran while one was open for 11% -> 0% of each run, Pallas kernels for 0% -> 3%
where the time goes in v1:
time: 683 us
  waiting for transfers between devices  618 us (90%)
  Pallas kernels  32.6 us (5%)
  between operations  13.8 us (2%)
  blocking collectives  10.3 us (2%)
    reduce_scatter x1, waiting for transfers between devices, body(): lax.psum_scatter(term, 'row', scatter_dimension=0, tiled=True)  339 us
    all_gather x1, waiting for transfers between devices, body(): gathered = lax.all_gather(features, 'row', axis=0, tiled=True)  127 us
    psum x1, waiting for transfers between devices, body(): lax.psum(local_grad, ('grp', 'row')) * (1.0 / math.sqrt(verts))  113 us
    reduce_scatter x1, waiting for transfers between devices, body(): lax.psum_scatter(partial_value, 'grp', scatter_dimension=0, tiled=True)  38.5 us
    pallas_call x1, Pallas kernels, spread(): pl.pallas_call(spread_kernel, out_shape=jax.ShapeDtypeStruct((col_blocks,...  19.7 us
  transfers between devices with their start and end apart: 4, of which 4 were waited for; matrix products, arithmetic and copies ran while one was open for 0% of the time, Pallas kernels for 3%

profile of v1, /device:TPU:0, one launch (start us, length us, event | category | flops | bytes accessed | tf_op | source)
XLA Modules:
  0.0 683.1 jit_solution(8598226333330042072)
XLA Ops:
  7.2 0.0 copy-start
  7.2 0.0 copy-start.1
  7.2 0.0 all-gather.2.cloned.1.call-start
  7.2 0.7 all-gather.2.cloned.1.call-update
  7.9 0.0 reduce-scatter.3.cloned.1.call-start
  8.0 127.3 %all-gather.2.cloned.1.call-done.panel_hbm = bf16[32768,256]{1,0:T(8,128)(2,1)} async-done(((bf16[512,256]{1,0:T(8,128)(2,1)}), bf16[32768,256]{1,0:T(8,128)(2,1)}) %all-gather.2.cloned.1.call-update) | async-done | bytes 16777232 | tf_op jit(solution)/shard_map/all_gather | solution.py:131
  135.3 12.8 %shard_map.85 = f32[8,128,256]{2,1,0:T(8,128)} custom-call(s32[8,16]{1,0:T(8,128)} %bitcast.15, s32[8]{0:T(128)} %bitcast.17, bf16[8,16,128,128]{3,2,1,0:T(8,128)(2,1)} %bitcast.11, bf16[32768,256]{1,0:T(8,128)(2,1)} %all-gather.2.cloned.1.call-done.panel_hbm), custom_call_target="tpu_custom_call" | custom-call | flops 1073741824 | bytes 22020096 | tf_op jit(solution)/shard_map/pallas_call | solution.py:74
  148.1 0.0 reduce-scatter.3.cloned.1.call-update
  148.2 0.0 all-reduce.2.cloned.1.call-start
  148.2 38.5 %reduce-scatter.3.cloned.1.call-done = f32[512,256]{1,0:T(8,128)} async-done(((f32[1024,256]{1,0:T(8,128)}), f32[512,256]{1,0:T(8,128)}) %reduce-scatter.3.cloned.1.call-update) | async-done | bytes 524304 | tf_op jit(solution)/shard_map/reduce_scatter | solution.py:138
  186.7 0.0 copy-done
  186.8 0.0 copy-done.1
  186.8 2.1 multiply_convert_fusion
  188.9 0.3 convolution_convert_fusion
  189.2 2.0 fusion
  191.2 0.0 all-reduce.2.cloned.1.call-update
  191.2 0.0 reduce-scatter.5.cloned.1.call-start
  191.3 10.3 %all_gather.7 = bf16[1024,256]{1,0:T(8,128)(2,1)} all-gather(bf16[512,256]{1,0:T(8,128)(2,1)S(1)} %convolution_convert_fusion), channel_id=1, replica_groups=mesh['grp'=2,'row'=64] {'grp'}, dimensions={0}, use_global_device_ids=true | all-gather | bytes 786432 | tf_op jit(solution)/shard_map/all_gather | solution.py:145
  201.6 19.7 %shard_map.86 = f32[256,128,256]{2,1,0:T(8,128)} custom-call(s32[8,16]{1,0:T(8,128)} %bitcast.16, s32[8]{0:T(128)} %bitcast.18, bf16[8,16,128,128]{3,2,1,0:T(8,128)(2,1)} %bitcast.12, bf16[8,128,256]{2,1,0:T(8,128)(2,1)} %bitcast.14), custom_call_target="tpu_custom_call" | custom-call | flops 1073741824 | bytes 38273024 | tf_op jit(solution)/shard_map/pallas_call | solution.py:101
  221.3 0.0 reduce-scatter.5.cloned.1.call-update
  221.4 113.2 %all-reduce.2.cloned.1.call-done = f32[256,256]{1,0:T(8,128)} async-done(((f32[256,256]{1,0:T(8,128)}), f32[256,256]{1,0:T(8,128)}) %all-reduce.2.cloned.1.call-update) | async-done | bytes 262160 | tf_op jit(solution)/shard_map/psum | solution.py:146
  334.5 1.7 broadcast_multiply_fusion
  336.2 338.6 %reduce-scatter.5.cloned.1.call-done = f32[512,256]{1,0:T(8,128)} async-done(((f32[32768,256]{1,0:T(8,128)}), f32[512,256]{1,0:T(8,128)}) %reduce-scatter.5.cloned.1.call-update) | async-done | bytes 524304 | tf_op jit(solution)/shard_map/reduce_scatter | solution.py:150
  674.8 1.8 convert_element_type.23
Async XLA Ops:
  7.2 179.6 %copy-start = (bf16[256,256]{1,0:T(8,128)(2,1)S(1)}, bf16[256,256]{1,0:T(8,128)(2,1)}, u32[]{:S(2)}) copy-start(bf16[256,256]{1,0:T(8,128)(2,1)} %param.7) | copy-start | bytes 393220
  7.2 179.6 %copy-start.1 = (bf16[512,256]{1,0:T(8,128)(2,1)S(1)}, bf16[512,256]{1,0:T(8,128)(2,1)}, u32[]{:S(2)}) copy-start(bf16[512,256]{1,0:T(8,128)(2,1)} %param.11) | copy-start | bytes 786436
  7.2 128.1 %all-gather.2.cloned.1.call-start = ((), (), s32[]{:S(2)}) async-start(), calls=%async_computation.2 | async-start | bytes 17039360 | tf_op jit(solution)/shard_map/all_gather | solution.py:131
  7.9 178.8 %reduce-scatter.3.cloned.1.call-start = ((), (), s32[]{:S(2)}) async-start(), calls=%async_computation.3 | async-start | bytes 1572864 | tf_op jit(solution)/shard_map/reduce_scatter | solution.py:138
  148.2 186.4 %all-reduce.2.cloned.1.call-start = ((), (), s32[]{:S(2)}) async-start(), calls=%async_computation.4 | async-start | bytes 524288 | tf_op jit(solution)/shard_map/psum | solution.py:146
  191.2 483.6 %reduce-scatter.5.cloned.1.call-start = ((), (), s32[]{:S(2)}) async-start(), calls=%async_computation.5 | async-start | bytes 34078720 | tf_op jit(solution)/shard_map/reduce_scatter | solution.py:150
Sparse Core Ops, SparseCore 0:
  9.7 125.4 all-gather.1
  148.3 38.4 reduce-scatter.2
  192.8 141.6 all-reduce.1
  336.9 337.8 reduce-scatter.4

commit v2 on v1

--- a/solution.py
+++ b/solution.py
@@ -38,8 +38,9 @@
         out_ref[t] = lax.fori_loop(0, live, body, jnp.zeros(out_ref.shape[1:], jnp.float32))
 
 
-def spread_kernel(cols_ref, count_ref, vals_hbm, grad_ref, out_hbm, vals, total, sems):
+def spread_kernel(side_ref, cols_ref, count_ref, vals_hbm, grad_ref, out_hbm, vals, total, sems):
     row_blocks, slot_total, block, _ = vals.shape
+    per_panel = grad_ref.shape[1]
     col_blocks = total.shape[0]
     load_vals = pltpu.make_async_copy(vals_hbm, vals, sems.at[0])
     load_vals.start()
@@ -52,7 +53,8 @@
     load_vals.wait()
     for t in range(row_blocks):
         live = jnp.clip(count_ref[t], 0, slot_total)
-        grad = grad_ref[t]
+        panel, within = divmod(t, per_panel)
+        grad = grad_ref[jnp.where(side_ref[0] == panel, 0, 1), within]
 
         def body(k, carry):
             col = jnp.clip(cols_ref[t, k], 0, col_blocks - 1)
@@ -95,13 +97,14 @@
     )(cols, count, vals, panel)
 
 
-def spread(cols, count, vals, grad, col_blocks):
+def spread(side, cols, count, vals, grad, col_blocks):
     row_blocks, slot_total, block, _ = vals.shape
     width = grad.shape[-1]
     return pl.pallas_call(
         spread_kernel,
         out_shape=jax.ShapeDtypeStruct((col_blocks, block, width), jnp.float32),
         in_specs=[
+            pl.BlockSpec(memory_space=pltpu.SMEM),
             pl.BlockSpec(memory_space=pltpu.SMEM),
             pl.BlockSpec(memory_space=pltpu.SMEM),
             pl.BlockSpec(memory_space=pl.ANY),
@@ -119,7 +122,21 @@
             bytes_accessed=vals.size * 2 + grad.size * 2 + col_blocks * block * width * 4,
             transcendentals=0,
         ),
-    )(cols, count, vals, grad)
+    )(side, cols, count, vals, grad)
+
+
+def swap(value, axis):
+    size = lax.axis_size(axis)
+    return lax.ppermute(value, axis, [(i, i ^ 1) for i in range(size)])
+
+
+def all_sum(value, axis):
+    size = lax.axis_size(axis)
+    step = 1
+    while step < size:
+        value = value + lax.ppermute(value, axis, [(i, i ^ step) for i in range(size)])
+        step *= 2
+    return value
 
 
 def body(features, weight, block_vals, block_cols, block_count, cotangent):
@@ -128,6 +145,7 @@
     groups = lax.axis_size("grp")
     members = lax.axis_size("row")
     verts = rows_dev * groups * members
+    side = lax.axis_index("grp")
     gathered = lax.all_gather(features, "row", axis=0, tiled=True)
     col_blocks = gathered.shape[0] // block
     cols = block_cols[0]
@@ -135,18 +153,19 @@
     vals = block_vals[0]
 
     partial_value = aggregate(cols, count, vals, gathered).reshape(-1, width)
-    summed = lax.psum_scatter(partial_value, "grp", scatter_dimension=0, tiled=True)
+    mine = lax.dynamic_slice_in_dim(partial_value, side * rows_dev, rows_dev)
+    theirs = lax.dynamic_slice_in_dim(partial_value, (1 - side) * rows_dev, rows_dev)
+    summed = mine + swap(theirs, "grp")
     aggregated = summed.astype(jnp.bfloat16)
     pre = jnp.dot(aggregated, weight, preferred_element_type=jnp.float32)
     activated = jax.nn.silu(pre).astype(jnp.bfloat16)
     pre_grad = (cotangent.astype(jnp.float32) * silu_slope(pre)).astype(jnp.bfloat16)
     local_grad = jnp.dot(aggregated.T, pre_grad, preferred_element_type=jnp.float32)
     own_grad = jnp.dot(pre_grad, weight.T, preferred_element_type=jnp.float32).astype(jnp.bfloat16)
-    rows_grad = lax.all_gather(own_grad, "grp", axis=0, tiled=True)
-    weight_grad = lax.psum(local_grad, ("grp", "row")) * (1.0 / math.sqrt(verts))
-    by_block = rows_grad.reshape(-1, block, width)
+    both_grad = jnp.stack([own_grad, swap(own_grad, "grp")]).reshape(2, -1, block, width)
+    weight_grad = all_sum(all_sum(local_grad, "row"), "grp") * (1.0 / math.sqrt(verts))
 
-    term = spread(cols, count, vals, by_block, col_blocks).reshape(-1, width)
+    term = spread(side.reshape(1), cols, count, vals, both_grad, col_blocks).reshape(-1, width)
     input_grad = lax.psum_scatter(term, "row", scatter_dimension=0, tiled=True).astype(jnp.bfloat16)
     return (activated, weight_grad, input_grad)
 

time: 683 us -> 584 us (0.86)
  waiting for transfers between devices: 618 us -> 476 us
  starting transfers between devices: 0.16 us -> 52 us
  blocking collectives: 10.3 us -> 0 us
    psum x1 -> x0, waiting for transfers between devices: 113 us -> none  [body(): lax.psum(local_grad, ('grp', 'row')) * (1.0 / math.sqrt(verts))]
    ppermute x0 -> x9, waiting for transfers between devices: none -> 91.8 us  [the longest x7 76.6 us: all_sum(): lax.ppermute(value, axis, [(i, i ^ step) for i in range(size)])]
    reduce_scatter x1, waiting for transfers between devices: 339 us -> 256 us  [body(): lax.psum_scatter(term, 'row', scatter_dimension=0, tiled=True)]
    ppermute x0 -> x9, starting transfers between devices: none -> 52 us  [the longest x7 46.5 us: all_sum(): lax.ppermute(value, axis, [(i, i ^ step) for i in range(size)])]
    reduce_scatter x1 -> x0, waiting for transfers between devices: 38.5 us -> none  [body(): lax.psum_scatter(partial_value, 'grp', scatter_dimension=0, tiled=True)]
    all_gather x1 -> x0, blocking collectives: 10.3 us -> none  [body(): rows_grad = lax.all_gather(own_grad, 'grp', axis=0, tiled=True)]
  transfers between devices with their start and end apart: 4 -> 11, of which waited for: 4 -> 11; matrix products, arithmetic and copies ran while one was open for 0% -> 0% of each run, Pallas kernels for 3% -> 0%
where the time goes in v2:
time: 584 us; the launch traced here: 582 us
  waiting for transfers between devices  476 us (82%)
  starting transfers between devices  52 us (9%)
  Pallas kernels  32.1 us (5%)
  between operations  14.2 us (2%)
    reduce_scatter x1, waiting for transfers between devices, body(): lax.psum_scatter(term, 'row', scatter_dimension=0, tiled=True)  256 us
    all_gather x1, waiting for transfers between devices, body(): gathered = lax.all_gather(features, 'row', axis=0, tiled=True)  127 us
    ppermute x7, waiting for transfers between devices, all_sum(): lax.ppermute(value, axis, [(i, i ^ step) for i in range(size)])  76.6 us
    ppermute x7, starting transfers between devices, all_sum(): lax.ppermute(value, axis, [(i, i ^ step) for i in range(size)])  46.5 us
    pallas_call x1, Pallas kernels, spread(): pl.pallas_call(spread_kernel, out_shape=jax.ShapeDtypeStruct((col_blocks,...  19.4 us
    ppermute x2, waiting for transfers between devices, swap(): return lax.ppermute(value, axis, [(i, i ^ 1) for i in range(size)])  15.1 us
    pallas_call x1, Pallas kernels, aggregate(): pl.pallas_call(aggregate_kernel, out_shape=jax.ShapeDtypeStruct((row_bloc...  12.7 us
  transfers between devices with their start and end apart: 11, of which 11 were waited for; matrix products, arithmetic and copies ran while one was open for 0% of the time, Pallas kernels for 0%

profile of v2, /device:TPU:0, one launch (start us, length us, event | category | flops | bytes accessed | tf_op | source)
XLA Modules:
  0.0 581.6 jit_solution(6232989626940688097)
XLA Ops:
  7.2 0.0 copy-start
  7.2 0.0 copy-start.1
  7.2 0.0 all-gather.2.cloned.1.call-start
  7.2 0.7 all-gather.2.cloned.1.call-update
  7.9 0.0 reduce-scatter.2.cloned.1.call-start
  8.0 127.3 %all-gather.2.cloned.1.call-done.panel_hbm = bf16[32768,256]{1,0:T(8,128)(2,1)} async-done(((bf16[512,256]{1,0:T(8,128)(2,1)}), bf16[32768,256]{1,0:T(8,128)(2,1)}) %all-gather.2.cloned.1.call-update) | async-done | bytes 16777232 | tf_op jit(solution)/shard_map/all_gather | solution.py:149
  135.3 12.7 %shard_map.85 = f32[8,128,256]{2,1,0:T(8,128)} custom-call(s32[8,16]{1,0:T(8,128)} %bitcast.21, s32[8]{0:T(128)} %bitcast.23, bf16[8,16,128,128]{3,2,1,0:T(8,128)(2,1)} %bitcast.15, bf16[32768,256]{1,0:T(8,128)(2,1)} %all-gather.2.cloned.1.call-done.panel_hbm), custom_call_target="tpu_custom_call" | custom-call | flops 1073741824 | bytes 22020096 | tf_op jit(solution)/shard_map/pallas_call | solution.py:76
  148.0 1.1 constant_dynamic-slice_fusion
  149.1 2.8 collective-permute-start
  151.8 8.0 %collective-permute-done = f32[512,256]{1,0:T(8,128)S(1)} collective-permute-done((f32[512,256]{1,0:T(8,128)S(1)}, f32[512,256]{1,0:T(8,128)S(1)}, u32[]{:S(2)}, u32[]{:S(2)}) %collective-permute-start) | collective-permute-done | bytes 524320 | tf_op jit(solution)/shard_map/ppermute | solution.py:130
  159.8 1.1 add_convert_fusion
  160.9 0.0 copy-done
  160.9 0.0 copy-done.1
  160.9 1.1 multiply_convert_fusion
  162.0 0.3 convolution_convert_fusion
  162.3 2.8 collective-permute-start.8
  165.1 7.1 %collective-permute-done.8 = bf16[512,256]{1,0:T(8,128)(2,1)S(1)} collective-permute-done((bf16[512,256]{1,0:T(8,128)(2,1)S(1)}, bf16[512,256]{1,0:T(8,128)(2,1)S(1)}, u32[]{:S(2)}, u32[]{:S(2)}) %collective-permute-start.8) | collective-permute-done | bytes 262176 | tf_op jit(solution)/shard_map/ppermute | solution.py:130
  172.2 0.8 pad_maximum_fusion.grad_ref
  173.0 19.4 %shard_map.86 = f32[256,128,256]{2,1,0:T(8,128)} custom-call(s32[1]{0:T(128)} %bitcast.4.side_ref, s32[8,16]{1,0:T(8,128)} %bitcast.22, s32[8]{0:T(128)} %bitcast.24, bf16[8,16,128,128]{3,2,1,0:T(8,128)(2,1)} %bitcast.16, bf16[2,4,128,256]{3,2,1,0:T(8,128)(2,1)} %pad_maximum_fusion.grad_ref), custom_call_target="tpu_custom_call" | custom-call | flops 1073741824 | bytes 38273024 | tf_op jit(solution)/shard_map/pallas_call | solution.py:103
  192.5 0.0 reduce-scatter.2.cloned.1.call-update
  192.5 0.3 fusion
  192.8 31.6 %collective-permute-start.1 = (f32[256,256]{1,0:T(8,128)S(1)}, f32[256,256]{1,0:T(8,128)S(1)}, u32[]{:S(2)}, u32[]{:S(2)}) collective-permute-start(f32[256,256]{1,0:T(8,128)S(1)} %fusion), channel_id=1, source_target_pairs={{0,1},{1,0},{2,3},{3,2},{4,5},{5,4},{6,7},{7,6},{8,9},{9,8},{10,11... | collective-permute-start | bytes 786440 | tf_op jit(solution)/shard_map/ppermute | solution.py:137
  224.4 1.2 collective-permute-done.1
  225.6 7.0 %collective-permute-start.2 = (f32[256,256]{1,0:T(8,128)S(1)}, f32[256,256]{1,0:T(8,128)S(1)}, u32[]{:S(2)}, u32[]{:S(2)}) collective-permute-start(f32[256,256]{1,0:T(8,128)S(1)} %add.45), channel_id=1, source_target_pairs={{0,2},{1,3},{2,0},{3,1},{4,6},{5,7},{6,4},{7,5},{8,10},{9,11},{10,... | collective-permute-start | bytes 786440 | tf_op jit(solution)/shard_map/ppermute | solution.py:137
  232.6 6.8 %collective-permute-done.2 = f32[256,256]{1,0:T(8,128)S(1)} collective-permute-done((f32[256,256]{1,0:T(8,128)S(1)}, f32[256,256]{1,0:T(8,128)S(1)}, u32[]{:S(2)}, u32[]{:S(2)}) %collective-permute-start.2) | collective-permute-done | bytes 262176 | tf_op jit(solution)/shard_map/ppermute | solution.py:137
  239.5 0.1 collective-permute-start.3
  239.5 12.9 %collective-permute-done.3 = f32[256,256]{1,0:T(8,128)S(1)} collective-permute-done((f32[256,256]{1,0:T(8,128)S(1)}, f32[256,256]{1,0:T(8,128)S(1)}, u32[]{:S(2)}, u32[]{:S(2)}) %collective-permute-start.3) | collective-permute-done | bytes 262176 | tf_op jit(solution)/shard_map/ppermute | solution.py:137
  252.4 0.1 collective-permute-start.4
  252.5 18.5 %collective-permute-done.4 = f32[256,256]{1,0:T(8,128)S(1)} collective-permute-done((f32[256,256]{1,0:T(8,128)S(1)}, f32[256,256]{1,0:T(8,128)S(1)}, u32[]{:S(2)}, u32[]{:S(2)}) %collective-permute-start.4) | collective-permute-done | bytes 262176 | tf_op jit(solution)/shard_map/ppermute | solution.py:137
  271.1 0.1 collective-permute-start.5
  271.1 10.1 %collective-permute-done.5 = f32[256,256]{1,0:T(8,128)S(1)} collective-permute-done((f32[256,256]{1,0:T(8,128)S(1)}, f32[256,256]{1,0:T(8,128)S(1)}, u32[]{:S(2)}, u32[]{:S(2)}) %collective-permute-start.5) | collective-permute-done | bytes 262176 | tf_op jit(solution)/shard_map/ppermute | solution.py:137
  281.3 1.8 collective-permute-start.6
  283.0 15.4 %collective-permute-done.6 = f32[256,256]{1,0:T(8,128)S(1)} collective-permute-done((f32[256,256]{1,0:T(8,128)S(1)}, f32[256,256]{1,0:T(8,128)S(1)}, u32[]{:S(2)}, u32[]{:S(2)}) %collective-permute-start.6) | collective-permute-done | bytes 262176 | tf_op jit(solution)/shard_map/ppermute | solution.py:137
  298.4 5.8 %collective-permute-start.7 = (f32[256,256]{1,0:T(8,128)S(1)}, f32[256,256]{1,0:T(8,128)S(1)}, u32[]{:S(2)}, u32[]{:S(2)}) collective-permute-start(f32[256,256]{1,0:T(8,128)S(1)} %add.50), channel_id=1, source_target_pairs={{0,64},{64,0},{1,65},{65,1},{2,66},{66,2},{3,67},{67,3},{4,68},{68... | collective-permute-start | bytes 786440 | tf_op jit(solution)/shard_map/ppermute | solution.py:137
  304.3 11.8 %collective-permute-done.7 = f32[256,256]{1,0:T(8,128)S(1)} collective-permute-done((f32[256,256]{1,0:T(8,128)S(1)}, f32[256,256]{1,0:T(8,128)S(1)}, u32[]{:S(2)}, u32[]{:S(2)}) %collective-permute-start.7) | collective-permute-done | bytes 262176 | tf_op jit(solution)/shard_map/ppermute | solution.py:137
  316.1 0.7 add_multiply_fusion
  316.8 256.1 %reduce-scatter.2.cloned.1.call-done = f32[512,256]{1,0:T(8,128)} async-done(((f32[32768,256]{1,0:T(8,128)}), f32[512,256]{1,0:T(8,128)}) %reduce-scatter.2.cloned.1.call-update) | async-done | bytes 524304 | tf_op jit(solution)/shard_map/reduce_scatter | solution.py:169
  573.0 1.8 convert_element_type.23
  (6 shorter events, 0.2 us)
Async XLA Ops:
  7.2 153.8 %copy-start = (bf16[256,256]{1,0:T(8,128)(2,1)S(1)}, bf16[256,256]{1,0:T(8,128)(2,1)}, u32[]{:S(2)}) copy-start(bf16[256,256]{1,0:T(8,128)(2,1)} %param.7) | copy-start | bytes 393220
  7.2 153.8 %copy-start.1 = (bf16[512,256]{1,0:T(8,128)(2,1)S(1)}, bf16[512,256]{1,0:T(8,128)(2,1)}, u32[]{:S(2)}) copy-start(bf16[512,256]{1,0:T(8,128)(2,1)} %param.11) | copy-start | bytes 786436
  7.2 128.1 %all-gather.2.cloned.1.call-start = ((), (), s32[]{:S(2)}) async-start(), calls=%async_computation.1 | async-start | bytes 17039360 | tf_op jit(solution)/shard_map/all_gather | solution.py:149
  7.9 565.0 %reduce-scatter.2.cloned.1.call-start = ((), (), s32[]{:S(2)}) async-start(), calls=%async_computation.2 | async-start | bytes 34078720 | tf_op jit(solution)/shard_map/reduce_scatter | solution.py:169
  149.1 10.8 %collective-permute-start = (f32[512,256]{1,0:T(8,128)S(1)}, f32[512,256]{1,0:T(8,128)S(1)}, u32[]{:S(2)}, u32[]{:S(2)}) collective-permute-start(f32[512,256]{1,0:T(8,128)S(1)} %constant_dynamic-slice_fusion), channel_id=1, source_target_pairs={{0,64},{64,0},{1,65},{65,1},{2,66},{66,2},{3,67},{67,3},{4,68},{68... | collective-permute-start | bytes 1572872 | tf_op jit(solution)/shard_map/ppermute | solution.py:130
  162.3 9.9 %collective-permute-start.8 = (bf16[512,256]{1,0:T(8,128)(2,1)S(1)}, bf16[512,256]{1,0:T(8,128)(2,1)S(1)}, u32[]{:S(2)}, u32[]{:S(2)}) collective-permute-start(bf16[512,256]{1,0:T(8,128)(2,1)S(1)} %convolution_convert_fusion), channel_id=1, source_target_pairs={{0,64},{64,0},{1,65},{65,1},{2,66},{66,2},{3,67},{67,3},{4,68},{68... | collective-permute-start | bytes 786440 | tf_op jit(solution)/shard_map/ppermute | solution.py:130
  192.8 32.8 %collective-permute-start.1 = (f32[256,256]{1,0:T(8,128)S(1)}, f32[256,256]{1,0:T(8,128)S(1)}, u32[]{:S(2)}, u32[]{:S(2)}) collective-permute-start(f32[256,256]{1,0:T(8,128)S(1)} %fusion), channel_id=1, source_target_pairs={{0,1},{1,0},{2,3},{3,2},{4,5},{5,4},{6,7},{7,6},{8,9},{9,8},{10,11... | collective-permute-start | bytes 786440 | tf_op jit(solution)/shard_map/ppermute | solution.py:137
  225.6 13.8 %collective-permute-start.2 = (f32[256,256]{1,0:T(8,128)S(1)}, f32[256,256]{1,0:T(8,128)S(1)}, u32[]{:S(2)}, u32[]{:S(2)}) collective-permute-start(f32[256,256]{1,0:T(8,128)S(1)} %add.45), channel_id=1, source_target_pairs={{0,2},{1,3},{2,0},{3,1},{4,6},{5,7},{6,4},{7,5},{8,10},{9,11},{10,... | collective-permute-start | bytes 786440 | tf_op jit(solution)/shard_map/ppermute | solution.py:137
  239.5 13.0 %collective-permute-start.3 = (f32[256,256]{1,0:T(8,128)S(1)}, f32[256,256]{1,0:T(8,128)S(1)}, u32[]{:S(2)}, u32[]{:S(2)}) collective-permute-start(f32[256,256]{1,0:T(8,128)S(1)} %add.46), channel_id=1, source_target_pairs={{0,4},{1,5},{2,6},{3,7},{4,0},{5,1},{6,2},{7,3},{8,12},{9,13},{10,... | collective-permute-start | bytes 786440 | tf_op jit(solution)/shard_map/ppermute | solution.py:137
  252.4 18.6 %collective-permute-start.4 = (f32[256,256]{1,0:T(8,128)S(1)}, f32[256,256]{1,0:T(8,128)S(1)}, u32[]{:S(2)}, u32[]{:S(2)}) collective-permute-start(f32[256,256]{1,0:T(8,128)S(1)} %add.47), channel_id=1, source_target_pairs={{0,8},{1,9},{2,10},{3,11},{4,12},{5,13},{6,14},{7,15},{8,0},{9,1},... | collective-permute-start | bytes 786440 | tf_op jit(solution)/shard_map/ppermute | solution.py:137
  271.1 10.2 %collective-permute-start.5 = (f32[256,256]{1,0:T(8,128)S(1)}, f32[256,256]{1,0:T(8,128)S(1)}, u32[]{:S(2)}, u32[]{:S(2)}) collective-permute-start(f32[256,256]{1,0:T(8,128)S(1)} %add.48), channel_id=1, source_target_pairs={{0,16},{1,17},{2,18},{3,19},{4,20},{5,21},{6,22},{7,23},{8,24},{9,... | collective-permute-start | bytes 786440 | tf_op jit(solution)/shard_map/ppermute | solution.py:137
  281.3 17.1 %collective-permute-start.6 = (f32[256,256]{1,0:T(8,128)S(1)}, f32[256,256]{1,0:T(8,128)S(1)}, u32[]{:S(2)}, u32[]{:S(2)}) collective-permute-start(f32[256,256]{1,0:T(8,128)S(1)} %add.49), channel_id=1, source_target_pairs={{0,32},{1,33},{2,34},{3,35},{4,36},{5,37},{6,38},{7,39},{8,40},{9,... | collective-permute-start | bytes 786440 | tf_op jit(solution)/shard_map/ppermute | solution.py:137
  298.4 17.7 %collective-permute-start.7 = (f32[256,256]{1,0:T(8,128)S(1)}, f32[256,256]{1,0:T(8,128)S(1)}, u32[]{:S(2)}, u32[]{:S(2)}) collective-permute-start(f32[256,256]{1,0:T(8,128)S(1)} %add.50), channel_id=1, source_target_pairs={{0,64},{64,0},{1,65},{65,1},{2,66},{66,2},{3,67},{67,3},{4,68},{68... | collective-permute-start | bytes 786440 | tf_op jit(solution)/shard_map/ppermute | solution.py:137
Sparse Core Ops, SparseCore 0:
  9.7 125.4 all-gather.1
  192.6 380.2 reduce-scatter.1

commit v3 on v2

--- a/solution.py
+++ b/solution.py
@@ -38,10 +38,24 @@
         out_ref[t] = lax.fori_loop(0, live, body, jnp.zeros(out_ref.shape[1:], jnp.float32))
 
 
+def owner_slot(col, me, per_dev):
+    owner, q = col // per_dev, col % per_dev
+    dk = (owner % 2) ^ (me % 2)
+    dx = ((owner // 2) % 4 - (me // 2) % 4 + 4) % 4
+    dy = ((owner // 8) % 2) ^ ((me // 8) % 2)
+    dz = ((owner // 16) - (me // 16) + 4) % 4
+    half, q2 = q // 2, q % 2
+    first = jnp.where(half == 0, dx, dz)
+    second = jnp.where(half == 0, dz, dx)
+    return (dk * 2 + half) * 64 + ((first * 4 + second) * 2 + dy) * 2 + q2
+
+
 def spread_kernel(side_ref, cols_ref, count_ref, vals_hbm, grad_ref, out_hbm, vals, total, sems):
     row_blocks, slot_total, block, _ = vals.shape
     per_panel = grad_ref.shape[1]
     col_blocks = total.shape[0]
+    per_dev = col_blocks // 64
+    me = side_ref[1]
     load_vals = pltpu.make_async_copy(vals_hbm, vals, sems.at[0])
     load_vals.start()
 
@@ -61,7 +75,8 @@
             contrib = lax.dot_general(
                 vals[t, k], grad, (((0,), (0,)), ((), ())), preferred_element_type=jnp.float32
             )
-            total[col] += contrib
+            slot = owner_slot(col, me, per_dev)
+            total[slot] += contrib
             return carry
 
         lax.fori_loop(0, live, body, 0)
@@ -128,6 +143,33 @@
 def swap(value, axis):
     size = lax.axis_size(axis)
     return lax.ppermute(value, axis, [(i, i ^ 1) for i in range(size)])
+
+
+def shifted(value, digit, size, shift):
+    def dest(r):
+        place = (r // digit) % size
+        return r + (((place + shift) % size) - place) * digit
+
+    return lax.ppermute(value, "row", [(r, dest(r)) for r in range(64)])
+
+
+def row_reduce_scatter(term):
+    _, block, width = term.shape
+    staged = term.reshape(2, 2, 64, block, width)
+    level = staged[0] + shifted(staged[1], 1, 2, 1)
+    first = level[0].reshape(4, 16, block, width)
+    second = level[1].reshape(4, 16, block, width)
+    first = first[0] + sum(shifted(first[s], 2, 4, s) for s in range(1, 4))
+    second = second[0] + sum(shifted(second[s], 16, 4, s) for s in range(1, 4))
+    first = first.reshape(4, 4, block, width)
+    second = second.reshape(4, 4, block, width)
+    first = first[0] + sum(shifted(first[s], 16, 4, s) for s in range(1, 4))
+    second = second[0] + sum(shifted(second[s], 2, 4, s) for s in range(1, 4))
+    first = first.reshape(2, 2, block, width)
+    second = second.reshape(2, 2, block, width)
+    first = first[0] + shifted(first[1], 8, 2, 1)
+    second = second[0] + shifted(second[1], 8, 2, 1)
+    return jnp.concatenate([first, second]).reshape(-1, width)
 
 
 def all_sum(value, axis):
@@ -165,8 +207,9 @@
     both_grad = jnp.stack([own_grad, swap(own_grad, "grp")]).reshape(2, -1, block, width)
     weight_grad = all_sum(all_sum(local_grad, "row"), "grp") * (1.0 / math.sqrt(verts))
 
-    term = spread(side.reshape(1), cols, count, vals, both_grad, col_blocks).reshape(-1, width)
-    input_grad = lax.psum_scatter(term, "row", scatter_dimension=0, tiled=True).astype(jnp.bfloat16)
+    where = jnp.stack([side, lax.axis_index("row")]).astype(jnp.int32)
+    term = spread(where, cols, count, vals, both_grad, col_blocks)
+    input_grad = row_reduce_scatter(term).astype(jnp.bfloat16)
     return (activated, weight_grad, input_grad)
 
 

time: 584 us -> 522 us (0.89)
  waiting for transfers between devices: 476 us -> 319 us
  starting transfers between devices: 52 us -> 100 us
  local copies, waits for them, and re-layouts: 1.1 us -> 30.7 us
  other arithmetic: 4.65 us -> 23.3 us
    reduce_scatter x1 -> x0, waiting for transfers between devices: 256 us -> none  [body(): lax.psum_scatter(term, 'row', scatter_dimension=0, tiled=True)]
    ppermute x0 -> x15, waiting for transfers between devices: none -> 86.6 us  [shifted(): return lax.ppermute(value, 'row', [(r, dest(r)) for r in range(64)])]
    ppermute x7, starting transfers between devices: 46.5 us -> 72.5 us  [all_sum(): lax.ppermute(value, axis, [(i, i ^ step) for i in range(size)])]
    ppermute x0 -> x15, starting transfers between devices: none -> 23.9 us  [shifted(): return lax.ppermute(value, 'row', [(r, dest(r)) for r in range(64)])]
    add x0 -> x4, other arithmetic: none -> 18.9 us  [the longest x1 11.8 us: row_reduce_scatter(): level = staged[0] + shifted(staged[1], 1, 2, 1)]
    slice x0 -> x5, local copies, waits for them, and re-layouts: none -> 18.1 us  [the longest x1 17.8 us: row_reduce_scatter(): level = staged[0] + shifted(staged[1], 1, 2, 1)]
    squeeze x0 -> x1, local copies, waits for them, and re-layouts: none -> 8.06 us  [row_reduce_scatter(): first = first[0] + sum((shifted(first[s], 2, 4, s) for s in range(1, 4)))]
    ppermute x7, waiting for transfers between devices: 76.6 us -> 84.2 us  [all_sum(): lax.ppermute(value, axis, [(i, i ^ step) for i in range(size)])]
  transfers between devices with their start and end apart: 11 -> 25, of which waited for: 11 -> 14; matrix products, arithmetic and copies ran while one was open for 0% -> 2% of each run, Pallas kernels for 0% -> 0%
where the time goes in v3:
time: 522 us; the launch traced here: 523 us
  waiting for transfers between devices  319 us (61%)
  starting transfers between devices  100 us (19%)
  Pallas kernels  32.8 us (6%)
  local copies, waits for them, and re-layouts  30.7 us (6%)
  other arithmetic  23.3 us (4%)
  between operations  14.2 us (3%)
    all_gather x1, waiting for transfers between devices, body(): gathered = lax.all_gather(features, 'row', axis=0, tiled=True)  127 us
    ppermute x15, waiting for transfers between devices, shifted(): return lax.ppermute(value, 'row', [(r, dest(r)) for r in range(64)])  86.6 us
    ppermute x7, waiting for transfers between devices, all_sum(): lax.ppermute(value, axis, [(i, i ^ step) for i in range(size)])  84.2 us
    ppermute x7, starting transfers between devices, all_sum(): lax.ppermute(value, axis, [(i, i ^ step) for i in range(size)])  72.5 us
    ppermute x15, starting transfers between devices, shifted(): return lax.ppermute(value, 'row', [(r, dest(r)) for r in range(64)])  23.9 us
    ppermute x2, waiting for transfers between devices, swap(): return lax.ppermute(value, axis, [(i, i ^ 1) for i in range(size)])  20.1 us
    pallas_call x1, Pallas kernels, spread(): pl.pallas_call(spread_kernel, out_shape=jax.ShapeDtypeStruct((col_blocks,...  19.8 us
    slice x1, local copies, waits for them, and re-layouts, row_reduce_scatter(): level = staged[0] + shifted(staged[1], 1, 2, 1)  17.8 us
  transfers between devices with their start and end apart: 25, of which 14 were waited for; matrix products, arithmetic and copies ran while one was open for 2% of the time, Pallas kernels for 0%

profile of v3, /device:TPU:0, one launch (start us, length us, event | category | flops | bytes accessed | tf_op | source)
XLA Modules:
  0.0 522.5 jit_solution(16583459874863341033)
XLA Ops:
  7.2 0.7 all-gather.2.cloned.1.call-update
  7.9 127.3 %all-gather.2.cloned.1.call-done.panel_hbm = bf16[32768,256]{1,0:T(8,128)(2,1)} async-done(((bf16[512,256]{1,0:T(8,128)(2,1)}), bf16[32768,256]{1,0:T(8,128)(2,1)}) %all-gather.2.cloned.1.call-update) | async-done | bytes 16777232 | tf_op jit(solution)/shard_map/all_gather | solution.py:191
  135.3 13.0 %shard_map.85 = f32[8,128,256]{2,1,0:T(8,128)} custom-call(s32[8,16]{1,0:T(8,128)} %bitcast.46, s32[8]{0:T(128)} %bitcast.48, bf16[8,16,128,128]{3,2,1,0:T(8,128)(2,1)} %bitcast.38, bf16[32768,256]{1,0:T(8,128)(2,1)} %all-gather.2.cloned.1.call-done.panel_hbm), custom_call_target="tpu_custom_call" | custom-call | flops 1073741824 | bytes 22020096 | tf_op jit(solution)/shard_map/pallas_call | solution.py:91
  148.3 1.1 constant_dynamic-slice_fusion
  149.4 2.6 collective-permute-start
  152.0 12.7 %collective-permute-done = f32[512,256]{1,0:T(8,128)S(1)} collective-permute-done((f32[512,256]{1,0:T(8,128)S(1)}, f32[512,256]{1,0:T(8,128)S(1)}, u32[]{:S(2)}, u32[]{:S(2)}) %collective-permute-start) | collective-permute-done | bytes 524320 | tf_op jit(solution)/shard_map/ppermute | solution.py:145
  164.8 1.1 add_convert_fusion
  165.9 1.1 multiply_convert_fusion
  167.0 0.7 copy-done.7
  167.9 0.9 collective-permute-start.8
  168.8 0.6 pad_add_fusion.side_ref
  169.4 7.4 %collective-permute-done.8 = bf16[512,256]{1,0:T(8,128)(2,1)S(1)} collective-permute-done((bf16[512,256]{1,0:T(8,128)(2,1)S(1)}, bf16[512,256]{1,0:T(8,128)(2,1)S(1)}, u32[]{:S(2)}, u32[]{:S(2)}) %collective-permute-start.8) | collective-permute-done | bytes 262176 | tf_op jit(solution)/shard_map/ppermute | solution.py:145
  176.8 0.9 pad_maximum_fusion.grad_ref
  177.7 19.8 %shard_map.86 = f32[256,128,256]{2,1,0:T(8,128)} custom-call(s32[2]{0:T(128)} %pad_add_fusion.side_ref, s32[8,16]{1,0:T(8,128)} %bitcast.47, s32[8]{0:T(128)} %bitcast.49, bf16[8,16,128,128]{3,2,1,0:T(8,128)(2,1)} %bitcast.39, bf16[2,4,128,256]{3,2,1,0:T(8,128)(2,1)} %pad_maximum_fusion.grad_ref), custom_call_target="tpu_custom_call" | custom-call | flops 1073741824 | bytes 38273024 | tf_op jit(solution)/shard_map/pallas_call | solution.py:118
  197.5 17.8 %fusion.4 = (f32[128,128,256]{2,1,0:T(8,128)}, f32[128,128,256]{2,1,0:T(8,128)S(1)}) fusion(f32[256,128,256]{2,1,0:T(8,128)} %shard_map.86), kind=kLoop, calls=%fused_computation.26 | loop fusion | bytes 67108864 | tf_op jit(solution)/shard_map/slice | solution.py:159
  215.3 25.5 %collective-permute-done.9 = f32[2,64,128,256]{3,2,1,0:T(8,128)} collective-permute-done((f32[2,64,128,256]{3,2,1,0:T(8,128)}, f32[2,64,128,256]{3,2,1,0:T(8,128)}, u32[]{:S(2)}, u32[]{:S(2)}) %collective-permute-start.9) | collective-permute-done | bytes 16777248 | tf_op jit(solution)/shard_map/ppermute | solution.py:153
  240.8 11.8 %add.95 = f32[2,64,128,256]{3,2,1,0:T(8,128)} add(f32[2,64,128,256]{3,2,1,0:T(8,128)S(1)} %bitcast.37, f32[2,64,128,256]{3,2,1,0:T(8,128)} %collective-permute-done.9) | non-fusion elementwise | flops 4194304 | bytes 50331648 | tf_op jit(solution)/shard_map/add | solution.py:159
  252.6 8.1 %slice_bitcast_fusion.5 = (f32[16,128,256]{2,1,0:T(8,128)}, f32[16,128,256]{2,1,0:T(8,128)}, f32[16,128,256]{2,1,0:T(8,128)}, f32[16,128,256]{2,1,0:T(8,128)S(1)...) fusion(f32[2,64,128,256]{3,2,1,0:T(8,128)} %add.95), kind=kLoop, calls=%fused_computation.6 | loop fusion | bytes 25165824 | tf_op jit(solution)/shard_map/squeeze | solution.py:162
  260.7 10.4 %collective-permute-start.11 = (f32[16,128,256]{2,1,0:T(8,128)}, f32[16,128,256]{2,1,0:T(8,128)S(1)}, u32[]{:S(2)}, u32[]{:S(2)}) collective-permute-start(f32[16,128,256]{2,1,0:T(8,128)} %get-tuple-element.7), channel_id=1, source_target_pairs={{0,4},{1,5},{2,6},{3,7},{4,0},{5,1},{6,2},{7,3},{8,12},{9,13},{10,... | collective-permute-start | bytes 6291464 | tf_op jit(solution)/shard_map/ppermute | solution.py:153
  271.1 1.2 fusion.7
  272.5 1.5 collective-permute-done.1
  274.0 4.3 collective-permute-start.2
  278.3 48.5 %collective-permute-done.2 = f32[256,256]{1,0:T(8,128)S(1)} collective-permute-done((f32[256,256]{1,0:T(8,128)S(1)}, f32[256,256]{1,0:T(8,128)S(1)}, u32[]{:S(2)}, u32[]{:S(2)}) %collective-permute-start.2) | collective-permute-done | bytes 262176 | tf_op jit(solution)/shard_map/ppermute | solution.py:179
  326.9 1.0 collective-permute-start.3
  327.8 8.1 %collective-permute-done.3 = f32[256,256]{1,0:T(8,128)S(1)} collective-permute-done((f32[256,256]{1,0:T(8,128)S(1)}, f32[256,256]{1,0:T(8,128)S(1)}, u32[]{:S(2)}, u32[]{:S(2)}) %collective-permute-start.3) | collective-permute-done | bytes 262176 | tf_op jit(solution)/shard_map/ppermute | solution.py:179
  336.0 23.6 %collective-permute-start.4 = (f32[256,256]{1,0:T(8,128)S(1)}, f32[256,256]{1,0:T(8,128)S(1)}, u32[]{:S(2)}, u32[]{:S(2)}) collective-permute-start(f32[256,256]{1,0:T(8,128)S(1)} %add.90), channel_id=1, source_target_pairs={{0,8},{1,9},{2,10},{3,11},{4,12},{5,13},{6,14},{7,15},{8,0},{9,1},... | collective-permute-start | bytes 786440 | tf_op jit(solution)/shard_map/ppermute | solution.py:179
  359.6 2.0 collective-permute-start.17
  361.6 3.1 collective-permute-done.4
  364.7 2.0 collective-permute-start.10
  366.8 41.6 %collective-permute-done.19 = f32[16,128,256]{2,1,0:T(8,128)S(1)} collective-permute-done((f32[16,128,256]{2,1,0:T(8,128)}, f32[16,128,256]{2,1,0:T(8,128)S(1)}, u32[]{:S(2)}, u32[]{:S(2)}) %collective-permute-start.19) | collective-permute-done | bytes 2097184 | tf_op jit(solution)/shard_map/ppermute | solution.py:153
  408.4 40.2 %collective-permute-start.5 = (f32[256,256]{1,0:T(8,128)S(1)}, f32[256,256]{1,0:T(8,128)S(1)}, u32[]{:S(2)}, u32[]{:S(2)}) collective-permute-start(f32[256,256]{1,0:T(8,128)S(1)} %add.91), channel_id=1, source_target_pairs={{0,16},{1,17},{2,18},{3,19},{4,20},{5,21},{6,22},{7,23},{8,24},{9,... | collective-permute-start | bytes 786440 | tf_op jit(solution)/shard_map/ppermute | solution.py:179
  448.6 3.4 collective-permute-done.17
  452.0 1.4 copy-done.5
  453.4 1.3 copy-done.6
  454.7 6.9 %fusion.1 = (f32[16,128,256]{2,1,0:T(8,128)S(1)}, f32[16,128,256]{2,1,0:T(8,128)S(1)}) fusion(f32[2,64,128,256]{3,2,1,0:T(8,128)} %add.95, f32[16,128,256]{2,1,0:T(8,128)} %copy-done.6, f32[16,128,256]{2,1,0:T(8,128)} %collective-permute-done.10, f32[16,128,256]{2,1,0:T(8,128)S(1)} %collective-permute-done.11, f32[16,128,256]{2,1,0:T(8,128)} %copy-done.3, ...), kind=kLoop, calls=%fused_computation.9 | loop fusion | flops 3145728 | bytes 20971520 | tf_op jit(solution)/shard_map/add | solution.py:162
  461.7 2.3 collective-permute-start.14
  464.0 2.5 collective-permute-start.15
  466.5 0.8 collective-permute-start.13
  467.3 2.3 collective-permute-start.6
  469.8 1.2 collective-permute-start.21
  471.0 23.0 %collective-permute-done.6 = f32[256,256]{1,0:T(8,128)S(1)} collective-permute-done((f32[256,256]{1,0:T(8,128)S(1)}, f32[256,256]{1,0:T(8,128)S(1)}, u32[]{:S(2)}, u32[]{:S(2)}) %collective-permute-start.6) | collective-permute-done | bytes 262176 | tf_op jit(solution)/shard_map/ppermute | solution.py:179
  494.0 2.0 collective-permute-start.20
  496.1 0.9 collective-permute-start.7
  497.3 9.7 %collective-permute-done.22 = f32[4,128,256]{2,1,0:T(8,128)S(1)} collective-permute-done((f32[4,128,256]{2,1,0:T(8,128)S(1)}, f32[4,128,256]{2,1,0:T(8,128)S(1)}, u32[]{:S(2)}, u32[]{:S(2)}) %collective-permute-start.22) | collective-permute-done | bytes 524320 | tf_op jit(solution)/shard_map/ppermute | solution.py:153
  507.0 1.2 collective-permute-done.20
  508.9 0.7 add_multiply_fusion
  509.7 5.2 collective-permute-done.23
  515.0 0.7 pad_maximum_fusion.1
  (50 shorter events, 1.9 us)
Async XLA Ops:
  7.2 158.7 %copy-start = (bf16[256,256]{1,0:T(8,128)(2,1)S(1)}, bf16[256,256]{1,0:T(8,128)(2,1)}, u32[]{:S(2)}) copy-start(bf16[256,256]{1,0:T(8,128)(2,1)} %param.7) | copy-start | bytes 393220
  7.2 128.1 %all-gather.2.cloned.1.call-start = ((), (), s32[]{:S(2)}) async-start(), calls=%async_computation | async-start | bytes 17039360 | tf_op jit(solution)/shard_map/all_gather | solution.py:191
  148.3 17.6 %copy-start.8 = (bf16[512,256]{1,0:T(8,128)(2,1)S(1)}, bf16[512,256]{1,0:T(8,128)(2,1)}, u32[]{:S(2)}) copy-start(bf16[512,256]{1,0:T(8,128)(2,1)} %param.11) | copy-start | bytes 786436
  149.4 15.3 %collective-permute-start = (f32[512,256]{1,0:T(8,128)S(1)}, f32[512,256]{1,0:T(8,128)S(1)}, u32[]{:S(2)}, u32[]{:S(2)}) collective-permute-start(f32[512,256]{1,0:T(8,128)S(1)} %constant_dynamic-slice_fusion), channel_id=1, source_target_pairs={{0,64},{64,0},{1,65},{65,1},{2,66},{66,2},{3,67},{67,3},{4,68},{68... | collective-permute-start | bytes 1572872 | tf_op jit(solution)/shard_map/ppermute | solution.py:145
  167.0 0.7 copy-start.7
  167.9 8.9 %collective-permute-start.8 = (bf16[512,256]{1,0:T(8,128)(2,1)S(1)}, bf16[512,256]{1,0:T(8,128)(2,1)S(1)}, u32[]{:S(2)}, u32[]{:S(2)}) collective-permute-start(bf16[512,256]{1,0:T(8,128)(2,1)S(1)} %convolution_convert_fusion), channel_id=1, source_target_pairs={{0,64},{64,0},{1,65},{65,1},{2,66},{66,2},{3,67},{67,3},{4,68},{68... | collective-permute-start | bytes 786440 | tf_op jit(solution)/shard_map/ppermute | solution.py:145
  215.3 25.5 %collective-permute-start.9 = (f32[2,64,128,256]{3,2,1,0:T(8,128)}, f32[2,64,128,256]{3,2,1,0:T(8,128)}, u32[]{:S(2)}, u32[]{:S(2)}) collective-permute-start(f32[2,64,128,256]{3,2,1,0:T(8,128)} %bitcast.40), channel_id=1, source_target_pairs={{0,1},{1,0},{2,3},{3,2},{4,5},{5,4},{6,7},{7,6},{8,9},{9,8},{10,11... | collective-permute-start | bytes 50331656 | tf_op jit(solution)/shard_map/ppermute | solution.py:153
  260.7 98.9 %copy-start.2 = (f32[16,128,256]{2,1,0:T(8,128)S(1)}, f32[16,128,256]{2,1,0:T(8,128)}, u32[]{:S(2)}) copy-start(f32[16,128,256]{2,1,0:T(8,128)} %get-tuple-element.9) | copy-start | bytes 6291460
  260.7 104.0 %collective-permute-start.11 = (f32[16,128,256]{2,1,0:T(8,128)}, f32[16,128,256]{2,1,0:T(8,128)S(1)}, u32[]{:S(2)}, u32[]{:S(2)}) collective-permute-start(f32[16,128,256]{2,1,0:T(8,128)} %get-tuple-element.7), channel_id=1, source_target_pairs={{0,4},{1,5},{2,6},{3,7},{4,0},{5,1},{6,2},{7,3},{8,12},{9,13},{10,... | collective-permute-start | bytes 6291464 | tf_op jit(solution)/shard_map/ppermute | solution.py:153
  272.3 1.6 collective-permute-start.1
  274.0 52.9 %collective-permute-start.2 = (f32[256,256]{1,0:T(8,128)S(1)}, f32[256,256]{1,0:T(8,128)S(1)}, u32[]{:S(2)}, u32[]{:S(2)}) collective-permute-start(f32[256,256]{1,0:T(8,128)S(1)} %add.88), channel_id=1, source_target_pairs={{0,2},{1,3},{2,0},{3,1},{4,6},{5,7},{6,4},{7,5},{8,10},{9,11},{10,... | collective-permute-start | bytes 786440 | tf_op jit(solution)/shard_map/ppermute | solution.py:179
  326.9 9.1 %collective-permute-start.3 = (f32[256,256]{1,0:T(8,128)S(1)}, f32[256,256]{1,0:T(8,128)S(1)}, u32[]{:S(2)}, u32[]{:S(2)}) collective-permute-start(f32[256,256]{1,0:T(8,128)S(1)} %add.89), channel_id=1, source_target_pairs={{0,4},{1,5},{2,6},{3,7},{4,0},{5,1},{6,2},{7,3},{8,12},{9,13},{10,... | collective-permute-start | bytes 786440 | tf_op jit(solution)/shard_map/ppermute | solution.py:179
  336.0 28.7 %collective-permute-start.4 = (f32[256,256]{1,0:T(8,128)S(1)}, f32[256,256]{1,0:T(8,128)S(1)}, u32[]{:S(2)}, u32[]{:S(2)}) collective-permute-start(f32[256,256]{1,0:T(8,128)S(1)} %add.90), channel_id=1, source_target_pairs={{0,8},{1,9},{2,10},{3,11},{4,12},{5,13},{6,14},{7,15},{8,0},{9,1},... | collective-permute-start | bytes 786440 | tf_op jit(solution)/shard_map/ppermute | solution.py:179
  359.6 48.8 %collective-permute-start.19 = (f32[16,128,256]{2,1,0:T(8,128)}, f32[16,128,256]{2,1,0:T(8,128)S(1)}, u32[]{:S(2)}, u32[]{:S(2)}) collective-permute-start(f32[16,128,256]{2,1,0:T(8,128)} %get-tuple-element.8), channel_id=1, source_target_pairs={{0,48},{1,49},{2,50},{3,51},{4,52},{5,53},{6,54},{7,55},{8,56},{9,... | collective-permute-start | bytes 6291464 | tf_op jit(solution)/shard_map/ppermute | solution.py:153
  359.6 89.0 %collective-permute-start.18 = (f32[16,128,256]{2,1,0:T(8,128)S(1)}, f32[16,128,256]{2,1,0:T(8,128)S(1)}, u32[]{:S(2)}, u32[]{:S(2)}) collective-permute-start(f32[16,128,256]{2,1,0:T(8,128)S(1)} %copy-done.2), channel_id=1, source_target_pairs={{0,32},{1,33},{2,34},{3,35},{4,36},{5,37},{6,38},{7,39},{8,40},{9,... | collective-permute-start | bytes 6291464 | tf_op jit(solution)/shard_map/ppermute | solution.py:153
  359.6 92.3 %collective-permute-start.17 = (f32[16,128,256]{2,1,0:T(8,128)S(1)}, f32[16,128,256]{2,1,0:T(8,128)S(1)}, u32[]{:S(2)}, u32[]{:S(2)}) collective-permute-start(f32[16,128,256]{2,1,0:T(8,128)S(1)} %get-tuple-element.10), channel_id=1, source_target_pairs={{0,16},{1,17},{2,18},{3,19},{4,20},{5,21},{6,22},{7,23},{8,24},{9,... | collective-permute-start | bytes 6291464 | tf_op jit(solution)/shard_map/ppermute | solution.py:153
  364.7 87.2 %collective-permute-start.12 = (f32[16,128,256]{2,1,0:T(8,128)S(1)}, f32[16,128,256]{2,1,0:T(8,128)S(1)}, u32[]{:S(2)}, u32[]{:S(2)}) collective-permute-start(f32[16,128,256]{2,1,0:T(8,128)S(1)} %get-tuple-element.11), channel_id=1, source_target_pairs={{0,6},{1,7},{2,0},{3,1},{4,2},{5,3},{6,4},{7,5},{8,14},{9,15},{10,... | collective-permute-start | bytes 6291464 | tf_op jit(solution)/shard_map/ppermute | solution.py:153
  364.7 90.0 %collective-permute-start.10 = (f32[16,128,256]{2,1,0:T(8,128)S(1)}, f32[16,128,256]{2,1,0:T(8,128)}, u32[]{:S(2)}, u32[]{:S(2)}) collective-permute-start(f32[16,128,256]{2,1,0:T(8,128)S(1)} %get-tuple-element.12), channel_id=1, source_target_pairs={{0,2},{1,3},{2,4},{3,5},{4,6},{5,7},{6,0},{7,1},{8,10},{9,11},{10,... | collective-permute-start | bytes 6291464 | tf_op jit(solution)/shard_map/ppermute | solution.py:153
  408.4 43.6 %copy-start.3 = (f32[16,128,256]{2,1,0:T(8,128)}, f32[16,128,256]{2,1,0:T(8,128)S(1)}, u32[]{:S(2)}) copy-start(f32[16,128,256]{2,1,0:T(8,128)S(1)} %collective-permute-done.19) | copy-start | bytes 6291460
  408.4 58.9 %collective-permute-start.5 = (f32[256,256]{1,0:T(8,128)S(1)}, f32[256,256]{1,0:T(8,128)S(1)}, u32[]{:S(2)}, u32[]{:S(2)}) collective-permute-start(f32[256,256]{1,0:T(8,128)S(1)} %add.91), channel_id=1, source_target_pairs={{0,16},{1,17},{2,18},{3,19},{4,20},{5,21},{6,22},{7,23},{8,24},{9,... | collective-permute-start | bytes 786440 | tf_op jit(solution)/shard_map/ppermute | solution.py:179
  448.6 3.4 copy-start.4
  451.9 1.4 copy-start.5
  453.4 1.3 copy-start.6
  461.7 32.3 %collective-permute-start.14 = (f32[4,128,256]{2,1,0:T(8,128)S(1)}, f32[4,128,256]{2,1,0:T(8,128)S(1)}, u32[]{:S(2)}, u32[]{:S(2)}) collective-permute-start(f32[4,128,256]{2,1,0:T(8,128)S(1)} %get-tuple-element.13), channel_id=1, source_target_pairs={{0,32},{1,33},{2,34},{3,35},{4,36},{5,37},{6,38},{7,39},{8,40},{9,... | collective-permute-start | bytes 1572872 | tf_op jit(solution)/shard_map/ppermute | solution.py:153
  464.0 32.1 %collective-permute-start.15 = (f32[4,128,256]{2,1,0:T(8,128)S(1)}, f32[4,128,256]{2,1,0:T(8,128)S(1)}, u32[]{:S(2)}, u32[]{:S(2)}) collective-permute-start(f32[4,128,256]{2,1,0:T(8,128)S(1)} %get-tuple-element.14), channel_id=1, source_target_pairs={{0,48},{1,49},{2,50},{3,51},{4,52},{5,53},{6,54},{7,55},{8,56},{9,... | collective-permute-start | bytes 1572872 | tf_op jit(solution)/shard_map/ppermute | solution.py:153
  466.5 30.5 %collective-permute-start.13 = (f32[4,128,256]{2,1,0:T(8,128)S(1)}, f32[4,128,256]{2,1,0:T(8,128)S(1)}, u32[]{:S(2)}, u32[]{:S(2)}) collective-permute-start(f32[4,128,256]{2,1,0:T(8,128)S(1)} %get-tuple-element.15), channel_id=1, source_target_pairs={{0,16},{1,17},{2,18},{3,19},{4,20},{5,21},{6,22},{7,23},{8,24},{9,... | collective-permute-start | bytes 1572872 | tf_op jit(solution)/shard_map/ppermute | solution.py:153
  467.3 26.7 %collective-permute-start.6 = (f32[256,256]{1,0:T(8,128)S(1)}, f32[256,256]{1,0:T(8,128)S(1)}, u32[]{:S(2)}, u32[]{:S(2)}) collective-permute-start(f32[256,256]{1,0:T(8,128)S(1)} %add.92), channel_id=1, source_target_pairs={{0,32},{1,33},{2,34},{3,35},{4,36},{5,37},{6,38},{7,39},{8,40},{9,... | collective-permute-start | bytes 786440 | tf_op jit(solution)/shard_map/ppermute | solution.py:179
  469.8 27.5 %collective-permute-start.21 = (f32[4,128,256]{2,1,0:T(8,128)S(1)}, f32[4,128,256]{2,1,0:T(8,128)S(1)}, u32[]{:S(2)}, u32[]{:S(2)}) collective-permute-start(f32[4,128,256]{2,1,0:T(8,128)S(1)} %get-tuple-element.16), channel_id=1, source_target_pairs={{0,4},{1,5},{2,6},{3,7},{4,0},{5,1},{6,2},{7,3},{8,12},{9,13},{10,... | collective-permute-start | bytes 1572872 | tf_op jit(solution)/shard_map/ppermute | solution.py:153
  494.0 13.0 %collective-permute-start.22 = (f32[4,128,256]{2,1,0:T(8,128)S(1)}, f32[4,128,256]{2,1,0:T(8,128)S(1)}, u32[]{:S(2)}, u32[]{:S(2)}) collective-permute-start(f32[4,128,256]{2,1,0:T(8,128)S(1)} %get-tuple-element.17), channel_id=1, source_target_pairs={{0,6},{1,7},{2,0},{3,1},{4,2},{5,3},{6,4},{7,5},{8,14},{9,15},{10,... | collective-permute-start | bytes 1572872 | tf_op jit(solution)/shard_map/ppermute | solution.py:153
  494.0 14.2 %collective-permute-start.20 = (f32[4,128,256]{2,1,0:T(8,128)S(1)}, f32[4,128,256]{2,1,0:T(8,128)S(1)}, u32[]{:S(2)}, u32[]{:S(2)}) collective-permute-start(f32[4,128,256]{2,1,0:T(8,128)S(1)} %get-tuple-element.18), channel_id=1, source_target_pairs={{0,2},{1,3},{2,4},{3,5},{4,6},{5,7},{6,0},{7,1},{8,10},{9,11},{10,... | collective-permute-start | bytes 1572872 | tf_op jit(solution)/shard_map/ppermute | solution.py:153
  496.1 12.9 %collective-permute-start.7 = (f32[256,256]{1,0:T(8,128)S(1)}, f32[256,256]{1,0:T(8,128)S(1)}, u32[]{:S(2)}, u32[]{:S(2)}) collective-permute-start(f32[256,256]{1,0:T(8,128)S(1)} %add.93), channel_id=1, source_target_pairs={{0,64},{64,0},{1,65},{65,1},{2,66},{66,2},{3,67},{67,3},{4,68},{68... | collective-permute-start | bytes 786440 | tf_op jit(solution)/shard_map/ppermute | solution.py:179
  497.2 12.5 %collective-permute-start.16 = (f32[2,128,256]{2,1,0:T(8,128)S(1)}, f32[2,128,256]{2,1,0:T(8,128)S(1)}, u32[]{:S(2)}, u32[]{:S(2)}) collective-permute-start(f32[2,128,256]{2,1,0:T(8,128)S(1)} %slice.131), channel_id=1, source_target_pairs={{0,8},{1,9},{2,10},{3,11},{4,12},{5,13},{6,14},{7,15},{8,0},{9,1},... | collective-permute-start | bytes 786440 | tf_op jit(solution)/shard_map/ppermute | solution.py:153
  508.2 7.5 %copy-start.1 = (bf16[256,256]{1,0:T(8,128)(2,1)S(1)}, bf16[256,256]{1,0:T(8,128)(2,1)}, u32[]{:S(2)}) copy-start(bf16[256,256]{1,0:T(8,128)(2,1)} %param.7) | copy-start | bytes 393220
  508.4 6.5 %collective-permute-start.23 = (f32[2,128,256]{2,1,0:T(8,128)S(1)}, f32[2,128,256]{2,1,0:T(8,128)S(1)}, u32[]{:S(2)}, u32[]{:S(2)}) collective-permute-start(f32[2,128,256]{2,1,0:T(8,128)S(1)} %slice.141), channel_id=1, source_target_pairs={{0,8},{1,9},{2,10},{3,11},{4,12},{5,13},{6,14},{7,15},{8,0},{9,1},... | collective-permute-start | bytes 786440 | tf_op jit(solution)/shard_map/ppermute | solution.py:153
Sparse Core Ops, SparseCore 0:
  9.7 125.4 all-gather.1

commit v4 on v3

--- a/solution.py
+++ b/solution.py
@@ -50,7 +50,7 @@
     return (dk * 2 + half) * 64 + ((first * 4 + second) * 2 + dy) * 2 + q2
 
 
-def spread_kernel(side_ref, cols_ref, count_ref, vals_hbm, grad_ref, out_hbm, vals, total, sems):
+def spread_kernel(side_ref, cols_ref, count_ref, vals_hbm, grad_ref, keep_hbm, send_hbm, vals, total, sems):
     row_blocks, slot_total, block, _ = vals.shape
     per_panel = grad_ref.shape[1]
     col_blocks = total.shape[0]
@@ -80,9 +80,13 @@
             return carry
 
         lax.fori_loop(0, live, body, 0)
-    store = pltpu.make_async_copy(total, out_hbm, sems.at[1])
-    store.start()
-    store.wait()
+    half = col_blocks // 2
+    keep = pltpu.make_async_copy(total.at[pl.ds(0, half)], keep_hbm, sems.at[1])
+    send = pltpu.make_async_copy(total.at[pl.ds(half, half)], send_hbm, sems.at[2])
+    send.start()
+    keep.start()
+    send.wait()
+    keep.wait()
 
 
 def aggregate(cols, count, vals, panel):
@@ -117,7 +121,7 @@
     width = grad.shape[-1]
     return pl.pallas_call(
         spread_kernel,
-        out_shape=jax.ShapeDtypeStruct((col_blocks, block, width), jnp.float32),
+        out_shape=[jax.ShapeDtypeStruct((col_blocks // 2, block, width), jnp.float32)] * 2,
         in_specs=[
             pl.BlockSpec(memory_space=pltpu.SMEM),
             pl.BlockSpec(memory_space=pltpu.SMEM),
@@ -125,11 +129,11 @@
             pl.BlockSpec(memory_space=pl.ANY),
             pl.BlockSpec(memory_space=pltpu.VMEM),
         ],
-        out_specs=pl.BlockSpec(memory_space=pl.ANY),
+        out_specs=[pl.BlockSpec(memory_space=pl.ANY)] * 2,
         scratch_shapes=[
             pltpu.VMEM(vals.shape, vals.dtype),
             pltpu.VMEM((col_blocks, block, width), jnp.float32),
-            pltpu.SemaphoreType.DMA((2,)),
+            pltpu.SemaphoreType.DMA((3,)),
         ],
         compiler_params=pltpu.CompilerParams(vmem_limit_bytes=VMEM_LIMIT),
         cost_estimate=pl.CostEstimate(
@@ -153,20 +157,16 @@
     return lax.ppermute(value, "row", [(r, dest(r)) for r in range(64)])
 
 
-def row_reduce_scatter(term):
-    _, block, width = term.shape
-    staged = term.reshape(2, 2, 64, block, width)
-    level = staged[0] + shifted(staged[1], 1, 2, 1)
-    first = level[0].reshape(4, 16, block, width)
-    second = level[1].reshape(4, 16, block, width)
-    first = first[0] + sum(shifted(first[s], 2, 4, s) for s in range(1, 4))
-    second = second[0] + sum(shifted(second[s], 16, 4, s) for s in range(1, 4))
-    first = first.reshape(4, 4, block, width)
-    second = second.reshape(4, 4, block, width)
-    first = first[0] + sum(shifted(first[s], 16, 4, s) for s in range(1, 4))
-    second = second[0] + sum(shifted(second[s], 2, 4, s) for s in range(1, 4))
-    first = first.reshape(2, 2, block, width)
-    second = second.reshape(2, 2, block, width)
+def row_reduce_scatter(keep, send):
+    _, block, width = keep.shape
+    keep = keep.reshape(2, 4, 16, block, width)
+    came = shifted(send, 1, 2, 1).reshape(2, 4, 16, block, width)
+    first = [keep[0, s] + came[0, s] for s in range(4)]
+    second = [keep[1, s] + came[1, s] for s in range(4)]
+    first = (first[0] + sum(shifted(first[s], 2, 4, s) for s in range(1, 4))).reshape(4, 4, block, width)
+    second = (second[0] + sum(shifted(second[s], 16, 4, s) for s in range(1, 4))).reshape(4, 4, block, width)
+    first = (first[0] + sum(shifted(first[s], 16, 4, s) for s in range(1, 4))).reshape(2, 2, block, width)
+    second = (second[0] + sum(shifted(second[s], 2, 4, s) for s in range(1, 4))).reshape(2, 2, block, width)
     first = first[0] + shifted(first[1], 8, 2, 1)
     second = second[0] + shifted(second[1], 8, 2, 1)
     return jnp.concatenate([first, second]).reshape(-1, width)
@@ -205,11 +205,11 @@
     local_grad = jnp.dot(aggregated.T, pre_grad, preferred_element_type=jnp.float32)
     own_grad = jnp.dot(pre_grad, weight.T, preferred_element_type=jnp.float32).astype(jnp.bfloat16)
     both_grad = jnp.stack([own_grad, swap(own_grad, "grp")]).reshape(2, -1, block, width)
-    weight_grad = all_sum(all_sum(local_grad, "row"), "grp") * (1.0 / math.sqrt(verts))
+    weight_grad = lax.psum(local_grad, ("grp", "row")) * (1.0 / math.sqrt(verts))
 
     where = jnp.stack([side, lax.axis_index("row")]).astype(jnp.int32)
-    term = spread(where, cols, count, vals, both_grad, col_blocks)
-    input_grad = row_reduce_scatter(term).astype(jnp.bfloat16)
+    keep, send = spread(where, cols, count, vals, both_grad, col_blocks)
+    input_grad = row_reduce_scatter(keep, send).astype(jnp.bfloat16)
     return (activated, weight_grad, input_grad)
 
 

time: 522 us -> 550 us (1.054)
  waiting for transfers between devices: 319 us -> 401 us
  starting transfers between devices: 100 us -> 27.7 us
  Pallas kernels: 32.8 us -> 63.3 us
  local copies, waits for them, and re-layouts: 30.7 us -> 7.79 us
  other arithmetic: 23.3 us -> 33.1 us
    psum x0 -> x1, waiting for transfers between devices: none -> 128 us  [body(): lax.psum(local_grad, ('grp', 'row')) * (1.0 / math.sqrt(verts))]
    ppermute x7 -> x0, waiting for transfers between devices: 84.2 us -> none  [all_sum(): lax.ppermute(value, axis, [(i, i ^ step) for i in range(size)])]
    ppermute x7 -> x0, starting transfers between devices: 72.5 us -> none  [all_sum(): lax.ppermute(value, axis, [(i, i ^ step) for i in range(size)])]
    ppermute x15, waiting for transfers between devices: 86.6 us -> 126 us  [shifted(): return lax.ppermute(value, 'row', [(r, dest(r)) for r in range(64)])]
    pallas_call x1, Pallas kernels: 19.8 us -> 36.7 us  [spread(): pl.pallas_call(spread_kernel, out_shape=[jax.ShapeDtypeStruct((col_blocks...]
    slice x3 -> x2, local copies, waits for them, and re-layouts: 18 us -> 2.48 us  [the longest x1 1.32 us: row_reduce_scatter(): first[s]]
    pallas_call x1, Pallas kernels: 13 us -> 26.6 us  [aggregate(): pl.pallas_call(aggregate_kernel, out_shape=jax.ShapeDtypeStruct((row_bloc...]
    add x10 -> x4, other arithmetic: 19.1 us -> 28 us  [the longest x1 15.7 us: row_reduce_scatter(): first = [keep[0, s] + came[0, s] for s in range(4)]]
  transfers between devices with their start and end apart: 25 -> 19, of which waited for: 14 -> 12; matrix products, arithmetic and copies ran while one was open for 2% -> 2% of each run, Pallas kernels for 0% -> 0%
where the time goes in v4:
time: 550 us; the launch traced here: 549 us
  waiting for transfers between devices  401 us (73%)
  Pallas kernels  63.3 us (12%)
  other arithmetic  33.1 us (6%)
  starting transfers between devices  27.7 us (5%)
  between operations  14.2 us (3%)
  local copies, waits for them, and re-layouts  7.79 us (1%)
    psum x1, waiting for transfers between devices, body(): lax.psum(local_grad, ('grp', 'row')) * (1.0 / math.sqrt(verts))  128 us
    all_gather x1, waiting for transfers between devices, body(): gathered = lax.all_gather(features, 'row', axis=0, tiled=True)  127 us
    ppermute x15, waiting for transfers between devices, shifted(): return lax.ppermute(value, 'row', [(r, dest(r)) for r in range(64)])  126 us
    pallas_call x1, Pallas kernels, spread(): pl.pallas_call(spread_kernel, out_shape=[jax.ShapeDtypeStruct((col_blocks...  36.7 us
    pallas_call x1, Pallas kernels, aggregate(): pl.pallas_call(aggregate_kernel, out_shape=jax.ShapeDtypeStruct((row_bloc...  26.6 us
    ppermute x15, starting transfers between devices, shifted(): return lax.ppermute(value, 'row', [(r, dest(r)) for r in range(64)])  22.1 us
    ppermute x2, waiting for transfers between devices, swap(): return lax.ppermute(value, axis, [(i, i ^ 1) for i in range(size)])  19 us
    add x1, other arithmetic, row_reduce_scatter(): first = [keep[0, s] + came[0, s] for s in range(4)]  15.7 us
  transfers between devices with their start and end apart: 19, of which 12 were waited for; matrix products, arithmetic and copies ran while one was open for 2% of the time, Pallas kernels for 0%

profile of v4, /device:TPU:0, one launch (start us, length us, event | category | flops | bytes accessed | tf_op | source)
XLA Modules:
  0.0 549.5 jit_solution(9770507521770591064)
XLA Ops:
  7.2 0.7 all-gather.2.cloned.1.call-update
  8.0 127.3 %all-gather.2.cloned.1.call-done.panel_hbm = bf16[32768,256]{1,0:T(8,128)(2,1)} async-done(((bf16[512,256]{1,0:T(8,128)(2,1)}), bf16[32768,256]{1,0:T(8,128)(2,1)}) %all-gather.2.cloned.1.call-update) | async-done | bytes 16777232 | tf_op jit(solution)/shard_map/all_gather | solution.py:191
  135.3 26.6 %shard_map.85 = f32[8,128,256]{2,1,0:T(8,128)} custom-call(s32[8,16]{1,0:T(8,128)} %bitcast.48, s32[8]{0:T(128)} %bitcast.50, bf16[8,16,128,128]{3,2,1,0:T(8,128)(2,1)} %bitcast.41, bf16[32768,256]{1,0:T(8,128)(2,1)} %all-gather.2.cloned.1.call-done.panel_hbm), custom_call_target="tpu_custom_call" | custom-call | flops 1073741824 | bytes 22020096 | tf_op jit(solution)/shard_map/pallas_call | solution.py:95
  161.9 1.1 constant_dynamic-slice_fusion
  163.0 3.2 collective-permute-start
  166.3 12.6 %collective-permute-done = f32[512,256]{1,0:T(8,128)S(1)} collective-permute-done((f32[512,256]{1,0:T(8,128)S(1)}, f32[512,256]{1,0:T(8,128)S(1)}, u32[]{:S(2)}, u32[]{:S(2)}) %collective-permute-start) | collective-permute-done | bytes 524320 | tf_op jit(solution)/shard_map/ppermute | solution.py:149
  178.8 1.1 add_convert_fusion
  179.9 1.1 multiply_convert_fusion
  181.1 0.7 copy-done.9
  181.8 0.3 convolution_convert_fusion
  182.0 2.3 collective-permute-start.1
  184.3 0.6 pad_add_fusion.side_ref
  184.9 6.5 %collective-permute-done.1 = bf16[512,256]{1,0:T(8,128)(2,1)S(1)} collective-permute-done((bf16[512,256]{1,0:T(8,128)(2,1)S(1)}, bf16[512,256]{1,0:T(8,128)(2,1)S(1)}, u32[]{:S(2)}, u32[]{:S(2)}) %collective-permute-start.1) | collective-permute-done | bytes 262176 | tf_op jit(solution)/shard_map/ppermute | solution.py:149
  191.4 0.9 pad_maximum_fusion.grad_ref
  192.2 36.7 %shard_map.86 = (f32[128,128,256]{2,1,0:T(8,128)}, f32[128,128,256]{2,1,0:T(8,128)}) custom-call(s32[2]{0:T(128)} %pad_add_fusion.side_ref, s32[8,16]{1,0:T(8,128)} %bitcast.49, s32[8]{0:T(128)} %bitcast.51, bf16[8,16,128,128]{3,2,1,0:T(8,128)(2,1)} %bitcast.42, bf16[2,4,128,256]{3,2,1,0:T(8,128)(2,1)} %pad_maximum_fusion.grad_ref), custom_call_target="tpu_custom_call" | custom-call | flops 1073741824 | bytes 38273024 | tf_op jit(solution)/shard_map/pallas_call | solution.py:122
  229.0 25.4 %collective-permute-done.2 = f32[128,128,256]{2,1,0:T(8,128)S(1)} collective-permute-done((f32[128,128,256]{2,1,0:T(8,128)}, f32[128,128,256]{2,1,0:T(8,128)S(1)}, u32[]{:S(2)}, u32[]{:S(2)}) %collective-permute-start.2) | collective-permute-done | bytes 16777248 | tf_op jit(solution)/shard_map/ppermute | solution.py:157
  254.4 15.7 %fusion.6 = (f32[16,128,256]{2,1,0:T(8,128)}, f32[16,128,256]{2,1,0:T(8,128)}, f32[16,128,256]{2,1,0:T(8,128)}, f32[16,128,256]{2,1,0:T(8,128)}, f32[16,128,256]{2,1,0:T(8,128)}, /*index=5*/f32[16,128,256]{2,1,0:T(8,128)S(1)}) fusion(f32[2,4,16,128,256]{4,3,2,1,0:T(8,128)S(1)} %bitcast.39, f32[2,4,16,128,256]{4,3,2,1,0:T(8,128)} %bitcast.37), kind=kLoop, calls=%fused_computation.12 | loop fusion | flops 3145728 | bytes 37748736 | tf_op jit(solution)/shard_map/add | solution.py:164
  270.0 1.4 collective-permute-start.4
  271.5 0.1 collective-permute-start.11
  271.6 1.9 collective-permute-start.10
  273.5 4.3 collective-permute-start.5
  277.8 41.7 %collective-permute-done.4 = f32[16,128,256]{2,1,0:T(8,128)S(1)} collective-permute-done((f32[16,128,256]{2,1,0:T(8,128)}, f32[16,128,256]{2,1,0:T(8,128)S(1)}, u32[]{:S(2)}, u32[]{:S(2)}) %collective-permute-start.4) | collective-permute-done | bytes 2097184 | tf_op jit(solution)/shard_map/ppermute | solution.py:157
  319.5 3.8 collective-permute-start.3
  323.3 42.2 %collective-permute-done.10 = f32[16,128,256]{2,1,0:T(8,128)S(1)} collective-permute-done((f32[16,128,256]{2,1,0:T(8,128)}, f32[16,128,256]{2,1,0:T(8,128)S(1)}, u32[]{:S(2)}, u32[]{:S(2)}) %collective-permute-start.10) | collective-permute-done | bytes 2097184 | tf_op jit(solution)/shard_map/ppermute | solution.py:157
  365.5 1.3 copy-done.7
  366.9 1.4 copy-done.8
  368.3 9.2 %fusion.9 = (f32[16,128,256]{2,1,0:T(8,128)S(1)}, f32[16,128,256]{2,1,0:T(8,128)S(1)}) fusion(f32[2,4,16,128,256]{4,3,2,1,0:T(8,128)} %bitcast.40, f32[2,4,16,128,256]{4,3,2,1,0:T(8,128)} %bitcast.38, f32[16,128,256]{2,1,0:T(8,128)} %copy-done.8, f32[16,128,256]{2,1,0:T(8,128)} %collective-permute-done.3, f32[16,128,256]{2,1,0:T(8,128)} %copy-done.4, ...), kind=kLoop, calls=%fused_computation.17 | loop fusion | flops 4194304 | bytes 25165824 | tf_op jit(solution)/shard_map/add | solution.py:166
  377.4 1.3 fusion.12
  378.8 0.3 collective-permute-start.7
  379.0 1.5 collective-permute-start.8
  380.6 0.9 collective-permute-start.6
  381.4 1.2 fusion.13
  382.6 2.2 collective-permute-start.14
  384.8 2.7 collective-permute-start.15
  387.5 7.6 %collective-permute-done.7 = f32[4,128,256]{2,1,0:T(8,128)S(1)} collective-permute-done((f32[4,128,256]{2,1,0:T(8,128)S(1)}, f32[4,128,256]{2,1,0:T(8,128)S(1)}, u32[]{:S(2)}, u32[]{:S(2)}) %collective-permute-start.7) | collective-permute-done | bytes 524320 | tf_op jit(solution)/shard_map/ppermute | solution.py:157
  395.1 2.3 collective-permute-start.13
  397.4 1.0 fusion.14
  398.4 5.2 collective-permute-done.8
  403.6 2.0 collective-permute-done.6
  405.6 1.7 slice_add_fusion.9
  407.2 0.7 slice.137
  407.9 0.6 collective-permute-start.9
  408.6 1.7 collective-permute-done.15
  410.3 0.1 collective-permute-done.13
  410.4 1.5 slice_add_fusion.8
  412.0 128.1 %all-reduce.2.cloned.1.call-done = f32[256,256]{1,0:T(8,128)} async-done(((f32[256,256]{1,0:T(8,128)}), f32[256,256]{1,0:T(8,128)}) %all-reduce.2.cloned.1.call-update) | async-done | bytes 262160 | tf_op jit(solution)/shard_map/psum | solution.py:208
  540.1 1.7 broadcast_multiply_fusion
  541.9 0.7 pad_maximum_fusion.1
  (39 shorter events, 0.4 us)
Async XLA Ops:
  7.2 172.8 %copy-start = (bf16[256,256]{1,0:T(8,128)(2,1)S(1)}, bf16[256,256]{1,0:T(8,128)(2,1)}, u32[]{:S(2)}) copy-start(bf16[256,256]{1,0:T(8,128)(2,1)} %param.7) | copy-start | bytes 393220
  7.2 128.1 %all-gather.2.cloned.1.call-start = ((), (), s32[]{:S(2)}) async-start(), calls=%async_computation | async-start | bytes 17039360 | tf_op jit(solution)/shard_map/all_gather | solution.py:191
  7.9 532.2 %all-reduce.2.cloned.1.call-start = ((), (), s32[]{:S(2)}) async-start(), calls=%async_computation.1 | async-start | bytes 524288 | tf_op jit(solution)/shard_map/psum | solution.py:208
  161.9 18.1 %copy-start.12 = (bf16[512,256]{1,0:T(8,128)(2,1)S(1)}, bf16[512,256]{1,0:T(8,128)(2,1)}, u32[]{:S(2)}) copy-start(bf16[512,256]{1,0:T(8,128)(2,1)} %param.11) | copy-start | bytes 786436
  163.0 15.8 %collective-permute-start = (f32[512,256]{1,0:T(8,128)S(1)}, f32[512,256]{1,0:T(8,128)S(1)}, u32[]{:S(2)}, u32[]{:S(2)}) collective-permute-start(f32[512,256]{1,0:T(8,128)S(1)} %constant_dynamic-slice_fusion), channel_id=1, source_target_pairs={{0,64},{64,0},{1,65},{65,1},{2,66},{66,2},{3,67},{67,3},{4,68},{68... | collective-permute-start | bytes 1572872 | tf_op jit(solution)/shard_map/ppermute | solution.py:149
  181.1 0.7 copy-start.9
  182.0 9.4 %collective-permute-start.1 = (bf16[512,256]{1,0:T(8,128)(2,1)S(1)}, bf16[512,256]{1,0:T(8,128)(2,1)S(1)}, u32[]{:S(2)}, u32[]{:S(2)}) collective-permute-start(bf16[512,256]{1,0:T(8,128)(2,1)S(1)} %convolution_convert_fusion), channel_id=1, source_target_pairs={{0,64},{64,0},{1,65},{65,1},{2,66},{66,2},{3,67},{67,3},{4,68},{68... | collective-permute-start | bytes 786440 | tf_op jit(solution)/shard_map/ppermute | solution.py:149
  228.9 25.4 %collective-permute-start.2 = (f32[128,128,256]{2,1,0:T(8,128)}, f32[128,128,256]{2,1,0:T(8,128)S(1)}, u32[]{:S(2)}, u32[]{:S(2)}) collective-permute-start(f32[128,128,256]{2,1,0:T(8,128)} %get-tuple-element.6), channel_id=1, source_target_pairs={{0,1},{1,0},{2,3},{3,2},{4,5},{5,4},{6,7},{7,6},{8,9},{9,8},{10,11... | collective-permute-start | bytes 50331656 | tf_op jit(solution)/shard_map/ppermute | solution.py:157
  254.4 15.7 %copy-start.2 = (f32[128,128,256]{2,1,0:T(8,128)}, f32[128,128,256]{2,1,0:T(8,128)S(1)}, u32[]{:S(2)}) copy-start(f32[128,128,256]{2,1,0:T(8,128)S(1)} %collective-permute-done.2) | copy-start | bytes 50331652
  270.0 49.5 %collective-permute-start.4 = (f32[16,128,256]{2,1,0:T(8,128)}, f32[16,128,256]{2,1,0:T(8,128)S(1)}, u32[]{:S(2)}, u32[]{:S(2)}) collective-permute-start(f32[16,128,256]{2,1,0:T(8,128)} %get-tuple-element.9), channel_id=1, source_target_pairs={{0,4},{1,5},{2,6},{3,7},{4,0},{5,1},{6,2},{7,3},{8,12},{9,13},{10,... | collective-permute-start | bytes 6291464 | tf_op jit(solution)/shard_map/ppermute | solution.py:157
  271.5 51.8 %collective-permute-start.12 = (f32[16,128,256]{2,1,0:T(8,128)}, f32[16,128,256]{2,1,0:T(8,128)S(1)}, u32[]{:S(2)}, u32[]{:S(2)}) collective-permute-start(f32[16,128,256]{2,1,0:T(8,128)} %get-tuple-element.10), channel_id=1, source_target_pairs={{0,48},{1,49},{2,50},{3,51},{4,52},{5,53},{6,54},{7,55},{8,56},{9,... | collective-permute-start | bytes 6291464 | tf_op jit(solution)/shard_map/ppermute | solution.py:157
  271.5 51.8 %collective-permute-start.11 = (f32[16,128,256]{2,1,0:T(8,128)}, f32[16,128,256]{2,1,0:T(8,128)S(1)}, u32[]{:S(2)}, u32[]{:S(2)}) collective-permute-start(f32[16,128,256]{2,1,0:T(8,128)} %get-tuple-element.11), channel_id=1, source_target_pairs={{0,32},{1,33},{2,34},{3,35},{4,36},{5,37},{6,38},{7,39},{8,40},{9,... | collective-permute-start | bytes 6291464 | tf_op jit(solution)/shard_map/ppermute | solution.py:157
  271.6 93.9 %collective-permute-start.10 = (f32[16,128,256]{2,1,0:T(8,128)}, f32[16,128,256]{2,1,0:T(8,128)S(1)}, u32[]{:S(2)}, u32[]{:S(2)}) collective-permute-start(f32[16,128,256]{2,1,0:T(8,128)} %get-tuple-element.12), channel_id=1, source_target_pairs={{0,16},{1,17},{2,18},{3,19},{4,20},{5,21},{6,22},{7,23},{8,24},{9,... | collective-permute-start | bytes 6291464 | tf_op jit(solution)/shard_map/ppermute | solution.py:157
  273.5 92.0 %collective-permute-start.5 = (f32[16,128,256]{2,1,0:T(8,128)}, f32[16,128,256]{2,1,0:T(8,128)S(1)}, u32[]{:S(2)}, u32[]{:S(2)}) collective-permute-start(f32[16,128,256]{2,1,0:T(8,128)} %get-tuple-element.13), channel_id=1, source_target_pairs={{0,6},{1,7},{2,0},{3,1},{4,2},{5,3},{6,4},{7,5},{8,14},{9,15},{10,... | collective-permute-start | bytes 6291464 | tf_op jit(solution)/shard_map/ppermute | solution.py:157
  319.5 46.0 %copy-start.4 = (f32[16,128,256]{2,1,0:T(8,128)}, f32[16,128,256]{2,1,0:T(8,128)S(1)}, u32[]{:S(2)}) copy-start(f32[16,128,256]{2,1,0:T(8,128)S(1)} %collective-permute-done.4) | copy-start | bytes 6291460
  319.5 48.7 %collective-permute-start.3 = (f32[16,128,256]{2,1,0:T(8,128)S(1)}, f32[16,128,256]{2,1,0:T(8,128)}, u32[]{:S(2)}, u32[]{:S(2)}) collective-permute-start(f32[16,128,256]{2,1,0:T(8,128)S(1)} %get-tuple-element.14), channel_id=1, source_target_pairs={{0,2},{1,3},{2,4},{3,5},{4,6},{5,7},{6,0},{7,1},{8,10},{9,11},{10,... | collective-permute-start | bytes 6291464 | tf_op jit(solution)/shard_map/ppermute | solution.py:157
  323.3 42.2 %copy-start.5 = (f32[16,128,256]{2,1,0:T(8,128)}, f32[16,128,256]{2,1,0:T(8,128)S(1)}, u32[]{:S(2)}) copy-start(f32[16,128,256]{2,1,0:T(8,128)S(1)} %collective-permute-done.12) | copy-start | bytes 6291460
  323.3 42.2 %copy-start.6 = (f32[16,128,256]{2,1,0:T(8,128)}, f32[16,128,256]{2,1,0:T(8,128)S(1)}, u32[]{:S(2)}) copy-start(f32[16,128,256]{2,1,0:T(8,128)S(1)} %collective-permute-done.11) | copy-start | bytes 6291460
  365.5 1.4 copy-start.7
  366.9 1.4 copy-start.8
  377.4 5.1 copy-start.3
  378.8 18.6 %copy-start.10 = (bf16[512,256]{1,0:T(8,128)(2,1)S(1)}, bf16[512,256]{1,0:T(8,128)(2,1)}, u32[]{:S(2)}) copy-start(bf16[512,256]{1,0:T(8,128)(2,1)} %copy-done.9) | copy-start | bytes 786436
  378.8 16.3 %collective-permute-start.7 = (f32[4,128,256]{2,1,0:T(8,128)S(1)}, f32[4,128,256]{2,1,0:T(8,128)S(1)}, u32[]{:S(2)}, u32[]{:S(2)}) collective-permute-start(f32[4,128,256]{2,1,0:T(8,128)S(1)} %get-tuple-element.15), channel_id=1, source_target_pairs={{0,32},{1,33},{2,34},{3,35},{4,36},{5,37},{6,38},{7,39},{8,40},{9,... | collective-permute-start | bytes 1572872 | tf_op jit(solution)/shard_map/ppermute | solution.py:157
  379.0 24.5 %collective-permute-start.8 = (f32[4,128,256]{2,1,0:T(8,128)}, f32[4,128,256]{2,1,0:T(8,128)}, u32[]{:S(2)}, u32[]{:S(2)}) collective-permute-start(f32[4,128,256]{2,1,0:T(8,128)} %get-tuple-element.16), channel_id=1, source_target_pairs={{0,48},{1,49},{2,50},{3,51},{4,52},{5,53},{6,54},{7,55},{8,56},{9,... | collective-permute-start | bytes 1572872 | tf_op jit(solution)/shard_map/ppermute | solution.py:157
  380.6 25.0 %collective-permute-start.6 = (f32[4,128,256]{2,1,0:T(8,128)}, f32[4,128,256]{2,1,0:T(8,128)}, u32[]{:S(2)}, u32[]{:S(2)}) collective-permute-start(f32[4,128,256]{2,1,0:T(8,128)} %get-tuple-element.17), channel_id=1, source_target_pairs={{0,16},{1,17},{2,18},{3,19},{4,20},{5,21},{6,22},{7,23},{8,24},{9,... | collective-permute-start | bytes 1572872 | tf_op jit(solution)/shard_map/ppermute | solution.py:157
  382.6 26.0 %collective-permute-start.14 = (f32[4,128,256]{2,1,0:T(8,128)}, f32[4,128,256]{2,1,0:T(8,128)}, u32[]{:S(2)}, u32[]{:S(2)}) collective-permute-start(f32[4,128,256]{2,1,0:T(8,128)} %get-tuple-element.18), channel_id=1, source_target_pairs={{0,4},{1,5},{2,6},{3,7},{4,0},{5,1},{6,2},{7,3},{8,12},{9,13},{10,... | collective-permute-start | bytes 1572872 | tf_op jit(solution)/shard_map/ppermute | solution.py:157
  384.8 25.5 %collective-permute-start.15 = (f32[4,128,256]{2,1,0:T(8,128)}, f32[4,128,256]{2,1,0:T(8,128)}, u32[]{:S(2)}, u32[]{:S(2)}) collective-permute-start(f32[4,128,256]{2,1,0:T(8,128)} %get-tuple-element.19), channel_id=1, source_target_pairs={{0,6},{1,7},{2,0},{3,1},{4,2},{5,3},{6,4},{7,5},{8,14},{9,15},{10,... | collective-permute-start | bytes 1572872 | tf_op jit(solution)/shard_map/ppermute | solution.py:157
  395.1 8.5 %copy-start.11 = (f32[4,128,256]{2,1,0:T(8,128)}, f32[4,128,256]{2,1,0:T(8,128)S(1)}, u32[]{:S(2)}) copy-start(f32[4,128,256]{2,1,0:T(8,128)S(1)} %collective-permute-done.7) | copy-start | bytes 1572868
  395.1 15.3 %collective-permute-start.13 = (f32[4,128,256]{2,1,0:T(8,128)}, f32[4,128,256]{2,1,0:T(8,128)}, u32[]{:S(2)}, u32[]{:S(2)}) collective-permute-start(f32[4,128,256]{2,1,0:T(8,128)} %get-tuple-element.20), channel_id=1, source_target_pairs={{0,2},{1,3},{2,4},{3,5},{4,6},{5,7},{6,0},{7,1},{8,10},{9,11},{10,... | collective-permute-start | bytes 1572872 | tf_op jit(solution)/shard_map/ppermute | solution.py:157
  407.9 133.9 %collective-permute-start.9 = (f32[2,128,256]{2,1,0:T(8,128)}, f32[2,128,256]{2,1,0:T(8,128)S(1)}, u32[]{:S(2)}, u32[]{:S(2)}) collective-permute-start(f32[2,128,256]{2,1,0:T(8,128)} %slice.137), channel_id=1, source_target_pairs={{0,8},{1,9},{2,10},{3,11},{4,12},{5,13},{6,14},{7,15},{8,0},{9,1},... | collective-permute-start | bytes 786440 | tf_op jit(solution)/shard_map/ppermute | solution.py:157
  410.4 132.3 %copy-start.1 = (bf16[256,256]{1,0:T(8,128)(2,1)S(1)}, bf16[256,256]{1,0:T(8,128)(2,1)}, u32[]{:S(2)}) copy-start(bf16[256,256]{1,0:T(8,128)(2,1)} %param.7) | copy-start | bytes 393220
  411.9 129.9 %collective-permute-start.16 = (f32[2,128,256]{2,1,0:T(8,128)S(1)}, f32[2,128,256]{2,1,0:T(8,128)S(1)}, u32[]{:S(2)}, u32[]{:S(2)}) collective-permute-start(f32[2,128,256]{2,1,0:T(8,128)S(1)} %slice.151), channel_id=1, source_target_pairs={{0,8},{1,9},{2,10},{3,11},{4,12},{5,13},{6,14},{7,15},{8,0},{9,1},... | collective-permute-start | bytes 786440 | tf_op jit(solution)/shard_map/ppermute | solution.py:157
Sparse Core Ops, SparseCore 0:
  9.7 125.4 all-gather.1
  398.5 141.5 all-reduce.1

commit v5 on v4

--- a/solution.py
+++ b/solution.py
@@ -205,7 +205,9 @@
     local_grad = jnp.dot(aggregated.T, pre_grad, preferred_element_type=jnp.float32)
     own_grad = jnp.dot(pre_grad, weight.T, preferred_element_type=jnp.float32).astype(jnp.bfloat16)
     both_grad = jnp.stack([own_grad, swap(own_grad, "grp")]).reshape(2, -1, block, width)
-    weight_grad = lax.psum(local_grad, ("grp", "row")) * (1.0 / math.sqrt(verts))
+    weight_grad = all_sum(all_sum(local_grad, "grp"), "row")
+    weight_grad, both_grad = lax.optimization_barrier((weight_grad, both_grad))
+    weight_grad = weight_grad * (1.0 / math.sqrt(verts))
 
     where = jnp.stack([side, lax.axis_index("row")]).astype(jnp.int32)
     keep, send = spread(where, cols, count, vals, both_grad, col_blocks)

time: 550 us -> 469 us (0.85)
  waiting for transfers between devices: 401 us -> 332 us
  Pallas kernels: 63.3 us -> 26.1 us
  starting transfers between devices: 27.7 us -> 59.6 us
    psum x1 -> x0, waiting for transfers between devices: 128 us -> none  [body(): lax.psum(local_grad, ('grp', 'row')) * (1.0 / math.sqrt(verts))]
    ppermute x0 -> x7, waiting for transfers between devices: none -> 37.6 us  [all_sum(): lax.ppermute(value, axis, [(i, i ^ step) for i in range(size)])]
    ppermute x15, waiting for transfers between devices: 126 us -> 153 us  [shifted(): return lax.ppermute(value, 'row', [(r, dest(r)) for r in range(64)])]
    pallas_call x1, Pallas kernels: 36.7 us -> 15.9 us  [spread(): pl.pallas_call(spread_kernel, out_shape=[jax.ShapeDtypeStruct((col_blocks...]
    ppermute x0 -> x7, starting transfers between devices: none -> 18.7 us  [all_sum(): lax.ppermute(value, axis, [(i, i ^ step) for i in range(size)])]
    pallas_call x1, Pallas kernels: 26.6 us -> 10.2 us  [aggregate(): pl.pallas_call(aggregate_kernel, out_shape=jax.ShapeDtypeStruct((row_bloc...]
    ppermute x15, starting transfers between devices: 22.1 us -> 30.4 us  [shifted(): return lax.ppermute(value, 'row', [(r, dest(r)) for r in range(64)])]
  transfers between devices with their start and end apart: 19 -> 25, of which waited for: 12 -> 21; matrix products, arithmetic and copies ran while one was open for 2% -> 1% of each run, Pallas kernels for 0% -> 0%
where the time goes in v5:
time: 469 us; the launch traced here: 468 us
  waiting for transfers between devices  332 us (71%)
  starting transfers between devices  59.6 us (13%)
  other arithmetic  29.3 us (6%)
  Pallas kernels  26.1 us (6%)
  between operations  14.3 us (3%)
    ppermute x15, waiting for transfers between devices, shifted(): return lax.ppermute(value, 'row', [(r, dest(r)) for r in range(64)])  153 us
    all_gather x1, waiting for transfers between devices, body(): gathered = lax.all_gather(features, 'row', axis=0, tiled=True)  127 us
    ppermute x7, waiting for transfers between devices, all_sum(): lax.ppermute(value, axis, [(i, i ^ step) for i in range(size)])  37.6 us
    ppermute x15, starting transfers between devices, shifted(): return lax.ppermute(value, 'row', [(r, dest(r)) for r in range(64)])  30.4 us
    ppermute x7, starting transfers between devices, all_sum(): lax.ppermute(value, axis, [(i, i ^ step) for i in range(size)])  18.7 us
    pallas_call x1, Pallas kernels, spread(): pl.pallas_call(spread_kernel, out_shape=[jax.ShapeDtypeStruct((col_blocks...  15.9 us
    add x1, other arithmetic, row_reduce_scatter(): first = [keep[0, s] + came[0, s] for s in range(4)]  15.9 us
    ppermute x2, waiting for transfers between devices, swap(): return lax.ppermute(value, axis, [(i, i ^ 1) for i in range(size)])  13.7 us
  transfers between devices with their start and end apart: 25, of which 21 were waited for; matrix products, arithmetic and copies ran while one was open for 1% of the time, Pallas kernels for 0%

profile of v5, /device:TPU:0, one launch (start us, length us, event | category | flops | bytes accessed | tf_op | source)
XLA Modules:
  0.0 467.5 jit_solution(8503286862774509999)
XLA Ops:
  7.2 0.7 all-gather.2.cloned.1.call-update
  7.9 127.3 %all-gather.2.cloned.1.call-done.panel_hbm = bf16[32768,256]{1,0:T(8,128)(2,1)} async-done(((bf16[512,256]{1,0:T(8,128)(2,1)}), bf16[32768,256]{1,0:T(8,128)(2,1)}) %all-gather.2.cloned.1.call-update) | async-done | bytes 16777232 | tf_op jit(solution)/shard_map/all_gather | solution.py:191
  135.3 10.2 %shard_map.85 = f32[8,128,256]{2,1,0:T(8,128)} custom-call(s32[8,16]{1,0:T(8,128)} %bitcast.48, s32[8]{0:T(128)} %bitcast.50, bf16[8,16,128,128]{3,2,1,0:T(8,128)(2,1)} %bitcast.41, bf16[32768,256]{1,0:T(8,128)(2,1)} %all-gather.2.cloned.1.call-done.panel_hbm), custom_call_target="tpu_custom_call" | custom-call | flops 1073741824 | bytes 22020096 | tf_op jit(solution)/shard_map/pallas_call | solution.py:95
  145.4 1.1 constant_dynamic-slice_fusion
  146.6 9.4 %collective-permute-start = (f32[512,256]{1,0:T(8,128)S(1)}, f32[512,256]{1,0:T(8,128)S(1)}, u32[]{:S(2)}, u32[]{:S(2)}) collective-permute-start(f32[512,256]{1,0:T(8,128)S(1)} %constant_dynamic-slice_fusion), channel_id=1, source_target_pairs={{0,64},{64,0},{1,65},{65,1},{2,66},{66,2},{3,67},{67,3},{4,68},{68... | collective-permute-start | bytes 1572872 | tf_op jit(solution)/shard_map/ppermute | solution.py:149
  156.0 11.7 %collective-permute-done = f32[512,256]{1,0:T(8,128)S(1)} collective-permute-done((f32[512,256]{1,0:T(8,128)S(1)}, f32[512,256]{1,0:T(8,128)S(1)}, u32[]{:S(2)}, u32[]{:S(2)}) %collective-permute-start) | collective-permute-done | bytes 524320 | tf_op jit(solution)/shard_map/ppermute | solution.py:149
  167.7 1.1 add_convert_fusion
  168.8 1.1 multiply_convert_fusion
  170.2 2.5 collective-permute-start.1
  172.7 8.2 %collective-permute-done.1 = f32[256,256]{1,0:T(8,128)S(1)} collective-permute-done((f32[256,256]{1,0:T(8,128)S(1)}, f32[256,256]{1,0:T(8,128)S(1)}, u32[]{:S(2)}, u32[]{:S(2)}) %collective-permute-start.1) | collective-permute-done | bytes 262176 | tf_op jit(solution)/shard_map/ppermute | solution.py:179
  181.1 1.5 collective-permute-done.2
  182.6 6.9 %collective-permute-start.3 = (f32[256,256]{1,0:T(8,128)S(1)}, f32[256,256]{1,0:T(8,128)S(1)}, u32[]{:S(2)}, u32[]{:S(2)}) collective-permute-start(f32[256,256]{1,0:T(8,128)S(1)} %add.134), channel_id=1, source_target_pairs={{0,2},{1,3},{2,0},{3,1},{4,6},{5,7},{6,4},{7,5},{8,10},{9,11},{10,... | collective-permute-start | bytes 786440 | tf_op jit(solution)/shard_map/ppermute | solution.py:179
  189.5 6.6 %collective-permute-done.3 = f32[256,256]{1,0:T(8,128)S(1)} collective-permute-done((f32[256,256]{1,0:T(8,128)S(1)}, f32[256,256]{1,0:T(8,128)S(1)}, u32[]{:S(2)}, u32[]{:S(2)}) %collective-permute-start.3) | collective-permute-done | bytes 262176 | tf_op jit(solution)/shard_map/ppermute | solution.py:179
  196.2 5.3 %collective-permute-start.4 = (f32[256,256]{1,0:T(8,128)S(1)}, f32[256,256]{1,0:T(8,128)S(1)}, u32[]{:S(2)}, u32[]{:S(2)}) collective-permute-start(f32[256,256]{1,0:T(8,128)S(1)} %add.135), channel_id=1, source_target_pairs={{0,4},{1,5},{2,6},{3,7},{4,0},{5,1},{6,2},{7,3},{8,12},{9,13},{10,... | collective-permute-start | bytes 786440 | tf_op jit(solution)/shard_map/ppermute | solution.py:179
  201.4 5.8 %collective-permute-done.4 = f32[256,256]{1,0:T(8,128)S(1)} collective-permute-done((f32[256,256]{1,0:T(8,128)S(1)}, f32[256,256]{1,0:T(8,128)S(1)}, u32[]{:S(2)}, u32[]{:S(2)}) %collective-permute-start.4) | collective-permute-done | bytes 262176 | tf_op jit(solution)/shard_map/ppermute | solution.py:179
  207.4 6.9 %collective-permute-done.5 = f32[256,256]{1,0:T(8,128)S(1)} collective-permute-done((f32[256,256]{1,0:T(8,128)S(1)}, f32[256,256]{1,0:T(8,128)S(1)}, u32[]{:S(2)}, u32[]{:S(2)}) %collective-permute-start.5) | collective-permute-done | bytes 262176 | tf_op jit(solution)/shard_map/ppermute | solution.py:179
  214.3 3.7 collective-permute-start.6
  218.2 1.0 collective-permute-start.8
  219.2 4.2 collective-permute-done.6
  223.6 0.6 pad_add_fusion.side_ref
  224.2 2.0 collective-permute-done.8
  226.2 0.9 pad_maximum_fusion.grad_ref
  227.0 4.4 collective-permute-done.7
  231.5 15.9 %shard_map.86 = (f32[128,128,256]{2,1,0:T(8,128)}, f32[128,128,256]{2,1,0:T(8,128)}) custom-call(s32[2]{0:T(128)} %pad_add_fusion.side_ref, s32[8,16]{1,0:T(8,128)} %bitcast.49, s32[8]{0:T(128)} %bitcast.51, bf16[8,16,128,128]{3,2,1,0:T(8,128)(2,1)} %bitcast.42, bf16[2,4,128,256]{3,2,1,0:T(8,128)(2,1)} %pad_maximum_fusion.grad_ref), custom_call_target="tpu_custom_call" | custom-call | flops 1073741824 | bytes 38273024 | tf_op jit(solution)/shard_map/pallas_call | solution.py:122
  247.4 4.6 collective-permute-start.9
  252.0 25.0 %collective-permute-done.9 = f32[128,128,256]{2,1,0:T(8,128)S(1)} collective-permute-done((f32[128,128,256]{2,1,0:T(8,128)}, f32[128,128,256]{2,1,0:T(8,128)S(1)}, u32[]{:S(2)}, u32[]{:S(2)}) %collective-permute-start.9) | collective-permute-done | bytes 16777248 | tf_op jit(solution)/shard_map/ppermute | solution.py:157
  277.0 15.9 %fusion.6 = (f32[16,128,256]{2,1,0:T(8,128)}, f32[16,128,256]{2,1,0:T(8,128)}, f32[16,128,256]{2,1,0:T(8,128)}, f32[16,128,256]{2,1,0:T(8,128)}, f32[16,128,256]{2,1,0:T(8,128)}, /*index=5*/f32[16,128,256]{2,1,0:T(8,128)}) fusion(f32[2,4,16,128,256]{4,3,2,1,0:T(8,128)S(1)} %bitcast.39, f32[2,4,16,128,256]{4,3,2,1,0:T(8,128)} %bitcast.37), kind=kLoop, calls=%fused_computation.12 | loop fusion | flops 3145728 | bytes 37748736 | tf_op jit(solution)/shard_map/add | solution.py:164
  292.9 20.4 %collective-permute-start.11 = (f32[16,128,256]{2,1,0:T(8,128)}, f32[16,128,256]{2,1,0:T(8,128)S(1)}, u32[]{:S(2)}, u32[]{:S(2)}) collective-permute-start(f32[16,128,256]{2,1,0:T(8,128)} %get-tuple-element.13), channel_id=1, source_target_pairs={{0,4},{1,5},{2,6},{3,7},{4,0},{5,1},{6,2},{7,3},{8,12},{9,13},{10,... | collective-permute-start | bytes 6291464 | tf_op jit(solution)/shard_map/ppermute | solution.py:157
  313.3 2.0 collective-permute-start.17
  315.3 44.1 %collective-permute-done.11 = f32[16,128,256]{2,1,0:T(8,128)S(1)} collective-permute-done((f32[16,128,256]{2,1,0:T(8,128)}, f32[16,128,256]{2,1,0:T(8,128)S(1)}, u32[]{:S(2)}, u32[]{:S(2)}) %collective-permute-start.11) | collective-permute-done | bytes 2097184 | tf_op jit(solution)/shard_map/ppermute | solution.py:157
  359.5 2.6 collective-permute-done.19
  362.0 1.5 collective-permute-done.18
  363.6 43.8 %collective-permute-done.17 = f32[16,128,256]{2,1,0:T(8,128)S(1)} collective-permute-done((f32[16,128,256]{2,1,0:T(8,128)}, f32[16,128,256]{2,1,0:T(8,128)S(1)}, u32[]{:S(2)}, u32[]{:S(2)}) %collective-permute-start.17) | collective-permute-done | bytes 2097184 | tf_op jit(solution)/shard_map/ppermute | solution.py:157
  407.4 1.3 copy-done.5
  408.7 1.4 copy-done.6
  410.1 8.7 %fusion.9 = (f32[16,128,256]{2,1,0:T(8,128)S(1)}, f32[16,128,256]{2,1,0:T(8,128)S(1)}) fusion(f32[2,4,16,128,256]{4,3,2,1,0:T(8,128)} %bitcast.40, f32[2,4,16,128,256]{4,3,2,1,0:T(8,128)} %bitcast.38, f32[16,128,256]{2,1,0:T(8,128)} %copy-done.6, f32[16,128,256]{2,1,0:T(8,128)} %collective-permute-done.10, f32[16,128,256]{2,1,0:T(8,128)S(1)} %collective-permute-done.11, ...), kind=kLoop, calls=%fused_computation.17 | loop fusion | flops 4194304 | bytes 25165824 | tf_op jit(solution)/shard_map/add | solution.py:166
  419.0 0.4 collective-permute-start.14
  419.4 1.6 collective-permute-start.15
  420.9 0.8 collective-permute-start.13
  421.9 0.4 collective-permute-start.21
  422.4 13.0 %collective-permute-done.14 = f32[4,128,256]{2,1,0:T(8,128)S(1)} collective-permute-done((f32[4,128,256]{2,1,0:T(8,128)S(1)}, f32[4,128,256]{2,1,0:T(8,128)S(1)}, u32[]{:S(2)}, u32[]{:S(2)}) %collective-permute-start.14) | collective-permute-done | bytes 524320 | tf_op jit(solution)/shard_map/ppermute | solution.py:157
  435.4 8.4 %collective-permute-done.15 = f32[4,128,256]{2,1,0:T(8,128)S(1)} collective-permute-done((f32[4,128,256]{2,1,0:T(8,128)S(1)}, f32[4,128,256]{2,1,0:T(8,128)S(1)}, u32[]{:S(2)}, u32[]{:S(2)}) %collective-permute-start.15) | collective-permute-done | bytes 524320 | tf_op jit(solution)/shard_map/ppermute | solution.py:157
  443.8 2.0 collective-permute-done.13
  446.1 2.8 collective-permute-done.20
  449.2 0.7 broadcast_multiply_fusion
  449.9 5.3 %collective-permute-done.16 = f32[2,128,256]{2,1,0:T(8,128)S(1)} collective-permute-done((f32[2,128,256]{2,1,0:T(8,128)S(1)}, f32[2,128,256]{2,1,0:T(8,128)S(1)}, u32[]{:S(2)}, u32[]{:S(2)}) %collective-permute-start.16) | collective-permute-done | bytes 262176 | tf_op jit(solution)/shard_map/ppermute | solution.py:157
  455.3 4.6 collective-permute-done.23
  459.9 0.7 pad_maximum_fusion.1
  (47 shorter events, 2.1 us)
Async XLA Ops:
  7.2 161.6 %copy-start = (bf16[256,256]{1,0:T(8,128)(2,1)S(1)}, bf16[256,256]{1,0:T(8,128)(2,1)}, u32[]{:S(2)}) copy-start(bf16[256,256]{1,0:T(8,128)(2,1)} %param.7) | copy-start | bytes 393220
  7.2 128.1 %all-gather.2.cloned.1.call-start = ((), (), s32[]{:S(2)}) async-start(), calls=%async_computation | async-start | bytes 17039360 | tf_op jit(solution)/shard_map/all_gather | solution.py:191
  145.4 23.4 %copy-start.7 = (bf16[512,256]{1,0:T(8,128)(2,1)S(1)}, bf16[512,256]{1,0:T(8,128)(2,1)}, u32[]{:S(2)}) copy-start(bf16[512,256]{1,0:T(8,128)(2,1)} %param.11) | copy-start | bytes 786436
  146.6 21.1 %collective-permute-start = (f32[512,256]{1,0:T(8,128)S(1)}, f32[512,256]{1,0:T(8,128)S(1)}, u32[]{:S(2)}, u32[]{:S(2)}) collective-permute-start(f32[512,256]{1,0:T(8,128)S(1)} %constant_dynamic-slice_fusion), channel_id=1, source_target_pairs={{0,64},{64,0},{1,65},{65,1},{2,66},{66,2},{3,67},{67,3},{4,68},{68... | collective-permute-start | bytes 1572872 | tf_op jit(solution)/shard_map/ppermute | solution.py:149
  170.2 10.7 %collective-permute-start.1 = (f32[256,256]{1,0:T(8,128)S(1)}, f32[256,256]{1,0:T(8,128)S(1)}, u32[]{:S(2)}, u32[]{:S(2)}) collective-permute-start(f32[256,256]{1,0:T(8,128)S(1)} %fusion.14), channel_id=1, source_target_pairs={{0,64},{64,0},{1,65},{65,1},{2,66},{66,2},{3,67},{67,3},{4,68},{68... | collective-permute-start | bytes 786440 | tf_op jit(solution)/shard_map/ppermute | solution.py:179
  180.9 1.6 collective-permute-start.2
  182.6 13.5 %collective-permute-start.3 = (f32[256,256]{1,0:T(8,128)S(1)}, f32[256,256]{1,0:T(8,128)S(1)}, u32[]{:S(2)}, u32[]{:S(2)}) collective-permute-start(f32[256,256]{1,0:T(8,128)S(1)} %add.134), channel_id=1, source_target_pairs={{0,2},{1,3},{2,0},{3,1},{4,6},{5,7},{6,4},{7,5},{8,10},{9,11},{10,... | collective-permute-start | bytes 786440 | tf_op jit(solution)/shard_map/ppermute | solution.py:179
  196.2 11.1 %collective-permute-start.4 = (f32[256,256]{1,0:T(8,128)S(1)}, f32[256,256]{1,0:T(8,128)S(1)}, u32[]{:S(2)}, u32[]{:S(2)}) collective-permute-start(f32[256,256]{1,0:T(8,128)S(1)} %add.135), channel_id=1, source_target_pairs={{0,4},{1,5},{2,6},{3,7},{4,0},{5,1},{6,2},{7,3},{8,12},{9,13},{10,... | collective-permute-start | bytes 786440 | tf_op jit(solution)/shard_map/ppermute | solution.py:179
  207.3 7.0 %collective-permute-start.5 = (f32[256,256]{1,0:T(8,128)S(1)}, f32[256,256]{1,0:T(8,128)S(1)}, u32[]{:S(2)}, u32[]{:S(2)}) collective-permute-start(f32[256,256]{1,0:T(8,128)S(1)} %add.136), channel_id=1, source_target_pairs={{0,8},{1,9},{2,10},{3,11},{4,12},{5,13},{6,14},{7,15},{8,0},{9,1},... | collective-permute-start | bytes 786440 | tf_op jit(solution)/shard_map/ppermute | solution.py:179
  214.3 9.2 %collective-permute-start.6 = (f32[256,256]{1,0:T(8,128)S(1)}, f32[256,256]{1,0:T(8,128)S(1)}, u32[]{:S(2)}, u32[]{:S(2)}) collective-permute-start(f32[256,256]{1,0:T(8,128)S(1)} %add.137), channel_id=1, source_target_pairs={{0,16},{1,17},{2,18},{3,19},{4,20},{5,21},{6,22},{7,23},{8,24},{9,... | collective-permute-start | bytes 786440 | tf_op jit(solution)/shard_map/ppermute | solution.py:179
  218.2 8.0 %collective-permute-start.8 = (bf16[512,256]{1,0:T(8,128)(2,1)S(1)}, bf16[512,256]{1,0:T(8,128)(2,1)S(1)}, u32[]{:S(2)}, u32[]{:S(2)}) collective-permute-start(bf16[512,256]{1,0:T(8,128)(2,1)S(1)} %convolution_convert_fusion), channel_id=1, source_target_pairs={{0,64},{64,0},{1,65},{65,1},{2,66},{66,2},{3,67},{67,3},{4,68},{68... | collective-permute-start | bytes 786440 | tf_op jit(solution)/shard_map/ppermute | solution.py:149
  223.5 8.0 %collective-permute-start.7 = (f32[256,256]{1,0:T(8,128)S(1)}, f32[256,256]{1,0:T(8,128)S(1)}, u32[]{:S(2)}, u32[]{:S(2)}) collective-permute-start(f32[256,256]{1,0:T(8,128)S(1)} %add.138), channel_id=1, source_target_pairs={{0,32},{1,33},{2,34},{3,35},{4,36},{5,37},{6,38},{7,39},{8,40},{9,... | collective-permute-start | bytes 786440 | tf_op jit(solution)/shard_map/ppermute | solution.py:179
  247.4 29.6 %collective-permute-start.9 = (f32[128,128,256]{2,1,0:T(8,128)}, f32[128,128,256]{2,1,0:T(8,128)S(1)}, u32[]{:S(2)}, u32[]{:S(2)}) collective-permute-start(f32[128,128,256]{2,1,0:T(8,128)} %get-tuple-element.10), channel_id=1, source_target_pairs={{0,1},{1,0},{2,3},{3,2},{4,5},{5,4},{6,7},{7,6},{8,9},{9,8},{10,11... | collective-permute-start | bytes 50331656 | tf_op jit(solution)/shard_map/ppermute | solution.py:157
  277.0 15.9 %copy-start.2 = (f32[128,128,256]{2,1,0:T(8,128)}, f32[128,128,256]{2,1,0:T(8,128)S(1)}, u32[]{:S(2)}) copy-start(f32[128,128,256]{2,1,0:T(8,128)S(1)} %collective-permute-done.9) | copy-start | bytes 50331652
  292.9 66.6 %collective-permute-start.11 = (f32[16,128,256]{2,1,0:T(8,128)}, f32[16,128,256]{2,1,0:T(8,128)S(1)}, u32[]{:S(2)}, u32[]{:S(2)}) collective-permute-start(f32[16,128,256]{2,1,0:T(8,128)} %get-tuple-element.13), channel_id=1, source_target_pairs={{0,4},{1,5},{2,6},{3,7},{4,0},{5,1},{6,2},{7,3},{8,12},{9,13},{10,... | collective-permute-start | bytes 6291464 | tf_op jit(solution)/shard_map/ppermute | solution.py:157
  313.3 48.7 %collective-permute-start.19 = (f32[16,128,256]{2,1,0:T(8,128)}, f32[16,128,256]{2,1,0:T(8,128)S(1)}, u32[]{:S(2)}, u32[]{:S(2)}) collective-permute-start(f32[16,128,256]{2,1,0:T(8,128)} %get-tuple-element.14), channel_id=1, source_target_pairs={{0,48},{1,49},{2,50},{3,51},{4,52},{5,53},{6,54},{7,55},{8,56},{9,... | collective-permute-start | bytes 6291464 | tf_op jit(solution)/shard_map/ppermute | solution.py:157
  313.3 50.3 %collective-permute-start.18 = (f32[16,128,256]{2,1,0:T(8,128)}, f32[16,128,256]{2,1,0:T(8,128)S(1)}, u32[]{:S(2)}, u32[]{:S(2)}) collective-permute-start(f32[16,128,256]{2,1,0:T(8,128)} %get-tuple-element.15), channel_id=1, source_target_pairs={{0,32},{1,33},{2,34},{3,35},{4,36},{5,37},{6,38},{7,39},{8,40},{9,... | collective-permute-start | bytes 6291464 | tf_op jit(solution)/shard_map/ppermute | solution.py:157
  313.3 94.0 %collective-permute-start.17 = (f32[16,128,256]{2,1,0:T(8,128)}, f32[16,128,256]{2,1,0:T(8,128)S(1)}, u32[]{:S(2)}, u32[]{:S(2)}) collective-permute-start(f32[16,128,256]{2,1,0:T(8,128)} %get-tuple-element.16), channel_id=1, source_target_pairs={{0,16},{1,17},{2,18},{3,19},{4,20},{5,21},{6,22},{7,23},{8,24},{9,... | collective-permute-start | bytes 6291464 | tf_op jit(solution)/shard_map/ppermute | solution.py:157
  315.3 92.0 %collective-permute-start.12 = (f32[16,128,256]{2,1,0:T(8,128)}, f32[16,128,256]{2,1,0:T(8,128)S(1)}, u32[]{:S(2)}, u32[]{:S(2)}) collective-permute-start(f32[16,128,256]{2,1,0:T(8,128)} %get-tuple-element.17), channel_id=1, source_target_pairs={{0,6},{1,7},{2,0},{3,1},{4,2},{5,3},{6,4},{7,5},{8,14},{9,15},{10,... | collective-permute-start | bytes 6291464 | tf_op jit(solution)/shard_map/ppermute | solution.py:157
  359.4 50.7 %collective-permute-start.10 = (f32[16,128,256]{2,1,0:T(8,128)}, f32[16,128,256]{2,1,0:T(8,128)}, u32[]{:S(2)}, u32[]{:S(2)}) collective-permute-start(f32[16,128,256]{2,1,0:T(8,128)} %get-tuple-element.18), channel_id=1, source_target_pairs={{0,2},{1,3},{2,4},{3,5},{4,6},{5,7},{6,0},{7,1},{8,10},{9,11},{10,... | collective-permute-start | bytes 6291464 | tf_op jit(solution)/shard_map/ppermute | solution.py:157
  362.0 45.3 %copy-start.3 = (f32[16,128,256]{2,1,0:T(8,128)}, f32[16,128,256]{2,1,0:T(8,128)S(1)}, u32[]{:S(2)}) copy-start(f32[16,128,256]{2,1,0:T(8,128)S(1)} %collective-permute-done.19) | copy-start | bytes 6291460
  363.6 43.8 %copy-start.4 = (f32[16,128,256]{2,1,0:T(8,128)}, f32[16,128,256]{2,1,0:T(8,128)S(1)}, u32[]{:S(2)}) copy-start(f32[16,128,256]{2,1,0:T(8,128)S(1)} %collective-permute-done.18) | copy-start | bytes 6291460
  407.4 1.4 copy-start.5
  408.7 1.4 copy-start.6
  419.0 16.4 %collective-permute-start.14 = (f32[4,128,256]{2,1,0:T(8,128)S(1)}, f32[4,128,256]{2,1,0:T(8,128)S(1)}, u32[]{:S(2)}, u32[]{:S(2)}) collective-permute-start(f32[4,128,256]{2,1,0:T(8,128)S(1)} %get-tuple-element.19), channel_id=1, source_target_pairs={{0,32},{1,33},{2,34},{3,35},{4,36},{5,37},{6,38},{7,39},{8,40},{9,... | collective-permute-start | bytes 1572872 | tf_op jit(solution)/shard_map/ppermute | solution.py:157
  419.4 24.4 %collective-permute-start.15 = (f32[4,128,256]{2,1,0:T(8,128)S(1)}, f32[4,128,256]{2,1,0:T(8,128)S(1)}, u32[]{:S(2)}, u32[]{:S(2)}) collective-permute-start(f32[4,128,256]{2,1,0:T(8,128)S(1)} %get-tuple-element.20), channel_id=1, source_target_pairs={{0,48},{1,49},{2,50},{3,51},{4,52},{5,53},{6,54},{7,55},{8,56},{9,... | collective-permute-start | bytes 1572872 | tf_op jit(solution)/shard_map/ppermute | solution.py:157
  420.9 24.8 %collective-permute-start.13 = (f32[4,128,256]{2,1,0:T(8,128)S(1)}, f32[4,128,256]{2,1,0:T(8,128)S(1)}, u32[]{:S(2)}, u32[]{:S(2)}) collective-permute-start(f32[4,128,256]{2,1,0:T(8,128)S(1)} %get-tuple-element.21), channel_id=1, source_target_pairs={{0,16},{1,17},{2,18},{3,19},{4,20},{5,21},{6,22},{7,23},{8,24},{9,... | collective-permute-start | bytes 1572872 | tf_op jit(solution)/shard_map/ppermute | solution.py:157
  421.9 24.1 %collective-permute-start.21 = (f32[4,128,256]{2,1,0:T(8,128)S(1)}, f32[4,128,256]{2,1,0:T(8,128)S(1)}, u32[]{:S(2)}, u32[]{:S(2)}) collective-permute-start(f32[4,128,256]{2,1,0:T(8,128)S(1)} %get-tuple-element.22), channel_id=1, source_target_pairs={{0,4},{1,5},{2,6},{3,7},{4,0},{5,1},{6,2},{7,3},{8,12},{9,13},{10,... | collective-permute-start | bytes 1572872 | tf_op jit(solution)/shard_map/ppermute | solution.py:157
  422.4 23.7 %collective-permute-start.22 = (f32[4,128,256]{2,1,0:T(8,128)S(1)}, f32[4,128,256]{2,1,0:T(8,128)S(1)}, u32[]{:S(2)}, u32[]{:S(2)}) collective-permute-start(f32[4,128,256]{2,1,0:T(8,128)S(1)} %get-tuple-element.23), channel_id=1, source_target_pairs={{0,6},{1,7},{2,0},{3,1},{4,2},{5,3},{6,4},{7,5},{8,14},{9,15},{10,... | collective-permute-start | bytes 1572872 | tf_op jit(solution)/shard_map/ppermute | solution.py:157
  435.4 13.5 %collective-permute-start.20 = (f32[4,128,256]{2,1,0:T(8,128)S(1)}, f32[4,128,256]{2,1,0:T(8,128)S(1)}, u32[]{:S(2)}, u32[]{:S(2)}) collective-permute-start(f32[4,128,256]{2,1,0:T(8,128)S(1)} %get-tuple-element.24), channel_id=1, source_target_pairs={{0,2},{1,3},{2,4},{3,5},{4,6},{5,7},{6,0},{7,1},{8,10},{9,11},{10,... | collective-permute-start | bytes 1572872 | tf_op jit(solution)/shard_map/ppermute | solution.py:157
  446.0 9.2 %collective-permute-start.16 = (f32[2,128,256]{2,1,0:T(8,128)S(1)}, f32[2,128,256]{2,1,0:T(8,128)S(1)}, u32[]{:S(2)}, u32[]{:S(2)}) collective-permute-start(f32[2,128,256]{2,1,0:T(8,128)S(1)} %slice.137), channel_id=1, source_target_pairs={{0,8},{1,9},{2,10},{3,11},{4,12},{5,13},{6,14},{7,15},{8,0},{9,1},... | collective-permute-start | bytes 786440 | tf_op jit(solution)/shard_map/ppermute | solution.py:157
  448.9 11.8 %copy-start.1 = (bf16[256,256]{1,0:T(8,128)(2,1)S(1)}, bf16[256,256]{1,0:T(8,128)(2,1)}, u32[]{:S(2)}) copy-start(bf16[256,256]{1,0:T(8,128)(2,1)} %param.7) | copy-start | bytes 393220
  449.1 10.8 %collective-permute-start.23 = (f32[2,128,256]{2,1,0:T(8,128)S(1)}, f32[2,128,256]{2,1,0:T(8,128)S(1)}, u32[]{:S(2)}, u32[]{:S(2)}) collective-permute-start(f32[2,128,256]{2,1,0:T(8,128)S(1)} %slice.151), channel_id=1, source_target_pairs={{0,8},{1,9},{2,10},{3,11},{4,12},{5,13},{6,14},{7,15},{8,0},{9,1},... | collective-permute-start | bytes 786440 | tf_op jit(solution)/shard_map/ppermute | solution.py:157
Sparse Core Ops, SparseCore 0:
  9.7 125.4 all-gather.1

commit v6 on v4

--- a/solution.py
+++ b/solution.py
@@ -50,7 +50,7 @@
     return (dk * 2 + half) * 64 + ((first * 4 + second) * 2 + dy) * 2 + q2
 
 
-def spread_kernel(side_ref, cols_ref, count_ref, vals_hbm, grad_ref, keep_hbm, send_hbm, vals, total, sems):
+def spread_kernel(side_ref, cols_ref, count_ref, vals_hbm, grad_ref, extra_ref, keep_hbm, send_hbm, vals, total, sems):
     row_blocks, slot_total, block, _ = vals.shape
     per_panel = grad_ref.shape[1]
     col_blocks = total.shape[0]
@@ -82,11 +82,14 @@
         lax.fori_loop(0, live, body, 0)
     half = col_blocks // 2
     keep = pltpu.make_async_copy(total.at[pl.ds(0, half)], keep_hbm, sems.at[1])
-    send = pltpu.make_async_copy(total.at[pl.ds(half, half)], send_hbm, sems.at[2])
+    send = pltpu.make_async_copy(total.at[pl.ds(half, half)], send_hbm.at[pl.ds(0, half)], sems.at[2])
+    tail = pltpu.make_async_copy(extra_ref, send_hbm.at[pl.ds(half, extra_ref.shape[0])], sems.at[3])
     send.start()
     keep.start()
+    tail.start()
     send.wait()
     keep.wait()
+    tail.wait()
 
 
 def aggregate(cols, count, vals, panel):
@@ -116,24 +119,28 @@
     )(cols, count, vals, panel)
 
 
-def spread(side, cols, count, vals, grad, col_blocks):
+def spread(side, cols, count, vals, grad, extra, col_blocks):
     row_blocks, slot_total, block, _ = vals.shape
     width = grad.shape[-1]
     return pl.pallas_call(
         spread_kernel,
-        out_shape=[jax.ShapeDtypeStruct((col_blocks // 2, block, width), jnp.float32)] * 2,
+        out_shape=[
+            jax.ShapeDtypeStruct((col_blocks // 2, block, width), jnp.float32),
+            jax.ShapeDtypeStruct((col_blocks // 2 + extra.shape[0], block, width), jnp.float32),
+        ],
         in_specs=[
             pl.BlockSpec(memory_space=pltpu.SMEM),
             pl.BlockSpec(memory_space=pltpu.SMEM),
             pl.BlockSpec(memory_space=pltpu.SMEM),
             pl.BlockSpec(memory_space=pl.ANY),
+            pl.BlockSpec(memory_space=pltpu.VMEM),
             pl.BlockSpec(memory_space=pltpu.VMEM),
         ],
         out_specs=[pl.BlockSpec(memory_space=pl.ANY)] * 2,
         scratch_shapes=[
             pltpu.VMEM(vals.shape, vals.dtype),
             pltpu.VMEM((col_blocks, block, width), jnp.float32),
-            pltpu.SemaphoreType.DMA((3,)),
+            pltpu.SemaphoreType.DMA((4,)),
         ],
         compiler_params=pltpu.CompilerParams(vmem_limit_bytes=VMEM_LIMIT),
         cost_estimate=pl.CostEstimate(
@@ -141,7 +148,7 @@
             bytes_accessed=vals.size * 2 + grad.size * 2 + col_blocks * block * width * 4,
             transcendentals=0,
         ),
-    )(side, cols, count, vals, grad)
+    )(side, cols, count, vals, grad, extra)
 
 
 def swap(value, axis):
@@ -157,19 +164,43 @@
     return lax.ppermute(value, "row", [(r, dest(r)) for r in range(64)])
 
 
-def row_reduce_scatter(keep, send):
-    _, block, width = keep.shape
+def ordered_sum(own, came, place, size):
+    values = [own, *came]
+    ordered = []
+    for position in range(size):
+        shift = (place - position + size) % size
+        picked = values[0]
+        for s in range(1, size):
+            picked = jnp.where(shift == s, values[s], picked)
+        ordered.append(picked)
+    return (ordered[0] + ordered[1]) + (ordered[2] + ordered[3])
+
+
+def row_reduce_scatter(keep, send, me):
+    half, block, width = keep.shape
+    extra = send.shape[0] - half
     keep = keep.reshape(2, 4, 16, block, width)
-    came = shifted(send, 1, 2, 1).reshape(2, 4, 16, block, width)
+    came = shifted(send, 1, 2, 1)
+    held = send[half:] + came[half:]
+    came = came[:half].reshape(2, 4, 16, block, width)
     first = [keep[0, s] + came[0, s] for s in range(4)]
     second = [keep[1, s] + came[1, s] for s in range(4)]
-    first = (first[0] + sum(shifted(first[s], 2, 4, s) for s in range(1, 4))).reshape(4, 4, block, width)
+
+    sent = [shifted(jnp.concatenate([first[s], held]), 2, 4, s) for s in range(1, 4)]
+    held = ordered_sum(held, [m[16:] for m in sent], (me // 2) % 4, 4)
+    first = (first[0] + sum(m[:16] for m in sent)).reshape(4, 4, block, width)
     second = (second[0] + sum(shifted(second[s], 16, 4, s) for s in range(1, 4))).reshape(4, 4, block, width)
-    first = (first[0] + sum(shifted(first[s], 16, 4, s) for s in range(1, 4))).reshape(2, 2, block, width)
+
+    sent = [shifted(jnp.concatenate([first[s], held]), 16, 4, s) for s in range(1, 4)]
+    held = ordered_sum(held, [m[4:] for m in sent], me // 16, 4)
+    first = (first[0] + sum(m[:4] for m in sent)).reshape(2, 2, block, width)
     second = (second[0] + sum(shifted(second[s], 2, 4, s) for s in range(1, 4))).reshape(2, 2, block, width)
-    first = first[0] + shifted(first[1], 8, 2, 1)
+
+    sent = shifted(jnp.concatenate([first[1], held]), 8, 2, 1)
+    held = held + sent[2:]
+    first = first[0] + sent[:2]
     second = second[0] + shifted(second[1], 8, 2, 1)
-    return jnp.concatenate([first, second]).reshape(-1, width)
+    return jnp.concatenate([first, second]).reshape(-1, width), held
 
 
 def all_sum(value, axis):
@@ -205,11 +236,14 @@
     local_grad = jnp.dot(aggregated.T, pre_grad, preferred_element_type=jnp.float32)
     own_grad = jnp.dot(pre_grad, weight.T, preferred_element_type=jnp.float32).astype(jnp.bfloat16)
     both_grad = jnp.stack([own_grad, swap(own_grad, "grp")]).reshape(2, -1, block, width)
-    weight_grad = lax.psum(local_grad, ("grp", "row")) * (1.0 / math.sqrt(verts))
 
     where = jnp.stack([side, lax.axis_index("row")]).astype(jnp.int32)
-    keep, send = spread(where, cols, count, vals, both_grad, col_blocks)
-    input_grad = row_reduce_scatter(keep, send).astype(jnp.bfloat16)
+    extra = local_grad.reshape(-1, block, width)
+    keep, send = spread(where, cols, count, vals, both_grad, extra, col_blocks)
+    input_grad, held = row_reduce_scatter(keep, send, lax.axis_index("row"))
+    input_grad = input_grad.astype(jnp.bfloat16)
+    held = held.reshape(-1, width)
+    weight_grad = (held + swap(held, "grp")) * (1.0 / math.sqrt(verts))
     return (activated, weight_grad, input_grad)
 
 

time: 550 us -> 480 us (0.87)
  waiting for transfers between devices: 401 us -> 309 us
  starting transfers between devices: 27.7 us -> 69 us
  Pallas kernels: 63.3 us -> 33.1 us
  other arithmetic: 33.1 us -> 41.3 us
    psum x1 -> x0, waiting for transfers between devices: 128 us -> none  [body(): lax.psum(local_grad, ('grp', 'row')) * (1.0 / math.sqrt(verts))]
    ppermute x15, starting transfers between devices: 22.1 us -> 60.8 us  [shifted(): return lax.ppermute(value, 'row', [(r, dest(r)) for r in range(64)])]
    ppermute x15, waiting for transfers between devices: 126 us -> 160 us  [shifted(): return lax.ppermute(value, 'row', [(r, dest(r)) for r in range(64)])]
    pallas_call x1, Pallas kernels: 36.7 us -> 20 us  [spread(): pl.pallas_call(spread_kernel, out_shape=[jax.ShapeDtypeStruct((col_blocks...]
    pallas_call x1, Pallas kernels: 26.6 us -> 13.2 us  [aggregate(): pl.pallas_call(aggregate_kernel, out_shape=jax.ShapeDtypeStruct((row_bloc...]
    concatenate x1 -> x4, other arithmetic: 0.73 us -> 7.75 us  [the longest x2 6.99 us: row_reduce_scatter(): jnp.concatenate([first[s], held])]
    add x3 -> x6, other arithmetic: 26.5 us -> 30 us  [the longest x1 15.3 us: row_reduce_scatter(): second = [keep[1, s] + came[1, s] for s in range(4)]]
    ppermute x2 -> x3, waiting for transfers between devices: 19 us -> 20.6 us  [swap(): return lax.ppermute(value, axis, [(i, i ^ 1) for i in range(size)])]
  transfers between devices with their start and end apart: 19 -> 19, of which waited for: 12 -> 15; matrix products, arithmetic and copies ran while one was open for 2% -> 2% of each run, Pallas kernels for 0% -> 0%
where the time goes in v6:
time: 480 us; the launch traced here: 479 us
  waiting for transfers between devices  309 us (64%)
  starting transfers between devices  69 us (14%)
  other arithmetic  41.3 us (9%)
  Pallas kernels  33.1 us (7%)
  between operations  14.2 us (3%)
  local copies, waits for them, and re-layouts  9.56 us (2%)
    ppermute x15, waiting for transfers between devices, shifted(): return lax.ppermute(value, 'row', [(r, dest(r)) for r in range(64)])  160 us
    all_gather x1, waiting for transfers between devices, body(): gathered = lax.all_gather(features, 'row', axis=0, tiled=True)  127 us
    ppermute x15, starting transfers between devices, shifted(): return lax.ppermute(value, 'row', [(r, dest(r)) for r in range(64)])  60.8 us
    ppermute x3, waiting for transfers between devices, swap(): return lax.ppermute(value, axis, [(i, i ^ 1) for i in range(size)])  20.6 us
    pallas_call x1, Pallas kernels, spread(): pl.pallas_call(spread_kernel, out_shape=[jax.ShapeDtypeStruct((col_blocks...  20 us
    add x1, other arithmetic, row_reduce_scatter(): second = [keep[1, s] + came[1, s] for s in range(4)]  15.3 us
    pallas_call x1, Pallas kernels, aggregate(): pl.pallas_call(aggregate_kernel, out_shape=jax.ShapeDtypeStruct((row_bloc...  13.2 us
  transfers between devices with their start and end apart: 19, of which 15 were waited for; matrix products, arithmetic and copies ran while one was open for 2% of the time, Pallas kernels for 0%

profile of v6, /device:TPU:0, one launch (start us, length us, event | category | flops | bytes accessed | tf_op | source)
XLA Modules:
  0.0 478.5 jit_solution(11963577219158914914)
XLA Ops:
  7.9 127.3 %all-gather.2.cloned.1.call-done.panel_hbm = bf16[32768,256]{1,0:T(8,128)(2,1)} async-done(((bf16[512,256]{1,0:T(8,128)(2,1)}), bf16[32768,256]{1,0:T(8,128)(2,1)}) %all-gather.2.cloned.1.call-update) | async-done | bytes 16777232 | tf_op jit(solution)/shard_map/all_gather | solution.py:222
  135.3 13.2 %shard_map.85 = f32[8,128,256]{2,1,0:T(8,128)} custom-call(s32[8,16]{1,0:T(8,128)} %bitcast.53, s32[8]{0:T(128)} %bitcast.55, bf16[8,16,128,128]{3,2,1,0:T(8,128)(2,1)} %bitcast.44, bf16[32768,256]{1,0:T(8,128)(2,1)} %all-gather.2.cloned.1.call-done.panel_hbm), custom_call_target="tpu_custom_call" | custom-call | flops 1073741824 | bytes 22020096 | tf_op jit(solution)/shard_map/pallas_call | solution.py:98
  148.5 1.1 constant_dynamic-slice_fusion
  149.6 2.8 collective-permute-start
  152.3 10.9 %collective-permute-done = f32[512,256]{1,0:T(8,128)S(1)} collective-permute-done((f32[512,256]{1,0:T(8,128)S(1)}, f32[512,256]{1,0:T(8,128)S(1)}, u32[]{:S(2)}, u32[]{:S(2)}) %collective-permute-start) | collective-permute-done | bytes 524320 | tf_op jit(solution)/shard_map/ppermute | solution.py:156
  163.2 1.1 add_convert_fusion
  164.4 1.1 multiply_convert_fusion
  165.7 4.1 collective-permute-start.1
  170.4 1.0 fusion.15
  171.4 4.9 %collective-permute-done.1 = bf16[512,256]{1,0:T(8,128)(2,1)S(1)} collective-permute-done((bf16[512,256]{1,0:T(8,128)(2,1)S(1)}, bf16[512,256]{1,0:T(8,128)(2,1)S(1)}, u32[]{:S(2)}, u32[]{:S(2)}) %collective-permute-start.1) | collective-permute-done | bytes 262176 | tf_op jit(solution)/shard_map/ppermute | solution.py:156
  176.2 0.8 pad_maximum_fusion.6.grad_ref
  177.1 20.0 %shard_map.86 = (f32[128,128,256]{2,1,0:T(8,128)}, f32[130,128,256]{2,1,0:T(8,128)}) custom-call(s32[2]{0:T(128)} %pad_add_fusion.side_ref, s32[8,16]{1,0:T(8,128)} %bitcast.54, s32[8]{0:T(128)} %bitcast.56, bf16[8,16,128,128]{3,2,1,0:T(8,128)(2,1)} %bitcast.45, bf16[2,4,128,256]{3,2,1,0:T(8,128)(2,1)} %pad_maximum_fusion.6.grad_ref, f32[2,128,256]{2,1,0:T(8,128)} %bitcast.48), custom_call_target="tpu_custom_call" | custom-call | flops 1073741824 | bytes 38273024 | tf_op jit(solution)/shard_map/pallas_call | solution.py:125
  197.1 6.3 %collective-permute-start.2 = (f32[130,128,256]{2,1,0:T(8,128)}, f32[130,128,256]{2,1,0:T(8,128)S(1)}, u32[]{:S(2)}, u32[]{:S(2)}) collective-permute-start(f32[130,128,256]{2,1,0:T(8,128)} %get-tuple-element.6), channel_id=1, source_target_pairs={{0,1},{1,0},{2,3},{3,2},{4,5},{5,4},{6,7},{7,6},{8,9},{9,8},{10,11... | collective-permute-start | bytes 51118088 | tf_op jit(solution)/shard_map/ppermute | solution.py:164
  203.3 25.4 %collective-permute-done.2 = f32[130,128,256]{2,1,0:T(8,128)S(1)} collective-permute-done((f32[130,128,256]{2,1,0:T(8,128)}, f32[130,128,256]{2,1,0:T(8,128)S(1)}, u32[]{:S(2)}, u32[]{:S(2)}) %collective-permute-start.2) | collective-permute-done | bytes 17039392 | tf_op jit(solution)/shard_map/ppermute | solution.py:164
  228.7 1.9 slice.193
  230.6 4.8 %copy-done.3 = f32[130,128,256]{2,1,0:T(8,128)} copy-done((f32[130,128,256]{2,1,0:T(8,128)}, f32[130,128,256]{2,1,0:T(8,128)S(1)}, u32[]{:S(2)}) %copy-start.3) | copy-done | bytes 17039384
  235.5 15.3 %fusion.1 = (f32[16,128,256]{2,1,0:T(8,128)}, f32[16,128,256]{2,1,0:T(8,128)}, f32[16,128,256]{2,1,0:T(8,128)}, f32[16,128,256]{2,1,0:T(8,128)S(1)}, f32[16,128,256]{2,1,0:T(8,128)}, /*index=5*/f32[16,128,256]{2,1,0:T(8,128)}) fusion(f32[2,4,16,128,256]{4,3,2,1,0:T(8,128)S(1)} %bitcast.40, f32[2,4,16,128,256]{4,3,2,1,0:T(8,128)} %bitcast.42), kind=kLoop, calls=%fused_computation.6 | loop fusion | flops 3145728 | bytes 37748736 | tf_op jit(solution)/shard_map/add | solution.py:187
  250.8 20.8 %collective-permute-start.13 = (f32[16,128,256]{2,1,0:T(8,128)}, f32[16,128,256]{2,1,0:T(8,128)}, u32[]{:S(2)}, u32[]{:S(2)}) collective-permute-start(f32[16,128,256]{2,1,0:T(8,128)} %get-tuple-element.10), channel_id=1, source_target_pairs={{0,48},{1,49},{2,50},{3,51},{4,52},{5,53},{6,54},{7,55},{8,56},{9,... | collective-permute-start | bytes 6291464 | tf_op jit(solution)/shard_map/ppermute | solution.py:164
  271.6 1.1 slice_add_fusion.16
  272.6 5.5 %pad_maximum_fusion.2 = (f32[18,128,256]{2,1,0:T(8,128)}, f32[18,128,256]{2,1,0:T(8,128)}, f32[18,128,256]{2,1,0:T(8,128)}) fusion(f32[2,128,256]{2,1,0:T(8,128)S(1)} %slice_add_fusion.16, f32[16,128,256]{2,1,0:T(8,128)} %get-tuple-element.14, f32[16,128,256]{2,1,0:T(8,128)S(1)} %get-tuple-element.12, f32[16,128,256]{2,1,0:T(8,128)} %get-tuple-element.13), kind=kLoop, calls=%fused_computation.2 | loop fusion | flops 1769472 | bytes 13631488 | tf_op jit(solution)/shard_map/concatenate | solution.py:189
  278.1 7.1 %collective-permute-start.5 = (f32[18,128,256]{2,1,0:T(8,128)}, f32[18,128,256]{2,1,0:T(8,128)S(1)}, u32[]{:S(2)}, u32[]{:S(2)}) collective-permute-start(f32[18,128,256]{2,1,0:T(8,128)} %get-tuple-element.29), channel_id=1, source_target_pairs={{0,6},{1,7},{2,0},{3,1},{4,2},{5,3},{6,4},{7,5},{8,14},{9,15},{10,... | collective-permute-start | bytes 7077896 | tf_op jit(solution)/shard_map/ppermute | solution.py:164
  285.2 0.9 collective-permute-start.3
  286.1 33.5 %collective-permute-done.13 = f32[16,128,256]{2,1,0:T(8,128)} collective-permute-done((f32[16,128,256]{2,1,0:T(8,128)}, f32[16,128,256]{2,1,0:T(8,128)}, u32[]{:S(2)}, u32[]{:S(2)}) %collective-permute-start.13) | collective-permute-done | bytes 2097184 | tf_op jit(solution)/shard_map/ppermute | solution.py:164
  319.6 1.3 collective-permute-start.12
  320.9 15.7 %collective-permute-done.11 = f32[16,128,256]{2,1,0:T(8,128)} collective-permute-done((f32[16,128,256]{2,1,0:T(8,128)}, f32[16,128,256]{2,1,0:T(8,128)}, u32[]{:S(2)}, u32[]{:S(2)}) %collective-permute-start.11) | collective-permute-done | bytes 2097184 | tf_op jit(solution)/shard_map/ppermute | solution.py:164
  336.6 45.5 %collective-permute-done.12 = f32[16,128,256]{2,1,0:T(8,128)} collective-permute-done((f32[16,128,256]{2,1,0:T(8,128)}, f32[16,128,256]{2,1,0:T(8,128)}, u32[]{:S(2)}, u32[]{:S(2)}) %collective-permute-start.12) | collective-permute-done | bytes 2097184 | tf_op jit(solution)/shard_map/ppermute | solution.py:164
  382.1 4.7 collective-permute-done.5
  386.8 1.4 copy-done.5
  388.2 2.0 collective-permute-done.3
  390.3 9.2 %fusion.4 = (f32[16,128,256]{2,1,0:T(8,128)S(1)}, f32[16,128,256]{2,1,0:T(8,128)S(1)}) fusion(f32[2,4,16,128,256]{4,3,2,1,0:T(8,128)} %bitcast.41, f32[2,4,16,128,256]{4,3,2,1,0:T(8,128)} %bitcast.43, f32[16,128,256]{2,1,0:T(8,128)} %collective-permute-done.13, f32[16,128,256]{2,1,0:T(8,128)} %collective-permute-done.11, ...), kind=kLoop, calls=%fused_computation.11 | loop fusion | flops 4194304 | bytes 25165824 | tf_op jit(solution)/shard_map/add | solution.py:192
  399.6 1.8 add_add_fusion.1
  401.4 1.5 pad_maximum_fusion.3
  402.9 1.4 collective-permute-start.6
  404.7 1.4 collective-permute-start.8
  406.2 1.3 collective-permute-start.16
  407.5 0.8 collective-permute-start.14
  408.3 15.3 %collective-permute-done.6 = f32[6,128,256]{2,1,0:T(8,128)S(1)} collective-permute-done((f32[6,128,256]{2,1,0:T(8,128)}, f32[6,128,256]{2,1,0:T(8,128)S(1)}, u32[]{:S(2)}, u32[]{:S(2)}) %collective-permute-start.6) | collective-permute-done | bytes 786464 | tf_op jit(solution)/shard_map/ppermute | solution.py:164
  423.6 17.4 %collective-permute-start.15 = (f32[4,128,256]{2,1,0:T(8,128)S(1)}, f32[4,128,256]{2,1,0:T(8,128)S(1)}, u32[]{:S(2)}, u32[]{:S(2)}) collective-permute-start(f32[4,128,256]{2,1,0:T(8,128)S(1)} %get-tuple-element.15), channel_id=1, source_target_pairs={{0,4},{1,5},{2,6},{3,7},{4,0},{5,1},{6,2},{7,3},{8,12},{9,13},{10,... | collective-permute-start | bytes 1572872 | tf_op jit(solution)/shard_map/ppermute | solution.py:164
  441.0 1.1 collective-permute-done.8
  442.1 1.5 fusion.10
  443.7 1.2 add_add_fusion
  445.1 6.6 %collective-permute-done.15 = f32[4,128,256]{2,1,0:T(8,128)S(1)} collective-permute-done((f32[4,128,256]{2,1,0:T(8,128)S(1)}, f32[4,128,256]{2,1,0:T(8,128)S(1)}, u32[]{:S(2)}, u32[]{:S(2)}) %collective-permute-start.15) | collective-permute-done | bytes 524320 | tf_op jit(solution)/shard_map/ppermute | solution.py:164
  451.9 1.6 collective-permute-start.17
  453.5 6.3 %collective-permute-done.9 = f32[4,128,256]{2,1,0:T(8,128)S(1)} collective-permute-done((f32[4,128,256]{2,1,0:T(8,128)S(1)}, f32[4,128,256]{2,1,0:T(8,128)S(1)}, u32[]{:S(2)}, u32[]{:S(2)}) %collective-permute-start.9) | collective-permute-done | bytes 524320 | tf_op jit(solution)/shard_map/ppermute | solution.py:164
  459.8 1.3 collective-permute-start.10
  461.1 4.2 collective-permute-done.17
  466.1 4.8 %collective-permute-done.10 = f32[256,256]{1,0:T(8,128)S(1)} collective-permute-done((f32[256,256]{1,0:T(8,128)S(1)}, f32[256,256]{1,0:T(8,128)S(1)}, u32[]{:S(2)}, u32[]{:S(2)}) %collective-permute-start.10) | collective-permute-done | bytes 262176 | tf_op jit(solution)/shard_map/ppermute | solution.py:156
  471.0 0.7 add_multiply_fusion
  (33 shorter events, 3.5 us)
Async XLA Ops:
  7.2 157.2 %copy-start = (bf16[256,256]{1,0:T(8,128)(2,1)S(1)}, bf16[256,256]{1,0:T(8,128)(2,1)}, u32[]{:S(2)}) copy-start(bf16[256,256]{1,0:T(8,128)(2,1)} %param.7) | copy-start | bytes 393220
  7.2 128.1 %all-gather.2.cloned.1.call-start = ((), (), s32[]{:S(2)}) async-start(), calls=%async_computation | async-start | bytes 17039360 | tf_op jit(solution)/shard_map/all_gather | solution.py:222
  148.4 15.9 %copy-start.6 = (bf16[512,256]{1,0:T(8,128)(2,1)S(1)}, bf16[512,256]{1,0:T(8,128)(2,1)}, u32[]{:S(2)}) copy-start(bf16[512,256]{1,0:T(8,128)(2,1)} %param.11) | copy-start | bytes 786436
  149.6 13.7 %collective-permute-start = (f32[512,256]{1,0:T(8,128)S(1)}, f32[512,256]{1,0:T(8,128)S(1)}, u32[]{:S(2)}, u32[]{:S(2)}) collective-permute-start(f32[512,256]{1,0:T(8,128)S(1)} %constant_dynamic-slice_fusion), channel_id=1, source_target_pairs={{0,64},{64,0},{1,65},{65,1},{2,66},{66,2},{3,67},{67,3},{4,68},{68... | collective-permute-start | bytes 1572872 | tf_op jit(solution)/shard_map/ppermute | solution.py:156
  165.7 10.5 %collective-permute-start.1 = (bf16[512,256]{1,0:T(8,128)(2,1)S(1)}, bf16[512,256]{1,0:T(8,128)(2,1)S(1)}, u32[]{:S(2)}, u32[]{:S(2)}) collective-permute-start(bf16[512,256]{1,0:T(8,128)(2,1)S(1)} %convolution_convert_fusion), channel_id=1, source_target_pairs={{0,64},{64,0},{1,65},{65,1},{2,66},{66,2},{3,67},{67,3},{4,68},{68... | collective-permute-start | bytes 786440 | tf_op jit(solution)/shard_map/ppermute | solution.py:156
  197.1 31.6 %collective-permute-start.2 = (f32[130,128,256]{2,1,0:T(8,128)}, f32[130,128,256]{2,1,0:T(8,128)S(1)}, u32[]{:S(2)}, u32[]{:S(2)}) collective-permute-start(f32[130,128,256]{2,1,0:T(8,128)} %get-tuple-element.6), channel_id=1, source_target_pairs={{0,1},{1,0},{2,3},{3,2},{4,5},{5,4},{6,7},{7,6},{8,9},{9,8},{10,11... | collective-permute-start | bytes 51118088 | tf_op jit(solution)/shard_map/ppermute | solution.py:164
  228.7 6.8 %copy-start.3 = (f32[130,128,256]{2,1,0:T(8,128)}, f32[130,128,256]{2,1,0:T(8,128)S(1)}, u32[]{:S(2)}) copy-start(f32[130,128,256]{2,1,0:T(8,128)S(1)} %collective-permute-done.2) | copy-start | bytes 51118084
  235.5 15.3 %copy-start.2 = (f32[128,128,256]{2,1,0:T(8,128)}, f32[128,128,256]{2,1,0:T(8,128)S(1)}, u32[]{:S(2)}) copy-start(f32[128,128,256]{2,1,0:T(8,128)S(1)} %slice.193) | copy-start | bytes 50331652
  250.8 68.8 %collective-permute-start.13 = (f32[16,128,256]{2,1,0:T(8,128)}, f32[16,128,256]{2,1,0:T(8,128)}, u32[]{:S(2)}, u32[]{:S(2)}) collective-permute-start(f32[16,128,256]{2,1,0:T(8,128)} %get-tuple-element.10), channel_id=1, source_target_pairs={{0,48},{1,49},{2,50},{3,51},{4,52},{5,53},{6,54},{7,55},{8,56},{9,... | collective-permute-start | bytes 6291464 | tf_op jit(solution)/shard_map/ppermute | solution.py:164
  278.1 108.7 %collective-permute-start.5 = (f32[18,128,256]{2,1,0:T(8,128)}, f32[18,128,256]{2,1,0:T(8,128)S(1)}, u32[]{:S(2)}, u32[]{:S(2)}) collective-permute-start(f32[18,128,256]{2,1,0:T(8,128)} %get-tuple-element.29), channel_id=1, source_target_pairs={{0,6},{1,7},{2,0},{3,1},{4,2},{5,3},{6,4},{7,5},{8,14},{9,15},{10,... | collective-permute-start | bytes 7077896 | tf_op jit(solution)/shard_map/ppermute | solution.py:164
  285.2 101.6 %collective-permute-start.4 = (f32[18,128,256]{2,1,0:T(8,128)}, f32[18,128,256]{2,1,0:T(8,128)}, u32[]{:S(2)}, u32[]{:S(2)}) collective-permute-start(f32[18,128,256]{2,1,0:T(8,128)} %get-tuple-element.30), channel_id=1, source_target_pairs={{0,4},{1,5},{2,6},{3,7},{4,0},{5,1},{6,2},{7,3},{8,12},{9,13},{10,... | collective-permute-start | bytes 7077896 | tf_op jit(solution)/shard_map/ppermute | solution.py:164
  285.2 105.0 %collective-permute-start.3 = (f32[18,128,256]{2,1,0:T(8,128)}, f32[18,128,256]{2,1,0:T(8,128)}, u32[]{:S(2)}, u32[]{:S(2)}) collective-permute-start(f32[18,128,256]{2,1,0:T(8,128)} %get-tuple-element.28), channel_id=1, source_target_pairs={{0,2},{1,3},{2,4},{3,5},{4,6},{5,7},{6,0},{7,1},{8,10},{9,11},{10,... | collective-permute-start | bytes 7077896 | tf_op jit(solution)/shard_map/ppermute | solution.py:164
  286.1 50.5 %collective-permute-start.11 = (f32[16,128,256]{2,1,0:T(8,128)}, f32[16,128,256]{2,1,0:T(8,128)}, u32[]{:S(2)}, u32[]{:S(2)}) collective-permute-start(f32[16,128,256]{2,1,0:T(8,128)} %get-tuple-element.11), channel_id=1, source_target_pairs={{0,16},{1,17},{2,18},{3,19},{4,20},{5,21},{6,22},{7,23},{8,24},{9,... | collective-permute-start | bytes 6291464 | tf_op jit(solution)/shard_map/ppermute | solution.py:164
  319.6 62.6 %collective-permute-start.12 = (f32[16,128,256]{2,1,0:T(8,128)}, f32[16,128,256]{2,1,0:T(8,128)}, u32[]{:S(2)}, u32[]{:S(2)}) collective-permute-start(f32[16,128,256]{2,1,0:T(8,128)} %get-tuple-element.9), channel_id=1, source_target_pairs={{0,32},{1,33},{2,34},{3,35},{4,36},{5,37},{6,38},{7,39},{8,40},{9,... | collective-permute-start | bytes 6291464 | tf_op jit(solution)/shard_map/ppermute | solution.py:164
  386.8 1.4 copy-start.5
  399.4 2.0 copy-start.4
  402.9 20.7 %collective-permute-start.6 = (f32[6,128,256]{2,1,0:T(8,128)}, f32[6,128,256]{2,1,0:T(8,128)S(1)}, u32[]{:S(2)}, u32[]{:S(2)}) collective-permute-start(f32[6,128,256]{2,1,0:T(8,128)} %get-tuple-element.27), channel_id=1, source_target_pairs={{0,48},{1,49},{2,50},{3,51},{4,52},{5,53},{6,54},{7,55},{8,56},{9,... | collective-permute-start | bytes 2359304 | tf_op jit(solution)/shard_map/ppermute | solution.py:164
  404.3 36.7 %collective-permute-start.7 = (f32[6,128,256]{2,1,0:T(8,128)}, f32[6,128,256]{2,1,0:T(8,128)}, u32[]{:S(2)}, u32[]{:S(2)}) collective-permute-start(f32[6,128,256]{2,1,0:T(8,128)} %get-tuple-element.26), channel_id=1, source_target_pairs={{0,32},{1,33},{2,34},{3,35},{4,36},{5,37},{6,38},{7,39},{8,40},{9,... | collective-permute-start | bytes 2359304 | tf_op jit(solution)/shard_map/ppermute | solution.py:164
  404.7 37.5 %collective-permute-start.8 = (f32[6,128,256]{2,1,0:T(8,128)}, f32[6,128,256]{2,1,0:T(8,128)}, u32[]{:S(2)}, u32[]{:S(2)}) collective-permute-start(f32[6,128,256]{2,1,0:T(8,128)} %get-tuple-element.25), channel_id=1, source_target_pairs={{0,16},{1,17},{2,18},{3,19},{4,20},{5,21},{6,22},{7,23},{8,24},{9,... | collective-permute-start | bytes 2359304 | tf_op jit(solution)/shard_map/ppermute | solution.py:164
  406.2 38.9 %collective-permute-start.16 = (f32[4,128,256]{2,1,0:T(8,128)S(1)}, f32[4,128,256]{2,1,0:T(8,128)S(1)}, u32[]{:S(2)}, u32[]{:S(2)}) collective-permute-start(f32[4,128,256]{2,1,0:T(8,128)S(1)} %get-tuple-element.16), channel_id=1, source_target_pairs={{0,6},{1,7},{2,0},{3,1},{4,2},{5,3},{6,4},{7,5},{8,14},{9,15},{10,... | collective-permute-start | bytes 1572872 | tf_op jit(solution)/shard_map/ppermute | solution.py:164
  407.5 37.6 %collective-permute-start.14 = (f32[4,128,256]{2,1,0:T(8,128)S(1)}, f32[4,128,256]{2,1,0:T(8,128)S(1)}, u32[]{:S(2)}, u32[]{:S(2)}) collective-permute-start(f32[4,128,256]{2,1,0:T(8,128)S(1)} %get-tuple-element.17), channel_id=1, source_target_pairs={{0,2},{1,3},{2,4},{3,5},{4,6},{5,7},{6,0},{7,1},{8,10},{9,11},{10,... | collective-permute-start | bytes 1572872 | tf_op jit(solution)/shard_map/ppermute | solution.py:164
  423.6 28.1 %collective-permute-start.15 = (f32[4,128,256]{2,1,0:T(8,128)S(1)}, f32[4,128,256]{2,1,0:T(8,128)S(1)}, u32[]{:S(2)}, u32[]{:S(2)}) collective-permute-start(f32[4,128,256]{2,1,0:T(8,128)S(1)} %get-tuple-element.15), channel_id=1, source_target_pairs={{0,4},{1,5},{2,6},{3,7},{4,0},{5,1},{6,2},{7,3},{8,12},{9,13},{10,... | collective-permute-start | bytes 1572872 | tf_op jit(solution)/shard_map/ppermute | solution.py:164
  444.9 14.9 %collective-permute-start.9 = (f32[4,128,256]{2,1,0:T(8,128)S(1)}, f32[4,128,256]{2,1,0:T(8,128)S(1)}, u32[]{:S(2)}, u32[]{:S(2)}) collective-permute-start(f32[4,128,256]{2,1,0:T(8,128)S(1)} %pad_maximum_fusion.7), channel_id=1, source_target_pairs={{0,8},{1,9},{2,10},{3,11},{4,12},{5,13},{6,14},{7,15},{8,0},{9,1},... | collective-permute-start | bytes 1572872 | tf_op jit(solution)/shard_map/ppermute | solution.py:164
  451.7 20.0 %copy-start.1 = (bf16[256,256]{1,0:T(8,128)(2,1)S(1)}, bf16[256,256]{1,0:T(8,128)(2,1)}, u32[]{:S(2)}) copy-start(bf16[256,256]{1,0:T(8,128)(2,1)} %param.7) | copy-start | bytes 393220
  451.9 13.5 %collective-permute-start.17 = (f32[2,128,256]{2,1,0:T(8,128)S(1)}, f32[2,128,256]{2,1,0:T(8,128)S(1)}, u32[]{:S(2)}, u32[]{:S(2)}) collective-permute-start(f32[2,128,256]{2,1,0:T(8,128)S(1)} %slice.235), channel_id=1, source_target_pairs={{0,8},{1,9},{2,10},{3,11},{4,12},{5,13},{6,14},{7,15},{8,0},{9,1},... | collective-permute-start | bytes 786440 | tf_op jit(solution)/shard_map/ppermute | solution.py:164
  459.8 11.1 %collective-permute-start.10 = (f32[256,256]{1,0:T(8,128)S(1)}, f32[256,256]{1,0:T(8,128)S(1)}, u32[]{:S(2)}, u32[]{:S(2)}) collective-permute-start(f32[256,256]{1,0:T(8,128)S(1)} %bitcast.49), channel_id=1, source_target_pairs={{0,64},{64,0},{1,65},{65,1},{2,66},{66,2},{3,67},{67,3},{4,68},{68... | collective-permute-start | bytes 786440 | tf_op jit(solution)/shard_map/ppermute | solution.py:156
Sparse Core Ops, SparseCore 0:
  9.7 125.4 all-gather.1

commit v7 on v5

--- a/solution.py
+++ b/solution.py
@@ -16,23 +16,39 @@
     return sigma * (1.0 + pre * (1.0 - sigma))
 
 
-def aggregate_kernel(cols_ref, count_ref, vals_hbm, panel_hbm, out_ref, vals, panel, sems):
-    row_blocks, slot_total, block, _ = vals.shape
-    col_blocks = panel.shape[0] // block
+def gathered_slot(owner, q2, me):
+    dk = (owner % 2) ^ (me % 2)
+    rx = ((me // 2) % 4 - (owner // 2) % 4 + 4) % 4
+    dy = ((owner // 8) % 2) ^ ((me // 8) % 2)
+    rz = ((me // 16) - (owner // 16) + 4) % 4
+    first = jnp.where(q2 == 0, rx, rz)
+    second = jnp.where(q2 == 0, rz, rx)
+    return (((dk * 2 + q2) * 4 + first) * 4 + second) * 2 + dy
+
+
+def aggregate_kernel(me_ref, cols_ref, count_ref, vals_hbm, low_hbm, high_hbm, out_ref, vals, panel, sems):
+    row_blocks, slot_total, block, _ = vals.shape
+    parts, part_rows, _ = panel.shape
+    col_blocks = parts * part_rows // block
     load_vals = pltpu.make_async_copy(vals_hbm, vals, sems.at[0])
-    load_panel = pltpu.make_async_copy(panel_hbm, panel, sems.at[1])
+    load_low = pltpu.make_async_copy(low_hbm, panel.at[0], sems.at[1])
+    load_high = pltpu.make_async_copy(high_hbm, panel.at[1], sems.at[2])
     load_vals.start()
-    load_panel.start()
+    load_low.start()
+    load_high.start()
     load_vals.wait()
-    load_panel.wait()
+    load_low.wait()
+    load_high.wait()
     for t in range(row_blocks):
         live = jnp.clip(count_ref[t], 0, slot_total)
 
         def body(k, acc):
             col = jnp.clip(cols_ref[t, k], 0, col_blocks - 1)
-            start = pl.multiple_of(col * block, block)
+            owner, q = col // 4, col % 4
+            place = jnp.where(q < 2, owner * 2 + q % 2, gathered_slot(owner, q % 2, me_ref[0]))
+            start = pl.multiple_of(place * block, block)
             return acc + jnp.dot(
-                vals[t, k], panel[pl.ds(start, block), :], preferred_element_type=jnp.float32
+                vals[t, k], panel[q // 2, pl.ds(start, block), :], preferred_element_type=jnp.float32
             )
 
         out_ref[t] = lax.fori_loop(0, live, body, jnp.zeros(out_ref.shape[1:], jnp.float32))
@@ -89,31 +105,33 @@
     keep.wait()
 
 
-def aggregate(cols, count, vals, panel):
-    row_blocks, slot_total, block, _ = vals.shape
-    width = panel.shape[1]
+def aggregate(me, cols, count, vals, low, high):
+    row_blocks, slot_total, block, _ = vals.shape
+    width = low.shape[1]
     return pl.pallas_call(
         aggregate_kernel,
         out_shape=jax.ShapeDtypeStruct((row_blocks, block, width), jnp.float32),
         in_specs=[
             pl.BlockSpec(memory_space=pltpu.SMEM),
             pl.BlockSpec(memory_space=pltpu.SMEM),
+            pl.BlockSpec(memory_space=pltpu.SMEM),
+            pl.BlockSpec(memory_space=pl.ANY),
             pl.BlockSpec(memory_space=pl.ANY),
             pl.BlockSpec(memory_space=pl.ANY),
         ],
         out_specs=pl.BlockSpec(memory_space=pltpu.VMEM),
         scratch_shapes=[
             pltpu.VMEM(vals.shape, vals.dtype),
-            pltpu.VMEM(panel.shape, panel.dtype),
-            pltpu.SemaphoreType.DMA((2,)),
+            pltpu.VMEM((2, *low.shape), low.dtype),
+            pltpu.SemaphoreType.DMA((3,)),
         ],
         compiler_params=pltpu.CompilerParams(vmem_limit_bytes=VMEM_LIMIT),
         cost_estimate=pl.CostEstimate(
             flops=2 * row_blocks * slot_total * block * block * width,
-            bytes_accessed=vals.size * 2 + panel.size * 2 + row_blocks * block * width * 4,
+            bytes_accessed=vals.size * 2 + low.size * 4 + row_blocks * block * width * 4,
             transcendentals=0,
         ),
-    )(cols, count, vals, panel)
+    )(me, cols, count, vals, low, high)
 
 
 def spread(side, cols, count, vals, grad, col_blocks):
@@ -172,6 +190,18 @@
     return jnp.concatenate([first, second]).reshape(-1, width)
 
 
+def row_all_gather(piece):
+    both = jnp.stack([piece, shifted(piece, 8, 2, 1)], axis=1)
+    first, second = both[0], both[1]
+    first = jnp.stack([first] + [shifted(first, 16, 4, s) for s in range(1, 4)])
+    second = jnp.stack([second] + [shifted(second, 2, 4, s) for s in range(1, 4)])
+    first = jnp.stack([first] + [shifted(first, 2, 4, s) for s in range(1, 4)])
+    second = jnp.stack([second] + [shifted(second, 16, 4, s) for s in range(1, 4)])
+    mine = jnp.stack([first, second])
+    whole = jnp.stack([mine, shifted(mine, 1, 2, 1)])
+    return whole.reshape(-1, piece.shape[-1])
+
+
 def all_sum(value, axis):
     size = lax.axis_size(axis)
     step = 1
@@ -188,13 +218,15 @@
     members = lax.axis_size("row")
     verts = rows_dev * groups * members
     side = lax.axis_index("grp")
-    gathered = lax.all_gather(features, "row", axis=0, tiled=True)
-    col_blocks = gathered.shape[0] // block
+    split = rows_dev // 2
+    low = lax.all_gather(features[:split], "row", axis=0, tiled=True)
+    high = row_all_gather(features[split:].reshape(2, block, width))
+    col_blocks = 2 * low.shape[0] // block
     cols = block_cols[0]
     count = block_count[0]
     vals = block_vals[0]
 
-    partial_value = aggregate(cols, count, vals, gathered).reshape(-1, width)
+    partial_value = aggregate(lax.axis_index("row").reshape(1).astype(jnp.int32), cols, count, vals, low, high).reshape(-1, width)
     mine = lax.dynamic_slice_in_dim(partial_value, side * rows_dev, rows_dev)
     theirs = lax.dynamic_slice_in_dim(partial_value, (1 - side) * rows_dev, rows_dev)
     summed = mine + swap(theirs, "grp")

time: 469 us -> 488 us (1.041)
  waiting for transfers between devices: 332 us -> 310 us
  Pallas kernels: 26.1 us -> 45.7 us
  other arithmetic: 29.3 us -> 41 us
  starting transfers between devices: 59.6 us -> 67.7 us
    all_gather x1, waiting for transfers between devices: 127 us -> 44.9 us  [body(): low = lax.all_gather(features[:split], 'row', axis=0, tiled=True)]
    ppermute x15 -> x29, waiting for transfers between devices: 153 us -> 216 us  [shifted(): return lax.ppermute(value, 'row', [(r, dest(r)) for r in range(64)])]
    another operation x2 -> x9, other arithmetic: 0.09 us -> 11.9 us  [the longest x2 11.1 us: row_all_gather(): whole = jnp.stack([mine, shifted(mine, 1, 2, 1)])]
    ppermute x15 -> x29, starting transfers between devices: 30.4 us -> 41.3 us  [shifted(): return lax.ppermute(value, 'row', [(r, dest(r)) for r in range(64)])]
    pallas_call x1, Pallas kernels: 10.2 us -> 20.1 us  [aggregate(): pl.pallas_call(aggregate_kernel, out_shape=jax.ShapeDtypeStruct((row_bloc...]
    pallas_call x1, Pallas kernels: 15.9 us -> 25.6 us  [spread(): pl.pallas_call(spread_kernel, out_shape=[jax.ShapeDtypeStruct((col_blocks...]
    ppermute x2, starting transfers between devices: 10.4 us -> 3.17 us  [swap(): return lax.ppermute(value, axis, [(i, i ^ 1) for i in range(size)])]
  transfers between devices with their start and end apart: 25 -> 39, of which waited for: 21 -> 32; matrix products, arithmetic and copies ran while one was open for 1% -> 3% of each run, Pallas kernels for 0% -> 0%
where the time goes in v7:
time: 488 us; the launch traced here: 486 us
  waiting for transfers between devices  310 us (64%)
  starting transfers between devices  67.7 us (14%)
  Pallas kernels  45.7 us (9%)
  other arithmetic  41 us (8%)
  between operations  14.3 us (3%)
  local copies, waits for them, and re-layouts  5.92 us (1%)
    ppermute x29, waiting for transfers between devices, shifted(): return lax.ppermute(value, 'row', [(r, dest(r)) for r in range(64)])  216 us
    all_gather x1, waiting for transfers between devices, body(): low = lax.all_gather(features[:split], 'row', axis=0, tiled=True)  44.9 us
    ppermute x29, starting transfers between devices, shifted(): return lax.ppermute(value, 'row', [(r, dest(r)) for r in range(64)])  41.3 us
    ppermute x7, waiting for transfers between devices, all_sum(): lax.ppermute(value, axis, [(i, i ^ step) for i in range(size)])  38.5 us
    pallas_call x1, Pallas kernels, spread(): pl.pallas_call(spread_kernel, out_shape=[jax.ShapeDtypeStruct((col_blocks...  25.6 us
    ppermute x7, starting transfers between devices, all_sum(): lax.ppermute(value, axis, [(i, i ^ step) for i in range(size)])  23.2 us
    pallas_call x1, Pallas kernels, aggregate(): pl.pallas_call(aggregate_kernel, out_shape=jax.ShapeDtypeStruct((row_bloc...  20.1 us
    add x1, other arithmetic, row_reduce_scatter(): first = [keep[0, s] + came[0, s] for s in range(4)]  15.8 us
  transfers between devices with their start and end apart: 39, of which 32 were waited for; matrix products, arithmetic and copies ran while one was open for 3% of the time, Pallas kernels for 0%

profile of v7, /device:TPU:0, one launch (start us, length us, event | category | flops | bytes accessed | tf_op | source)
XLA Modules:
  0.0 486.1 jit_solution(14288149753487561099)
XLA Ops:
  7.2 1.7 fusion.18
  8.9 1.7 collective-permute-start
  10.7 3.5 collective-permute-done
  14.2 3.0 collective-permute-start.9
  18.9 3.1 collective-permute-done.9
  21.9 2.3 collective-permute-done.8
  25.7 4.0 collective-permute-start.11
  30.3 2.4 collective-permute-start.2
  33.8 15.7 %collective-permute-done.3 = bf16[2,128,256]{2,1,0:T(8,128)(2,1)S(1)} collective-permute-done((bf16[2,128,256]{2,1,0:T(8,128)(2,1)S(1)}, bf16[2,128,256]{2,1,0:T(8,128)(2,1)S(1)}, u32[]{:S(2)}, u32[]{:S(2)}) %collective-permute-start.3) | collective-permute-done | bytes 131104 | tf_op jit(solution)/shard_map/ppermute | solution.py:175
  50.6 2.3 collective-permute-done.1
  53.2 3.2 collective-permute-start.6
  56.4 11.5 %collective-permute-done.10 = bf16[4,2,128,256]{3,2,1,0:T(8,128)(2,1)S(1)} collective-permute-done((bf16[4,2,128,256]{3,2,1,0:T(8,128)(2,1)S(1)}, bf16[4,2,128,256]{3,2,1,0:T(8,128)(2,1)S(1)}, u32[]{:S(2)}, u32[]{:S(2)}) %collective-permute-start.10) | collective-permute-done | bytes 524320 | tf_op jit(solution)/shard_map/ppermute | solution.py:175
  67.9 2.9 collective-permute-done.12
  71.1 1.5 collective-permute-done.5
  72.6 12.2 %collective-permute-done.4 = bf16[4,2,128,256]{3,2,1,0:T(8,128)(2,1)S(1)} collective-permute-done((bf16[4,2,128,256]{3,2,1,0:T(8,128)(2,1)S(1)}, bf16[4,2,128,256]{3,2,1,0:T(8,128)(2,1)S(1)}, u32[]{:S(2)}, u32[]{:S(2)}) %collective-permute-start.4) | collective-permute-done | bytes 524320 | tf_op jit(solution)/shard_map/ppermute | solution.py:175
  85.0 3.6 fusion.15
  88.6 7.5 %collective-permute-done.13 = bf16[2,4,4,2,128,256]{5,4,3,2,1,0:T(8,128)(2,1)} collective-permute-done((bf16[2,4,4,2,128,256]{5,4,3,2,1,0:T(8,128)(2,1)}, bf16[2,4,4,2,128,256]{5,4,3,2,1,0:T(8,128)(2,1)}, u32[]{:S(2)}, u32[]{:S(2)}) %collective-permute-start.13) | collective-permute-done | bytes 4194336 | tf_op jit(solution)/shard_map/ppermute | solution.py:175
  96.1 7.6 %pad_maximum_fusion = bf16[2,2,4,4,2,128,256]{6,5,4,3,2,1,0:T(8,128)(2,1)} fusion(bf16[1,2,4,4,2,128,256]{6,5,4,3,2,1,0:T(8,128)(2,1)} %bitcast.27, bf16[1,2,4,4,2,128,256]{6,5,4,3,2,1,0:T(8,128)(2,1)} %get-tuple-element.19), kind=kLoop, calls=%fused_computation | loop fusion | flops 4194304 | bytes 16777216 | tf_op jit(solution)/shard_map/stack | solution.py:201
  103.7 44.9 %all-gather.2.cloned.1.call-done.low_hbm = bf16[16384,256]{1,0:T(8,128)(2,1)} async-done(((bf16[256,256]{1,0:T(8,128)(2,1)}), bf16[16384,256]{1,0:T(8,128)(2,1)}) %all-gather.2.cloned.1.call-update) | async-done | bytes 8388624 | tf_op jit(solution)/shard_map/all_gather | solution.py:222
  148.6 20.1 %shard_map.85 = f32[8,128,256]{2,1,0:T(8,128)} custom-call(s32[1]{0:T(128)} %bitcast.me_ref, s32[8,16]{1,0:T(8,128)} %bitcast.101, s32[8]{0:T(128)} %bitcast.103, bf16[8,16,128,128]{3,2,1,0:T(8,128)(2,1)} %bitcast.73, bf16[16384,256]{1,0:T(8,128)(2,1)} %all-gather.2.cloned.1.call-done.low_hbm, bf16[16384,256]{1,0:T(8,128)(2,1)} %bitcast.68), custom_call_target="tpu_custom_call" | custom-call | flops 1073741824 | bytes 22020096 | tf_op jit(solution)/shard_map/pallas_call | solution.py:111
  169.9 10.7 %collective-permute-done.14 = f32[512,256]{1,0:T(8,128)S(1)} collective-permute-done((f32[512,256]{1,0:T(8,128)S(1)}, f32[512,256]{1,0:T(8,128)S(1)}, u32[]{:S(2)}, u32[]{:S(2)}) %collective-permute-start.14) | collective-permute-done | bytes 524320 | tf_op jit(solution)/shard_map/ppermute | solution.py:167
  183.2 10.2 %collective-permute-done.15 = f32[256,256]{1,0:T(8,128)S(1)} collective-permute-done((f32[256,256]{1,0:T(8,128)S(1)}, f32[256,256]{1,0:T(8,128)S(1)}, u32[]{:S(2)}, u32[]{:S(2)}) %collective-permute-start.15) | collective-permute-done | bytes 262176 | tf_op jit(solution)/shard_map/ppermute | solution.py:209
  193.5 9.2 %collective-permute-start.16 = (f32[256,256]{1,0:T(8,128)S(1)}, f32[256,256]{1,0:T(8,128)S(1)}, u32[]{:S(2)}, u32[]{:S(2)}) collective-permute-start(f32[256,256]{1,0:T(8,128)S(1)} %add.133), channel_id=1, source_target_pairs={{0,1},{1,0},{2,3},{3,2},{4,5},{5,4},{6,7},{7,6},{8,9},{9,8},{10,11... | collective-permute-start | bytes 786440 | tf_op jit(solution)/shard_map/ppermute | solution.py:209
  203.9 3.2 collective-permute-start.17
  207.1 6.6 %collective-permute-done.17 = f32[256,256]{1,0:T(8,128)S(1)} collective-permute-done((f32[256,256]{1,0:T(8,128)S(1)}, f32[256,256]{1,0:T(8,128)S(1)}, u32[]{:S(2)}, u32[]{:S(2)}) %collective-permute-start.17) | collective-permute-done | bytes 262176 | tf_op jit(solution)/shard_map/ppermute | solution.py:209
  213.7 8.4 %collective-permute-start.18 = (f32[256,256]{1,0:T(8,128)S(1)}, f32[256,256]{1,0:T(8,128)S(1)}, u32[]{:S(2)}, u32[]{:S(2)}) collective-permute-start(f32[256,256]{1,0:T(8,128)S(1)} %add.135), channel_id=1, source_target_pairs={{0,4},{1,5},{2,6},{3,7},{4,0},{5,1},{6,2},{7,3},{8,12},{9,13},{10,... | collective-permute-start | bytes 786440 | tf_op jit(solution)/shard_map/ppermute | solution.py:209
  222.1 5.8 %collective-permute-done.18 = f32[256,256]{1,0:T(8,128)S(1)} collective-permute-done((f32[256,256]{1,0:T(8,128)S(1)}, f32[256,256]{1,0:T(8,128)S(1)}, u32[]{:S(2)}, u32[]{:S(2)}) %collective-permute-start.18) | collective-permute-done | bytes 262176 | tf_op jit(solution)/shard_map/ppermute | solution.py:209
  227.9 1.6 collective-permute-start.19
  229.5 5.4 %collective-permute-done.19 = f32[256,256]{1,0:T(8,128)S(1)} collective-permute-done((f32[256,256]{1,0:T(8,128)S(1)}, f32[256,256]{1,0:T(8,128)S(1)}, u32[]{:S(2)}, u32[]{:S(2)}) %collective-permute-start.19) | collective-permute-done | bytes 262176 | tf_op jit(solution)/shard_map/ppermute | solution.py:209
  235.3 3.1 collective-permute-start.22
  238.4 3.5 collective-permute-done.20
  244.1 5.8 %collective-permute-done.21 = f32[256,256]{1,0:T(8,128)S(1)} collective-permute-done((f32[256,256]{1,0:T(8,128)S(1)}, f32[256,256]{1,0:T(8,128)S(1)}, u32[]{:S(2)}, u32[]{:S(2)}) %collective-permute-start.21) | collective-permute-done | bytes 262176 | tf_op jit(solution)/shard_map/ppermute | solution.py:209
  250.0 25.6 %shard_map.86 = (f32[128,128,256]{2,1,0:T(8,128)}, f32[128,128,256]{2,1,0:T(8,128)}) custom-call(s32[2]{0:T(128)} %pad_add_fusion.side_ref, s32[8,16]{1,0:T(8,128)} %bitcast.102, s32[8]{0:T(128)} %bitcast.104, bf16[8,16,128,128]{3,2,1,0:T(8,128)(2,1)} %bitcast.74, bf16[2,4,128,256]{3,2,1,0:T(8,128)(2,1)} %pad_maximum_fusion.4.grad_ref), custom_call_target="tpu_custom_call" | custom-call | flops 1073741824 | bytes 38273024 | tf_op jit(solution)/shard_map/pallas_call | solution.py:140
  275.6 5.7 %collective-permute-start.23 = (f32[128,128,256]{2,1,0:T(8,128)}, f32[128,128,256]{2,1,0:T(8,128)S(1)}, u32[]{:S(2)}, u32[]{:S(2)}) collective-permute-start(f32[128,128,256]{2,1,0:T(8,128)} %get-tuple-element.10), channel_id=1, source_target_pairs={{0,1},{1,0},{2,3},{3,2},{4,5},{5,4},{6,7},{7,6},{8,9},{9,8},{10,11... | collective-permute-start | bytes 50331656 | tf_op jit(solution)/shard_map/ppermute | solution.py:175
  281.3 25.0 %collective-permute-done.23 = f32[128,128,256]{2,1,0:T(8,128)S(1)} collective-permute-done((f32[128,128,256]{2,1,0:T(8,128)}, f32[128,128,256]{2,1,0:T(8,128)S(1)}, u32[]{:S(2)}, u32[]{:S(2)}) %collective-permute-start.23) | collective-permute-done | bytes 16777248 | tf_op jit(solution)/shard_map/ppermute | solution.py:175
  306.3 15.8 %fusion.6 = (f32[16,128,256]{2,1,0:T(8,128)}, f32[16,128,256]{2,1,0:T(8,128)}, f32[16,128,256]{2,1,0:T(8,128)}, f32[16,128,256]{2,1,0:T(8,128)}, f32[16,128,256]{2,1,0:T(8,128)}, /*index=5*/f32[16,128,256]{2,1,0:T(8,128)}) fusion(f32[2,4,16,128,256]{4,3,2,1,0:T(8,128)S(1)} %bitcast.71, f32[2,4,16,128,256]{4,3,2,1,0:T(8,128)} %bitcast.69), kind=kLoop, calls=%fused_computation.14 | loop fusion | flops 3145728 | bytes 37748736 | tf_op jit(solution)/shard_map/add | solution.py:182
  322.1 9.8 %collective-permute-start.25 = (f32[16,128,256]{2,1,0:T(8,128)}, f32[16,128,256]{2,1,0:T(8,128)S(1)}, u32[]{:S(2)}, u32[]{:S(2)}) collective-permute-start(f32[16,128,256]{2,1,0:T(8,128)} %get-tuple-element.13), channel_id=1, source_target_pairs={{0,4},{1,5},{2,6},{3,7},{4,0},{5,1},{6,2},{7,3},{8,12},{9,13},{10,... | collective-permute-start | bytes 6291464 | tf_op jit(solution)/shard_map/ppermute | solution.py:175
  333.9 44.1 %collective-permute-done.25 = f32[16,128,256]{2,1,0:T(8,128)S(1)} collective-permute-done((f32[16,128,256]{2,1,0:T(8,128)}, f32[16,128,256]{2,1,0:T(8,128)S(1)}, u32[]{:S(2)}, u32[]{:S(2)}) %collective-permute-start.25) | collective-permute-done | bytes 2097184 | tf_op jit(solution)/shard_map/ppermute | solution.py:175
  378.0 2.6 collective-permute-done.33
  380.6 1.5 collective-permute-done.32
  382.2 43.8 %collective-permute-done.31 = f32[16,128,256]{2,1,0:T(8,128)S(1)} collective-permute-done((f32[16,128,256]{2,1,0:T(8,128)}, f32[16,128,256]{2,1,0:T(8,128)S(1)}, u32[]{:S(2)}, u32[]{:S(2)}) %collective-permute-start.31) | collective-permute-done | bytes 2097184 | tf_op jit(solution)/shard_map/ppermute | solution.py:175
  428.7 8.7 %fusion.9 = (f32[16,128,256]{2,1,0:T(8,128)S(1)}, f32[16,128,256]{2,1,0:T(8,128)S(1)}) fusion(f32[2,4,16,128,256]{4,3,2,1,0:T(8,128)} %bitcast.72, f32[2,4,16,128,256]{4,3,2,1,0:T(8,128)} %bitcast.70, f32[16,128,256]{2,1,0:T(8,128)} %copy-done.6, f32[16,128,256]{2,1,0:T(8,128)} %collective-permute-done.24, f32[16,128,256]{2,1,0:T(8,128)S(1)} %collective-permute-done.25, ...), kind=kLoop, calls=%fused_computation.19 | loop fusion | flops 4194304 | bytes 25165824 | tf_op jit(solution)/shard_map/add | solution.py:184
  442.4 11.6 %collective-permute-done.28 = f32[4,128,256]{2,1,0:T(8,128)S(1)} collective-permute-done((f32[4,128,256]{2,1,0:T(8,128)S(1)}, f32[4,128,256]{2,1,0:T(8,128)S(1)}, u32[]{:S(2)}, u32[]{:S(2)}) %collective-permute-start.28) | collective-permute-done | bytes 524320 | tf_op jit(solution)/shard_map/ppermute | solution.py:175
  454.0 8.4 %collective-permute-done.29 = f32[4,128,256]{2,1,0:T(8,128)S(1)} collective-permute-done((f32[4,128,256]{2,1,0:T(8,128)S(1)}, f32[4,128,256]{2,1,0:T(8,128)S(1)}, u32[]{:S(2)}, u32[]{:S(2)}) %collective-permute-start.29) | collective-permute-done | bytes 524320 | tf_op jit(solution)/shard_map/ppermute | solution.py:175
  462.4 1.9 collective-permute-done.27
  464.6 3.3 collective-permute-done.34
  468.9 4.8 collective-permute-done.30
  473.8 4.6 collective-permute-done.37
  (83 shorter events, 26.3 us)
Async XLA Ops:
  7.2 174.5 %copy-start = (bf16[256,256]{1,0:T(8,128)(2,1)S(1)}, bf16[256,256]{1,0:T(8,128)(2,1)}, u32[]{:S(2)}) copy-start(bf16[256,256]{1,0:T(8,128)(2,1)} %param.7) | copy-start | bytes 393220
  7.2 141.4 %all-gather.2.cloned.1.call-start = ((), (), s32[]{:S(2)}) async-start(), calls=%async_computation | async-start | bytes 8519680 | tf_op jit(solution)/shard_map/all_gather | solution.py:222
  8.9 5.2 %collective-permute-start = (bf16[2,128,256]{2,1,0:T(8,128)(2,1)S(1)}, bf16[2,128,256]{2,1,0:T(8,128)(2,1)S(1)}, u32[]{:S(2)}, u32[]{:S(2)}) collective-permute-start(bf16[2,128,256]{2,1,0:T(8,128)(2,1)S(1)} %bitcast.84), channel_id=1, source_target_pairs={{0,8},{1,9},{2,10},{3,11},{4,12},{5,13},{6,14},{7,15},{8,0},{9,1},... | collective-permute-start | bytes 393224 | tf_op jit(solution)/shard_map/ppermute | solution.py:175
  14.2 7.7 %collective-permute-start.9 = (bf16[2,128,256]{2,1,0:T(8,128)(2,1)S(1)}, bf16[2,128,256]{2,1,0:T(8,128)(2,1)S(1)}, u32[]{:S(2)}, u32[]{:S(2)}) collective-permute-start(bf16[2,128,256]{2,1,0:T(8,128)(2,1)S(1)} %bitcast.81), channel_id=1, source_target_pairs={{0,6},{1,7},{2,0},{3,1},{4,2},{5,3},{6,4},{7,5},{8,14},{9,15},{10,... | collective-permute-start | bytes 393224 | tf_op jit(solution)/shard_map/ppermute | solution.py:175
  17.2 7.1 %collective-permute-start.8 = (bf16[2,128,256]{2,1,0:T(8,128)(2,1)S(1)}, bf16[2,128,256]{2,1,0:T(8,128)(2,1)S(1)}, u32[]{:S(2)}, u32[]{:S(2)}) collective-permute-start(bf16[2,128,256]{2,1,0:T(8,128)(2,1)S(1)} %bitcast.82), channel_id=1, source_target_pairs={{0,4},{1,5},{2,6},{3,7},{4,0},{5,1},{6,2},{7,3},{8,12},{9,13},{10,... | collective-permute-start | bytes 393224 | tf_op jit(solution)/shard_map/ppermute | solution.py:175
  18.0 7.6 %collective-permute-start.7 = (bf16[2,128,256]{2,1,0:T(8,128)(2,1)S(1)}, bf16[2,128,256]{2,1,0:T(8,128)(2,1)S(1)}, u32[]{:S(2)}, u32[]{:S(2)}) collective-permute-start(bf16[2,128,256]{2,1,0:T(8,128)(2,1)S(1)} %bitcast.83), channel_id=1, source_target_pairs={{0,2},{1,3},{2,4},{3,5},{4,6},{5,7},{6,0},{7,1},{8,10},{9,11},{10,... | collective-permute-start | bytes 393224 | tf_op jit(solution)/shard_map/ppermute | solution.py:175
  25.7 27.5 %collective-permute-start.11 = (bf16[4,2,128,256]{3,2,1,0:T(8,128)(2,1)S(1)}, bf16[4,2,128,256]{3,2,1,0:T(8,128)(2,1)S(1)}, u32[]{:S(2)}, u32[]{:S(2)}) collective-permute-start(bf16[4,2,128,256]{3,2,1,0:T(8,128)(2,1)S(1)} %get-tuple-element.32), channel_id=1, source_target_pairs={{0,32},{1,33},{2,34},{3,35},{4,36},{5,37},{6,38},{7,39},{8,40},{9,... | collective-permute-start | bytes 1572872 | tf_op jit(solution)/shard_map/ppermute | solution.py:175
  29.6 20.0 %collective-permute-start.3 = (bf16[2,128,256]{2,1,0:T(8,128)(2,1)S(1)}, bf16[2,128,256]{2,1,0:T(8,128)(2,1)S(1)}, u32[]{:S(2)}, u32[]{:S(2)}) collective-permute-start(bf16[2,128,256]{2,1,0:T(8,128)(2,1)S(1)} %bitcast.78), channel_id=1, source_target_pairs={{0,48},{1,49},{2,50},{3,51},{4,52},{5,53},{6,54},{7,55},{8,56},{9,... | collective-permute-start | bytes 393224 | tf_op jit(solution)/shard_map/ppermute | solution.py:175
  30.3 20.3 %collective-permute-start.2 = (bf16[2,128,256]{2,1,0:T(8,128)(2,1)S(1)}, bf16[2,128,256]{2,1,0:T(8,128)(2,1)S(1)}, u32[]{:S(2)}, u32[]{:S(2)}) collective-permute-start(bf16[2,128,256]{2,1,0:T(8,128)(2,1)S(1)} %bitcast.79), channel_id=1, source_target_pairs={{0,32},{1,33},{2,34},{3,35},{4,36},{5,37},{6,38},{7,39},{8,40},{9,... | collective-permute-start | bytes 393224 | tf_op jit(solution)/shard_map/ppermute | solution.py:175
  32.7 20.2 %collective-permute-start.1 = (bf16[2,128,256]{2,1,0:T(8,128)(2,1)S(1)}, bf16[2,128,256]{2,1,0:T(8,128)(2,1)S(1)}, u32[]{:S(2)}, u32[]{:S(2)}) collective-permute-start(bf16[2,128,256]{2,1,0:T(8,128)(2,1)S(1)} %bitcast.80), channel_id=1, source_target_pairs={{0,16},{1,17},{2,18},{3,19},{4,20},{5,21},{6,22},{7,23},{8,24},{9,... | collective-permute-start | bytes 393224 | tf_op jit(solution)/shard_map/ppermute | solution.py:175
  32.7 35.2 %collective-permute-start.10 = (bf16[4,2,128,256]{3,2,1,0:T(8,128)(2,1)S(1)}, bf16[4,2,128,256]{3,2,1,0:T(8,128)(2,1)S(1)}, u32[]{:S(2)}, u32[]{:S(2)}) collective-permute-start(bf16[4,2,128,256]{3,2,1,0:T(8,128)(2,1)S(1)} %get-tuple-element.32), channel_id=1, source_target_pairs={{0,16},{1,17},{2,18},{3,19},{4,20},{5,21},{6,22},{7,23},{8,24},{9,... | collective-permute-start | bytes 1572872 | tf_op jit(solution)/shard_map/ppermute | solution.py:175
  49.6 21.2 %collective-permute-start.12 = (bf16[4,2,128,256]{3,2,1,0:T(8,128)(2,1)S(1)}, bf16[4,2,128,256]{3,2,1,0:T(8,128)(2,1)S(1)}, u32[]{:S(2)}, u32[]{:S(2)}) collective-permute-start(bf16[4,2,128,256]{3,2,1,0:T(8,128)(2,1)S(1)} %get-tuple-element.32), channel_id=1, source_target_pairs={{0,48},{1,49},{2,50},{3,51},{4,52},{5,53},{6,54},{7,55},{8,56},{9,... | collective-permute-start | bytes 1572872 | tf_op jit(solution)/shard_map/ppermute | solution.py:175
  53.0 19.6 %collective-permute-start.5 = (bf16[4,2,128,256]{3,2,1,0:T(8,128)(2,1)S(1)}, bf16[4,2,128,256]{3,2,1,0:T(8,128)(2,1)S(1)}, u32[]{:S(2)}, u32[]{:S(2)}) collective-permute-start(bf16[4,2,128,256]{3,2,1,0:T(8,128)(2,1)S(1)} %get-tuple-element.30), channel_id=1, source_target_pairs={{0,4},{1,5},{2,6},{3,7},{4,0},{5,1},{6,2},{7,3},{8,12},{9,13},{10,... | collective-permute-start | bytes 1572872 | tf_op jit(solution)/shard_map/ppermute | solution.py:175
  53.1 31.7 %collective-permute-start.4 = (bf16[4,2,128,256]{3,2,1,0:T(8,128)(2,1)S(1)}, bf16[4,2,128,256]{3,2,1,0:T(8,128)(2,1)S(1)}, u32[]{:S(2)}, u32[]{:S(2)}) collective-permute-start(bf16[4,2,128,256]{3,2,1,0:T(8,128)(2,1)S(1)} %get-tuple-element.30), channel_id=1, source_target_pairs={{0,2},{1,3},{2,4},{3,5},{4,6},{5,7},{6,0},{7,1},{8,10},{9,11},{10,... | collective-permute-start | bytes 1572872 | tf_op jit(solution)/shard_map/ppermute | solution.py:175
  53.2 31.6 %collective-permute-start.6 = (bf16[4,2,128,256]{3,2,1,0:T(8,128)(2,1)S(1)}, bf16[4,2,128,256]{3,2,1,0:T(8,128)(2,1)S(1)}, u32[]{:S(2)}, u32[]{:S(2)}) collective-permute-start(bf16[4,2,128,256]{3,2,1,0:T(8,128)(2,1)S(1)} %get-tuple-element.30), channel_id=1, source_target_pairs={{0,6},{1,7},{2,0},{3,1},{4,2},{5,3},{6,4},{7,5},{8,14},{9,15},{10,... | collective-permute-start | bytes 1572872 | tf_op jit(solution)/shard_map/ppermute | solution.py:175
  88.6 7.5 %collective-permute-start.13 = (bf16[2,4,4,2,128,256]{5,4,3,2,1,0:T(8,128)(2,1)}, bf16[2,4,4,2,128,256]{5,4,3,2,1,0:T(8,128)(2,1)}, u32[]{:S(2)}, u32[]{:S(2)}) collective-permute-start(bf16[2,4,4,2,128,256]{5,4,3,2,1,0:T(8,128)(2,1)} %get-tuple-element.20), channel_id=1, source_target_pairs={{0,1},{1,0},{2,3},{3,2},{4,5},{5,4},{6,7},{7,6},{8,9},{9,8},{10,11... | collective-permute-start | bytes 12582920 | tf_op jit(solution)/shard_map/ppermute | solution.py:175
  168.7 13.0 %copy-start.7 = (bf16[512,256]{1,0:T(8,128)(2,1)S(1)}, bf16[512,256]{1,0:T(8,128)(2,1)}, u32[]{:S(2)}) copy-start(bf16[512,256]{1,0:T(8,128)(2,1)} %param.11) | copy-start | bytes 786436
  169.8 10.8 %collective-permute-start.14 = (f32[512,256]{1,0:T(8,128)S(1)}, f32[512,256]{1,0:T(8,128)S(1)}, u32[]{:S(2)}, u32[]{:S(2)}) collective-permute-start(f32[512,256]{1,0:T(8,128)S(1)} %constant_dynamic-slice_fusion), channel_id=1, source_target_pairs={{0,64},{64,0},{1,65},{65,1},{2,66},{66,2},{3,67},{67,3},{4,68},{68... | collective-permute-start | bytes 1572872 | tf_op jit(solution)/shard_map/ppermute | solution.py:167
  183.1 10.3 %collective-permute-start.15 = (f32[256,256]{1,0:T(8,128)S(1)}, f32[256,256]{1,0:T(8,128)S(1)}, u32[]{:S(2)}, u32[]{:S(2)}) collective-permute-start(f32[256,256]{1,0:T(8,128)S(1)} %fusion.19), channel_id=1, source_target_pairs={{0,64},{64,0},{1,65},{65,1},{2,66},{66,2},{3,67},{67,3},{4,68},{68... | collective-permute-start | bytes 786440 | tf_op jit(solution)/shard_map/ppermute | solution.py:209
  193.5 10.4 %collective-permute-start.16 = (f32[256,256]{1,0:T(8,128)S(1)}, f32[256,256]{1,0:T(8,128)S(1)}, u32[]{:S(2)}, u32[]{:S(2)}) collective-permute-start(f32[256,256]{1,0:T(8,128)S(1)} %add.133), channel_id=1, source_target_pairs={{0,1},{1,0},{2,3},{3,2},{4,5},{5,4},{6,7},{7,6},{8,9},{9,8},{10,11... | collective-permute-start | bytes 786440 | tf_op jit(solution)/shard_map/ppermute | solution.py:209
  203.9 9.8 %collective-permute-start.17 = (f32[256,256]{1,0:T(8,128)S(1)}, f32[256,256]{1,0:T(8,128)S(1)}, u32[]{:S(2)}, u32[]{:S(2)}) collective-permute-start(f32[256,256]{1,0:T(8,128)S(1)} %add.134), channel_id=1, source_target_pairs={{0,2},{1,3},{2,0},{3,1},{4,6},{5,7},{6,4},{7,5},{8,10},{9,11},{10,... | collective-permute-start | bytes 786440 | tf_op jit(solution)/shard_map/ppermute | solution.py:209
  213.7 14.2 %collective-permute-start.18 = (f32[256,256]{1,0:T(8,128)S(1)}, f32[256,256]{1,0:T(8,128)S(1)}, u32[]{:S(2)}, u32[]{:S(2)}) collective-permute-start(f32[256,256]{1,0:T(8,128)S(1)} %add.135), channel_id=1, source_target_pairs={{0,4},{1,5},{2,6},{3,7},{4,0},{5,1},{6,2},{7,3},{8,12},{9,13},{10,... | collective-permute-start | bytes 786440 | tf_op jit(solution)/shard_map/ppermute | solution.py:209
  227.9 7.0 %collective-permute-start.19 = (f32[256,256]{1,0:T(8,128)S(1)}, f32[256,256]{1,0:T(8,128)S(1)}, u32[]{:S(2)}, u32[]{:S(2)}) collective-permute-start(f32[256,256]{1,0:T(8,128)S(1)} %add.136), channel_id=1, source_target_pairs={{0,8},{1,9},{2,10},{3,11},{4,12},{5,13},{6,14},{7,15},{8,0},{9,1},... | collective-permute-start | bytes 786440 | tf_op jit(solution)/shard_map/ppermute | solution.py:209
  234.9 7.0 %collective-permute-start.20 = (f32[256,256]{1,0:T(8,128)S(1)}, f32[256,256]{1,0:T(8,128)S(1)}, u32[]{:S(2)}, u32[]{:S(2)}) collective-permute-start(f32[256,256]{1,0:T(8,128)S(1)} %add.137), channel_id=1, source_target_pairs={{0,16},{1,17},{2,18},{3,19},{4,20},{5,21},{6,22},{7,23},{8,24},{9,... | collective-permute-start | bytes 786440 | tf_op jit(solution)/shard_map/ppermute | solution.py:209
  235.3 8.0 %collective-permute-start.22 = (bf16[512,256]{1,0:T(8,128)(2,1)S(1)}, bf16[512,256]{1,0:T(8,128)(2,1)S(1)}, u32[]{:S(2)}, u32[]{:S(2)}) collective-permute-start(bf16[512,256]{1,0:T(8,128)(2,1)S(1)} %convolution_convert_fusion), channel_id=1, source_target_pairs={{0,64},{64,0},{1,65},{65,1},{2,66},{66,2},{3,67},{67,3},{4,68},{68... | collective-permute-start | bytes 786440 | tf_op jit(solution)/shard_map/ppermute | solution.py:167
  242.0 8.0 %collective-permute-start.21 = (f32[256,256]{1,0:T(8,128)S(1)}, f32[256,256]{1,0:T(8,128)S(1)}, u32[]{:S(2)}, u32[]{:S(2)}) collective-permute-start(f32[256,256]{1,0:T(8,128)S(1)} %add.138), channel_id=1, source_target_pairs={{0,32},{1,33},{2,34},{3,35},{4,36},{5,37},{6,38},{7,39},{8,40},{9,... | collective-permute-start | bytes 786440 | tf_op jit(solution)/shard_map/ppermute | solution.py:209
  275.6 30.7 %collective-permute-start.23 = (f32[128,128,256]{2,1,0:T(8,128)}, f32[128,128,256]{2,1,0:T(8,128)S(1)}, u32[]{:S(2)}, u32[]{:S(2)}) collective-permute-start(f32[128,128,256]{2,1,0:T(8,128)} %get-tuple-element.10), channel_id=1, source_target_pairs={{0,1},{1,0},{2,3},{3,2},{4,5},{5,4},{6,7},{7,6},{8,9},{9,8},{10,11... | collective-permute-start | bytes 50331656 | tf_op jit(solution)/shard_map/ppermute | solution.py:175
  306.3 15.8 %copy-start.2 = (f32[128,128,256]{2,1,0:T(8,128)}, f32[128,128,256]{2,1,0:T(8,128)S(1)}, u32[]{:S(2)}) copy-start(f32[128,128,256]{2,1,0:T(8,128)S(1)} %collective-permute-done.23) | copy-start | bytes 50331652
  322.1 55.9 %collective-permute-start.25 = (f32[16,128,256]{2,1,0:T(8,128)}, f32[16,128,256]{2,1,0:T(8,128)S(1)}, u32[]{:S(2)}, u32[]{:S(2)}) collective-permute-start(f32[16,128,256]{2,1,0:T(8,128)} %get-tuple-element.13), channel_id=1, source_target_pairs={{0,4},{1,5},{2,6},{3,7},{4,0},{5,1},{6,2},{7,3},{8,12},{9,13},{10,... | collective-permute-start | bytes 6291464 | tf_op jit(solution)/shard_map/ppermute | solution.py:175
  331.9 48.7 %collective-permute-start.33 = (f32[16,128,256]{2,1,0:T(8,128)}, f32[16,128,256]{2,1,0:T(8,128)S(1)}, u32[]{:S(2)}, u32[]{:S(2)}) collective-permute-start(f32[16,128,256]{2,1,0:T(8,128)} %get-tuple-element.14), channel_id=1, source_target_pairs={{0,48},{1,49},{2,50},{3,51},{4,52},{5,53},{6,54},{7,55},{8,56},{9,... | collective-permute-start | bytes 6291464 | tf_op jit(solution)/shard_map/ppermute | solution.py:175
  331.9 50.3 %collective-permute-start.32 = (f32[16,128,256]{2,1,0:T(8,128)}, f32[16,128,256]{2,1,0:T(8,128)S(1)}, u32[]{:S(2)}, u32[]{:S(2)}) collective-permute-start(f32[16,128,256]{2,1,0:T(8,128)} %get-tuple-element.15), channel_id=1, source_target_pairs={{0,32},{1,33},{2,34},{3,35},{4,36},{5,37},{6,38},{7,39},{8,40},{9,... | collective-permute-start | bytes 6291464 | tf_op jit(solution)/shard_map/ppermute | solution.py:175
  333.1 92.8 %collective-permute-start.31 = (f32[16,128,256]{2,1,0:T(8,128)}, f32[16,128,256]{2,1,0:T(8,128)S(1)}, u32[]{:S(2)}, u32[]{:S(2)}) collective-permute-start(f32[16,128,256]{2,1,0:T(8,128)} %get-tuple-element.16), channel_id=1, source_target_pairs={{0,16},{1,17},{2,18},{3,19},{4,20},{5,21},{6,22},{7,23},{8,24},{9,... | collective-permute-start | bytes 6291464 | tf_op jit(solution)/shard_map/ppermute | solution.py:175
  333.9 92.0 %collective-permute-start.26 = (f32[16,128,256]{2,1,0:T(8,128)}, f32[16,128,256]{2,1,0:T(8,128)S(1)}, u32[]{:S(2)}, u32[]{:S(2)}) collective-permute-start(f32[16,128,256]{2,1,0:T(8,128)} %get-tuple-element.17), channel_id=1, source_target_pairs={{0,6},{1,7},{2,0},{3,1},{4,2},{5,3},{6,4},{7,5},{8,14},{9,15},{10,... | collective-permute-start | bytes 6291464 | tf_op jit(solution)/shard_map/ppermute | solution.py:175
  378.0 50.6 %collective-permute-start.24 = (f32[16,128,256]{2,1,0:T(8,128)}, f32[16,128,256]{2,1,0:T(8,128)}, u32[]{:S(2)}, u32[]{:S(2)}) collective-permute-start(f32[16,128,256]{2,1,0:T(8,128)} %get-tuple-element.18), channel_id=1, source_target_pairs={{0,2},{1,3},{2,4},{3,5},{4,6},{5,7},{6,0},{7,1},{8,10},{9,11},{10,... | collective-permute-start | bytes 6291464 | tf_op jit(solution)/shard_map/ppermute | solution.py:175
  380.6 45.3 %copy-start.3 = (f32[16,128,256]{2,1,0:T(8,128)}, f32[16,128,256]{2,1,0:T(8,128)S(1)}, u32[]{:S(2)}) copy-start(f32[16,128,256]{2,1,0:T(8,128)S(1)} %collective-permute-done.33) | copy-start | bytes 6291460
  382.2 43.8 %copy-start.4 = (f32[16,128,256]{2,1,0:T(8,128)}, f32[16,128,256]{2,1,0:T(8,128)S(1)}, u32[]{:S(2)}) copy-start(f32[16,128,256]{2,1,0:T(8,128)S(1)} %collective-permute-done.32) | copy-start | bytes 6291460
  425.9 1.4 copy-start.5
  427.3 1.4 copy-start.6
  437.6 16.4 %collective-permute-start.28 = (f32[4,128,256]{2,1,0:T(8,128)S(1)}, f32[4,128,256]{2,1,0:T(8,128)S(1)}, u32[]{:S(2)}, u32[]{:S(2)}) collective-permute-start(f32[4,128,256]{2,1,0:T(8,128)S(1)} %get-tuple-element.21), channel_id=1, source_target_pairs={{0,32},{1,33},{2,34},{3,35},{4,36},{5,37},{6,38},{7,39},{8,40},{9,... | collective-permute-start | bytes 1572872 | tf_op jit(solution)/shard_map/ppermute | solution.py:175
  438.6 23.8 %collective-permute-start.29 = (f32[4,128,256]{2,1,0:T(8,128)S(1)}, f32[4,128,256]{2,1,0:T(8,128)S(1)}, u32[]{:S(2)}, u32[]{:S(2)}) collective-permute-start(f32[4,128,256]{2,1,0:T(8,128)S(1)} %get-tuple-element.22), channel_id=1, source_target_pairs={{0,48},{1,49},{2,50},{3,51},{4,52},{5,53},{6,54},{7,55},{8,56},{9,... | collective-permute-start | bytes 1572872 | tf_op jit(solution)/shard_map/ppermute | solution.py:175
  439.8 24.6 %collective-permute-start.27 = (f32[4,128,256]{2,1,0:T(8,128)S(1)}, f32[4,128,256]{2,1,0:T(8,128)S(1)}, u32[]{:S(2)}, u32[]{:S(2)}) collective-permute-start(f32[4,128,256]{2,1,0:T(8,128)S(1)} %get-tuple-element.23), channel_id=1, source_target_pairs={{0,16},{1,17},{2,18},{3,19},{4,20},{5,21},{6,22},{7,23},{8,24},{9,... | collective-permute-start | bytes 1572872 | tf_op jit(solution)/shard_map/ppermute | solution.py:175
  440.8 23.8 %collective-permute-start.35 = (f32[4,128,256]{2,1,0:T(8,128)S(1)}, f32[4,128,256]{2,1,0:T(8,128)S(1)}, u32[]{:S(2)}, u32[]{:S(2)}) collective-permute-start(f32[4,128,256]{2,1,0:T(8,128)S(1)} %get-tuple-element.24), channel_id=1, source_target_pairs={{0,4},{1,5},{2,6},{3,7},{4,0},{5,1},{6,2},{7,3},{8,12},{9,13},{10,... | collective-permute-start | bytes 1572872 | tf_op jit(solution)/shard_map/ppermute | solution.py:175
  441.2 23.4 %collective-permute-start.36 = (f32[4,128,256]{2,1,0:T(8,128)S(1)}, f32[4,128,256]{2,1,0:T(8,128)S(1)}, u32[]{:S(2)}, u32[]{:S(2)}) collective-permute-start(f32[4,128,256]{2,1,0:T(8,128)S(1)} %get-tuple-element.25), channel_id=1, source_target_pairs={{0,6},{1,7},{2,0},{3,1},{4,2},{5,3},{6,4},{7,5},{8,14},{9,15},{10,... | collective-permute-start | bytes 1572872 | tf_op jit(solution)/shard_map/ppermute | solution.py:175
  454.0 14.0 %collective-permute-start.34 = (f32[4,128,256]{2,1,0:T(8,128)S(1)}, f32[4,128,256]{2,1,0:T(8,128)S(1)}, u32[]{:S(2)}, u32[]{:S(2)}) collective-permute-start(f32[4,128,256]{2,1,0:T(8,128)S(1)} %get-tuple-element.26), channel_id=1, source_target_pairs={{0,2},{1,3},{2,4},{3,5},{4,6},{5,7},{6,0},{7,1},{8,10},{9,11},{10,... | collective-permute-start | bytes 1572872 | tf_op jit(solution)/shard_map/ppermute | solution.py:175
  464.5 9.2 %collective-permute-start.30 = (f32[2,128,256]{2,1,0:T(8,128)S(1)}, f32[2,128,256]{2,1,0:T(8,128)S(1)}, u32[]{:S(2)}, u32[]{:S(2)}) collective-permute-start(f32[2,128,256]{2,1,0:T(8,128)S(1)} %slice.155), channel_id=1, source_target_pairs={{0,8},{1,9},{2,10},{3,11},{4,12},{5,13},{6,14},{7,15},{8,0},{9,1},... | collective-permute-start | bytes 786440 | tf_op jit(solution)/shard_map/ppermute | solution.py:175
  467.9 11.3 %copy-start.1 = (bf16[256,256]{1,0:T(8,128)(2,1)S(1)}, bf16[256,256]{1,0:T(8,128)(2,1)}, u32[]{:S(2)}) copy-start(bf16[256,256]{1,0:T(8,128)(2,1)} %param.7) | copy-start | bytes 393220
  468.1 10.3 %collective-permute-start.37 = (f32[2,128,256]{2,1,0:T(8,128)S(1)}, f32[2,128,256]{2,1,0:T(8,128)S(1)}, u32[]{:S(2)}, u32[]{:S(2)}) collective-permute-start(f32[2,128,256]{2,1,0:T(8,128)S(1)} %slice.169), channel_id=1, source_target_pairs={{0,8},{1,9},{2,10},{3,11},{4,12},{5,13},{6,14},{7,15},{8,0},{9,1},... | collective-permute-start | bytes 786440 | tf_op jit(solution)/shard_map/ppermute | solution.py:175
Sparse Core Ops, SparseCore 0:
  10.3 138.2 all-gather.1

commit v8 on v6

--- a/solution.py
+++ b/solution.py
@@ -186,19 +186,16 @@
     first = [keep[0, s] + came[0, s] for s in range(4)]
     second = [keep[1, s] + came[1, s] for s in range(4)]
 
-    sent = [shifted(jnp.concatenate([first[s], held]), 2, 4, s) for s in range(1, 4)]
-    held = ordered_sum(held, [m[16:] for m in sent], (me // 2) % 4, 4)
-    first = (first[0] + sum(m[:16] for m in sent)).reshape(4, 4, block, width)
+    held = ordered_sum(held, [shifted(held, 2, 4, s) for s in range(1, 4)], (me // 2) % 4, 4)
+    first = (first[0] + sum(shifted(first[s], 2, 4, s) for s in range(1, 4))).reshape(4, 4, block, width)
     second = (second[0] + sum(shifted(second[s], 16, 4, s) for s in range(1, 4))).reshape(4, 4, block, width)
 
-    sent = [shifted(jnp.concatenate([first[s], held]), 16, 4, s) for s in range(1, 4)]
-    held = ordered_sum(held, [m[4:] for m in sent], me // 16, 4)
-    first = (first[0] + sum(m[:4] for m in sent)).reshape(2, 2, block, width)
+    held = ordered_sum(held, [shifted(held, 16, 4, s) for s in range(1, 4)], me // 16, 4)
+    first = (first[0] + sum(shifted(first[s], 16, 4, s) for s in range(1, 4))).reshape(2, 2, block, width)
     second = (second[0] + sum(shifted(second[s], 2, 4, s) for s in range(1, 4))).reshape(2, 2, block, width)
 
-    sent = shifted(jnp.concatenate([first[1], held]), 8, 2, 1)
-    held = held + sent[2:]
-    first = first[0] + sent[:2]
+    held = held + shifted(held, 8, 2, 1)
+    first = first[0] + shifted(first[1], 8, 2, 1)
     second = second[0] + shifted(second[1], 8, 2, 1)
     return jnp.concatenate([first, second]).reshape(-1, width), held
 

time: 480 us -> 492 us (1.025)
  starting transfers between devices: 69 us -> 79.4 us
  waiting for transfers between devices: 309 us -> 319 us
  other arithmetic: 41.3 us -> 32.3 us
    ppermute x15 -> x22, waiting for transfers between devices: 160 us -> 180 us  [shifted(): return lax.ppermute(value, 'row', [(r, dest(r)) for r in range(64)])]
    ppermute x3, starting transfers between devices: 8.12 us -> 22.9 us  [swap(): return lax.ppermute(value, axis, [(i, i ^ 1) for i in range(size)])]
    ppermute x3, waiting for transfers between devices: 20.6 us -> 10.6 us  [swap(): return lax.ppermute(value, axis, [(i, i ^ 1) for i in range(size)])]
    concatenate x3 -> x0, other arithmetic: 7.02 us -> none  [the longest x2 6.99 us: row_reduce_scatter(): jnp.concatenate([first[s], held])]
    ppermute x15 -> x22, starting transfers between devices: 60.8 us -> 56.5 us  [shifted(): return lax.ppermute(value, 'row', [(r, dest(r)) for r in range(64)])]
    add x3 -> x4, other arithmetic: 25.9 us -> 24.6 us  [the longest x1 15.8 us: row_reduce_scatter(): first = [keep[0, s] + came[0, s] for s in range(4)]]
  transfers between devices with their start and end apart: 19 -> 26, of which waited for: 15 -> 13; matrix products, arithmetic and copies ran while one was open for 2% -> 3% of each run, Pallas kernels for 0% -> 0%
where the time goes in v8:
time: 492 us; the launch traced here: 488 us
  waiting for transfers between devices  319 us (65%)
  starting transfers between devices  79.4 us (16%)
  Pallas kernels  32.7 us (7%)
  other arithmetic  32.3 us (7%)
  between operations  14.3 us (3%)
  local copies, waits for them, and re-layouts  8.31 us (2%)
    ppermute x22, waiting for transfers between devices, shifted(): return lax.ppermute(value, 'row', [(r, dest(r)) for r in range(64)])  180 us
    all_gather x1, waiting for transfers between devices, body(): gathered = lax.all_gather(features, 'row', axis=0, tiled=True)  127 us
    ppermute x22, starting transfers between devices, shifted(): return lax.ppermute(value, 'row', [(r, dest(r)) for r in range(64)])  56.5 us
    ppermute x3, starting transfers between devices, swap(): return lax.ppermute(value, axis, [(i, i ^ 1) for i in range(size)])  22.9 us
    pallas_call x1, Pallas kernels, spread(): pl.pallas_call(spread_kernel, out_shape=[jax.ShapeDtypeStruct((col_blocks...  19.7 us
    add x1, other arithmetic, row_reduce_scatter(): first = [keep[0, s] + came[0, s] for s in range(4)]  15.8 us
    pallas_call x1, Pallas kernels, aggregate(): pl.pallas_call(aggregate_kernel, out_shape=jax.ShapeDtypeStruct((row_bloc...  13 us
    ppermute x3, waiting for transfers between devices, swap(): return lax.ppermute(value, axis, [(i, i ^ 1) for i in range(size)])  10.6 us
  transfers between devices with their start and end apart: 26, of which 13 were waited for; matrix products, arithmetic and copies ran while one was open for 3% of the time, Pallas kernels for 0%

profile of v8, /device:TPU:0, one launch (start us, length us, event | category | flops | bytes accessed | tf_op | source)
XLA Modules:
  0.0 488.2 jit_solution(5401783365854925188)
XLA Ops:
  7.2 0.7 all-gather.2.cloned.1.call-update
  7.9 127.3 %all-gather.2.cloned.1.call-done.panel_hbm = bf16[32768,256]{1,0:T(8,128)(2,1)} async-done(((bf16[512,256]{1,0:T(8,128)(2,1)}), bf16[32768,256]{1,0:T(8,128)(2,1)}) %all-gather.2.cloned.1.call-update) | async-done | bytes 16777232 | tf_op jit(solution)/shard_map/all_gather | solution.py:219
  135.3 13.0 %shard_map.85 = f32[8,128,256]{2,1,0:T(8,128)} custom-call(s32[8,16]{1,0:T(8,128)} %bitcast.53, s32[8]{0:T(128)} %bitcast.55, bf16[8,16,128,128]{3,2,1,0:T(8,128)(2,1)} %bitcast.44, bf16[32768,256]{1,0:T(8,128)(2,1)} %all-gather.2.cloned.1.call-done.panel_hbm), custom_call_target="tpu_custom_call" | custom-call | flops 1073741824 | bytes 22020096 | tf_op jit(solution)/shard_map/pallas_call | solution.py:98
  148.3 1.1 constant_dynamic-slice_fusion
  149.4 16.7 %collective-permute-start = (f32[512,256]{1,0:T(8,128)S(1)}, f32[512,256]{1,0:T(8,128)S(1)}, u32[]{:S(2)}, u32[]{:S(2)}) collective-permute-start(f32[512,256]{1,0:T(8,128)S(1)} %constant_dynamic-slice_fusion), channel_id=1, source_target_pairs={{0,64},{64,0},{1,65},{65,1},{2,66},{66,2},{3,67},{67,3},{4,68},{68... | collective-permute-start | bytes 1572872 | tf_op jit(solution)/shard_map/ppermute | solution.py:156
  166.1 7.5 %collective-permute-done = f32[512,256]{1,0:T(8,128)S(1)} collective-permute-done((f32[512,256]{1,0:T(8,128)S(1)}, f32[512,256]{1,0:T(8,128)S(1)}, u32[]{:S(2)}, u32[]{:S(2)}) %collective-permute-start) | collective-permute-done | bytes 524320 | tf_op jit(solution)/shard_map/ppermute | solution.py:156
  173.6 1.1 add_convert_fusion
  174.8 1.1 multiply_convert_fusion
  175.9 0.3 convolution_convert_fusion
  176.1 3.3 collective-permute-start.1
  179.4 0.7 pad_add_fusion.side_ref
  180.1 1.0 fusion.14
  181.1 3.0 collective-permute-done.1
  184.1 0.8 pad_maximum_fusion.grad_ref
  184.9 19.7 %shard_map.86 = (f32[128,128,256]{2,1,0:T(8,128)}, f32[130,128,256]{2,1,0:T(8,128)}) custom-call(s32[2]{0:T(128)} %pad_add_fusion.side_ref, s32[8,16]{1,0:T(8,128)} %bitcast.54, s32[8]{0:T(128)} %bitcast.56, bf16[8,16,128,128]{3,2,1,0:T(8,128)(2,1)} %bitcast.45, bf16[2,4,128,256]{3,2,1,0:T(8,128)(2,1)} %pad_maximum_fusion.grad_ref, f32[2,128,256]{2,1,0:T(8,128)} %bitcast.49), custom_call_target="tpu_custom_call" | custom-call | flops 1073741824 | bytes 38273024 | tf_op jit(solution)/shard_map/pallas_call | solution.py:125
  204.8 25.7 %collective-permute-done.2 = f32[130,128,256]{2,1,0:T(8,128)S(1)} collective-permute-done((f32[130,128,256]{2,1,0:T(8,128)}, f32[130,128,256]{2,1,0:T(8,128)S(1)}, u32[]{:S(2)}, u32[]{:S(2)}) %collective-permute-start.2) | collective-permute-done | bytes 17039392 | tf_op jit(solution)/shard_map/ppermute | solution.py:164
  230.5 1.9 slice.138
  232.4 4.8 copy-done.3
  237.3 15.8 %fusion.6 = (f32[16,128,256]{2,1,0:T(8,128)}, f32[16,128,256]{2,1,0:T(8,128)}, f32[16,128,256]{2,1,0:T(8,128)}, f32[16,128,256]{2,1,0:T(8,128)}, f32[16,128,256]{2,1,0:T(8,128)}, /*index=5*/f32[16,128,256]{2,1,0:T(8,128)}) fusion(f32[2,4,16,128,256]{4,3,2,1,0:T(8,128)S(1)} %bitcast.40, f32[2,4,16,128,256]{4,3,2,1,0:T(8,128)} %bitcast.42), kind=kLoop, calls=%fused_computation.12 | loop fusion | flops 3145728 | bytes 37748736 | tf_op jit(solution)/shard_map/add | solution.py:186
  253.2 1.1 slice_add_fusion.12
  254.3 23.0 %collective-permute-start.4 = (f32[2,128,256]{2,1,0:T(8,128)S(1)}, f32[2,128,256]{2,1,0:T(8,128)S(1)}, u32[]{:S(2)}, u32[]{:S(2)}) collective-permute-start(f32[2,128,256]{2,1,0:T(8,128)S(1)} %slice_add_fusion.12), channel_id=1, source_target_pairs={{0,4},{1,5},{2,6},{3,7},{4,0},{5,1},{6,2},{7,3},{8,12},{9,13},{10,... | collective-permute-start | bytes 786440 | tf_op jit(solution)/shard_map/ppermute | solution.py:164
  277.3 1.3 collective-permute-start.5
  278.7 47.6 %collective-permute-done.3 = f32[2,128,256]{2,1,0:T(8,128)S(1)} collective-permute-done((f32[2,128,256]{2,1,0:T(8,128)S(1)}, f32[2,128,256]{2,1,0:T(8,128)S(1)}, u32[]{:S(2)}, u32[]{:S(2)}) %collective-permute-start.3) | collective-permute-done | bytes 262176 | tf_op jit(solution)/shard_map/ppermute | solution.py:164
  326.3 6.5 %collective-permute-start.12 = (f32[16,128,256]{2,1,0:T(8,128)}, f32[16,128,256]{2,1,0:T(8,128)}, u32[]{:S(2)}, u32[]{:S(2)}) collective-permute-start(f32[16,128,256]{2,1,0:T(8,128)} %get-tuple-element.9), channel_id=1, source_target_pairs={{0,4},{1,5},{2,6},{3,7},{4,0},{5,1},{6,2},{7,3},{8,12},{9,13},{10,... | collective-permute-start | bytes 6291464 | tf_op jit(solution)/shard_map/ppermute | solution.py:164
  332.7 2.0 collective-permute-start.18
  335.0 1.1 add_add_fusion.1
  336.1 3.2 collective-permute-start.6
  339.3 40.0 %collective-permute-done.12 = f32[16,128,256]{2,1,0:T(8,128)} collective-permute-done((f32[16,128,256]{2,1,0:T(8,128)}, f32[16,128,256]{2,1,0:T(8,128)}, u32[]{:S(2)}, u32[]{:S(2)}) %collective-permute-start.12) | collective-permute-done | bytes 2097184 | tf_op jit(solution)/shard_map/ppermute | solution.py:164
  379.3 6.1 %collective-permute-start.7 = (f32[2,128,256]{2,1,0:T(8,128)S(1)}, f32[2,128,256]{2,1,0:T(8,128)}, u32[]{:S(2)}, u32[]{:S(2)}) collective-permute-start(f32[2,128,256]{2,1,0:T(8,128)S(1)} %add_add_fusion.1), channel_id=1, source_target_pairs={{0,32},{1,33},{2,34},{3,35},{4,36},{5,37},{6,38},{7,39},{8,40},{9,... | collective-permute-start | bytes 786440 | tf_op jit(solution)/shard_map/ppermute | solution.py:164
  385.4 36.6 %collective-permute-done.20 = f32[16,128,256]{2,1,0:T(8,128)} collective-permute-done((f32[16,128,256]{2,1,0:T(8,128)}, f32[16,128,256]{2,1,0:T(8,128)}, u32[]{:S(2)}, u32[]{:S(2)}) %collective-permute-start.20) | collective-permute-done | bytes 2097184 | tf_op jit(solution)/shard_map/ppermute | solution.py:164
  422.1 1.5 collective-permute-start.8
  423.6 9.6 %collective-permute-done.18 = f32[16,128,256]{2,1,0:T(8,128)} collective-permute-done((f32[16,128,256]{2,1,0:T(8,128)}, f32[16,128,256]{2,1,0:T(8,128)}, u32[]{:S(2)}, u32[]{:S(2)}) %collective-permute-start.18) | collective-permute-done | bytes 2097184 | tf_op jit(solution)/shard_map/ppermute | solution.py:164
  433.2 8.6 %fusion.9 = (f32[16,128,256]{2,1,0:T(8,128)S(1)}, f32[16,128,256]{2,1,0:T(8,128)S(1)}) fusion(f32[2,4,16,128,256]{4,3,2,1,0:T(8,128)} %bitcast.41, f32[2,4,16,128,256]{4,3,2,1,0:T(8,128)} %bitcast.43, f32[16,128,256]{2,1,0:T(8,128)S(1)} %collective-permute-done.13, f32[16,128,256]{2,1,0:T(8,128)} %collective-permute-done.11, ...), kind=kLoop, calls=%fused_computation.17 | loop fusion | flops 4194304 | bytes 25165824 | tf_op jit(solution)/shard_map/add | solution.py:190
  441.9 1.9 collective-permute-start.23
  444.0 1.6 collective-permute-start.22
  445.6 1.2 add_add_fusion
  446.8 5.2 %collective-permute-start.9 = (f32[2,128,256]{2,1,0:T(8,128)S(1)}, f32[2,128,256]{2,1,0:T(8,128)S(1)}, u32[]{:S(2)}, u32[]{:S(2)}) collective-permute-start(f32[2,128,256]{2,1,0:T(8,128)S(1)} %add_add_fusion), channel_id=1, source_target_pairs={{0,8},{1,9},{2,10},{3,11},{4,12},{5,13},{6,14},{7,15},{8,0},{9,1},... | collective-permute-start | bytes 786440 | tf_op jit(solution)/shard_map/ppermute | solution.py:164
  452.3 5.3 %collective-permute-done.9 = f32[2,128,256]{2,1,0:T(8,128)S(1)} collective-permute-done((f32[2,128,256]{2,1,0:T(8,128)S(1)}, f32[2,128,256]{2,1,0:T(8,128)S(1)}, u32[]{:S(2)}, u32[]{:S(2)}) %collective-permute-start.9) | collective-permute-done | bytes 262176 | tf_op jit(solution)/shard_map/ppermute | solution.py:164
  457.6 3.3 collective-permute-done.23
  460.9 2.3 collective-permute-start.15
  463.2 1.1 collective-permute-done.21
  464.3 2.9 collective-permute-start.10
  467.2 0.2 slice_add_fusion.8
  467.5 6.5 %collective-permute-done.14 = f32[4,128,256]{2,1,0:T(8,128)S(1)} collective-permute-done((f32[4,128,256]{2,1,0:T(8,128)S(1)}, f32[4,128,256]{2,1,0:T(8,128)S(1)}, u32[]{:S(2)}, u32[]{:S(2)}) %collective-permute-start.14) | collective-permute-done | bytes 524320 | tf_op jit(solution)/shard_map/ppermute | solution.py:164
  474.2 1.1 collective-permute-start.17
  475.3 0.7 add_multiply_fusion
  476.1 4.5 collective-permute-done.17
  480.7 0.7 pad_maximum_fusion.1
  (43 shorter events, 1.5 us)
Async XLA Ops:
  7.2 167.6 %copy-start = (bf16[256,256]{1,0:T(8,128)(2,1)S(1)}, bf16[256,256]{1,0:T(8,128)(2,1)}, u32[]{:S(2)}) copy-start(bf16[256,256]{1,0:T(8,128)(2,1)} %param.7) | copy-start | bytes 393220
  7.2 128.1 %all-gather.2.cloned.1.call-start = ((), (), s32[]{:S(2)}) async-start(), calls=%async_computation | async-start | bytes 17039360 | tf_op jit(solution)/shard_map/all_gather | solution.py:219
  148.3 26.5 %copy-start.5 = (bf16[512,256]{1,0:T(8,128)(2,1)S(1)}, bf16[512,256]{1,0:T(8,128)(2,1)}, u32[]{:S(2)}) copy-start(bf16[512,256]{1,0:T(8,128)(2,1)} %param.11) | copy-start | bytes 786436
  149.4 24.2 %collective-permute-start = (f32[512,256]{1,0:T(8,128)S(1)}, f32[512,256]{1,0:T(8,128)S(1)}, u32[]{:S(2)}, u32[]{:S(2)}) collective-permute-start(f32[512,256]{1,0:T(8,128)S(1)} %constant_dynamic-slice_fusion), channel_id=1, source_target_pairs={{0,64},{64,0},{1,65},{65,1},{2,66},{66,2},{3,67},{67,3},{4,68},{68... | collective-permute-start | bytes 1572872 | tf_op jit(solution)/shard_map/ppermute | solution.py:156
  176.1 8.0 %collective-permute-start.1 = (bf16[512,256]{1,0:T(8,128)(2,1)S(1)}, bf16[512,256]{1,0:T(8,128)(2,1)S(1)}, u32[]{:S(2)}, u32[]{:S(2)}) collective-permute-start(bf16[512,256]{1,0:T(8,128)(2,1)S(1)} %convolution_convert_fusion), channel_id=1, source_target_pairs={{0,64},{64,0},{1,65},{65,1},{2,66},{66,2},{3,67},{67,3},{4,68},{68... | collective-permute-start | bytes 786440 | tf_op jit(solution)/shard_map/ppermute | solution.py:156
  204.7 25.8 %collective-permute-start.2 = (f32[130,128,256]{2,1,0:T(8,128)}, f32[130,128,256]{2,1,0:T(8,128)S(1)}, u32[]{:S(2)}, u32[]{:S(2)}) collective-permute-start(f32[130,128,256]{2,1,0:T(8,128)} %get-tuple-element.5), channel_id=1, source_target_pairs={{0,1},{1,0},{2,3},{3,2},{4,5},{5,4},{6,7},{7,6},{8,9},{9,8},{10,11... | collective-permute-start | bytes 51118088 | tf_op jit(solution)/shard_map/ppermute | solution.py:164
  230.5 6.8 %copy-start.3 = (f32[130,128,256]{2,1,0:T(8,128)}, f32[130,128,256]{2,1,0:T(8,128)S(1)}, u32[]{:S(2)}) copy-start(f32[130,128,256]{2,1,0:T(8,128)S(1)} %collective-permute-done.2) | copy-start | bytes 51118084
  237.3 15.8 %copy-start.2 = (f32[128,128,256]{2,1,0:T(8,128)}, f32[128,128,256]{2,1,0:T(8,128)S(1)}, u32[]{:S(2)}) copy-start(f32[128,128,256]{2,1,0:T(8,128)S(1)} %slice.138) | copy-start | bytes 50331652
  253.1 81.7 %collective-permute-start.13 = (f32[16,128,256]{2,1,0:T(8,128)}, f32[16,128,256]{2,1,0:T(8,128)S(1)}, u32[]{:S(2)}, u32[]{:S(2)}) collective-permute-start(f32[16,128,256]{2,1,0:T(8,128)} %get-tuple-element.13), channel_id=1, source_target_pairs={{0,6},{1,7},{2,0},{3,1},{4,2},{5,3},{6,4},{7,5},{8,14},{9,15},{10,... | collective-permute-start | bytes 6291464 | tf_op jit(solution)/shard_map/ppermute | solution.py:164
  254.2 72.0 %collective-permute-start.3 = (f32[2,128,256]{2,1,0:T(8,128)S(1)}, f32[2,128,256]{2,1,0:T(8,128)S(1)}, u32[]{:S(2)}, u32[]{:S(2)}) collective-permute-start(f32[2,128,256]{2,1,0:T(8,128)S(1)} %slice_add_fusion.12), channel_id=1, source_target_pairs={{0,6},{1,7},{2,0},{3,1},{4,2},{5,3},{6,4},{7,5},{8,14},{9,15},{10,... | collective-permute-start | bytes 786440 | tf_op jit(solution)/shard_map/ppermute | solution.py:164
  254.3 78.4 %collective-permute-start.4 = (f32[2,128,256]{2,1,0:T(8,128)S(1)}, f32[2,128,256]{2,1,0:T(8,128)S(1)}, u32[]{:S(2)}, u32[]{:S(2)}) collective-permute-start(f32[2,128,256]{2,1,0:T(8,128)S(1)} %slice_add_fusion.12), channel_id=1, source_target_pairs={{0,4},{1,5},{2,6},{3,7},{4,0},{5,1},{6,2},{7,3},{8,12},{9,13},{10,... | collective-permute-start | bytes 786440 | tf_op jit(solution)/shard_map/ppermute | solution.py:164
  277.3 55.4 %collective-permute-start.5 = (f32[2,128,256]{2,1,0:T(8,128)S(1)}, f32[2,128,256]{2,1,0:T(8,128)S(1)}, u32[]{:S(2)}, u32[]{:S(2)}) collective-permute-start(f32[2,128,256]{2,1,0:T(8,128)S(1)} %slice_add_fusion.12), channel_id=1, source_target_pairs={{0,2},{1,3},{2,4},{3,5},{4,6},{5,7},{6,0},{7,1},{8,10},{9,11},{10,... | collective-permute-start | bytes 786440 | tf_op jit(solution)/shard_map/ppermute | solution.py:164
  278.6 57.4 %collective-permute-start.11 = (f32[16,128,256]{2,1,0:T(8,128)}, f32[16,128,256]{2,1,0:T(8,128)}, u32[]{:S(2)}, u32[]{:S(2)}) collective-permute-start(f32[16,128,256]{2,1,0:T(8,128)} %get-tuple-element.14), channel_id=1, source_target_pairs={{0,2},{1,3},{2,4},{3,5},{4,6},{5,7},{6,0},{7,1},{8,10},{9,11},{10,... | collective-permute-start | bytes 6291464 | tf_op jit(solution)/shard_map/ppermute | solution.py:164
  326.3 53.0 %collective-permute-start.12 = (f32[16,128,256]{2,1,0:T(8,128)}, f32[16,128,256]{2,1,0:T(8,128)}, u32[]{:S(2)}, u32[]{:S(2)}) collective-permute-start(f32[16,128,256]{2,1,0:T(8,128)} %get-tuple-element.9), channel_id=1, source_target_pairs={{0,4},{1,5},{2,6},{3,7},{4,0},{5,1},{6,2},{7,3},{8,12},{9,13},{10,... | collective-permute-start | bytes 6291464 | tf_op jit(solution)/shard_map/ppermute | solution.py:164
  332.7 89.3 %collective-permute-start.20 = (f32[16,128,256]{2,1,0:T(8,128)}, f32[16,128,256]{2,1,0:T(8,128)}, u32[]{:S(2)}, u32[]{:S(2)}) collective-permute-start(f32[16,128,256]{2,1,0:T(8,128)} %get-tuple-element.10), channel_id=1, source_target_pairs={{0,48},{1,49},{2,50},{3,51},{4,52},{5,53},{6,54},{7,55},{8,56},{9,... | collective-permute-start | bytes 6291464 | tf_op jit(solution)/shard_map/ppermute | solution.py:164
  332.7 2.0 copy-start.4
  332.7 100.4 %collective-permute-start.18 = (f32[16,128,256]{2,1,0:T(8,128)}, f32[16,128,256]{2,1,0:T(8,128)}, u32[]{:S(2)}, u32[]{:S(2)}) collective-permute-start(f32[16,128,256]{2,1,0:T(8,128)} %get-tuple-element.12), channel_id=1, source_target_pairs={{0,16},{1,17},{2,18},{3,19},{4,20},{5,21},{6,22},{7,23},{8,24},{9,... | collective-permute-start | bytes 6291464 | tf_op jit(solution)/shard_map/ppermute | solution.py:164
  334.8 98.4 %collective-permute-start.19 = (f32[16,128,256]{2,1,0:T(8,128)}, f32[16,128,256]{2,1,0:T(8,128)}, u32[]{:S(2)}, u32[]{:S(2)}) collective-permute-start(f32[16,128,256]{2,1,0:T(8,128)} %get-tuple-element.11), channel_id=1, source_target_pairs={{0,32},{1,33},{2,34},{3,35},{4,36},{5,37},{6,38},{7,39},{8,40},{9,... | collective-permute-start | bytes 6291464 | tf_op jit(solution)/shard_map/ppermute | solution.py:164
  336.1 108.0 %collective-permute-start.6 = (f32[2,128,256]{2,1,0:T(8,128)S(1)}, f32[2,128,256]{2,1,0:T(8,128)}, u32[]{:S(2)}, u32[]{:S(2)}) collective-permute-start(f32[2,128,256]{2,1,0:T(8,128)S(1)} %add_add_fusion.1), channel_id=1, source_target_pairs={{0,48},{1,49},{2,50},{3,51},{4,52},{5,53},{6,54},{7,55},{8,56},{9,... | collective-permute-start | bytes 786440 | tf_op jit(solution)/shard_map/ppermute | solution.py:164
  379.3 66.3 %collective-permute-start.7 = (f32[2,128,256]{2,1,0:T(8,128)S(1)}, f32[2,128,256]{2,1,0:T(8,128)}, u32[]{:S(2)}, u32[]{:S(2)}) collective-permute-start(f32[2,128,256]{2,1,0:T(8,128)S(1)} %add_add_fusion.1), channel_id=1, source_target_pairs={{0,32},{1,33},{2,34},{3,35},{4,36},{5,37},{6,38},{7,39},{8,40},{9,... | collective-permute-start | bytes 786440 | tf_op jit(solution)/shard_map/ppermute | solution.py:164
  422.1 23.5 %collective-permute-start.8 = (f32[2,128,256]{2,1,0:T(8,128)S(1)}, f32[2,128,256]{2,1,0:T(8,128)}, u32[]{:S(2)}, u32[]{:S(2)}) collective-permute-start(f32[2,128,256]{2,1,0:T(8,128)S(1)} %add_add_fusion.1), channel_id=1, source_target_pairs={{0,16},{1,17},{2,18},{3,19},{4,20},{5,21},{6,22},{7,23},{8,24},{9,... | collective-permute-start | bytes 786440 | tf_op jit(solution)/shard_map/ppermute | solution.py:164
  441.9 19.0 %collective-permute-start.23 = (f32[4,128,256]{2,1,0:T(8,128)S(1)}, f32[4,128,256]{2,1,0:T(8,128)S(1)}, u32[]{:S(2)}, u32[]{:S(2)}) collective-permute-start(f32[4,128,256]{2,1,0:T(8,128)S(1)} %get-tuple-element.19), channel_id=1, source_target_pairs={{0,6},{1,7},{2,0},{3,1},{4,2},{5,3},{6,4},{7,5},{8,14},{9,15},{10,... | collective-permute-start | bytes 1572872 | tf_op jit(solution)/shard_map/ppermute | solution.py:164
  443.9 20.4 %collective-permute-start.21 = (f32[4,128,256]{2,1,0:T(8,128)S(1)}, f32[4,128,256]{2,1,0:T(8,128)S(1)}, u32[]{:S(2)}, u32[]{:S(2)}) collective-permute-start(f32[4,128,256]{2,1,0:T(8,128)S(1)} %get-tuple-element.20), channel_id=1, source_target_pairs={{0,2},{1,3},{2,4},{3,5},{4,6},{5,7},{6,0},{7,1},{8,10},{9,11},{10,... | collective-permute-start | bytes 1572872 | tf_op jit(solution)/shard_map/ppermute | solution.py:164
  444.0 23.1 %collective-permute-start.22 = (f32[4,128,256]{2,1,0:T(8,128)S(1)}, f32[4,128,256]{2,1,0:T(8,128)S(1)}, u32[]{:S(2)}, u32[]{:S(2)}) collective-permute-start(f32[4,128,256]{2,1,0:T(8,128)S(1)} %get-tuple-element.18), channel_id=1, source_target_pairs={{0,4},{1,5},{2,6},{3,7},{4,0},{5,1},{6,2},{7,3},{8,12},{9,13},{10,... | collective-permute-start | bytes 1572872 | tf_op jit(solution)/shard_map/ppermute | solution.py:164
  446.8 10.7 %collective-permute-start.9 = (f32[2,128,256]{2,1,0:T(8,128)S(1)}, f32[2,128,256]{2,1,0:T(8,128)S(1)}, u32[]{:S(2)}, u32[]{:S(2)}) collective-permute-start(f32[2,128,256]{2,1,0:T(8,128)S(1)} %add_add_fusion), channel_id=1, source_target_pairs={{0,8},{1,9},{2,10},{3,11},{4,12},{5,13},{6,14},{7,15},{8,0},{9,1},... | collective-permute-start | bytes 786440 | tf_op jit(solution)/shard_map/ppermute | solution.py:164
  452.2 15.3 %collective-permute-start.16 = (f32[4,128,256]{2,1,0:T(8,128)S(1)}, f32[4,128,256]{2,1,0:T(8,128)S(1)}, u32[]{:S(2)}, u32[]{:S(2)}) collective-permute-start(f32[4,128,256]{2,1,0:T(8,128)S(1)} %get-tuple-element.16), channel_id=1, source_target_pairs={{0,48},{1,49},{2,50},{3,51},{4,52},{5,53},{6,54},{7,55},{8,56},{9,... | collective-permute-start | bytes 1572872 | tf_op jit(solution)/shard_map/ppermute | solution.py:164
  457.6 16.4 %collective-permute-start.14 = (f32[4,128,256]{2,1,0:T(8,128)S(1)}, f32[4,128,256]{2,1,0:T(8,128)S(1)}, u32[]{:S(2)}, u32[]{:S(2)}) collective-permute-start(f32[4,128,256]{2,1,0:T(8,128)S(1)} %get-tuple-element.17), channel_id=1, source_target_pairs={{0,16},{1,17},{2,18},{3,19},{4,20},{5,21},{6,22},{7,23},{8,24},{9,... | collective-permute-start | bytes 1572872 | tf_op jit(solution)/shard_map/ppermute | solution.py:164
  460.9 13.1 %collective-permute-start.15 = (f32[4,128,256]{2,1,0:T(8,128)S(1)}, f32[4,128,256]{2,1,0:T(8,128)S(1)}, u32[]{:S(2)}, u32[]{:S(2)}) collective-permute-start(f32[4,128,256]{2,1,0:T(8,128)S(1)} %get-tuple-element.15), channel_id=1, source_target_pairs={{0,32},{1,33},{2,34},{3,35},{4,36},{5,37},{6,38},{7,39},{8,40},{9,... | collective-permute-start | bytes 1572872 | tf_op jit(solution)/shard_map/ppermute | solution.py:164
  464.3 11.0 %collective-permute-start.10 = (f32[256,256]{1,0:T(8,128)S(1)}, f32[256,256]{1,0:T(8,128)S(1)}, u32[]{:S(2)}, u32[]{:S(2)}) collective-permute-start(f32[256,256]{1,0:T(8,128)S(1)} %bitcast.48), channel_id=1, source_target_pairs={{0,64},{64,0},{1,65},{65,1},{2,66},{66,2},{3,67},{67,3},{4,68},{68... | collective-permute-start | bytes 786440 | tf_op jit(solution)/shard_map/ppermute | solution.py:156
  467.4 8.6 %collective-permute-start.24 = (f32[2,128,256]{2,1,0:T(8,128)S(1)}, f32[2,128,256]{2,1,0:T(8,128)S(1)}, u32[]{:S(2)}, u32[]{:S(2)}) collective-permute-start(f32[2,128,256]{2,1,0:T(8,128)S(1)} %slice.165), channel_id=1, source_target_pairs={{0,8},{1,9},{2,10},{3,11},{4,12},{5,13},{6,14},{7,15},{8,0},{9,1},... | collective-permute-start | bytes 786440 | tf_op jit(solution)/shard_map/ppermute | solution.py:164
  473.9 7.4 %copy-start.1 = (bf16[256,256]{1,0:T(8,128)(2,1)S(1)}, bf16[256,256]{1,0:T(8,128)(2,1)}, u32[]{:S(2)}) copy-start(bf16[256,256]{1,0:T(8,128)(2,1)} %param.7) | copy-start | bytes 393220
  474.2 6.5 %collective-permute-start.17 = (f32[2,128,256]{2,1,0:T(8,128)S(1)}, f32[2,128,256]{2,1,0:T(8,128)S(1)}, u32[]{:S(2)}, u32[]{:S(2)}) collective-permute-start(f32[2,128,256]{2,1,0:T(8,128)S(1)} %slice.151), channel_id=1, source_target_pairs={{0,8},{1,9},{2,10},{3,11},{4,12},{5,13},{6,14},{7,15},{8,0},{9,1},... | collective-permute-start | bytes 786440 | tf_op jit(solution)/shard_map/ppermute | solution.py:164
Sparse Core Ops, SparseCore 0:
  9.7 125.4 all-gather.1

commit v9 on v5

--- a/solution.py
+++ b/solution.py
@@ -1,4 +1,5 @@
 import functools
+import itertools
 import math
 
 import jax
@@ -172,6 +173,36 @@
     return jnp.concatenate([first, second]).reshape(-1, width)
 
 
+def group_sum(value, axes, digits):
+    size_all = 1
+    for axis in axes:
+        size_all *= lax.axis_size(axis)
+    me = lax.axis_index(axes)
+    combos = list(itertools.product(*[range(size) for _, size in digits]))
+    came = [value]
+    for combo in combos[1:]:
+        pairs = []
+        for r in range(size_all):
+            dest = r
+            for (digit, size), shift in zip(digits, combo):
+                place = (r // digit) % size
+                dest += (((place + shift) % size) - place) * digit
+            pairs.append((r, dest))
+        came.append(lax.ppermute(value, axes, pairs))
+    ordered = []
+    for target in combos:
+        code = 0
+        for (digit, size), spot in zip(digits, target):
+            code = code * size + ((me // digit) % size - spot + size) % size
+        picked = came[0]
+        for index in range(1, len(combos)):
+            picked = jnp.where(code == index, came[index], picked)
+        ordered.append(picked)
+    while len(ordered) > 1:
+        ordered = [ordered[i] + ordered[i + 1] for i in range(0, len(ordered), 2)]
+    return ordered[0]
+
+
 def all_sum(value, axis):
     size = lax.axis_size(axis)
     step = 1
@@ -205,7 +236,9 @@
     local_grad = jnp.dot(aggregated.T, pre_grad, preferred_element_type=jnp.float32)
     own_grad = jnp.dot(pre_grad, weight.T, preferred_element_type=jnp.float32).astype(jnp.bfloat16)
     both_grad = jnp.stack([own_grad, swap(own_grad, "grp")]).reshape(2, -1, block, width)
-    weight_grad = all_sum(all_sum(local_grad, "grp"), "row")
+    weight_grad = group_sum(local_grad, ("row",), [(2, 4), (1, 2)])
+    weight_grad = group_sum(weight_grad, ("row",), [(16, 4)])
+    weight_grad = group_sum(weight_grad, ("grp", "row"), [(64, 2), (8, 2)])
     weight_grad, both_grad = lax.optimization_barrier((weight_grad, both_grad))
     weight_grad = weight_grad * (1.0 / math.sqrt(verts))
 

time: 469 us -> 479 us (1.021)
  starting transfers between devices: 59.6 us -> 82.7 us
  waiting for transfers between devices: 332 us -> 320 us
    ppermute x7 -> x13, starting transfers between devices: 18.7 us -> 34.7 us  [group_sum(): came.append(lax.ppermute(value, axes, pairs))]
    ppermute x2, waiting for transfers between devices: 13.7 us -> 7.85 us  [swap(): return lax.ppermute(value, axis, [(i, i ^ 1) for i in range(size)])]
    ppermute x15, waiting for transfers between devices: 153 us -> 148 us  [shifted(): return lax.ppermute(value, 'row', [(r, dest(r)) for r in range(64)])]
    ppermute x7 -> x13, waiting for transfers between devices: 37.6 us -> 36.2 us  [group_sum(): came.append(lax.ppermute(value, axes, pairs))]
  transfers between devices with their start and end apart: 25 -> 31, of which waited for: 21 -> 21; matrix products, arithmetic and copies ran while one was open for 1% -> 1% of each run, Pallas kernels for 0% -> 0%
where the time goes in v9:
time: 479 us
  waiting for transfers between devices  320 us (67%)
  starting transfers between devices  82.7 us (17%)
  other arithmetic  30.8 us (6%)
  Pallas kernels  26.1 us (5%)
  between operations  14.2 us (3%)
    ppermute x15, waiting for transfers between devices, shifted(): return lax.ppermute(value, 'row', [(r, dest(r)) for r in range(64)])  148 us
    all_gather x1, waiting for transfers between devices, body(): gathered = lax.all_gather(features, 'row', axis=0, tiled=True)  127 us
    ppermute x13, waiting for transfers between devices, group_sum(): came.append(lax.ppermute(value, axes, pairs))  36.2 us
    ppermute x15, starting transfers between devices, shifted(): return lax.ppermute(value, 'row', [(r, dest(r)) for r in range(64)])  35 us
    ppermute x13, starting transfers between devices, group_sum(): came.append(lax.ppermute(value, axes, pairs))  34.7 us
    pallas_call x1, Pallas kernels, spread(): pl.pallas_call(spread_kernel, out_shape=[jax.ShapeDtypeStruct((col_blocks...  15.9 us
    add x1, other arithmetic, row_reduce_scatter(): first = [keep[0, s] + came[0, s] for s in range(4)]  15.9 us
    ppermute x2, starting transfers between devices, swap(): return lax.ppermute(value, axis, [(i, i ^ 1) for i in range(size)])  13.1 us
  transfers between devices with their start and end apart: 31, of which 21 were waited for; matrix products, arithmetic and copies ran while one was open for 1% of the time, Pallas kernels for 0%

profile of v9, /device:TPU:0, one launch (start us, length us, event | category | flops | bytes accessed | tf_op | source)
XLA Modules:
  0.0 479.4 jit_solution(6534613678797541068)
XLA Ops:
  7.9 127.3 %all-gather.2.cloned.1.call-done.panel_hbm = bf16[32768,256]{1,0:T(8,128)(2,1)} async-done(((bf16[512,256]{1,0:T(8,128)(2,1)}), bf16[32768,256]{1,0:T(8,128)(2,1)}) %all-gather.2.cloned.1.call-update) | async-done | bytes 16777232 | tf_op jit(solution)/shard_map/all_gather | solution.py:222
  135.3 10.2 %shard_map.85 = f32[8,128,256]{2,1,0:T(8,128)} custom-call(s32[8,16]{1,0:T(8,128)} %bitcast.48, s32[8]{0:T(128)} %bitcast.50, bf16[8,16,128,128]{3,2,1,0:T(8,128)(2,1)} %bitcast.41, bf16[32768,256]{1,0:T(8,128)(2,1)} %all-gather.2.cloned.1.call-done.panel_hbm), custom_call_target="tpu_custom_call" | custom-call | flops 1073741824 | bytes 22020096 | tf_op jit(solution)/shard_map/pallas_call | solution.py:96
  145.5 1.1 constant_dynamic-slice_fusion
  146.6 9.9 %collective-permute-start = (f32[512,256]{1,0:T(8,128)S(1)}, f32[512,256]{1,0:T(8,128)S(1)}, u32[]{:S(2)}, u32[]{:S(2)}) collective-permute-start(f32[512,256]{1,0:T(8,128)S(1)} %constant_dynamic-slice_fusion), channel_id=1, source_target_pairs={{0,64},{64,0},{1,65},{65,1},{2,66},{66,2},{3,67},{67,3},{4,68},{68... | collective-permute-start | bytes 1572872 | tf_op jit(solution)/shard_map/ppermute | solution.py:150
  156.5 7.8 %collective-permute-done = f32[512,256]{1,0:T(8,128)S(1)} collective-permute-done((f32[512,256]{1,0:T(8,128)S(1)}, f32[512,256]{1,0:T(8,128)S(1)}, u32[]{:S(2)}, u32[]{:S(2)}) %collective-permute-start) | collective-permute-done | bytes 524320 | tf_op jit(solution)/shard_map/ppermute | solution.py:150
  164.4 1.1 add_convert_fusion
  165.5 1.1 multiply_convert_fusion
  167.0 0.8 collective-permute-start.6
  167.8 9.5 %collective-permute-start.5 = (f32[256,256]{1,0:T(8,128)S(1)}, f32[256,256]{1,0:T(8,128)S(1)}, u32[]{:S(2)}, u32[]{:S(2)}) collective-permute-start(f32[256,256]{1,0:T(8,128)S(1)} %fusion.14), channel_id=1, source_target_pairs={{0,3},{1,2},{2,5},{3,4},{4,7},{5,6},{6,1},{7,0},{8,11},{9,10},{10,... | collective-permute-start | bytes 786440 | tf_op jit(solution)/shard_map/ppermute | solution.py:191
  177.9 2.9 collective-permute-start.3
  180.9 3.3 collective-permute-start.1
  184.2 12.0 %collective-permute-done.4 = f32[256,256]{1,0:T(8,128)S(1)} collective-permute-done((f32[256,256]{1,0:T(8,128)S(1)}, f32[256,256]{1,0:T(8,128)S(1)}, u32[]{:S(2)}, u32[]{:S(2)}) %collective-permute-start.4) | collective-permute-done | bytes 262176 | tf_op jit(solution)/shard_map/ppermute | solution.py:191
  196.2 4.5 collective-permute-done.3
  200.9 1.4 add_add_fusion.2
  202.3 7.9 %collective-permute-start.10 = (f32[256,256]{1,0:T(8,128)S(1)}, f32[256,256]{1,0:T(8,128)S(1)}, u32[]{:S(2)}, u32[]{:S(2)}) collective-permute-start(f32[256,256]{1,0:T(8,128)S(1)} %add_add_fusion.2), channel_id=1, source_target_pairs={{0,16},{1,17},{2,18},{3,19},{4,20},{5,21},{6,22},{7,23},{8,24},{9,... | collective-permute-start | bytes 786440 | tf_op jit(solution)/shard_map/ppermute | solution.py:191
  210.2 4.3 collective-permute-start.9
  215.2 3.1 collective-permute-start.14
  218.3 1.2 collective-permute-done.10
  219.6 6.8 %collective-permute-done.9 = f32[256,256]{1,0:T(8,128)S(1)} collective-permute-done((f32[256,256]{1,0:T(8,128)S(1)}, f32[256,256]{1,0:T(8,128)S(1)}, u32[]{:S(2)}, u32[]{:S(2)}) %collective-permute-start.9) | collective-permute-done | bytes 262176 | tf_op jit(solution)/shard_map/ppermute | solution.py:191
  226.5 1.5 collective-permute-start.13
  228.0 2.2 collective-permute-start.12
  230.2 1.1 collective-permute-start.11
  231.9 0.9 pad_maximum_fusion.grad_ref
  232.8 3.0 collective-permute-done.13
  235.8 5.8 %collective-permute-done.12 = f32[256,256]{1,0:T(8,128)S(1)} collective-permute-done((f32[256,256]{1,0:T(8,128)S(1)}, f32[256,256]{1,0:T(8,128)S(1)}, u32[]{:S(2)}, u32[]{:S(2)}) %collective-permute-start.12) | collective-permute-done | bytes 262176 | tf_op jit(solution)/shard_map/ppermute | solution.py:191
  241.6 2.7 collective-permute-done.11
  244.4 15.9 %shard_map.86 = (f32[128,128,256]{2,1,0:T(8,128)}, f32[128,128,256]{2,1,0:T(8,128)}) custom-call(s32[2]{0:T(128)} %pad_add_fusion.side_ref, s32[8,16]{1,0:T(8,128)} %bitcast.49, s32[8]{0:T(128)} %bitcast.51, bf16[8,16,128,128]{3,2,1,0:T(8,128)(2,1)} %bitcast.42, bf16[2,4,128,256]{3,2,1,0:T(8,128)(2,1)} %pad_maximum_fusion.grad_ref), custom_call_target="tpu_custom_call" | custom-call | flops 1073741824 | bytes 38273024 | tf_op jit(solution)/shard_map/pallas_call | solution.py:123
  260.4 25.4 %collective-permute-done.15 = f32[128,128,256]{2,1,0:T(8,128)S(1)} collective-permute-done((f32[128,128,256]{2,1,0:T(8,128)}, f32[128,128,256]{2,1,0:T(8,128)S(1)}, u32[]{:S(2)}, u32[]{:S(2)}) %collective-permute-start.15) | collective-permute-done | bytes 16777248 | tf_op jit(solution)/shard_map/ppermute | solution.py:158
  285.8 15.9 %fusion.6 = (f32[16,128,256]{2,1,0:T(8,128)}, f32[16,128,256]{2,1,0:T(8,128)}, f32[16,128,256]{2,1,0:T(8,128)}, f32[16,128,256]{2,1,0:T(8,128)}, f32[16,128,256]{2,1,0:T(8,128)}, /*index=5*/f32[16,128,256]{2,1,0:T(8,128)}) fusion(f32[2,4,16,128,256]{4,3,2,1,0:T(8,128)S(1)} %bitcast.39, f32[2,4,16,128,256]{4,3,2,1,0:T(8,128)} %bitcast.37), kind=kLoop, calls=%fused_computation.12 | loop fusion | flops 3145728 | bytes 37748736 | tf_op jit(solution)/shard_map/add | solution.py:165
  301.7 20.4 %collective-permute-start.17 = (f32[16,128,256]{2,1,0:T(8,128)}, f32[16,128,256]{2,1,0:T(8,128)S(1)}, u32[]{:S(2)}, u32[]{:S(2)}) collective-permute-start(f32[16,128,256]{2,1,0:T(8,128)} %get-tuple-element.13), channel_id=1, source_target_pairs={{0,4},{1,5},{2,6},{3,7},{4,0},{5,1},{6,2},{7,3},{8,12},{9,13},{10,... | collective-permute-start | bytes 6291464 | tf_op jit(solution)/shard_map/ppermute | solution.py:158
  322.1 4.0 collective-permute-start.25
  326.9 3.2 collective-permute-start.18
  330.1 38.3 %collective-permute-done.17 = f32[16,128,256]{2,1,0:T(8,128)S(1)} collective-permute-done((f32[16,128,256]{2,1,0:T(8,128)}, f32[16,128,256]{2,1,0:T(8,128)S(1)}, u32[]{:S(2)}, u32[]{:S(2)}) %collective-permute-start.17) | collective-permute-done | bytes 2097184 | tf_op jit(solution)/shard_map/ppermute | solution.py:158
  368.4 48.0 %collective-permute-done.25 = f32[16,128,256]{2,1,0:T(8,128)S(1)} collective-permute-done((f32[16,128,256]{2,1,0:T(8,128)}, f32[16,128,256]{2,1,0:T(8,128)S(1)}, u32[]{:S(2)}, u32[]{:S(2)}) %collective-permute-start.25) | collective-permute-done | bytes 2097184 | tf_op jit(solution)/shard_map/ppermute | solution.py:158
  416.4 3.3 collective-permute-done.23
  419.8 1.4 copy-done.5
  421.1 1.4 copy-done.6
  422.5 8.7 %fusion.9 = (f32[16,128,256]{2,1,0:T(8,128)S(1)}, f32[16,128,256]{2,1,0:T(8,128)S(1)}) fusion(f32[2,4,16,128,256]{4,3,2,1,0:T(8,128)} %bitcast.40, f32[2,4,16,128,256]{4,3,2,1,0:T(8,128)} %bitcast.38, f32[16,128,256]{2,1,0:T(8,128)} %copy-done.6, f32[16,128,256]{2,1,0:T(8,128)} %collective-permute-done.16, f32[16,128,256]{2,1,0:T(8,128)S(1)} %collective-permute-done.17, ...), kind=kLoop, calls=%fused_computation.17 | loop fusion | flops 4194304 | bytes 25165824 | tf_op jit(solution)/shard_map/add | solution.py:167
  432.0 1.5 collective-permute-start.21
  434.2 3.1 collective-permute-start.27
  437.8 10.0 %collective-permute-done.20 = f32[4,128,256]{2,1,0:T(8,128)S(1)} collective-permute-done((f32[4,128,256]{2,1,0:T(8,128)S(1)}, f32[4,128,256]{2,1,0:T(8,128)S(1)}, u32[]{:S(2)}, u32[]{:S(2)}) %collective-permute-start.20) | collective-permute-done | bytes 524320 | tf_op jit(solution)/shard_map/ppermute | solution.py:158
  447.8 8.4 %collective-permute-done.21 = f32[4,128,256]{2,1,0:T(8,128)S(1)} collective-permute-done((f32[4,128,256]{2,1,0:T(8,128)S(1)}, f32[4,128,256]{2,1,0:T(8,128)S(1)}, u32[]{:S(2)}, u32[]{:S(2)}) %collective-permute-start.21) | collective-permute-done | bytes 524320 | tf_op jit(solution)/shard_map/ppermute | solution.py:158
  456.3 1.4 collective-permute-done.19
  458.0 1.7 collective-permute-done.28
  460.6 0.7 broadcast_multiply_fusion
  461.3 5.8 %collective-permute-done.22 = f32[2,128,256]{2,1,0:T(8,128)S(1)} collective-permute-done((f32[2,128,256]{2,1,0:T(8,128)S(1)}, f32[2,128,256]{2,1,0:T(8,128)S(1)}, u32[]{:S(2)}, u32[]{:S(2)}) %collective-permute-start.22) | collective-permute-done | bytes 262176 | tf_op jit(solution)/shard_map/ppermute | solution.py:158
  467.2 4.6 collective-permute-done.29
  471.9 0.7 pad_maximum_fusion.1
  (55 shorter events, 7.8 us)
Async XLA Ops:
  7.2 158.3 %copy-start = (bf16[256,256]{1,0:T(8,128)(2,1)S(1)}, bf16[256,256]{1,0:T(8,128)(2,1)}, u32[]{:S(2)}) copy-start(bf16[256,256]{1,0:T(8,128)(2,1)} %param.7) | copy-start | bytes 393220
  7.2 128.1 %all-gather.2.cloned.1.call-start = ((), (), s32[]{:S(2)}) async-start(), calls=%async_computation | async-start | bytes 17039360 | tf_op jit(solution)/shard_map/all_gather | solution.py:222
  145.5 20.0 %copy-start.7 = (bf16[512,256]{1,0:T(8,128)(2,1)S(1)}, bf16[512,256]{1,0:T(8,128)(2,1)}, u32[]{:S(2)}) copy-start(bf16[512,256]{1,0:T(8,128)(2,1)} %param.11) | copy-start | bytes 786436
  146.6 17.8 %collective-permute-start = (f32[512,256]{1,0:T(8,128)S(1)}, f32[512,256]{1,0:T(8,128)S(1)}, u32[]{:S(2)}, u32[]{:S(2)}) collective-permute-start(f32[512,256]{1,0:T(8,128)S(1)} %constant_dynamic-slice_fusion), channel_id=1, source_target_pairs={{0,64},{64,0},{1,65},{65,1},{2,66},{66,2},{3,67},{67,3},{4,68},{68... | collective-permute-start | bytes 1572872 | tf_op jit(solution)/shard_map/ppermute | solution.py:150
  166.9 14.0 %collective-permute-start.7 = (f32[256,256]{1,0:T(8,128)S(1)}, f32[256,256]{1,0:T(8,128)S(1)}, u32[]{:S(2)}, u32[]{:S(2)}) collective-permute-start(f32[256,256]{1,0:T(8,128)S(1)} %fusion.14), channel_id=1, source_target_pairs={{0,1},{1,0},{2,3},{3,2},{4,5},{5,4},{6,7},{7,6},{8,9},{9,8},{10,11... | collective-permute-start | bytes 786440 | tf_op jit(solution)/shard_map/ppermute | solution.py:191
  167.0 13.9 %collective-permute-start.6 = (f32[256,256]{1,0:T(8,128)S(1)}, f32[256,256]{1,0:T(8,128)S(1)}, u32[]{:S(2)}, u32[]{:S(2)}) collective-permute-start(f32[256,256]{1,0:T(8,128)S(1)} %fusion.14), channel_id=1, source_target_pairs={{0,2},{1,3},{2,4},{3,5},{4,6},{5,7},{6,0},{7,1},{8,10},{9,11},{10,... | collective-permute-start | bytes 786440 | tf_op jit(solution)/shard_map/ppermute | solution.py:191
  167.8 16.4 %collective-permute-start.5 = (f32[256,256]{1,0:T(8,128)S(1)}, f32[256,256]{1,0:T(8,128)S(1)}, u32[]{:S(2)}, u32[]{:S(2)}) collective-permute-start(f32[256,256]{1,0:T(8,128)S(1)} %fusion.14), channel_id=1, source_target_pairs={{0,3},{1,2},{2,5},{3,4},{4,7},{5,6},{6,1},{7,0},{8,11},{9,10},{10,... | collective-permute-start | bytes 786440 | tf_op jit(solution)/shard_map/ppermute | solution.py:191
  177.3 19.0 %collective-permute-start.4 = (f32[256,256]{1,0:T(8,128)S(1)}, f32[256,256]{1,0:T(8,128)S(1)}, u32[]{:S(2)}, u32[]{:S(2)}) collective-permute-start(f32[256,256]{1,0:T(8,128)S(1)} %fusion.14), channel_id=1, source_target_pairs={{0,4},{1,5},{2,6},{3,7},{4,0},{5,1},{6,2},{7,3},{8,12},{9,13},{10,... | collective-permute-start | bytes 786440 | tf_op jit(solution)/shard_map/ppermute | solution.py:191
  177.9 22.9 %collective-permute-start.3 = (f32[256,256]{1,0:T(8,128)S(1)}, f32[256,256]{1,0:T(8,128)S(1)}, u32[]{:S(2)}, u32[]{:S(2)}) collective-permute-start(f32[256,256]{1,0:T(8,128)S(1)} %fusion.14), channel_id=1, source_target_pairs={{0,5},{1,4},{2,7},{3,6},{4,1},{5,0},{6,3},{7,2},{8,13},{9,12},{10,... | collective-permute-start | bytes 786440 | tf_op jit(solution)/shard_map/ppermute | solution.py:191
  180.8 19.9 %collective-permute-start.2 = (f32[256,256]{1,0:T(8,128)S(1)}, f32[256,256]{1,0:T(8,128)S(1)}, u32[]{:S(2)}, u32[]{:S(2)}) collective-permute-start(f32[256,256]{1,0:T(8,128)S(1)} %fusion.14), channel_id=1, source_target_pairs={{0,6},{1,7},{2,0},{3,1},{4,2},{5,3},{6,4},{7,5},{8,14},{9,15},{10,... | collective-permute-start | bytes 786440 | tf_op jit(solution)/shard_map/ppermute | solution.py:191
  180.9 20.0 %collective-permute-start.1 = (f32[256,256]{1,0:T(8,128)S(1)}, f32[256,256]{1,0:T(8,128)S(1)}, u32[]{:S(2)}, u32[]{:S(2)}) collective-permute-start(f32[256,256]{1,0:T(8,128)S(1)} %fusion.14), channel_id=1, source_target_pairs={{0,7},{1,6},{2,1},{3,0},{4,3},{5,2},{6,5},{7,4},{8,15},{9,14},{10,... | collective-permute-start | bytes 786440 | tf_op jit(solution)/shard_map/ppermute | solution.py:191
  202.3 17.3 %collective-permute-start.10 = (f32[256,256]{1,0:T(8,128)S(1)}, f32[256,256]{1,0:T(8,128)S(1)}, u32[]{:S(2)}, u32[]{:S(2)}) collective-permute-start(f32[256,256]{1,0:T(8,128)S(1)} %add_add_fusion.2), channel_id=1, source_target_pairs={{0,16},{1,17},{2,18},{3,19},{4,20},{5,21},{6,22},{7,23},{8,24},{9,... | collective-permute-start | bytes 786440 | tf_op jit(solution)/shard_map/ppermute | solution.py:191
  210.2 16.2 %collective-permute-start.9 = (f32[256,256]{1,0:T(8,128)S(1)}, f32[256,256]{1,0:T(8,128)S(1)}, u32[]{:S(2)}, u32[]{:S(2)}) collective-permute-start(f32[256,256]{1,0:T(8,128)S(1)} %add_add_fusion.2), channel_id=1, source_target_pairs={{0,32},{1,33},{2,34},{3,35},{4,36},{5,37},{6,38},{7,39},{8,40},{9,... | collective-permute-start | bytes 786440 | tf_op jit(solution)/shard_map/ppermute | solution.py:191
  214.5 11.9 %collective-permute-start.8 = (f32[256,256]{1,0:T(8,128)S(1)}, f32[256,256]{1,0:T(8,128)S(1)}, u32[]{:S(2)}, u32[]{:S(2)}) collective-permute-start(f32[256,256]{1,0:T(8,128)S(1)} %add_add_fusion.2), channel_id=1, source_target_pairs={{0,48},{1,49},{2,50},{3,51},{4,52},{5,53},{6,54},{7,55},{8,56},{9,... | collective-permute-start | bytes 786440 | tf_op jit(solution)/shard_map/ppermute | solution.py:191
  215.2 16.7 %collective-permute-start.14 = (bf16[512,256]{1,0:T(8,128)(2,1)S(1)}, bf16[512,256]{1,0:T(8,128)(2,1)S(1)}, u32[]{:S(2)}, u32[]{:S(2)}) collective-permute-start(bf16[512,256]{1,0:T(8,128)(2,1)S(1)} %convolution_convert_fusion), channel_id=1, source_target_pairs={{0,64},{64,0},{1,65},{65,1},{2,66},{66,2},{3,67},{67,3},{4,68},{68... | collective-permute-start | bytes 786440 | tf_op jit(solution)/shard_map/ppermute | solution.py:150
  226.5 9.3 %collective-permute-start.13 = (f32[256,256]{1,0:T(8,128)S(1)}, f32[256,256]{1,0:T(8,128)S(1)}, u32[]{:S(2)}, u32[]{:S(2)}) collective-permute-start(f32[256,256]{1,0:T(8,128)S(1)} %add_add_fusion.1), channel_id=1, source_target_pairs={{0,8},{1,9},{2,10},{3,11},{4,12},{5,13},{6,14},{7,15},{8,0},{9,1},... | collective-permute-start | bytes 786440 | tf_op jit(solution)/shard_map/ppermute | solution.py:191
  228.0 13.6 %collective-permute-start.12 = (f32[256,256]{1,0:T(8,128)S(1)}, f32[256,256]{1,0:T(8,128)S(1)}, u32[]{:S(2)}, u32[]{:S(2)}) collective-permute-start(f32[256,256]{1,0:T(8,128)S(1)} %add_add_fusion.1), channel_id=1, source_target_pairs={{0,64},{1,65},{2,66},{3,67},{4,68},{5,69},{6,70},{7,71},{8,72},{9,... | collective-permute-start | bytes 786440 | tf_op jit(solution)/shard_map/ppermute | solution.py:191
  230.2 14.0 %collective-permute-start.11 = (f32[256,256]{1,0:T(8,128)S(1)}, f32[256,256]{1,0:T(8,128)S(1)}, u32[]{:S(2)}, u32[]{:S(2)}) collective-permute-start(f32[256,256]{1,0:T(8,128)S(1)} %add_add_fusion.1), channel_id=1, source_target_pairs={{0,72},{1,73},{2,74},{3,75},{4,76},{5,77},{6,78},{7,79},{8,64},{9,... | collective-permute-start | bytes 786440 | tf_op jit(solution)/shard_map/ppermute | solution.py:191
  260.3 25.4 %collective-permute-start.15 = (f32[128,128,256]{2,1,0:T(8,128)}, f32[128,128,256]{2,1,0:T(8,128)S(1)}, u32[]{:S(2)}, u32[]{:S(2)}) collective-permute-start(f32[128,128,256]{2,1,0:T(8,128)} %get-tuple-element.10), channel_id=1, source_target_pairs={{0,1},{1,0},{2,3},{3,2},{4,5},{5,4},{6,7},{7,6},{8,9},{9,8},{10,11... | collective-permute-start | bytes 50331656 | tf_op jit(solution)/shard_map/ppermute | solution.py:158
  285.8 15.9 %copy-start.2 = (f32[128,128,256]{2,1,0:T(8,128)}, f32[128,128,256]{2,1,0:T(8,128)S(1)}, u32[]{:S(2)}) copy-start(f32[128,128,256]{2,1,0:T(8,128)S(1)} %collective-permute-done.15) | copy-start | bytes 50331652
  301.7 66.8 %collective-permute-start.17 = (f32[16,128,256]{2,1,0:T(8,128)}, f32[16,128,256]{2,1,0:T(8,128)S(1)}, u32[]{:S(2)}, u32[]{:S(2)}) collective-permute-start(f32[16,128,256]{2,1,0:T(8,128)} %get-tuple-element.13), channel_id=1, source_target_pairs={{0,4},{1,5},{2,6},{3,7},{4,0},{5,1},{6,2},{7,3},{8,12},{9,13},{10,... | collective-permute-start | bytes 6291464 | tf_op jit(solution)/shard_map/ppermute | solution.py:158
  322.1 94.4 %collective-permute-start.25 = (f32[16,128,256]{2,1,0:T(8,128)}, f32[16,128,256]{2,1,0:T(8,128)S(1)}, u32[]{:S(2)}, u32[]{:S(2)}) collective-permute-start(f32[16,128,256]{2,1,0:T(8,128)} %get-tuple-element.14), channel_id=1, source_target_pairs={{0,48},{1,49},{2,50},{3,51},{4,52},{5,53},{6,54},{7,55},{8,56},{9,... | collective-permute-start | bytes 6291464 | tf_op jit(solution)/shard_map/ppermute | solution.py:158
  326.1 90.4 %collective-permute-start.24 = (f32[16,128,256]{2,1,0:T(8,128)}, f32[16,128,256]{2,1,0:T(8,128)S(1)}, u32[]{:S(2)}, u32[]{:S(2)}) collective-permute-start(f32[16,128,256]{2,1,0:T(8,128)} %get-tuple-element.15), channel_id=1, source_target_pairs={{0,32},{1,33},{2,34},{3,35},{4,36},{5,37},{6,38},{7,39},{8,40},{9,... | collective-permute-start | bytes 6291464 | tf_op jit(solution)/shard_map/ppermute | solution.py:158
  326.3 93.5 %collective-permute-start.23 = (f32[16,128,256]{2,1,0:T(8,128)}, f32[16,128,256]{2,1,0:T(8,128)S(1)}, u32[]{:S(2)}, u32[]{:S(2)}) collective-permute-start(f32[16,128,256]{2,1,0:T(8,128)} %get-tuple-element.16), channel_id=1, source_target_pairs={{0,16},{1,17},{2,18},{3,19},{4,20},{5,21},{6,22},{7,23},{8,24},{9,... | collective-permute-start | bytes 6291464 | tf_op jit(solution)/shard_map/ppermute | solution.py:158
  326.9 92.8 %collective-permute-start.18 = (f32[16,128,256]{2,1,0:T(8,128)}, f32[16,128,256]{2,1,0:T(8,128)S(1)}, u32[]{:S(2)}, u32[]{:S(2)}) collective-permute-start(f32[16,128,256]{2,1,0:T(8,128)} %get-tuple-element.17), channel_id=1, source_target_pairs={{0,6},{1,7},{2,0},{3,1},{4,2},{5,3},{6,4},{7,5},{8,14},{9,15},{10,... | collective-permute-start | bytes 6291464 | tf_op jit(solution)/shard_map/ppermute | solution.py:158
  368.4 54.1 %collective-permute-start.16 = (f32[16,128,256]{2,1,0:T(8,128)}, f32[16,128,256]{2,1,0:T(8,128)}, u32[]{:S(2)}, u32[]{:S(2)}) collective-permute-start(f32[16,128,256]{2,1,0:T(8,128)} %get-tuple-element.18), channel_id=1, source_target_pairs={{0,2},{1,3},{2,4},{3,5},{4,6},{5,7},{6,0},{7,1},{8,10},{9,11},{10,... | collective-permute-start | bytes 6291464 | tf_op jit(solution)/shard_map/ppermute | solution.py:158
  416.4 3.3 copy-start.3
  416.4 3.3 copy-start.4
  419.8 1.4 copy-start.5
  421.1 1.4 copy-start.6
  431.4 16.5 %collective-permute-start.20 = (f32[4,128,256]{2,1,0:T(8,128)S(1)}, f32[4,128,256]{2,1,0:T(8,128)S(1)}, u32[]{:S(2)}, u32[]{:S(2)}) collective-permute-start(f32[4,128,256]{2,1,0:T(8,128)S(1)} %get-tuple-element.19), channel_id=1, source_target_pairs={{0,32},{1,33},{2,34},{3,35},{4,36},{5,37},{6,38},{7,39},{8,40},{9,... | collective-permute-start | bytes 1572872 | tf_op jit(solution)/shard_map/ppermute | solution.py:158
  432.0 24.2 %collective-permute-start.21 = (f32[4,128,256]{2,1,0:T(8,128)S(1)}, f32[4,128,256]{2,1,0:T(8,128)S(1)}, u32[]{:S(2)}, u32[]{:S(2)}) collective-permute-start(f32[4,128,256]{2,1,0:T(8,128)S(1)} %get-tuple-element.20), channel_id=1, source_target_pairs={{0,48},{1,49},{2,50},{3,51},{4,52},{5,53},{6,54},{7,55},{8,56},{9,... | collective-permute-start | bytes 1572872 | tf_op jit(solution)/shard_map/ppermute | solution.py:158
  433.5 24.2 %collective-permute-start.19 = (f32[4,128,256]{2,1,0:T(8,128)S(1)}, f32[4,128,256]{2,1,0:T(8,128)S(1)}, u32[]{:S(2)}, u32[]{:S(2)}) collective-permute-start(f32[4,128,256]{2,1,0:T(8,128)S(1)} %get-tuple-element.21), channel_id=1, source_target_pairs={{0,16},{1,17},{2,18},{3,19},{4,20},{5,21},{6,22},{7,23},{8,24},{9,... | collective-permute-start | bytes 1572872 | tf_op jit(solution)/shard_map/ppermute | solution.py:158
  434.2 23.8 %collective-permute-start.27 = (f32[4,128,256]{2,1,0:T(8,128)S(1)}, f32[4,128,256]{2,1,0:T(8,128)S(1)}, u32[]{:S(2)}, u32[]{:S(2)}) collective-permute-start(f32[4,128,256]{2,1,0:T(8,128)S(1)} %get-tuple-element.22), channel_id=1, source_target_pairs={{0,4},{1,5},{2,6},{3,7},{4,0},{5,1},{6,2},{7,3},{8,12},{9,13},{10,... | collective-permute-start | bytes 1572872 | tf_op jit(solution)/shard_map/ppermute | solution.py:158
  437.4 22.3 %collective-permute-start.28 = (f32[4,128,256]{2,1,0:T(8,128)S(1)}, f32[4,128,256]{2,1,0:T(8,128)S(1)}, u32[]{:S(2)}, u32[]{:S(2)}) collective-permute-start(f32[4,128,256]{2,1,0:T(8,128)S(1)} %get-tuple-element.23), channel_id=1, source_target_pairs={{0,6},{1,7},{2,0},{3,1},{4,2},{5,3},{6,4},{7,5},{8,14},{9,15},{10,... | collective-permute-start | bytes 1572872 | tf_op jit(solution)/shard_map/ppermute | solution.py:158
  447.8 12.5 %collective-permute-start.26 = (f32[4,128,256]{2,1,0:T(8,128)S(1)}, f32[4,128,256]{2,1,0:T(8,128)S(1)}, u32[]{:S(2)}, u32[]{:S(2)}) collective-permute-start(f32[4,128,256]{2,1,0:T(8,128)S(1)} %get-tuple-element.24), channel_id=1, source_target_pairs={{0,2},{1,3},{2,4},{3,5},{4,6},{5,7},{6,0},{7,1},{8,10},{9,11},{10,... | collective-permute-start | bytes 1572872 | tf_op jit(solution)/shard_map/ppermute | solution.py:158
  457.9 9.2 %collective-permute-start.22 = (f32[2,128,256]{2,1,0:T(8,128)S(1)}, f32[2,128,256]{2,1,0:T(8,128)S(1)}, u32[]{:S(2)}, u32[]{:S(2)}) collective-permute-start(f32[2,128,256]{2,1,0:T(8,128)S(1)} %slice.137), channel_id=1, source_target_pairs={{0,8},{1,9},{2,10},{3,11},{4,12},{5,13},{6,14},{7,15},{8,0},{9,1},... | collective-permute-start | bytes 786440 | tf_op jit(solution)/shard_map/ppermute | solution.py:158
  460.3 12.3 %copy-start.1 = (bf16[256,256]{1,0:T(8,128)(2,1)S(1)}, bf16[256,256]{1,0:T(8,128)(2,1)}, u32[]{:S(2)}) copy-start(bf16[256,256]{1,0:T(8,128)(2,1)} %param.7) | copy-start | bytes 393220
  460.5 11.3 %collective-permute-start.29 = (f32[2,128,256]{2,1,0:T(8,128)S(1)}, f32[2,128,256]{2,1,0:T(8,128)S(1)}, u32[]{:S(2)}, u32[]{:S(2)}) collective-permute-start(f32[2,128,256]{2,1,0:T(8,128)S(1)} %slice.151), channel_id=1, source_target_pairs={{0,8},{1,9},{2,10},{3,11},{4,12},{5,13},{6,14},{7,15},{8,0},{9,1},... | collective-permute-start | bytes 786440 | tf_op jit(solution)/shard_map/ppermute | solution.py:158
Sparse Core Ops, SparseCore 0:
  9.7 125.4 all-gather.1

commit v10 on v5

--- a/solution.py
+++ b/solution.py
@@ -28,14 +28,13 @@
     for t in range(row_blocks):
         live = jnp.clip(count_ref[t], 0, slot_total)
 
-        def body(k, acc):
+        acc = jnp.zeros(out_ref.shape[1:], jnp.float32)
+        for k in range(slot_total):
             col = jnp.clip(cols_ref[t, k], 0, col_blocks - 1)
             start = pl.multiple_of(col * block, block)
-            return acc + jnp.dot(
-                vals[t, k], panel[pl.ds(start, block), :], preferred_element_type=jnp.float32
-            )
-
-        out_ref[t] = lax.fori_loop(0, live, body, jnp.zeros(out_ref.shape[1:], jnp.float32))
+            picked = jnp.where(k < live, vals[t, k], jnp.zeros_like(vals[t, k]))
+            acc = acc + jnp.dot(picked, panel[pl.ds(start, block), :], preferred_element_type=jnp.float32)
+        out_ref[t] = acc
 
 
 def owner_slot(col, me, per_dev):
@@ -70,16 +69,12 @@
         panel, within = divmod(t, per_panel)
         grad = grad_ref[jnp.where(side_ref[0] == panel, 0, 1), within]
 
-        def body(k, carry):
+        for k in range(slot_total):
             col = jnp.clip(cols_ref[t, k], 0, col_blocks - 1)
-            contrib = lax.dot_general(
-                vals[t, k], grad, (((0,), (0,)), ((), ())), preferred_element_type=jnp.float32
-            )
+            picked = jnp.where(k < live, vals[t, k], jnp.zeros_like(vals[t, k]))
+            contrib = jnp.dot(picked, grad, preferred_element_type=jnp.float32)
             slot = owner_slot(col, me, per_dev)
             total[slot] += contrib
-            return carry
-
-        lax.fori_loop(0, live, body, 0)
     half = col_blocks // 2
     keep = pltpu.make_async_copy(total.at[pl.ds(0, half)], keep_hbm, sems.at[1])
     send = pltpu.make_async_copy(total.at[pl.ds(half, half)], send_hbm, sems.at[2])
@@ -210,7 +205,7 @@
     weight_grad = weight_grad * (1.0 / math.sqrt(verts))
 
     where = jnp.stack([side, lax.axis_index("row")]).astype(jnp.int32)
-    keep, send = spread(where, cols, count, vals, both_grad, col_blocks)
+    keep, send = spread(where, cols, count, jnp.swapaxes(vals, 2, 3), both_grad, col_blocks)
     input_grad = row_reduce_scatter(keep, send).astype(jnp.bfloat16)
     return (activated, weight_grad, input_grad)
 

time: 469 us -> 437 us (0.932)
  starting transfers between devices: 59.6 us -> 36.9 us
  waiting for transfers between devices: 332 us -> 313 us
  local copies, waits for them, and re-layouts: 4.27 us -> 10.7 us
  Pallas kernels: 26.1 us -> 31 us
    ppermute x15, waiting for transfers between devices: 153 us -> 142 us  [shifted(): return lax.ppermute(value, 'row', [(r, dest(r)) for r in range(64)])]
    ppermute x15, starting transfers between devices: 30.4 us -> 20.6 us  [shifted(): return lax.ppermute(value, 'row', [(r, dest(r)) for r in range(64)])]
    ppermute x7, starting transfers between devices: 18.7 us -> 10.3 us  [all_sum(): lax.ppermute(value, axis, [(i, i ^ step) for i in range(size)])]
    ppermute x7, waiting for transfers between devices: 37.6 us -> 30.1 us  [all_sum(): lax.ppermute(value, axis, [(i, i ^ step) for i in range(size)])]
    unnamed x16 -> x17, local copies, waits for them, and re-layouts: 2.75 us -> 9.2 us
  transfers between devices with their start and end apart: 25 -> 25, of which waited for: 21 -> 19; matrix products, arithmetic and copies ran while one was open for 1% -> 2% of each run, Pallas kernels for 0% -> 0%
where the time goes in v10:
time: 437 us
  waiting for transfers between devices  313 us (72%)
  starting transfers between devices  36.9 us (8%)
  Pallas kernels  31 us (7%)
  other arithmetic  29.3 us (7%)
  between operations  14.2 us (3%)
  local copies, waits for them, and re-layouts  10.7 us (2%)
    ppermute x15, waiting for transfers between devices, shifted(): return lax.ppermute(value, 'row', [(r, dest(r)) for r in range(64)])  142 us
    all_gather x1, waiting for transfers between devices, body(): gathered = lax.all_gather(features, 'row', axis=0, tiled=True)  127 us
    ppermute x7, waiting for transfers between devices, all_sum(): lax.ppermute(value, axis, [(i, i ^ step) for i in range(size)])  30.1 us
    ppermute x15, starting transfers between devices, shifted(): return lax.ppermute(value, 'row', [(r, dest(r)) for r in range(64)])  20.6 us
    pallas_call x1, Pallas kernels, spread(): pl.pallas_call(spread_kernel, out_shape=[jax.ShapeDtypeStruct((col_blocks...  19.9 us
    add x1, other arithmetic, row_reduce_scatter(): first = [keep[0, s] + came[0, s] for s in range(4)]  15.9 us
    ppermute x2, waiting for transfers between devices, swap(): return lax.ppermute(value, axis, [(i, i ^ 1) for i in range(size)])  12.9 us
    pallas_call x1, Pallas kernels, aggregate(): pl.pallas_call(aggregate_kernel, out_shape=jax.ShapeDtypeStruct((row_bloc...  11.1 us
  transfers between devices with their start and end apart: 25, of which 19 were waited for; matrix products, arithmetic and copies ran while one was open for 2% of the time, Pallas kernels for 0%

profile of v10, /device:TPU:0, one launch (start us, length us, event | category | flops | bytes accessed | tf_op | source)
XLA Modules:
  0.0 436.6 jit_solution(75904674289468943)
XLA Ops:
  7.9 127.3 %all-gather.2.cloned.1.call-done.panel_hbm = bf16[32768,256]{1,0:T(8,128)(2,1)} async-done(((bf16[512,256]{1,0:T(8,128)(2,1)}), bf16[32768,256]{1,0:T(8,128)(2,1)}) %all-gather.2.cloned.1.call-update) | async-done | bytes 16777232 | tf_op jit(solution)/shard_map/all_gather | solution.py:186
  135.3 11.1 %shard_map.85 = f32[8,128,256]{2,1,0:T(8,128)} custom-call(s32[8,16]{1,0:T(8,128)} %bitcast.51, s32[8]{0:T(128)} %bitcast.53, bf16[8,16,128,128]{3,2,1,0:T(8,128)(2,1)} %bitcast.45, bf16[32768,256]{1,0:T(8,128)(2,1)} %all-gather.2.cloned.1.call-done.panel_hbm), custom_call_target="tpu_custom_call" | custom-call | flops 1073741824 | bytes 22020096 | tf_op jit(solution)/shard_map/pallas_call | solution.py:90
  146.4 1.1 constant_dynamic-slice_fusion
  147.5 2.8 collective-permute-start
  150.3 12.9 %collective-permute-done = f32[512,256]{1,0:T(8,128)S(1)} collective-permute-done((f32[512,256]{1,0:T(8,128)S(1)}, f32[512,256]{1,0:T(8,128)S(1)}, u32[]{:S(2)}, u32[]{:S(2)}) %collective-permute-start) | collective-permute-done | bytes 524320 | tf_op jit(solution)/shard_map/ppermute | solution.py:144
  163.1 1.1 add_convert_fusion
  164.3 1.1 multiply_convert_fusion
  165.6 2.8 collective-permute-start.1
  168.4 6.5 %collective-permute-done.1 = f32[256,256]{1,0:T(8,128)S(1)} collective-permute-done((f32[256,256]{1,0:T(8,128)S(1)}, f32[256,256]{1,0:T(8,128)S(1)}, u32[]{:S(2)}, u32[]{:S(2)}) %collective-permute-start.1) | collective-permute-done | bytes 262176 | tf_op jit(solution)/shard_map/ppermute | solution.py:174
  175.0 1.5 collective-permute-done.2
  176.5 1.5 collective-permute-start.3
  178.0 7.0 %collective-permute-done.3 = f32[256,256]{1,0:T(8,128)S(1)} collective-permute-done((f32[256,256]{1,0:T(8,128)S(1)}, f32[256,256]{1,0:T(8,128)S(1)}, u32[]{:S(2)}, u32[]{:S(2)}) %collective-permute-start.3) | collective-permute-done | bytes 262176 | tf_op jit(solution)/shard_map/ppermute | solution.py:174
  185.0 2.2 collective-permute-start.4
  187.2 6.9 %collective-permute-done.4 = f32[256,256]{1,0:T(8,128)S(1)} collective-permute-done((f32[256,256]{1,0:T(8,128)S(1)}, f32[256,256]{1,0:T(8,128)S(1)}, u32[]{:S(2)}, u32[]{:S(2)}) %collective-permute-start.4) | collective-permute-done | bytes 262176 | tf_op jit(solution)/shard_map/ppermute | solution.py:174
  194.1 1.0 collective-permute-start.5
  195.1 5.7 %collective-permute-done.5 = f32[256,256]{1,0:T(8,128)S(1)} collective-permute-done((f32[256,256]{1,0:T(8,128)S(1)}, f32[256,256]{1,0:T(8,128)S(1)}, u32[]{:S(2)}, u32[]{:S(2)}) %collective-permute-start.5) | collective-permute-done | bytes 262176 | tf_op jit(solution)/shard_map/ppermute | solution.py:174
  200.9 1.0 collective-permute-start.6
  202.1 3.2 collective-permute-start.8
  205.3 2.5 collective-permute-done.6
  207.8 1.9 collective-permute-start.7
  209.7 6.4 %copy.9 = bf16[1,8,16,128,128]{3,4,2,1,0:T(8,128)(2,1)} copy(bf16[1,8,16,128,128]{4,3,2,1,0:T(8,128)(2,1)} %param.8) | data formatting | bytes 8388608 | tf_op args[2]
  217.7 19.9 %shard_map.86 = (f32[128,128,256]{2,1,0:T(8,128)}, f32[128,128,256]{2,1,0:T(8,128)}) custom-call(s32[2]{0:T(128)} %pad_add_fusion.side_ref, s32[8,16]{1,0:T(8,128)} %bitcast.52, s32[8]{0:T(128)} %bitcast.54, bf16[8,16,128,128]{3,2,1,0:T(8,128)(2,1)} %bitcast.40, bf16[2,4,128,256]{3,2,1,0:T(8,128)(2,1)} %pad_maximum_fusion.grad_ref), custom_call_target="tpu_custom_call" | custom-call | flops 1073741824 | bytes 38273024 | tf_op jit(solution)/shard_map/pallas_call | solution.py:117
  237.9 25.4 %collective-permute-done.9 = f32[128,128,256]{2,1,0:T(8,128)S(1)} collective-permute-done((f32[128,128,256]{2,1,0:T(8,128)}, f32[128,128,256]{2,1,0:T(8,128)S(1)}, u32[]{:S(2)}, u32[]{:S(2)}) %collective-permute-start.9) | collective-permute-done | bytes 16777248 | tf_op jit(solution)/shard_map/ppermute | solution.py:152
  263.3 15.9 %fusion.6 = (f32[16,128,256]{2,1,0:T(8,128)}, f32[16,128,256]{2,1,0:T(8,128)}, f32[16,128,256]{2,1,0:T(8,128)}, f32[16,128,256]{2,1,0:T(8,128)}, f32[16,128,256]{2,1,0:T(8,128)}, /*index=5*/f32[16,128,256]{2,1,0:T(8,128)}) fusion(f32[2,4,16,128,256]{4,3,2,1,0:T(8,128)S(1)} %bitcast.43, f32[2,4,16,128,256]{4,3,2,1,0:T(8,128)} %bitcast.41), kind=kLoop, calls=%fused_computation.12 | loop fusion | flops 3145728 | bytes 37748736 | tf_op jit(solution)/shard_map/add | solution.py:159
  279.2 2.3 collective-permute-start.11
  281.5 1.2 collective-permute-start.19
  282.7 1.0 collective-permute-start.18
  283.7 0.9 collective-permute-start.17
  284.6 2.1 collective-permute-start.12
  286.7 41.9 %collective-permute-done.11 = f32[16,128,256]{2,1,0:T(8,128)S(1)} collective-permute-done((f32[16,128,256]{2,1,0:T(8,128)}, f32[16,128,256]{2,1,0:T(8,128)S(1)}, u32[]{:S(2)}, u32[]{:S(2)}) %collective-permute-start.11) | collective-permute-done | bytes 2097184 | tf_op jit(solution)/shard_map/ppermute | solution.py:152
  328.7 1.6 collective-permute-start.10
  330.2 2.8 collective-permute-done.18
  333.0 43.4 %collective-permute-done.17 = f32[16,128,256]{2,1,0:T(8,128)S(1)} collective-permute-done((f32[16,128,256]{2,1,0:T(8,128)}, f32[16,128,256]{2,1,0:T(8,128)S(1)}, u32[]{:S(2)}, u32[]{:S(2)}) %collective-permute-start.17) | collective-permute-done | bytes 2097184 | tf_op jit(solution)/shard_map/ppermute | solution.py:152
  376.5 1.3 copy-done.5
  377.8 1.4 copy-done.6
  379.2 8.7 %fusion.9 = (f32[16,128,256]{2,1,0:T(8,128)S(1)}, f32[16,128,256]{2,1,0:T(8,128)S(1)}) fusion(f32[2,4,16,128,256]{4,3,2,1,0:T(8,128)} %bitcast.44, f32[2,4,16,128,256]{4,3,2,1,0:T(8,128)} %bitcast.42, f32[16,128,256]{2,1,0:T(8,128)} %copy-done.6, f32[16,128,256]{2,1,0:T(8,128)} %collective-permute-done.10, f32[16,128,256]{2,1,0:T(8,128)S(1)} %collective-permute-done.11, ...), kind=kLoop, calls=%fused_computation.17 | loop fusion | flops 4194304 | bytes 25165824 | tf_op jit(solution)/shard_map/add | solution.py:161
  388.1 1.1 collective-permute-start.14
  389.2 1.2 collective-permute-start.15
  391.4 1.8 collective-permute-start.21
  393.2 2.4 collective-permute-start.22
  395.7 8.8 %collective-permute-done.14 = f32[4,128,256]{2,1,0:T(8,128)S(1)} collective-permute-done((f32[4,128,256]{2,1,0:T(8,128)S(1)}, f32[4,128,256]{2,1,0:T(8,128)S(1)}, u32[]{:S(2)}, u32[]{:S(2)}) %collective-permute-start.14) | collective-permute-done | bytes 524320 | tf_op jit(solution)/shard_map/ppermute | solution.py:152
  405.3 6.7 %collective-permute-done.15 = f32[4,128,256]{2,1,0:T(8,128)S(1)} collective-permute-done((f32[4,128,256]{2,1,0:T(8,128)S(1)}, f32[4,128,256]{2,1,0:T(8,128)S(1)}, u32[]{:S(2)}, u32[]{:S(2)}) %collective-permute-start.15) | collective-permute-done | bytes 524320 | tf_op jit(solution)/shard_map/ppermute | solution.py:152
  411.9 2.9 collective-permute-done.13
  415.0 1.4 collective-permute-start.16
  416.5 1.5 collective-permute-done.20
  418.2 1.6 collective-permute-start.23
  420.5 3.8 collective-permute-done.16
  424.3 4.6 %collective-permute-done.23 = f32[2,128,256]{2,1,0:T(8,128)S(1)} collective-permute-done((f32[2,128,256]{2,1,0:T(8,128)S(1)}, f32[2,128,256]{2,1,0:T(8,128)S(1)}, u32[]{:S(2)}, u32[]{:S(2)}) %collective-permute-start.23) | collective-permute-done | bytes 262176 | tf_op jit(solution)/shard_map/ppermute | solution.py:152
  (48 shorter events, 7.4 us)
Async XLA Ops:
  7.2 157.1 %copy-start = (bf16[256,256]{1,0:T(8,128)(2,1)S(1)}, bf16[256,256]{1,0:T(8,128)(2,1)}, u32[]{:S(2)}) copy-start(bf16[256,256]{1,0:T(8,128)(2,1)} %param.7) | copy-start | bytes 393220
  7.2 128.1 %all-gather.2.cloned.1.call-start = ((), (), s32[]{:S(2)}) async-start(), calls=%async_computation | async-start | bytes 17039360 | tf_op jit(solution)/shard_map/all_gather | solution.py:186
  146.4 17.9 %copy-start.7 = (bf16[512,256]{1,0:T(8,128)(2,1)S(1)}, bf16[512,256]{1,0:T(8,128)(2,1)}, u32[]{:S(2)}) copy-start(bf16[512,256]{1,0:T(8,128)(2,1)} %param.11) | copy-start | bytes 786436
  147.5 15.7 %collective-permute-start = (f32[512,256]{1,0:T(8,128)S(1)}, f32[512,256]{1,0:T(8,128)S(1)}, u32[]{:S(2)}, u32[]{:S(2)}) collective-permute-start(f32[512,256]{1,0:T(8,128)S(1)} %constant_dynamic-slice_fusion), channel_id=1, source_target_pairs={{0,64},{64,0},{1,65},{65,1},{2,66},{66,2},{3,67},{67,3},{4,68},{68... | collective-permute-start | bytes 1572872 | tf_op jit(solution)/shard_map/ppermute | solution.py:144
  165.6 9.2 %collective-permute-start.1 = (f32[256,256]{1,0:T(8,128)S(1)}, f32[256,256]{1,0:T(8,128)S(1)}, u32[]{:S(2)}, u32[]{:S(2)}) collective-permute-start(f32[256,256]{1,0:T(8,128)S(1)} %fusion.14), channel_id=1, source_target_pairs={{0,64},{64,0},{1,65},{65,1},{2,66},{66,2},{3,67},{67,3},{4,68},{68... | collective-permute-start | bytes 786440 | tf_op jit(solution)/shard_map/ppermute | solution.py:174
  174.9 1.6 collective-permute-start.2
  176.5 8.4 %collective-permute-start.3 = (f32[256,256]{1,0:T(8,128)S(1)}, f32[256,256]{1,0:T(8,128)S(1)}, u32[]{:S(2)}, u32[]{:S(2)}) collective-permute-start(f32[256,256]{1,0:T(8,128)S(1)} %add.134), channel_id=1, source_target_pairs={{0,2},{1,3},{2,0},{3,1},{4,6},{5,7},{6,4},{7,5},{8,10},{9,11},{10,... | collective-permute-start | bytes 786440 | tf_op jit(solution)/shard_map/ppermute | solution.py:174
  185.0 9.1 %collective-permute-start.4 = (f32[256,256]{1,0:T(8,128)S(1)}, f32[256,256]{1,0:T(8,128)S(1)}, u32[]{:S(2)}, u32[]{:S(2)}) collective-permute-start(f32[256,256]{1,0:T(8,128)S(1)} %add.135), channel_id=1, source_target_pairs={{0,4},{1,5},{2,6},{3,7},{4,0},{5,1},{6,2},{7,3},{8,12},{9,13},{10,... | collective-permute-start | bytes 786440 | tf_op jit(solution)/shard_map/ppermute | solution.py:174
  194.1 6.7 %collective-permute-start.5 = (f32[256,256]{1,0:T(8,128)S(1)}, f32[256,256]{1,0:T(8,128)S(1)}, u32[]{:S(2)}, u32[]{:S(2)}) collective-permute-start(f32[256,256]{1,0:T(8,128)S(1)} %add.136), channel_id=1, source_target_pairs={{0,8},{1,9},{2,10},{3,11},{4,12},{5,13},{6,14},{7,15},{8,0},{9,1},... | collective-permute-start | bytes 786440 | tf_op jit(solution)/shard_map/ppermute | solution.py:174
  200.9 6.9 %collective-permute-start.6 = (f32[256,256]{1,0:T(8,128)S(1)}, f32[256,256]{1,0:T(8,128)S(1)}, u32[]{:S(2)}, u32[]{:S(2)}) collective-permute-start(f32[256,256]{1,0:T(8,128)S(1)} %add.137), channel_id=1, source_target_pairs={{0,16},{1,17},{2,18},{3,19},{4,20},{5,21},{6,22},{7,23},{8,24},{9,... | collective-permute-start | bytes 786440 | tf_op jit(solution)/shard_map/ppermute | solution.py:174
  202.1 14.7 %collective-permute-start.8 = (bf16[512,256]{1,0:T(8,128)(2,1)S(1)}, bf16[512,256]{1,0:T(8,128)(2,1)S(1)}, u32[]{:S(2)}, u32[]{:S(2)}) collective-permute-start(bf16[512,256]{1,0:T(8,128)(2,1)S(1)} %convolution_convert_fusion), channel_id=1, source_target_pairs={{0,64},{64,0},{1,65},{65,1},{2,66},{66,2},{3,67},{67,3},{4,68},{68... | collective-permute-start | bytes 786440 | tf_op jit(solution)/shard_map/ppermute | solution.py:144
  207.8 9.9 %collective-permute-start.7 = (f32[256,256]{1,0:T(8,128)S(1)}, f32[256,256]{1,0:T(8,128)S(1)}, u32[]{:S(2)}, u32[]{:S(2)}) collective-permute-start(f32[256,256]{1,0:T(8,128)S(1)} %add.138), channel_id=1, source_target_pairs={{0,32},{1,33},{2,34},{3,35},{4,36},{5,37},{6,38},{7,39},{8,40},{9,... | collective-permute-start | bytes 786440 | tf_op jit(solution)/shard_map/ppermute | solution.py:174
  237.7 25.6 %collective-permute-start.9 = (f32[128,128,256]{2,1,0:T(8,128)}, f32[128,128,256]{2,1,0:T(8,128)S(1)}, u32[]{:S(2)}, u32[]{:S(2)}) collective-permute-start(f32[128,128,256]{2,1,0:T(8,128)} %get-tuple-element.10), channel_id=1, source_target_pairs={{0,1},{1,0},{2,3},{3,2},{4,5},{5,4},{6,7},{7,6},{8,9},{9,8},{10,11... | collective-permute-start | bytes 50331656 | tf_op jit(solution)/shard_map/ppermute | solution.py:152
  263.3 15.9 %copy-start.2 = (f32[128,128,256]{2,1,0:T(8,128)}, f32[128,128,256]{2,1,0:T(8,128)S(1)}, u32[]{:S(2)}) copy-start(f32[128,128,256]{2,1,0:T(8,128)S(1)} %collective-permute-done.9) | copy-start | bytes 50331652
  279.2 49.5 %collective-permute-start.11 = (f32[16,128,256]{2,1,0:T(8,128)}, f32[16,128,256]{2,1,0:T(8,128)S(1)}, u32[]{:S(2)}, u32[]{:S(2)}) collective-permute-start(f32[16,128,256]{2,1,0:T(8,128)} %get-tuple-element.13), channel_id=1, source_target_pairs={{0,4},{1,5},{2,6},{3,7},{4,0},{5,1},{6,2},{7,3},{8,12},{9,13},{10,... | collective-permute-start | bytes 6291464 | tf_op jit(solution)/shard_map/ppermute | solution.py:152
  281.5 48.8 %collective-permute-start.19 = (f32[16,128,256]{2,1,0:T(8,128)}, f32[16,128,256]{2,1,0:T(8,128)S(1)}, u32[]{:S(2)}, u32[]{:S(2)}) collective-permute-start(f32[16,128,256]{2,1,0:T(8,128)} %get-tuple-element.14), channel_id=1, source_target_pairs={{0,48},{1,49},{2,50},{3,51},{4,52},{5,53},{6,54},{7,55},{8,56},{9,... | collective-permute-start | bytes 6291464 | tf_op jit(solution)/shard_map/ppermute | solution.py:152
  282.7 50.3 %collective-permute-start.18 = (f32[16,128,256]{2,1,0:T(8,128)}, f32[16,128,256]{2,1,0:T(8,128)S(1)}, u32[]{:S(2)}, u32[]{:S(2)}) collective-permute-start(f32[16,128,256]{2,1,0:T(8,128)} %get-tuple-element.15), channel_id=1, source_target_pairs={{0,32},{1,33},{2,34},{3,35},{4,36},{5,37},{6,38},{7,39},{8,40},{9,... | collective-permute-start | bytes 6291464 | tf_op jit(solution)/shard_map/ppermute | solution.py:152
  283.7 92.7 %collective-permute-start.17 = (f32[16,128,256]{2,1,0:T(8,128)}, f32[16,128,256]{2,1,0:T(8,128)S(1)}, u32[]{:S(2)}, u32[]{:S(2)}) collective-permute-start(f32[16,128,256]{2,1,0:T(8,128)} %get-tuple-element.16), channel_id=1, source_target_pairs={{0,16},{1,17},{2,18},{3,19},{4,20},{5,21},{6,22},{7,23},{8,24},{9,... | collective-permute-start | bytes 6291464 | tf_op jit(solution)/shard_map/ppermute | solution.py:152
  284.6 91.8 %collective-permute-start.12 = (f32[16,128,256]{2,1,0:T(8,128)}, f32[16,128,256]{2,1,0:T(8,128)S(1)}, u32[]{:S(2)}, u32[]{:S(2)}) collective-permute-start(f32[16,128,256]{2,1,0:T(8,128)} %get-tuple-element.17), channel_id=1, source_target_pairs={{0,6},{1,7},{2,0},{3,1},{4,2},{5,3},{6,4},{7,5},{8,14},{9,15},{10,... | collective-permute-start | bytes 6291464 | tf_op jit(solution)/shard_map/ppermute | solution.py:152
  328.7 50.5 %collective-permute-start.10 = (f32[16,128,256]{2,1,0:T(8,128)}, f32[16,128,256]{2,1,0:T(8,128)}, u32[]{:S(2)}, u32[]{:S(2)}) collective-permute-start(f32[16,128,256]{2,1,0:T(8,128)} %get-tuple-element.18), channel_id=1, source_target_pairs={{0,2},{1,3},{2,4},{3,5},{4,6},{5,7},{6,0},{7,1},{8,10},{9,11},{10,... | collective-permute-start | bytes 6291464 | tf_op jit(solution)/shard_map/ppermute | solution.py:152
  330.2 46.2 %copy-start.3 = (f32[16,128,256]{2,1,0:T(8,128)}, f32[16,128,256]{2,1,0:T(8,128)S(1)}, u32[]{:S(2)}) copy-start(f32[16,128,256]{2,1,0:T(8,128)S(1)} %collective-permute-done.19) | copy-start | bytes 6291460
  333.0 43.5 %copy-start.4 = (f32[16,128,256]{2,1,0:T(8,128)}, f32[16,128,256]{2,1,0:T(8,128)S(1)}, u32[]{:S(2)}) copy-start(f32[16,128,256]{2,1,0:T(8,128)S(1)} %collective-permute-done.18) | copy-start | bytes 6291460
  376.4 1.4 copy-start.5
  377.8 1.4 copy-start.6
  388.1 16.4 %collective-permute-start.14 = (f32[4,128,256]{2,1,0:T(8,128)S(1)}, f32[4,128,256]{2,1,0:T(8,128)S(1)}, u32[]{:S(2)}, u32[]{:S(2)}) collective-permute-start(f32[4,128,256]{2,1,0:T(8,128)S(1)} %get-tuple-element.19), channel_id=1, source_target_pairs={{0,32},{1,33},{2,34},{3,35},{4,36},{5,37},{6,38},{7,39},{8,40},{9,... | collective-permute-start | bytes 1572872 | tf_op jit(solution)/shard_map/ppermute | solution.py:152
  389.2 22.7 %collective-permute-start.15 = (f32[4,128,256]{2,1,0:T(8,128)S(1)}, f32[4,128,256]{2,1,0:T(8,128)S(1)}, u32[]{:S(2)}, u32[]{:S(2)}) collective-permute-start(f32[4,128,256]{2,1,0:T(8,128)S(1)} %get-tuple-element.20), channel_id=1, source_target_pairs={{0,48},{1,49},{2,50},{3,51},{4,52},{5,53},{6,54},{7,55},{8,56},{9,... | collective-permute-start | bytes 1572872 | tf_op jit(solution)/shard_map/ppermute | solution.py:152
  390.4 24.4 %collective-permute-start.13 = (f32[4,128,256]{2,1,0:T(8,128)S(1)}, f32[4,128,256]{2,1,0:T(8,128)S(1)}, u32[]{:S(2)}, u32[]{:S(2)}) collective-permute-start(f32[4,128,256]{2,1,0:T(8,128)S(1)} %get-tuple-element.21), channel_id=1, source_target_pairs={{0,16},{1,17},{2,18},{3,19},{4,20},{5,21},{6,22},{7,23},{8,24},{9,... | collective-permute-start | bytes 1572872 | tf_op jit(solution)/shard_map/ppermute | solution.py:152
  391.4 25.0 %collective-permute-start.21 = (f32[4,128,256]{2,1,0:T(8,128)S(1)}, f32[4,128,256]{2,1,0:T(8,128)S(1)}, u32[]{:S(2)}, u32[]{:S(2)}) collective-permute-start(f32[4,128,256]{2,1,0:T(8,128)S(1)} %get-tuple-element.22), channel_id=1, source_target_pairs={{0,4},{1,5},{2,6},{3,7},{4,0},{5,1},{6,2},{7,3},{8,12},{9,13},{10,... | collective-permute-start | bytes 1572872 | tf_op jit(solution)/shard_map/ppermute | solution.py:152
  393.2 23.3 %collective-permute-start.22 = (f32[4,128,256]{2,1,0:T(8,128)S(1)}, f32[4,128,256]{2,1,0:T(8,128)S(1)}, u32[]{:S(2)}, u32[]{:S(2)}) collective-permute-start(f32[4,128,256]{2,1,0:T(8,128)S(1)} %get-tuple-element.23), channel_id=1, source_target_pairs={{0,6},{1,7},{2,0},{3,1},{4,2},{5,3},{6,4},{7,5},{8,14},{9,15},{10,... | collective-permute-start | bytes 1572872 | tf_op jit(solution)/shard_map/ppermute | solution.py:152
  404.5 13.5 %collective-permute-start.20 = (f32[4,128,256]{2,1,0:T(8,128)S(1)}, f32[4,128,256]{2,1,0:T(8,128)S(1)}, u32[]{:S(2)}, u32[]{:S(2)}) collective-permute-start(f32[4,128,256]{2,1,0:T(8,128)S(1)} %get-tuple-element.24), channel_id=1, source_target_pairs={{0,2},{1,3},{2,4},{3,5},{4,6},{5,7},{6,0},{7,1},{8,10},{9,11},{10,... | collective-permute-start | bytes 1572872 | tf_op jit(solution)/shard_map/ppermute | solution.py:152
  415.0 9.2 %collective-permute-start.16 = (f32[2,128,256]{2,1,0:T(8,128)S(1)}, f32[2,128,256]{2,1,0:T(8,128)S(1)}, u32[]{:S(2)}, u32[]{:S(2)}) collective-permute-start(f32[2,128,256]{2,1,0:T(8,128)S(1)} %slice.137), channel_id=1, source_target_pairs={{0,8},{1,9},{2,10},{3,11},{4,12},{5,13},{6,14},{7,15},{8,0},{9,1},... | collective-permute-start | bytes 786440 | tf_op jit(solution)/shard_map/ppermute | solution.py:152
  418.0 11.8 %copy-start.1 = (bf16[256,256]{1,0:T(8,128)(2,1)S(1)}, bf16[256,256]{1,0:T(8,128)(2,1)}, u32[]{:S(2)}) copy-start(bf16[256,256]{1,0:T(8,128)(2,1)} %param.7) | copy-start | bytes 393220
  418.2 10.8 %collective-permute-start.23 = (f32[2,128,256]{2,1,0:T(8,128)S(1)}, f32[2,128,256]{2,1,0:T(8,128)S(1)}, u32[]{:S(2)}, u32[]{:S(2)}) collective-permute-start(f32[2,128,256]{2,1,0:T(8,128)S(1)} %slice.151), channel_id=1, source_target_pairs={{0,8},{1,9},{2,10},{3,11},{4,12},{5,13},{6,14},{7,15},{8,0},{9,1},... | collective-permute-start | bytes 786440 | tf_op jit(solution)/shard_map/ppermute | solution.py:152
Sparse Core Ops, SparseCore 0:
  9.7 125.4 all-gather.1

commit v11 on v10

--- a/solution.py
+++ b/solution.py
@@ -49,10 +49,12 @@
     return (dk * 2 + half) * 64 + ((first * 4 + second) * 2 + dy) * 2 + q2
 
 
-def spread_kernel(side_ref, cols_ref, count_ref, vals_hbm, grad_ref, keep_hbm, send_hbm, vals, total, sems):
-    row_blocks, slot_total, block, _ = vals.shape
-    per_panel = grad_ref.shape[1]
-    col_blocks = total.shape[0]
+def spread_kernel(side_ref, cols_ref, count_ref, vals_hbm, grad_ref, *rest):
+    outs, (vals, total, sems) = rest[:-3], rest[-3:]
+    sources, row_blocks, slot_total, block, _ = vals.shape
+    per_panel = grad_ref.shape[2]
+    kept = total.shape[0]
+    col_blocks = 2 * kept
     per_dev = col_blocks // 64
     me = side_ref[1]
     load_vals = pltpu.make_async_copy(vals_hbm, vals, sems.at[0])
@@ -62,26 +64,36 @@
         total[c] = jnp.zeros(total.shape[1:], total.dtype)
         return carry
 
-    lax.fori_loop(0, col_blocks, clear, 0)
+    lax.fori_loop(0, kept, clear, 0)
     load_vals.wait()
-    for t in range(row_blocks):
-        live = jnp.clip(count_ref[t], 0, slot_total)
-        panel, within = divmod(t, per_panel)
-        grad = grad_ref[jnp.where(side_ref[0] == panel, 0, 1), within]
-
-        for k in range(slot_total):
-            col = jnp.clip(cols_ref[t, k], 0, col_blocks - 1)
-            picked = jnp.where(k < live, vals[t, k], jnp.zeros_like(vals[t, k]))
-            contrib = jnp.dot(picked, grad, preferred_element_type=jnp.float32)
-            slot = owner_slot(col, me, per_dev)
-            total[slot] += contrib
-    half = col_blocks // 2
-    keep = pltpu.make_async_copy(total.at[pl.ds(0, half)], keep_hbm, sems.at[1])
-    send = pltpu.make_async_copy(total.at[pl.ds(half, half)], send_hbm, sems.at[2])
-    send.start()
-    keep.start()
-    send.wait()
-    keep.wait()
+    for src in range(sources):
+
+        def row_block(t, carry):
+            live = jnp.clip(count_ref[src, t], 0, slot_total)
+            panel, within = t // per_panel, t % per_panel
+            grad = grad_ref[src, jnp.where(side_ref[0] == panel, 0, 1), within]
+            for k in range(slot_total):
+                col = jnp.clip(cols_ref[src, t, k], 0, col_blocks - 1)
+                slot = owner_slot(col, me, per_dev)
+
+                @pl.when((k < live) & (slot < kept))
+                def _():
+                    contrib = jnp.dot(vals[src, t, k], grad, preferred_element_type=jnp.float32)
+                    total[jnp.minimum(slot, kept - 1)] += contrib
+
+            return carry
+
+        lax.fori_loop(0, row_blocks, row_block, 0)
+
+    chunk = kept // len(outs)
+    copies = [
+        pltpu.make_async_copy(total.at[pl.ds(i * chunk, chunk)], out, sems.at[1 + i])
+        for i, out in enumerate(outs)
+    ]
+    for copy in copies:
+        copy.start()
+    for copy in copies:
+        copy.wait()
 
 
 def aggregate(cols, count, vals, panel):
@@ -112,11 +124,13 @@
 
 
 def spread(side, cols, count, vals, grad, col_blocks):
-    row_blocks, slot_total, block, _ = vals.shape
+    sources, row_blocks, slot_total, block, _ = vals.shape
     width = grad.shape[-1]
+    kept = col_blocks // 2
+    pieces = 8
     return pl.pallas_call(
         spread_kernel,
-        out_shape=[jax.ShapeDtypeStruct((col_blocks // 2, block, width), jnp.float32)] * 2,
+        out_shape=[jax.ShapeDtypeStruct((kept // pieces, block, width), jnp.float32)] * pieces,
         in_specs=[
             pl.BlockSpec(memory_space=pltpu.SMEM),
             pl.BlockSpec(memory_space=pltpu.SMEM),
@@ -124,16 +138,16 @@
             pl.BlockSpec(memory_space=pl.ANY),
             pl.BlockSpec(memory_space=pltpu.VMEM),
         ],
-        out_specs=[pl.BlockSpec(memory_space=pl.ANY)] * 2,
+        out_specs=[pl.BlockSpec(memory_space=pl.ANY)] * pieces,
         scratch_shapes=[
             pltpu.VMEM(vals.shape, vals.dtype),
-            pltpu.VMEM((col_blocks, block, width), jnp.float32),
-            pltpu.SemaphoreType.DMA((3,)),
+            pltpu.VMEM((kept, block, width), jnp.float32),
+            pltpu.SemaphoreType.DMA((1 + pieces,)),
         ],
         compiler_params=pltpu.CompilerParams(vmem_limit_bytes=VMEM_LIMIT),
         cost_estimate=pl.CostEstimate(
-            flops=2 * row_blocks * slot_total * block * block * width,
-            bytes_accessed=vals.size * 2 + grad.size * 2 + col_blocks * block * width * 4,
+            flops=sources * row_blocks * slot_total * block * block * width,
+            bytes_accessed=vals.size * 2 + grad.size * 2 + kept * block * width * 4,
             transcendentals=0,
         ),
     )(side, cols, count, vals, grad)
@@ -152,12 +166,9 @@
     return lax.ppermute(value, "row", [(r, dest(r)) for r in range(64)])
 
 
-def row_reduce_scatter(keep, send):
-    _, block, width = keep.shape
-    keep = keep.reshape(2, 4, 16, block, width)
-    came = shifted(send, 1, 2, 1).reshape(2, 4, 16, block, width)
-    first = [keep[0, s] + came[0, s] for s in range(4)]
-    second = [keep[1, s] + came[1, s] for s in range(4)]
+def row_reduce_scatter(pieces):
+    _, block, width = pieces[0].shape
+    first, second = pieces[:4], pieces[4:]
     first = (first[0] + sum(shifted(first[s], 2, 4, s) for s in range(1, 4))).reshape(4, 4, block, width)
     second = (second[0] + sum(shifted(second[s], 16, 4, s) for s in range(1, 4))).reshape(4, 4, block, width)
     first = (first[0] + sum(shifted(first[s], 16, 4, s) for s in range(1, 4))).reshape(2, 2, block, width)
@@ -188,6 +199,9 @@
     cols = block_cols[0]
     count = block_count[0]
     vals = block_vals[0]
+    chip_vals = jnp.swapaxes(vals, 2, 3)
+    chip_vals = jnp.stack([chip_vals, shifted(chip_vals, 1, 2, 1)])
+    chip_vals, gathered = lax.optimization_barrier((chip_vals, gathered))
 
     partial_value = aggregate(cols, count, vals, gathered).reshape(-1, width)
     mine = lax.dynamic_slice_in_dim(partial_value, side * rows_dev, rows_dev)
@@ -205,8 +219,9 @@
     weight_grad = weight_grad * (1.0 / math.sqrt(verts))
 
     where = jnp.stack([side, lax.axis_index("row")]).astype(jnp.int32)
-    keep, send = spread(where, cols, count, jnp.swapaxes(vals, 2, 3), both_grad, col_blocks)
-    input_grad = row_reduce_scatter(keep, send).astype(jnp.bfloat16)
+    pair = lambda value: jnp.stack([value, shifted(value, 1, 2, 1)])
+    pieces = spread(where, pair(cols), pair(count), chip_vals, pair(both_grad), col_blocks)
+    input_grad = row_reduce_scatter(pieces).astype(jnp.bfloat16)
     return (activated, weight_grad, input_grad)
 
 

time: 437 us -> 441 us (level)
  starting transfers between devices: 36.9 us -> 82.9 us
  waiting for transfers between devices: 313 us -> 272 us
  other arithmetic: 29.3 us -> 16.3 us
  Pallas kernels: 31 us -> 43.9 us
    ppermute x15 -> x18, starting transfers between devices: 20.6 us -> 66.5 us  [shifted(): return lax.ppermute(value, 'row', [(r, dest(r)) for r in range(64)])]
    ppermute x15 -> x18, waiting for transfers between devices: 142 us -> 117 us  [shifted(): return lax.ppermute(value, 'row', [(r, dest(r)) for r in range(64)])]
    all_gather x1, waiting for transfers between devices: 127 us -> 106 us  [body(): gathered = lax.all_gather(features, 'row', axis=0, tiled=True)]
    add x1, other arithmetic: 15.9 us -> 2.15 us  [row_reduce_scatter(): second[0] + sum((shifted(second[s], 16, 4, s) for s in range(1, 4)))]
    pallas_call x1, Pallas kernels: 19.9 us -> 32.8 us  [spread(): pl.pallas_call(spread_kernel, out_shape=[jax.ShapeDtypeStruct((kept // pi...]
    another operation x2 -> x6, other arithmetic: 0.09 us -> 9.85 us  [the longest x1 7.52 us: body(): chip_vals = jnp.stack([chip_vals, shifted(chip_vals, 1, 2, 1)])]
    add x1, other arithmetic: 8.7 us -> 0.6 us  [row_reduce_scatter(): first[0] + sum((shifted(first[s], 2, 4, s) for s in range(1, 4)))]
    ppermute x7, waiting for transfers between devices: 30.1 us -> 35.7 us  [all_sum(): lax.ppermute(value, axis, [(i, i ^ step) for i in range(size)])]
  transfers between devices with their start and end apart: 25 -> 28, of which waited for: 19 -> 17; matrix products, arithmetic and copies ran while one was open for 2% -> 5% of each run, Pallas kernels for 0% -> 0%
where the time goes in v11:
time: 441 us; the launch traced here: 439 us
  waiting for transfers between devices  272 us (62%)
  starting transfers between devices  82.9 us (19%)
  Pallas kernels  43.9 us (10%)
  other arithmetic  16.3 us (4%)
  between operations  14.3 us (3%)
  local copies, waits for them, and re-layouts  7.93 us (2%)
    ppermute x18, waiting for transfers between devices, shifted(): return lax.ppermute(value, 'row', [(r, dest(r)) for r in range(64)])  117 us
    all_gather x1, waiting for transfers between devices, body(): gathered = lax.all_gather(features, 'row', axis=0, tiled=True)  106 us
    ppermute x18, starting transfers between devices, shifted(): return lax.ppermute(value, 'row', [(r, dest(r)) for r in range(64)])  66.5 us
    ppermute x7, waiting for transfers between devices, all_sum(): lax.ppermute(value, axis, [(i, i ^ step) for i in range(size)])  35.7 us
    pallas_call x1, Pallas kernels, spread(): pl.pallas_call(spread_kernel, out_shape=[jax.ShapeDtypeStruct((kept // pi...  32.8 us
    ppermute x2, waiting for transfers between devices, swap(): return lax.ppermute(value, axis, [(i, i ^ 1) for i in range(size)])  13.2 us
    pallas_call x1, Pallas kernels, aggregate(): pl.pallas_call(aggregate_kernel, out_shape=jax.ShapeDtypeStruct((row_bloc...  11.1 us
    ppermute x7, starting transfers between devices, all_sum(): lax.ppermute(value, axis, [(i, i ^ step) for i in range(size)])  10.4 us
  transfers between devices with their start and end apart: 28, of which 17 were waited for; matrix products, arithmetic and copies ran while one was open for 5% of the time, Pallas kernels for 0%

profile of v11, /device:TPU:0, one launch (start us, length us, event | category | flops | bytes accessed | tf_op | source)
XLA Modules:
  0.0 439.2 jit_solution(429596257261058330)
XLA Ops:
  7.2 0.7 all-gather.2.cloned.1.call-update
  7.9 6.5 %copy.9 = bf16[1,8,16,128,128]{3,4,2,1,0:T(8,128)(2,1)} copy(bf16[1,8,16,128,128]{4,3,2,1,0:T(8,128)(2,1)} %param.8) | data formatting | bytes 8388608 | tf_op args[2]
  14.4 7.5 %collective-permute-done = bf16[8,16,128,128]{3,2,1,0:T(8,128)(2,1)} collective-permute-done((bf16[8,16,128,128]{3,2,1,0:T(8,128)(2,1)}, bf16[8,16,128,128]{3,2,1,0:T(8,128)(2,1)}, u32[]{:S(2)}, u32[]{:S(2)}) %collective-permute-start) | collective-permute-done | bytes 4194336 | tf_op jit(solution)/shard_map/ppermute | solution.py:166
  21.9 7.5 %pad_maximum_fusion.vals_hbm = bf16[2,8,16,128,128]{4,3,2,1,0:T(8,128)(2,1)} fusion(bf16[1,8,16,128,128]{4,3,2,1,0:T(8,128)(2,1)} %bitcast.7, bf16[1,8,16,128,128]{4,3,2,1,0:T(8,128)(2,1)} %bitcast.27), kind=kLoop, calls=%fused_computation | loop fusion | flops 4194304 | bytes 16777216 | tf_op jit(solution)/shard_map/stack | solution.py:203
  29.5 105.8 %all-gather.2.cloned.1.call-done.panel_hbm = bf16[32768,256]{1,0:T(8,128)(2,1)} async-done(((bf16[512,256]{1,0:T(8,128)(2,1)}), bf16[32768,256]{1,0:T(8,128)(2,1)}) %all-gather.2.cloned.1.call-update) | async-done | bytes 16777232 | tf_op jit(solution)/shard_map/all_gather | solution.py:197
  135.3 11.1 %shard_map.85 = f32[8,128,256]{2,1,0:T(8,128)} custom-call(s32[8,16]{1,0:T(8,128)} %bitcast.35, s32[8]{0:T(128)} %bitcast.38, bf16[8,16,128,128]{3,2,1,0:T(8,128)(2,1)} %bitcast.25, bf16[32768,256]{1,0:T(8,128)(2,1)} %all-gather.2.cloned.1.call-done.panel_hbm), custom_call_target="tpu_custom_call" | custom-call | flops 1073741824 | bytes 22020096 | tf_op jit(solution)/shard_map/pallas_call | solution.py:102
  146.4 1.1 constant_dynamic-slice_fusion
  147.5 2.8 collective-permute-start.1
  150.3 12.9 %collective-permute-done.1 = f32[512,256]{1,0:T(8,128)S(1)} collective-permute-done((f32[512,256]{1,0:T(8,128)S(1)}, f32[512,256]{1,0:T(8,128)S(1)}, u32[]{:S(2)}, u32[]{:S(2)}) %collective-permute-start.1) | collective-permute-done | bytes 524320 | tf_op jit(solution)/shard_map/ppermute | solution.py:158
  163.2 1.1 add_convert_fusion
  164.3 1.1 multiply_convert_fusion
  165.7 2.8 collective-permute-start.2
  168.4 6.5 %collective-permute-done.2 = f32[256,256]{1,0:T(8,128)S(1)} collective-permute-done((f32[256,256]{1,0:T(8,128)S(1)}, f32[256,256]{1,0:T(8,128)S(1)}, u32[]{:S(2)}, u32[]{:S(2)}) %collective-permute-start.2) | collective-permute-done | bytes 262176 | tf_op jit(solution)/shard_map/ppermute | solution.py:185
  175.0 1.5 collective-permute-done.3
  176.6 1.5 collective-permute-start.4
  178.0 7.0 %collective-permute-done.4 = f32[256,256]{1,0:T(8,128)S(1)} collective-permute-done((f32[256,256]{1,0:T(8,128)S(1)}, f32[256,256]{1,0:T(8,128)S(1)}, u32[]{:S(2)}, u32[]{:S(2)}) %collective-permute-start.4) | collective-permute-done | bytes 262176 | tf_op jit(solution)/shard_map/ppermute | solution.py:185
  185.0 2.2 collective-permute-start.5
  187.2 6.9 %collective-permute-done.5 = f32[256,256]{1,0:T(8,128)S(1)} collective-permute-done((f32[256,256]{1,0:T(8,128)S(1)}, f32[256,256]{1,0:T(8,128)S(1)}, u32[]{:S(2)}, u32[]{:S(2)}) %collective-permute-start.5) | collective-permute-done | bytes 262176 | tf_op jit(solution)/shard_map/ppermute | solution.py:185
  194.2 1.0 collective-permute-start.6
  195.2 5.7 %collective-permute-done.6 = f32[256,256]{1,0:T(8,128)S(1)} collective-permute-done((f32[256,256]{1,0:T(8,128)S(1)}, f32[256,256]{1,0:T(8,128)S(1)}, u32[]{:S(2)}, u32[]{:S(2)}) %collective-permute-start.6) | collective-permute-done | bytes 262176 | tf_op jit(solution)/shard_map/ppermute | solution.py:185
  200.9 1.0 collective-permute-start.7
  202.2 3.2 collective-permute-start.9
  205.3 2.5 collective-permute-done.7
  207.9 1.9 collective-permute-start.8
  210.2 5.7 %collective-permute-done.8 = f32[256,256]{1,0:T(8,128)S(1)} collective-permute-done((f32[256,256]{1,0:T(8,128)S(1)}, f32[256,256]{1,0:T(8,128)S(1)}, u32[]{:S(2)}, u32[]{:S(2)}) %collective-permute-start.8) | collective-permute-done | bytes 262176 | tf_op jit(solution)/shard_map/ppermute | solution.py:185
  216.6 0.6 pad_add_fusion.2.side_ref
  217.2 0.7 collective-permute-done.11
  218.4 0.6 pad_add_fusion.cols_ref
  219.0 1.1 pad_maximum_fusion.1.grad_ref
  220.1 32.8 %shard_map.86 = (f32[16,128,256]{2,1,0:T(8,128)}, f32[16,128,256]{2,1,0:T(8,128)}, f32[16,128,256]{2,1,0:T(8,128)}, f32[16,128,256]{2,1,0:T(8,128)}, f32[16,128,...) custom-call(s32[2]{0:T(128)} %pad_add_fusion.2.side_ref, ...), custom_call_target="tpu_custom_call" | custom-call | flops 1073741824 | bytes 26214400 | tf_op jit(solution)/shard_map/pallas_call | solution.py:131
  253.1 2.0 collective-permute-start.20
  255.6 9.2 %collective-permute-start.15 = (f32[16,128,256]{2,1,0:T(8,128)}, f32[16,128,256]{2,1,0:T(8,128)S(1)}, u32[]{:S(2)}, u32[]{:S(2)}) collective-permute-start(f32[16,128,256]{2,1,0:T(8,128)} %get-tuple-element.22), channel_id=1, source_target_pairs={{0,6},{1,7},{2,0},{3,1},{4,2},{5,3},{6,4},{7,5},{8,14},{9,15},{10,... | collective-permute-start | bytes 6291464 | tf_op jit(solution)/shard_map/ppermute | solution.py:166
  264.8 37.0 %collective-permute-done.22 = f32[16,128,256]{2,1,0:T(8,128)S(1)} collective-permute-done((f32[16,128,256]{2,1,0:T(8,128)}, f32[16,128,256]{2,1,0:T(8,128)S(1)}, u32[]{:S(2)}, u32[]{:S(2)}) %collective-permute-start.22) | collective-permute-done | bytes 2097184 | tf_op jit(solution)/shard_map/ppermute | solution.py:166
  301.7 0.7 collective-permute-start.14
  302.4 44.7 %collective-permute-done.20 = f32[16,128,256]{2,1,0:T(8,128)S(1)} collective-permute-done((f32[16,128,256]{2,1,0:T(8,128)}, f32[16,128,256]{2,1,0:T(8,128)S(1)}, u32[]{:S(2)}, u32[]{:S(2)}) %collective-permute-start.20) | collective-permute-done | bytes 2097184 | tf_op jit(solution)/shard_map/ppermute | solution.py:166
  347.1 2.2 add_add_fusion
  349.4 8.6 %collective-permute-start.25 = (f32[4,128,256]{2,1,0:T(8,128)S(1)}, f32[4,128,256]{2,1,0:T(8,128)S(1)}, u32[]{:S(2)}, u32[]{:S(2)}) collective-permute-start(f32[4,128,256]{2,1,0:T(8,128)S(1)} %get-tuple-element.31), channel_id=1, source_target_pairs={{0,6},{1,7},{2,0},{3,1},{4,2},{5,3},{6,4},{7,5},{8,14},{9,15},{10,... | collective-permute-start | bytes 1572872 | tf_op jit(solution)/shard_map/ppermute | solution.py:166
  358.0 1.5 collective-permute-start.24
  359.6 0.6 add_add_fusion.1
  360.3 1.7 collective-permute-start.18
  362.1 31.6 %collective-permute-start.16 = (f32[4,128,256]{2,1,0:T(8,128)S(1)}, f32[4,128,256]{2,1,0:T(8,128)S(1)}, u32[]{:S(2)}, u32[]{:S(2)}) collective-permute-start(f32[4,128,256]{2,1,0:T(8,128)S(1)} %get-tuple-element.29), channel_id=1, source_target_pairs={{0,16},{1,17},{2,18},{3,19},{4,20},{5,21},{6,22},{7,23},{8,24},{9,... | collective-permute-start | bytes 1572872 | tf_op jit(solution)/shard_map/ppermute | solution.py:166
  393.7 17.6 %collective-permute-done.25 = f32[4,128,256]{2,1,0:T(8,128)S(1)} collective-permute-done((f32[4,128,256]{2,1,0:T(8,128)S(1)}, f32[4,128,256]{2,1,0:T(8,128)S(1)}, u32[]{:S(2)}, u32[]{:S(2)}) %collective-permute-start.25) | collective-permute-done | bytes 524320 | tf_op jit(solution)/shard_map/ppermute | solution.py:166
  411.5 8.1 %collective-permute-start.26 = (f32[2,128,256]{2,1,0:T(8,128)S(1)}, f32[2,128,256]{2,1,0:T(8,128)S(1)}, u32[]{:S(2)}, u32[]{:S(2)}) collective-permute-start(f32[2,128,256]{2,1,0:T(8,128)S(1)} %slice.71), channel_id=1, source_target_pairs={{0,8},{1,9},{2,10},{3,11},{4,12},{5,13},{6,14},{7,15},{8,0},{9,1},... | collective-permute-start | bytes 786440 | tf_op jit(solution)/shard_map/ppermute | solution.py:166
  419.6 5.3 %collective-permute-done.17 = f32[4,128,256]{2,1,0:T(8,128)S(1)} collective-permute-done((f32[4,128,256]{2,1,0:T(8,128)S(1)}, f32[4,128,256]{2,1,0:T(8,128)S(1)}, u32[]{:S(2)}, u32[]{:S(2)}) %collective-permute-start.17) | collective-permute-done | bytes 524320 | tf_op jit(solution)/shard_map/ppermute | solution.py:166
  425.1 1.7 collective-permute-start.19
  426.8 0.7 broadcast_multiply_fusion
  427.6 4.0 collective-permute-done.19
  431.6 0.7 pad_maximum_fusion.3
  (54 shorter events, 3.7 us)
Async XLA Ops:
  7.2 157.1 %copy-start = (bf16[256,256]{1,0:T(8,128)(2,1)S(1)}, bf16[256,256]{1,0:T(8,128)(2,1)}, u32[]{:S(2)}) copy-start(bf16[256,256]{1,0:T(8,128)(2,1)} %param.7) | copy-start | bytes 393220
  7.2 128.1 %all-gather.2.cloned.1.call-start = ((), (), s32[]{:S(2)}) async-start(), calls=%async_computation | async-start | bytes 17039360 | tf_op jit(solution)/shard_map/all_gather | solution.py:197
  14.4 7.5 %collective-permute-start = (bf16[8,16,128,128]{3,2,1,0:T(8,128)(2,1)}, bf16[8,16,128,128]{3,2,1,0:T(8,128)(2,1)}, u32[]{:S(2)}, u32[]{:S(2)}) collective-permute-start(bf16[8,16,128,128]{3,2,1,0:T(8,128)(2,1)} %bitcast.26), channel_id=1, source_target_pairs={{0,1},{1,0},{2,3},{3,2},{4,5},{5,4},{6,7},{7,6},{8,9},{9,8},{10,11... | collective-permute-start | bytes 12582920 | tf_op jit(solution)/shard_map/ppermute | solution.py:166
  146.4 17.9 %copy-start.5 = (bf16[512,256]{1,0:T(8,128)(2,1)S(1)}, bf16[512,256]{1,0:T(8,128)(2,1)}, u32[]{:S(2)}) copy-start(bf16[512,256]{1,0:T(8,128)(2,1)} %param.11) | copy-start | bytes 786436
  147.5 15.7 %collective-permute-start.1 = (f32[512,256]{1,0:T(8,128)S(1)}, f32[512,256]{1,0:T(8,128)S(1)}, u32[]{:S(2)}, u32[]{:S(2)}) collective-permute-start(f32[512,256]{1,0:T(8,128)S(1)} %constant_dynamic-slice_fusion), channel_id=1, source_target_pairs={{0,64},{64,0},{1,65},{65,1},{2,66},{66,2},{3,67},{67,3},{4,68},{68... | collective-permute-start | bytes 1572872 | tf_op jit(solution)/shard_map/ppermute | solution.py:158
  165.7 9.2 %collective-permute-start.2 = (f32[256,256]{1,0:T(8,128)S(1)}, f32[256,256]{1,0:T(8,128)S(1)}, u32[]{:S(2)}, u32[]{:S(2)}) collective-permute-start(f32[256,256]{1,0:T(8,128)S(1)} %fusion.4), channel_id=1, source_target_pairs={{0,64},{64,0},{1,65},{65,1},{2,66},{66,2},{3,67},{67,3},{4,68},{68... | collective-permute-start | bytes 786440 | tf_op jit(solution)/shard_map/ppermute | solution.py:185
  174.9 1.6 collective-permute-start.3
  176.6 8.4 %collective-permute-start.4 = (f32[256,256]{1,0:T(8,128)S(1)}, f32[256,256]{1,0:T(8,128)S(1)}, u32[]{:S(2)}, u32[]{:S(2)}) collective-permute-start(f32[256,256]{1,0:T(8,128)S(1)} %add.86), channel_id=1, source_target_pairs={{0,2},{1,3},{2,0},{3,1},{4,6},{5,7},{6,4},{7,5},{8,10},{9,11},{10,... | collective-permute-start | bytes 786440 | tf_op jit(solution)/shard_map/ppermute | solution.py:185
  185.0 9.1 %collective-permute-start.5 = (f32[256,256]{1,0:T(8,128)S(1)}, f32[256,256]{1,0:T(8,128)S(1)}, u32[]{:S(2)}, u32[]{:S(2)}) collective-permute-start(f32[256,256]{1,0:T(8,128)S(1)} %add.87), channel_id=1, source_target_pairs={{0,4},{1,5},{2,6},{3,7},{4,0},{5,1},{6,2},{7,3},{8,12},{9,13},{10,... | collective-permute-start | bytes 786440 | tf_op jit(solution)/shard_map/ppermute | solution.py:185
  194.2 21.8 %copy-start.3 = (s32[1,8,16]{2,1,0:T(8,128)S(1)}, s32[1,8,16]{2,1,0:T(8,128)}, u32[]{:S(2)}) copy-start(s32[1,8,16]{2,1,0:T(8,128)} %param.9) | copy-start | bytes 1540
  194.2 22.3 %copy-start.4 = (s32[1,8]{1,0:T(1,128)S(1)}, s32[1,8]{1,0:T(1,128)}, u32[]{:S(2)}) copy-start(s32[1,8]{1,0:T(1,128)} %param.10) | copy-start | bytes 100
  194.2 6.7 %collective-permute-start.6 = (f32[256,256]{1,0:T(8,128)S(1)}, f32[256,256]{1,0:T(8,128)S(1)}, u32[]{:S(2)}, u32[]{:S(2)}) collective-permute-start(f32[256,256]{1,0:T(8,128)S(1)} %add.88), channel_id=1, source_target_pairs={{0,8},{1,9},{2,10},{3,11},{4,12},{5,13},{6,14},{7,15},{8,0},{9,1},... | collective-permute-start | bytes 786440 | tf_op jit(solution)/shard_map/ppermute | solution.py:185
  200.9 6.9 %collective-permute-start.7 = (f32[256,256]{1,0:T(8,128)S(1)}, f32[256,256]{1,0:T(8,128)S(1)}, u32[]{:S(2)}, u32[]{:S(2)}) collective-permute-start(f32[256,256]{1,0:T(8,128)S(1)} %add.89), channel_id=1, source_target_pairs={{0,16},{1,17},{2,18},{3,19},{4,20},{5,21},{6,22},{7,23},{8,24},{9,... | collective-permute-start | bytes 786440 | tf_op jit(solution)/shard_map/ppermute | solution.py:185
  202.2 8.0 %collective-permute-start.9 = (bf16[512,256]{1,0:T(8,128)(2,1)S(1)}, bf16[512,256]{1,0:T(8,128)(2,1)S(1)}, u32[]{:S(2)}, u32[]{:S(2)}) collective-permute-start(bf16[512,256]{1,0:T(8,128)(2,1)S(1)} %convolution_convert_fusion), channel_id=1, source_target_pairs={{0,64},{64,0},{1,65},{65,1},{2,66},{66,2},{3,67},{67,3},{4,68},{68... | collective-permute-start | bytes 786440 | tf_op jit(solution)/shard_map/ppermute | solution.py:158
  207.9 8.0 %collective-permute-start.8 = (f32[256,256]{1,0:T(8,128)S(1)}, f32[256,256]{1,0:T(8,128)S(1)}, u32[]{:S(2)}, u32[]{:S(2)}) collective-permute-start(f32[256,256]{1,0:T(8,128)S(1)} %add.90), channel_id=1, source_target_pairs={{0,32},{1,33},{2,34},{3,35},{4,36},{5,37},{6,38},{7,39},{8,40},{9,... | collective-permute-start | bytes 786440 | tf_op jit(solution)/shard_map/ppermute | solution.py:185
  215.9 3.2 collective-permute-start.12
  216.0 2.5 collective-permute-start.10
  216.5 1.4 collective-permute-start.11
  253.0 48.8 %collective-permute-start.22 = (f32[16,128,256]{2,1,0:T(8,128)}, f32[16,128,256]{2,1,0:T(8,128)S(1)}, u32[]{:S(2)}, u32[]{:S(2)}) collective-permute-start(f32[16,128,256]{2,1,0:T(8,128)} %get-tuple-element.26), channel_id=1, source_target_pairs={{0,48},{1,49},{2,50},{3,51},{4,52},{5,53},{6,54},{7,55},{8,56},{9,... | collective-permute-start | bytes 6291464 | tf_op jit(solution)/shard_map/ppermute | solution.py:166
  253.1 94.1 %collective-permute-start.20 = (f32[16,128,256]{2,1,0:T(8,128)}, f32[16,128,256]{2,1,0:T(8,128)S(1)}, u32[]{:S(2)}, u32[]{:S(2)}) collective-permute-start(f32[16,128,256]{2,1,0:T(8,128)} %get-tuple-element.24), channel_id=1, source_target_pairs={{0,16},{1,17},{2,18},{3,19},{4,20},{5,21},{6,22},{7,23},{8,24},{9,... | collective-permute-start | bytes 6291464 | tf_op jit(solution)/shard_map/ppermute | solution.py:166
  255.1 92.0 %collective-permute-start.21 = (f32[16,128,256]{2,1,0:T(8,128)}, f32[16,128,256]{2,1,0:T(8,128)S(1)}, u32[]{:S(2)}, u32[]{:S(2)}) collective-permute-start(f32[16,128,256]{2,1,0:T(8,128)} %get-tuple-element.25), channel_id=1, source_target_pairs={{0,32},{1,33},{2,34},{3,35},{4,36},{5,37},{6,38},{7,39},{8,40},{9,... | collective-permute-start | bytes 6291464 | tf_op jit(solution)/shard_map/ppermute | solution.py:166
  255.6 102.5 %collective-permute-start.15 = (f32[16,128,256]{2,1,0:T(8,128)}, f32[16,128,256]{2,1,0:T(8,128)S(1)}, u32[]{:S(2)}, u32[]{:S(2)}) collective-permute-start(f32[16,128,256]{2,1,0:T(8,128)} %get-tuple-element.22), channel_id=1, source_target_pairs={{0,6},{1,7},{2,0},{3,1},{4,2},{5,3},{6,4},{7,5},{8,14},{9,15},{10,... | collective-permute-start | bytes 6291464 | tf_op jit(solution)/shard_map/ppermute | solution.py:166
  264.7 94.8 %collective-permute-start.13 = (f32[16,128,256]{2,1,0:T(8,128)}, f32[16,128,256]{2,1,0:T(8,128)S(1)}, u32[]{:S(2)}, u32[]{:S(2)}) collective-permute-start(f32[16,128,256]{2,1,0:T(8,128)} %get-tuple-element.20), channel_id=1, source_target_pairs={{0,2},{1,3},{2,4},{3,5},{4,6},{5,7},{6,0},{7,1},{8,10},{9,11},{10,... | collective-permute-start | bytes 6291464 | tf_op jit(solution)/shard_map/ppermute | solution.py:166
  301.7 57.8 %collective-permute-start.14 = (f32[16,128,256]{2,1,0:T(8,128)}, f32[16,128,256]{2,1,0:T(8,128)S(1)}, u32[]{:S(2)}, u32[]{:S(2)}) collective-permute-start(f32[16,128,256]{2,1,0:T(8,128)} %get-tuple-element.21), channel_id=1, source_target_pairs={{0,4},{1,5},{2,6},{3,7},{4,0},{5,1},{6,2},{7,3},{8,12},{9,13},{10,... | collective-permute-start | bytes 6291464 | tf_op jit(solution)/shard_map/ppermute | solution.py:166
  349.3 10.3 %copy-start.2 = (f32[16,128,256]{2,1,0:T(8,128)S(1)}, f32[16,128,256]{2,1,0:T(8,128)}, u32[]{:S(2)}) copy-start(f32[16,128,256]{2,1,0:T(8,128)} %get-tuple-element.19) | copy-start | bytes 6291460
  349.4 61.9 %collective-permute-start.25 = (f32[4,128,256]{2,1,0:T(8,128)S(1)}, f32[4,128,256]{2,1,0:T(8,128)S(1)}, u32[]{:S(2)}, u32[]{:S(2)}) collective-permute-start(f32[4,128,256]{2,1,0:T(8,128)S(1)} %get-tuple-element.31), channel_id=1, source_target_pairs={{0,6},{1,7},{2,0},{3,1},{4,2},{5,3},{6,4},{7,5},{8,14},{9,15},{10,... | collective-permute-start | bytes 1572872 | tf_op jit(solution)/shard_map/ppermute | solution.py:166
  358.0 53.2 %collective-permute-start.23 = (f32[4,128,256]{2,1,0:T(8,128)S(1)}, f32[4,128,256]{2,1,0:T(8,128)S(1)}, u32[]{:S(2)}, u32[]{:S(2)}) collective-permute-start(f32[4,128,256]{2,1,0:T(8,128)S(1)} %get-tuple-element.32), channel_id=1, source_target_pairs={{0,2},{1,3},{2,4},{3,5},{4,6},{5,7},{6,0},{7,1},{8,10},{9,11},{10,... | collective-permute-start | bytes 1572872 | tf_op jit(solution)/shard_map/ppermute | solution.py:166
  358.0 53.2 %collective-permute-start.24 = (f32[4,128,256]{2,1,0:T(8,128)S(1)}, f32[4,128,256]{2,1,0:T(8,128)S(1)}, u32[]{:S(2)}, u32[]{:S(2)}) collective-permute-start(f32[4,128,256]{2,1,0:T(8,128)S(1)} %get-tuple-element.30), channel_id=1, source_target_pairs={{0,4},{1,5},{2,6},{3,7},{4,0},{5,1},{6,2},{7,3},{8,12},{9,13},{10,... | collective-permute-start | bytes 1572872 | tf_op jit(solution)/shard_map/ppermute | solution.py:166
  360.3 59.3 %collective-permute-start.18 = (f32[4,128,256]{2,1,0:T(8,128)S(1)}, f32[4,128,256]{2,1,0:T(8,128)S(1)}, u32[]{:S(2)}, u32[]{:S(2)}) collective-permute-start(f32[4,128,256]{2,1,0:T(8,128)S(1)} %get-tuple-element.28), channel_id=1, source_target_pairs={{0,48},{1,49},{2,50},{3,51},{4,52},{5,53},{6,54},{7,55},{8,56},{9,... | collective-permute-start | bytes 1572872 | tf_op jit(solution)/shard_map/ppermute | solution.py:166
  362.1 57.5 %collective-permute-start.16 = (f32[4,128,256]{2,1,0:T(8,128)S(1)}, f32[4,128,256]{2,1,0:T(8,128)S(1)}, u32[]{:S(2)}, u32[]{:S(2)}) collective-permute-start(f32[4,128,256]{2,1,0:T(8,128)S(1)} %get-tuple-element.29), channel_id=1, source_target_pairs={{0,16},{1,17},{2,18},{3,19},{4,20},{5,21},{6,22},{7,23},{8,24},{9,... | collective-permute-start | bytes 1572872 | tf_op jit(solution)/shard_map/ppermute | solution.py:166
  411.3 13.7 %collective-permute-start.17 = (f32[4,128,256]{2,1,0:T(8,128)S(1)}, f32[4,128,256]{2,1,0:T(8,128)S(1)}, u32[]{:S(2)}, u32[]{:S(2)}) collective-permute-start(f32[4,128,256]{2,1,0:T(8,128)S(1)} %get-tuple-element.27), channel_id=1, source_target_pairs={{0,32},{1,33},{2,34},{3,35},{4,36},{5,37},{6,38},{7,39},{8,40},{9,... | collective-permute-start | bytes 1572872 | tf_op jit(solution)/shard_map/ppermute | solution.py:166
  411.5 16.1 %collective-permute-start.26 = (f32[2,128,256]{2,1,0:T(8,128)S(1)}, f32[2,128,256]{2,1,0:T(8,128)S(1)}, u32[]{:S(2)}, u32[]{:S(2)}) collective-permute-start(f32[2,128,256]{2,1,0:T(8,128)S(1)} %slice.71), channel_id=1, source_target_pairs={{0,8},{1,9},{2,10},{3,11},{4,12},{5,13},{6,14},{7,15},{8,0},{9,1},... | collective-permute-start | bytes 786440 | tf_op jit(solution)/shard_map/ppermute | solution.py:166
  424.9 7.4 %copy-start.1 = (bf16[256,256]{1,0:T(8,128)(2,1)S(1)}, bf16[256,256]{1,0:T(8,128)(2,1)}, u32[]{:S(2)}) copy-start(bf16[256,256]{1,0:T(8,128)(2,1)} %param.7) | copy-start | bytes 393220
  425.1 6.5 %collective-permute-start.19 = (f32[2,128,256]{2,1,0:T(8,128)S(1)}, f32[2,128,256]{2,1,0:T(8,128)S(1)}, u32[]{:S(2)}, u32[]{:S(2)}) collective-permute-start(f32[2,128,256]{2,1,0:T(8,128)S(1)} %slice.65), channel_id=1, source_target_pairs={{0,8},{1,9},{2,10},{3,11},{4,12},{5,13},{6,14},{7,15},{8,0},{9,1},... | collective-permute-start | bytes 786440 | tf_op jit(solution)/shard_map/ppermute | solution.py:166
Sparse Core Ops, SparseCore 0:
  9.7 125.4 all-gather.1

commit v12 on v10

--- a/solution.py
+++ b/solution.py
@@ -188,6 +188,7 @@
     cols = block_cols[0]
     count = block_count[0]
     vals = block_vals[0]
+    flipped, gathered = lax.optimization_barrier((jnp.swapaxes(vals, 2, 3), gathered))
 
     partial_value = aggregate(cols, count, vals, gathered).reshape(-1, width)
     mine = lax.dynamic_slice_in_dim(partial_value, side * rows_dev, rows_dev)
@@ -205,7 +206,7 @@
     weight_grad = weight_grad * (1.0 / math.sqrt(verts))
 
     where = jnp.stack([side, lax.axis_index("row")]).astype(jnp.int32)
-    keep, send = spread(where, cols, count, jnp.swapaxes(vals, 2, 3), both_grad, col_blocks)
+    keep, send = spread(where, cols, count, flipped, both_grad, col_blocks)
     input_grad = row_reduce_scatter(keep, send).astype(jnp.bfloat16)
     return (activated, weight_grad, input_grad)
 

time: 437 us -> 435 us (level)
    all_gather x1, waiting for transfers between devices: 127 us -> 121 us  [body(): gathered = lax.all_gather(features, 'row', axis=0, tiled=True)]
    ppermute x7, waiting for transfers between devices: 30.1 us -> 34.6 us  [all_sum(): lax.ppermute(value, axis, [(i, i ^ step) for i in range(size)])]
where the time goes in v12:
time: 435 us
  waiting for transfers between devices  310 us (71%)
  starting transfers between devices  38 us (9%)
  Pallas kernels  31 us (7%)
  other arithmetic  29.3 us (7%)
  between operations  14.2 us (3%)
  local copies, waits for them, and re-layouts  10.7 us (2%)
    ppermute x15, waiting for transfers between devices, shifted(): return lax.ppermute(value, 'row', [(r, dest(r)) for r in range(64)])  141 us
    all_gather x1, waiting for transfers between devices, body(): gathered = lax.all_gather(features, 'row', axis=0, tiled=True)  121 us
    ppermute x7, waiting for transfers between devices, all_sum(): lax.ppermute(value, axis, [(i, i ^ step) for i in range(size)])  34.6 us
    ppermute x15, starting transfers between devices, shifted(): return lax.ppermute(value, 'row', [(r, dest(r)) for r in range(64)])  21.7 us
    pallas_call x1, Pallas kernels, spread(): pl.pallas_call(spread_kernel, out_shape=[jax.ShapeDtypeStruct((col_blocks...  19.9 us
    add x1, other arithmetic, row_reduce_scatter(): first = [keep[0, s] + came[0, s] for s in range(4)]  15.9 us
    ppermute x2, waiting for transfers between devices, swap(): return lax.ppermute(value, axis, [(i, i ^ 1) for i in range(size)])  12.9 us
    pallas_call x1, Pallas kernels, aggregate(): pl.pallas_call(aggregate_kernel, out_shape=jax.ShapeDtypeStruct((row_bloc...  11.1 us
  transfers between devices with their start and end apart: 25, of which 19 were waited for; matrix products, arithmetic and copies ran while one was open for 2% of the time, Pallas kernels for 0%

profile of v12, /device:TPU:0, one launch (start us, length us, event | category | flops | bytes accessed | tf_op | source)
XLA Modules:
  0.0 434.7 jit_solution(15574290585058906715)
XLA Ops:
  7.9 6.5 %copy.9 = bf16[1,8,16,128,128]{3,4,2,1,0:T(8,128)(2,1)} copy(bf16[1,8,16,128,128]{4,3,2,1,0:T(8,128)(2,1)} %param.8) | data formatting | bytes 8388608 | tf_op args[2]
  14.4 120.9 %all-gather.2.cloned.1.call-done.panel_hbm = bf16[32768,256]{1,0:T(8,128)(2,1)} async-done(((bf16[512,256]{1,0:T(8,128)(2,1)}), bf16[32768,256]{1,0:T(8,128)(2,1)}) %all-gather.2.cloned.1.call-update) | async-done | bytes 16777232 | tf_op jit(solution)/shard_map/all_gather | solution.py:186
  135.3 11.1 %shard_map.85 = f32[8,128,256]{2,1,0:T(8,128)} custom-call(s32[8,16]{1,0:T(8,128)} %bitcast.51, s32[8]{0:T(128)} %bitcast.53, bf16[8,16,128,128]{3,2,1,0:T(8,128)(2,1)} %bitcast.45, bf16[32768,256]{1,0:T(8,128)(2,1)} %all-gather.2.cloned.1.call-done.panel_hbm), custom_call_target="tpu_custom_call" | custom-call | flops 1073741824 | bytes 22020096 | tf_op jit(solution)/shard_map/pallas_call | solution.py:90
  146.4 1.1 constant_dynamic-slice_fusion
  147.5 2.8 collective-permute-start
  150.3 12.9 %collective-permute-done = f32[512,256]{1,0:T(8,128)S(1)} collective-permute-done((f32[512,256]{1,0:T(8,128)S(1)}, f32[512,256]{1,0:T(8,128)S(1)}, u32[]{:S(2)}, u32[]{:S(2)}) %collective-permute-start) | collective-permute-done | bytes 524320 | tf_op jit(solution)/shard_map/ppermute | solution.py:144
  163.1 1.1 add_convert_fusion
  164.3 1.1 multiply_convert_fusion
  165.6 2.8 collective-permute-start.1
  168.4 6.5 %collective-permute-done.1 = f32[256,256]{1,0:T(8,128)S(1)} collective-permute-done((f32[256,256]{1,0:T(8,128)S(1)}, f32[256,256]{1,0:T(8,128)S(1)}, u32[]{:S(2)}, u32[]{:S(2)}) %collective-permute-start.1) | collective-permute-done | bytes 262176 | tf_op jit(solution)/shard_map/ppermute | solution.py:174
  175.0 1.5 collective-permute-done.2
  176.5 1.5 collective-permute-start.3
  178.0 7.0 %collective-permute-done.3 = f32[256,256]{1,0:T(8,128)S(1)} collective-permute-done((f32[256,256]{1,0:T(8,128)S(1)}, f32[256,256]{1,0:T(8,128)S(1)}, u32[]{:S(2)}, u32[]{:S(2)}) %collective-permute-start.3) | collective-permute-done | bytes 262176 | tf_op jit(solution)/shard_map/ppermute | solution.py:174
  185.0 2.2 collective-permute-start.4
  187.2 6.9 %collective-permute-done.4 = f32[256,256]{1,0:T(8,128)S(1)} collective-permute-done((f32[256,256]{1,0:T(8,128)S(1)}, f32[256,256]{1,0:T(8,128)S(1)}, u32[]{:S(2)}, u32[]{:S(2)}) %collective-permute-start.4) | collective-permute-done | bytes 262176 | tf_op jit(solution)/shard_map/ppermute | solution.py:174
  194.1 1.0 collective-permute-start.5
  195.1 5.7 %collective-permute-done.5 = f32[256,256]{1,0:T(8,128)S(1)} collective-permute-done((f32[256,256]{1,0:T(8,128)S(1)}, f32[256,256]{1,0:T(8,128)S(1)}, u32[]{:S(2)}, u32[]{:S(2)}) %collective-permute-start.5) | collective-permute-done | bytes 262176 | tf_op jit(solution)/shard_map/ppermute | solution.py:174
  202.1 3.2 collective-permute-start.8
  205.3 2.5 collective-permute-done.6
  207.8 1.9 collective-permute-start.7
  211.3 4.5 %collective-permute-done.7 = f32[256,256]{1,0:T(8,128)S(1)} collective-permute-done((f32[256,256]{1,0:T(8,128)S(1)}, f32[256,256]{1,0:T(8,128)S(1)}, u32[]{:S(2)}, u32[]{:S(2)}) %collective-permute-start.7) | collective-permute-done | bytes 262176 | tf_op jit(solution)/shard_map/ppermute | solution.py:174
  215.8 19.9 %shard_map.86 = (f32[128,128,256]{2,1,0:T(8,128)}, f32[128,128,256]{2,1,0:T(8,128)}) custom-call(s32[2]{0:T(128)} %pad_add_fusion.side_ref, s32[8,16]{1,0:T(8,128)} %bitcast.52, s32[8]{0:T(128)} %bitcast.54, bf16[8,16,128,128]{3,2,1,0:T(8,128)(2,1)} %bitcast.40, bf16[2,4,128,256]{3,2,1,0:T(8,128)(2,1)} %pad_maximum_fusion.grad_ref), custom_call_target="tpu_custom_call" | custom-call | flops 1073741824 | bytes 38273024 | tf_op jit(solution)/shard_map/pallas_call | solution.py:117
  236.0 25.4 %collective-permute-done.9 = f32[128,128,256]{2,1,0:T(8,128)S(1)} collective-permute-done((f32[128,128,256]{2,1,0:T(8,128)}, f32[128,128,256]{2,1,0:T(8,128)S(1)}, u32[]{:S(2)}, u32[]{:S(2)}) %collective-permute-start.9) | collective-permute-done | bytes 16777248 | tf_op jit(solution)/shard_map/ppermute | solution.py:152
  261.4 15.9 %fusion.6 = (f32[16,128,256]{2,1,0:T(8,128)}, f32[16,128,256]{2,1,0:T(8,128)}, f32[16,128,256]{2,1,0:T(8,128)}, f32[16,128,256]{2,1,0:T(8,128)}, f32[16,128,256]{2,1,0:T(8,128)}, /*index=5*/f32[16,128,256]{2,1,0:T(8,128)}) fusion(f32[2,4,16,128,256]{4,3,2,1,0:T(8,128)S(1)} %bitcast.43, f32[2,4,16,128,256]{4,3,2,1,0:T(8,128)} %bitcast.41), kind=kLoop, calls=%fused_computation.12 | loop fusion | flops 3145728 | bytes 37748736 | tf_op jit(solution)/shard_map/add | solution.py:159
  277.3 2.3 collective-permute-start.11
  279.6 1.1 collective-permute-start.19
  280.7 1.3 collective-permute-start.18
  282.8 1.2 collective-permute-start.12
  284.0 42.8 %collective-permute-done.11 = f32[16,128,256]{2,1,0:T(8,128)S(1)} collective-permute-done((f32[16,128,256]{2,1,0:T(8,128)}, f32[16,128,256]{2,1,0:T(8,128)S(1)}, u32[]{:S(2)}, u32[]{:S(2)}) %collective-permute-start.11) | collective-permute-done | bytes 2097184 | tf_op jit(solution)/shard_map/ppermute | solution.py:152
  326.8 2.5 collective-permute-start.10
  329.3 1.8 collective-permute-done.18
  331.0 43.4 %collective-permute-done.17 = f32[16,128,256]{2,1,0:T(8,128)S(1)} collective-permute-done((f32[16,128,256]{2,1,0:T(8,128)}, f32[16,128,256]{2,1,0:T(8,128)S(1)}, u32[]{:S(2)}, u32[]{:S(2)}) %collective-permute-start.17) | collective-permute-done | bytes 2097184 | tf_op jit(solution)/shard_map/ppermute | solution.py:152
  374.5 1.3 copy-done.5
  375.8 1.4 copy-done.6
  377.2 8.7 %fusion.9 = (f32[16,128,256]{2,1,0:T(8,128)S(1)}, f32[16,128,256]{2,1,0:T(8,128)S(1)}) fusion(f32[2,4,16,128,256]{4,3,2,1,0:T(8,128)} %bitcast.44, f32[2,4,16,128,256]{4,3,2,1,0:T(8,128)} %bitcast.42, f32[16,128,256]{2,1,0:T(8,128)} %copy-done.6, f32[16,128,256]{2,1,0:T(8,128)} %collective-permute-done.10, f32[16,128,256]{2,1,0:T(8,128)S(1)} %collective-permute-done.11, ...), kind=kLoop, calls=%fused_computation.17 | loop fusion | flops 4194304 | bytes 25165824 | tf_op jit(solution)/shard_map/add | solution.py:161
  386.1 1.3 collective-permute-start.14
  387.4 1.2 collective-permute-start.15
  389.6 1.5 collective-permute-start.21
  391.2 2.1 collective-permute-start.22
  393.2 9.3 %collective-permute-done.14 = f32[4,128,256]{2,1,0:T(8,128)S(1)} collective-permute-done((f32[4,128,256]{2,1,0:T(8,128)S(1)}, f32[4,128,256]{2,1,0:T(8,128)S(1)}, u32[]{:S(2)}, u32[]{:S(2)}) %collective-permute-start.14) | collective-permute-done | bytes 524320 | tf_op jit(solution)/shard_map/ppermute | solution.py:152
  402.5 1.6 collective-permute-start.20
  404.1 6.0 %collective-permute-done.15 = f32[4,128,256]{2,1,0:T(8,128)S(1)} collective-permute-done((f32[4,128,256]{2,1,0:T(8,128)S(1)}, f32[4,128,256]{2,1,0:T(8,128)S(1)}, u32[]{:S(2)}, u32[]{:S(2)}) %collective-permute-start.15) | collective-permute-done | bytes 524320 | tf_op jit(solution)/shard_map/ppermute | solution.py:152
  410.1 2.8 collective-permute-done.13
  413.1 1.9 collective-permute-start.16
  415.0 1.0 collective-permute-done.20
  416.2 1.8 collective-permute-start.23
  418.7 3.6 collective-permute-done.16
  422.3 4.8 %collective-permute-done.23 = f32[2,128,256]{2,1,0:T(8,128)S(1)} collective-permute-done((f32[2,128,256]{2,1,0:T(8,128)S(1)}, f32[2,128,256]{2,1,0:T(8,128)S(1)}, u32[]{:S(2)}, u32[]{:S(2)}) %collective-permute-start.23) | collective-permute-done | bytes 262176 | tf_op jit(solution)/shard_map/ppermute | solution.py:152
  (48 shorter events, 8.3 us)
Async XLA Ops:
  7.2 157.1 %copy-start = (bf16[256,256]{1,0:T(8,128)(2,1)S(1)}, bf16[256,256]{1,0:T(8,128)(2,1)}, u32[]{:S(2)}) copy-start(bf16[256,256]{1,0:T(8,128)(2,1)} %param.7) | copy-start | bytes 393220
  7.2 128.1 %all-gather.2.cloned.1.call-start = ((), (), s32[]{:S(2)}) async-start(), calls=%async_computation | async-start | bytes 17039360 | tf_op jit(solution)/shard_map/all_gather | solution.py:186
  146.4 17.9 %copy-start.7 = (bf16[512,256]{1,0:T(8,128)(2,1)S(1)}, bf16[512,256]{1,0:T(8,128)(2,1)}, u32[]{:S(2)}) copy-start(bf16[512,256]{1,0:T(8,128)(2,1)} %param.11) | copy-start | bytes 786436
  147.5 15.7 %collective-permute-start = (f32[512,256]{1,0:T(8,128)S(1)}, f32[512,256]{1,0:T(8,128)S(1)}, u32[]{:S(2)}, u32[]{:S(2)}) collective-permute-start(f32[512,256]{1,0:T(8,128)S(1)} %constant_dynamic-slice_fusion), channel_id=1, source_target_pairs={{0,64},{64,0},{1,65},{65,1},{2,66},{66,2},{3,67},{67,3},{4,68},{68... | collective-permute-start | bytes 1572872 | tf_op jit(solution)/shard_map/ppermute | solution.py:144
  165.6 9.2 %collective-permute-start.1 = (f32[256,256]{1,0:T(8,128)S(1)}, f32[256,256]{1,0:T(8,128)S(1)}, u32[]{:S(2)}, u32[]{:S(2)}) collective-permute-start(f32[256,256]{1,0:T(8,128)S(1)} %fusion.14), channel_id=1, source_target_pairs={{0,64},{64,0},{1,65},{65,1},{2,66},{66,2},{3,67},{67,3},{4,68},{68... | collective-permute-start | bytes 786440 | tf_op jit(solution)/shard_map/ppermute | solution.py:174
  174.9 1.6 collective-permute-start.2
  176.5 8.4 %collective-permute-start.3 = (f32[256,256]{1,0:T(8,128)S(1)}, f32[256,256]{1,0:T(8,128)S(1)}, u32[]{:S(2)}, u32[]{:S(2)}) collective-permute-start(f32[256,256]{1,0:T(8,128)S(1)} %add.134), channel_id=1, source_target_pairs={{0,2},{1,3},{2,0},{3,1},{4,6},{5,7},{6,4},{7,5},{8,10},{9,11},{10,... | collective-permute-start | bytes 786440 | tf_op jit(solution)/shard_map/ppermute | solution.py:174
  185.0 9.1 %collective-permute-start.4 = (f32[256,256]{1,0:T(8,128)S(1)}, f32[256,256]{1,0:T(8,128)S(1)}, u32[]{:S(2)}, u32[]{:S(2)}) collective-permute-start(f32[256,256]{1,0:T(8,128)S(1)} %add.135), channel_id=1, source_target_pairs={{0,4},{1,5},{2,6},{3,7},{4,0},{5,1},{6,2},{7,3},{8,12},{9,13},{10,... | collective-permute-start | bytes 786440 | tf_op jit(solution)/shard_map/ppermute | solution.py:174
  194.1 6.7 %collective-permute-start.5 = (f32[256,256]{1,0:T(8,128)S(1)}, f32[256,256]{1,0:T(8,128)S(1)}, u32[]{:S(2)}, u32[]{:S(2)}) collective-permute-start(f32[256,256]{1,0:T(8,128)S(1)} %add.136), channel_id=1, source_target_pairs={{0,8},{1,9},{2,10},{3,11},{4,12},{5,13},{6,14},{7,15},{8,0},{9,1},... | collective-permute-start | bytes 786440 | tf_op jit(solution)/shard_map/ppermute | solution.py:174
  200.9 6.9 %collective-permute-start.6 = (f32[256,256]{1,0:T(8,128)S(1)}, f32[256,256]{1,0:T(8,128)S(1)}, u32[]{:S(2)}, u32[]{:S(2)}) collective-permute-start(f32[256,256]{1,0:T(8,128)S(1)} %add.137), channel_id=1, source_target_pairs={{0,16},{1,17},{2,18},{3,19},{4,20},{5,21},{6,22},{7,23},{8,24},{9,... | collective-permute-start | bytes 786440 | tf_op jit(solution)/shard_map/ppermute | solution.py:174
  202.1 8.3 %collective-permute-start.8 = (bf16[512,256]{1,0:T(8,128)(2,1)S(1)}, bf16[512,256]{1,0:T(8,128)(2,1)S(1)}, u32[]{:S(2)}, u32[]{:S(2)}) collective-permute-start(bf16[512,256]{1,0:T(8,128)(2,1)S(1)} %convolution_convert_fusion), channel_id=1, source_target_pairs={{0,64},{64,0},{1,65},{65,1},{2,66},{66,2},{3,67},{67,3},{4,68},{68... | collective-permute-start | bytes 786440 | tf_op jit(solution)/shard_map/ppermute | solution.py:144
  207.8 8.0 %collective-permute-start.7 = (f32[256,256]{1,0:T(8,128)S(1)}, f32[256,256]{1,0:T(8,128)S(1)}, u32[]{:S(2)}, u32[]{:S(2)}) collective-permute-start(f32[256,256]{1,0:T(8,128)S(1)} %add.138), channel_id=1, source_target_pairs={{0,32},{1,33},{2,34},{3,35},{4,36},{5,37},{6,38},{7,39},{8,40},{9,... | collective-permute-start | bytes 786440 | tf_op jit(solution)/shard_map/ppermute | solution.py:174
  235.8 25.6 %collective-permute-start.9 = (f32[128,128,256]{2,1,0:T(8,128)}, f32[128,128,256]{2,1,0:T(8,128)S(1)}, u32[]{:S(2)}, u32[]{:S(2)}) collective-permute-start(f32[128,128,256]{2,1,0:T(8,128)} %get-tuple-element.14), channel_id=1, source_target_pairs={{0,1},{1,0},{2,3},{3,2},{4,5},{5,4},{6,7},{7,6},{8,9},{9,8},{10,11... | collective-permute-start | bytes 50331656 | tf_op jit(solution)/shard_map/ppermute | solution.py:152
  261.4 15.9 %copy-start.2 = (f32[128,128,256]{2,1,0:T(8,128)}, f32[128,128,256]{2,1,0:T(8,128)S(1)}, u32[]{:S(2)}) copy-start(f32[128,128,256]{2,1,0:T(8,128)S(1)} %collective-permute-done.9) | copy-start | bytes 50331652
  277.3 49.5 %collective-permute-start.11 = (f32[16,128,256]{2,1,0:T(8,128)}, f32[16,128,256]{2,1,0:T(8,128)S(1)}, u32[]{:S(2)}, u32[]{:S(2)}) collective-permute-start(f32[16,128,256]{2,1,0:T(8,128)} %get-tuple-element.17), channel_id=1, source_target_pairs={{0,4},{1,5},{2,6},{3,7},{4,0},{5,1},{6,2},{7,3},{8,12},{9,13},{10,... | collective-permute-start | bytes 6291464 | tf_op jit(solution)/shard_map/ppermute | solution.py:152
  279.6 49.7 %collective-permute-start.19 = (f32[16,128,256]{2,1,0:T(8,128)}, f32[16,128,256]{2,1,0:T(8,128)S(1)}, u32[]{:S(2)}, u32[]{:S(2)}) collective-permute-start(f32[16,128,256]{2,1,0:T(8,128)} %get-tuple-element.18), channel_id=1, source_target_pairs={{0,48},{1,49},{2,50},{3,51},{4,52},{5,53},{6,54},{7,55},{8,56},{9,... | collective-permute-start | bytes 6291464 | tf_op jit(solution)/shard_map/ppermute | solution.py:152
  280.7 50.3 %collective-permute-start.18 = (f32[16,128,256]{2,1,0:T(8,128)}, f32[16,128,256]{2,1,0:T(8,128)S(1)}, u32[]{:S(2)}, u32[]{:S(2)}) collective-permute-start(f32[16,128,256]{2,1,0:T(8,128)} %get-tuple-element.19), channel_id=1, source_target_pairs={{0,32},{1,33},{2,34},{3,35},{4,36},{5,37},{6,38},{7,39},{8,40},{9,... | collective-permute-start | bytes 6291464 | tf_op jit(solution)/shard_map/ppermute | solution.py:152
  282.0 92.5 %collective-permute-start.17 = (f32[16,128,256]{2,1,0:T(8,128)}, f32[16,128,256]{2,1,0:T(8,128)S(1)}, u32[]{:S(2)}, u32[]{:S(2)}) collective-permute-start(f32[16,128,256]{2,1,0:T(8,128)} %get-tuple-element.20), channel_id=1, source_target_pairs={{0,16},{1,17},{2,18},{3,19},{4,20},{5,21},{6,22},{7,23},{8,24},{9,... | collective-permute-start | bytes 6291464 | tf_op jit(solution)/shard_map/ppermute | solution.py:152
  282.8 91.7 %collective-permute-start.12 = (f32[16,128,256]{2,1,0:T(8,128)}, f32[16,128,256]{2,1,0:T(8,128)S(1)}, u32[]{:S(2)}, u32[]{:S(2)}) collective-permute-start(f32[16,128,256]{2,1,0:T(8,128)} %get-tuple-element.21), channel_id=1, source_target_pairs={{0,6},{1,7},{2,0},{3,1},{4,2},{5,3},{6,4},{7,5},{8,14},{9,15},{10,... | collective-permute-start | bytes 6291464 | tf_op jit(solution)/shard_map/ppermute | solution.py:152
  326.8 50.5 %collective-permute-start.10 = (f32[16,128,256]{2,1,0:T(8,128)}, f32[16,128,256]{2,1,0:T(8,128)}, u32[]{:S(2)}, u32[]{:S(2)}) collective-permute-start(f32[16,128,256]{2,1,0:T(8,128)} %get-tuple-element.22), channel_id=1, source_target_pairs={{0,2},{1,3},{2,4},{3,5},{4,6},{5,7},{6,0},{7,1},{8,10},{9,11},{10,... | collective-permute-start | bytes 6291464 | tf_op jit(solution)/shard_map/ppermute | solution.py:152
  329.3 45.2 %copy-start.3 = (f32[16,128,256]{2,1,0:T(8,128)}, f32[16,128,256]{2,1,0:T(8,128)S(1)}, u32[]{:S(2)}) copy-start(f32[16,128,256]{2,1,0:T(8,128)S(1)} %collective-permute-done.19) | copy-start | bytes 6291460
  331.0 43.5 %copy-start.4 = (f32[16,128,256]{2,1,0:T(8,128)}, f32[16,128,256]{2,1,0:T(8,128)S(1)}, u32[]{:S(2)}) copy-start(f32[16,128,256]{2,1,0:T(8,128)S(1)} %collective-permute-done.18) | copy-start | bytes 6291460
  374.5 1.4 copy-start.5
  375.8 1.4 copy-start.6
  386.1 16.4 %collective-permute-start.14 = (f32[4,128,256]{2,1,0:T(8,128)S(1)}, f32[4,128,256]{2,1,0:T(8,128)S(1)}, u32[]{:S(2)}, u32[]{:S(2)}) collective-permute-start(f32[4,128,256]{2,1,0:T(8,128)S(1)} %get-tuple-element.23), channel_id=1, source_target_pairs={{0,32},{1,33},{2,34},{3,35},{4,36},{5,37},{6,38},{7,39},{8,40},{9,... | collective-permute-start | bytes 1572872 | tf_op jit(solution)/shard_map/ppermute | solution.py:152
  387.4 22.6 %collective-permute-start.15 = (f32[4,128,256]{2,1,0:T(8,128)S(1)}, f32[4,128,256]{2,1,0:T(8,128)S(1)}, u32[]{:S(2)}, u32[]{:S(2)}) collective-permute-start(f32[4,128,256]{2,1,0:T(8,128)S(1)} %get-tuple-element.24), channel_id=1, source_target_pairs={{0,48},{1,49},{2,50},{3,51},{4,52},{5,53},{6,54},{7,55},{8,56},{9,... | collective-permute-start | bytes 1572872 | tf_op jit(solution)/shard_map/ppermute | solution.py:152
  388.6 24.2 %collective-permute-start.13 = (f32[4,128,256]{2,1,0:T(8,128)S(1)}, f32[4,128,256]{2,1,0:T(8,128)S(1)}, u32[]{:S(2)}, u32[]{:S(2)}) collective-permute-start(f32[4,128,256]{2,1,0:T(8,128)S(1)} %get-tuple-element.25), channel_id=1, source_target_pairs={{0,16},{1,17},{2,18},{3,19},{4,20},{5,21},{6,22},{7,23},{8,24},{9,... | collective-permute-start | bytes 1572872 | tf_op jit(solution)/shard_map/ppermute | solution.py:152
  389.6 25.4 %collective-permute-start.21 = (f32[4,128,256]{2,1,0:T(8,128)S(1)}, f32[4,128,256]{2,1,0:T(8,128)S(1)}, u32[]{:S(2)}, u32[]{:S(2)}) collective-permute-start(f32[4,128,256]{2,1,0:T(8,128)S(1)} %get-tuple-element.26), channel_id=1, source_target_pairs={{0,4},{1,5},{2,6},{3,7},{4,0},{5,1},{6,2},{7,3},{8,12},{9,13},{10,... | collective-permute-start | bytes 1572872 | tf_op jit(solution)/shard_map/ppermute | solution.py:152
  391.2 23.9 %collective-permute-start.22 = (f32[4,128,256]{2,1,0:T(8,128)S(1)}, f32[4,128,256]{2,1,0:T(8,128)S(1)}, u32[]{:S(2)}, u32[]{:S(2)}) collective-permute-start(f32[4,128,256]{2,1,0:T(8,128)S(1)} %get-tuple-element.27), channel_id=1, source_target_pairs={{0,6},{1,7},{2,0},{3,1},{4,2},{5,3},{6,4},{7,5},{8,14},{9,15},{10,... | collective-permute-start | bytes 1572872 | tf_op jit(solution)/shard_map/ppermute | solution.py:152
  402.5 13.5 %collective-permute-start.20 = (f32[4,128,256]{2,1,0:T(8,128)S(1)}, f32[4,128,256]{2,1,0:T(8,128)S(1)}, u32[]{:S(2)}, u32[]{:S(2)}) collective-permute-start(f32[4,128,256]{2,1,0:T(8,128)S(1)} %get-tuple-element.28), channel_id=1, source_target_pairs={{0,2},{1,3},{2,4},{3,5},{4,6},{5,7},{6,0},{7,1},{8,10},{9,11},{10,... | collective-permute-start | bytes 1572872 | tf_op jit(solution)/shard_map/ppermute | solution.py:152
  413.1 9.2 %collective-permute-start.16 = (f32[2,128,256]{2,1,0:T(8,128)S(1)}, f32[2,128,256]{2,1,0:T(8,128)S(1)}, u32[]{:S(2)}, u32[]{:S(2)}) collective-permute-start(f32[2,128,256]{2,1,0:T(8,128)S(1)} %slice.137), channel_id=1, source_target_pairs={{0,8},{1,9},{2,10},{3,11},{4,12},{5,13},{6,14},{7,15},{8,0},{9,1},... | collective-permute-start | bytes 786440 | tf_op jit(solution)/shard_map/ppermute | solution.py:152
  416.0 11.9 %copy-start.1 = (bf16[256,256]{1,0:T(8,128)(2,1)S(1)}, bf16[256,256]{1,0:T(8,128)(2,1)}, u32[]{:S(2)}) copy-start(bf16[256,256]{1,0:T(8,128)(2,1)} %param.7) | copy-start | bytes 393220
  416.2 10.9 %collective-permute-start.23 = (f32[2,128,256]{2,1,0:T(8,128)S(1)}, f32[2,128,256]{2,1,0:T(8,128)S(1)}, u32[]{:S(2)}, u32[]{:S(2)}) collective-permute-start(f32[2,128,256]{2,1,0:T(8,128)S(1)} %slice.151), channel_id=1, source_target_pairs={{0,8},{1,9},{2,10},{3,11},{4,12},{5,13},{6,14},{7,15},{8,0},{9,1},... | collective-permute-start | bytes 786440 | tf_op jit(solution)/shard_map/ppermute | solution.py:152
Sparse Core Ops, SparseCore 0:
  9.7 125.4 all-gather.1

commit v13 on v12

--- a/solution.py
+++ b/solution.py
@@ -49,7 +49,7 @@
     return (dk * 2 + half) * 64 + ((first * 4 + second) * 2 + dy) * 2 + q2
 
 
-def spread_kernel(side_ref, cols_ref, count_ref, vals_hbm, grad_ref, keep_hbm, send_hbm, vals, total, sems):
+def spread_kernel(side_ref, cols_ref, count_ref, vals_hbm, grad_ref, keep_hbm, send_hbm, later_hbm, vals, total, sems):
     row_blocks, slot_total, block, _ = vals.shape
     per_panel = grad_ref.shape[1]
     col_blocks = total.shape[0]
@@ -76,11 +76,15 @@
             slot = owner_slot(col, me, per_dev)
             total[slot] += contrib
     half = col_blocks // 2
+    quarter = half // 2
     keep = pltpu.make_async_copy(total.at[pl.ds(0, half)], keep_hbm, sems.at[1])
-    send = pltpu.make_async_copy(total.at[pl.ds(half, half)], send_hbm, sems.at[2])
+    send = pltpu.make_async_copy(total.at[pl.ds(half, quarter)], send_hbm, sems.at[2])
+    later = pltpu.make_async_copy(total.at[pl.ds(half + quarter, quarter)], later_hbm, sems.at[3])
     send.start()
+    later.start()
     keep.start()
     send.wait()
+    later.wait()
     keep.wait()
 
 
@@ -116,7 +120,11 @@
     width = grad.shape[-1]
     return pl.pallas_call(
         spread_kernel,
-        out_shape=[jax.ShapeDtypeStruct((col_blocks // 2, block, width), jnp.float32)] * 2,
+        out_shape=[
+            jax.ShapeDtypeStruct((col_blocks // 2, block, width), jnp.float32),
+            jax.ShapeDtypeStruct((col_blocks // 4, block, width), jnp.float32),
+            jax.ShapeDtypeStruct((col_blocks // 4, block, width), jnp.float32),
+        ],
         in_specs=[
             pl.BlockSpec(memory_space=pltpu.SMEM),
             pl.BlockSpec(memory_space=pltpu.SMEM),
@@ -124,11 +132,11 @@
             pl.BlockSpec(memory_space=pl.ANY),
             pl.BlockSpec(memory_space=pltpu.VMEM),
         ],
-        out_specs=[pl.BlockSpec(memory_space=pl.ANY)] * 2,
+        out_specs=[pl.BlockSpec(memory_space=pl.ANY)] * 3,
         scratch_shapes=[
             pltpu.VMEM(vals.shape, vals.dtype),
             pltpu.VMEM((col_blocks, block, width), jnp.float32),
-            pltpu.SemaphoreType.DMA((3,)),
+            pltpu.SemaphoreType.DMA((4,)),
         ],
         compiler_params=pltpu.CompilerParams(vmem_limit_bytes=VMEM_LIMIT),
         cost_estimate=pl.CostEstimate(
@@ -152,12 +160,13 @@
     return lax.ppermute(value, "row", [(r, dest(r)) for r in range(64)])
 
 
-def row_reduce_scatter(keep, send):
+def row_reduce_scatter(keep, send, later):
     _, block, width = keep.shape
     keep = keep.reshape(2, 4, 16, block, width)
-    came = shifted(send, 1, 2, 1).reshape(2, 4, 16, block, width)
-    first = [keep[0, s] + came[0, s] for s in range(4)]
-    second = [keep[1, s] + came[1, s] for s in range(4)]
+    came = shifted(send, 1, 2, 1).reshape(4, 16, block, width)
+    first = [keep[0, s] + came[s] for s in range(4)]
+    came = shifted(later, 1, 2, 1).reshape(4, 16, block, width)
+    second = [keep[1, s] + came[s] for s in range(4)]
     first = (first[0] + sum(shifted(first[s], 2, 4, s) for s in range(1, 4))).reshape(4, 4, block, width)
     second = (second[0] + sum(shifted(second[s], 16, 4, s) for s in range(1, 4))).reshape(4, 4, block, width)
     first = (first[0] + sum(shifted(first[s], 16, 4, s) for s in range(1, 4))).reshape(2, 2, block, width)
@@ -206,8 +215,8 @@
     weight_grad = weight_grad * (1.0 / math.sqrt(verts))
 
     where = jnp.stack([side, lax.axis_index("row")]).astype(jnp.int32)
-    keep, send = spread(where, cols, count, flipped, both_grad, col_blocks)
-    input_grad = row_reduce_scatter(keep, send).astype(jnp.bfloat16)
+    keep, send, later = spread(where, cols, count, flipped, both_grad, col_blocks)
+    input_grad = row_reduce_scatter(keep, send, later).astype(jnp.bfloat16)
     return (activated, weight_grad, input_grad)
 
 

time: 435 us -> 516 us (1.19)
  waiting for transfers between devices: 310 us -> 402 us
  starting transfers between devices: 38 us -> 30.7 us
  other arithmetic: 29.3 us -> 22.4 us
    ppermute x15 -> x16, waiting for transfers between devices: 141 us -> 233 us  [shifted(): return lax.ppermute(value, 'row', [(r, dest(r)) for r in range(64)])]
    ppermute x15 -> x16, starting transfers between devices: 21.7 us -> 14.3 us  [shifted(): return lax.ppermute(value, 'row', [(r, dest(r)) for r in range(64)])]
    add x2 -> x3, other arithmetic: 24.6 us -> 17.7 us  [the longest x1 8.24 us: row_reduce_scatter(): first = [keep[0, s] + came[s] for s in range(4)]]
    unnamed x17 -> x13, local copies, waits for them, and re-layouts: 9.21 us -> 11.1 us
  transfers between devices with their start and end apart: 25 -> 26, of which waited for: 19 -> 18; matrix products, arithmetic and copies ran while one was open for 2% -> 4% of each run, Pallas kernels for 0% -> 0%
where the time goes in v13:
time: 516 us; the launch traced here: 515 us
  waiting for transfers between devices  402 us (78%)
  Pallas kernels  31.1 us (6%)
  starting transfers between devices  30.7 us (6%)
  other arithmetic  22.4 us (4%)
  between operations  14.2 us (3%)
  local copies, waits for them, and re-layouts  13.6 us (3%)
    ppermute x16, waiting for transfers between devices, shifted(): return lax.ppermute(value, 'row', [(r, dest(r)) for r in range(64)])  233 us
    all_gather x1, waiting for transfers between devices, body(): gathered = lax.all_gather(features, 'row', axis=0, tiled=True)  121 us
    ppermute x7, waiting for transfers between devices, all_sum(): lax.ppermute(value, axis, [(i, i ^ step) for i in range(size)])  34.6 us
    pallas_call x1, Pallas kernels, spread(): pl.pallas_call(spread_kernel, out_shape=[jax.ShapeDtypeStruct((col_blocks...  19.9 us
    ppermute x16, starting transfers between devices, shifted(): return lax.ppermute(value, 'row', [(r, dest(r)) for r in range(64)])  14.3 us
    ppermute x2, waiting for transfers between devices, swap(): return lax.ppermute(value, axis, [(i, i ^ 1) for i in range(size)])  12.9 us
    pallas_call x1, Pallas kernels, aggregate(): pl.pallas_call(aggregate_kernel, out_shape=jax.ShapeDtypeStruct((row_bloc...  11.1 us
    unnamed x13, local copies, waits for them, and re-layouts  11.1 us
  transfers between devices with their start and end apart: 26, of which 18 were waited for; matrix products, arithmetic and copies ran while one was open for 4% of the time, Pallas kernels for 0%

profile of v13, /device:TPU:0, one launch (start us, length us, event | category | flops | bytes accessed | tf_op | source)
XLA Modules:
  0.0 515.5 jit_solution(8209357043709001433)
XLA Ops:
  7.9 6.5 %copy.9 = bf16[1,8,16,128,128]{3,4,2,1,0:T(8,128)(2,1)} copy(bf16[1,8,16,128,128]{4,3,2,1,0:T(8,128)(2,1)} %param.8) | data formatting | bytes 8388608 | tf_op args[2]
  14.4 120.9 %all-gather.2.cloned.1.call-done.panel_hbm = bf16[32768,256]{1,0:T(8,128)(2,1)} async-done(((bf16[512,256]{1,0:T(8,128)(2,1)}), bf16[32768,256]{1,0:T(8,128)(2,1)}) %all-gather.2.cloned.1.call-update) | async-done | bytes 16777232 | tf_op jit(solution)/shard_map/all_gather | solution.py:195
  135.3 11.1 %shard_map.85 = f32[8,128,256]{2,1,0:T(8,128)} custom-call(s32[8,16]{1,0:T(8,128)} %bitcast.61, s32[8]{0:T(128)} %bitcast.63, bf16[8,16,128,128]{3,2,1,0:T(8,128)(2,1)} %bitcast.52, bf16[32768,256]{1,0:T(8,128)(2,1)} %all-gather.2.cloned.1.call-done.panel_hbm), custom_call_target="tpu_custom_call" | custom-call | flops 1073741824 | bytes 22020096 | tf_op jit(solution)/shard_map/pallas_call | solution.py:94
  146.4 1.1 constant_dynamic-slice_fusion
  147.5 2.8 collective-permute-start
  150.3 12.9 %collective-permute-done = f32[512,256]{1,0:T(8,128)S(1)} collective-permute-done((f32[512,256]{1,0:T(8,128)S(1)}, f32[512,256]{1,0:T(8,128)S(1)}, u32[]{:S(2)}, u32[]{:S(2)}) %collective-permute-start) | collective-permute-done | bytes 524320 | tf_op jit(solution)/shard_map/ppermute | solution.py:152
  163.2 1.1 add_convert_fusion
  164.3 1.1 multiply_convert_fusion
  165.7 2.8 collective-permute-start.1
  168.4 6.5 %collective-permute-done.1 = f32[256,256]{1,0:T(8,128)S(1)} collective-permute-done((f32[256,256]{1,0:T(8,128)S(1)}, f32[256,256]{1,0:T(8,128)S(1)}, u32[]{:S(2)}, u32[]{:S(2)}) %collective-permute-start.1) | collective-permute-done | bytes 262176 | tf_op jit(solution)/shard_map/ppermute | solution.py:183
  175.0 1.5 collective-permute-done.2
  176.6 1.5 collective-permute-start.3
  178.1 7.0 %collective-permute-done.3 = f32[256,256]{1,0:T(8,128)S(1)} collective-permute-done((f32[256,256]{1,0:T(8,128)S(1)}, f32[256,256]{1,0:T(8,128)S(1)}, u32[]{:S(2)}, u32[]{:S(2)}) %collective-permute-start.3) | collective-permute-done | bytes 262176 | tf_op jit(solution)/shard_map/ppermute | solution.py:183
  185.0 2.2 collective-permute-start.4
  187.2 6.9 %collective-permute-done.4 = f32[256,256]{1,0:T(8,128)S(1)} collective-permute-done((f32[256,256]{1,0:T(8,128)S(1)}, f32[256,256]{1,0:T(8,128)S(1)}, u32[]{:S(2)}, u32[]{:S(2)}) %collective-permute-start.4) | collective-permute-done | bytes 262176 | tf_op jit(solution)/shard_map/ppermute | solution.py:183
  194.2 1.0 collective-permute-start.5
  195.2 5.7 %collective-permute-done.5 = f32[256,256]{1,0:T(8,128)S(1)} collective-permute-done((f32[256,256]{1,0:T(8,128)S(1)}, f32[256,256]{1,0:T(8,128)S(1)}, u32[]{:S(2)}, u32[]{:S(2)}) %collective-permute-start.5) | collective-permute-done | bytes 262176 | tf_op jit(solution)/shard_map/ppermute | solution.py:183
  200.9 1.0 collective-permute-start.6
  202.2 3.2 collective-permute-start.8
  205.3 2.5 collective-permute-done.6
  207.9 1.9 collective-permute-start.7
  210.4 0.8 pad_maximum_fusion.grad_ref
  211.3 4.6 collective-permute-done.7
  215.9 19.9 %shard_map.86 = (f32[128,128,256]{2,1,0:T(8,128)}, f32[64,128,256]{2,1,0:T(8,128)}, f32[64,128,256]{2,1,0:T(8,128)}) custom-call(s32[2]{0:T(128)} %pad_add_fusion.side_ref, s32[8,16]{1,0:T(8,128)} %bitcast.62, s32[8]{0:T(128)} %bitcast.64, bf16[8,16,128,128]{3,2,1,0:T(8,128)(2,1)} %bitcast.51, bf16[2,4,128,256]{3,2,1,0:T(8,128)(2,1)} %pad_maximum_fusion.grad_ref), custom_call_target="tpu_custom_call" | custom-call | flops 1073741824 | bytes 38273024 | tf_op jit(solution)/shard_map/pallas_call | solution.py:121
  236.4 22.1 %collective-permute-done.9 = f32[64,128,256]{2,1,0:T(8,128)S(1)} collective-permute-done((f32[64,128,256]{2,1,0:T(8,128)}, f32[64,128,256]{2,1,0:T(8,128)S(1)}, u32[]{:S(2)}, u32[]{:S(2)}) %collective-permute-start.9) | collective-permute-done | bytes 8388640 | tf_op jit(solution)/shard_map/ppermute | solution.py:160
  258.5 3.3 copy-done.3
  261.8 8.2 %slice_add_fusion.5 = (f32[16,128,256]{2,1,0:T(8,128)S(1)}, f32[16,128,256]{2,1,0:T(8,128)}, f32[16,128,256]{2,1,0:T(8,128)}) fusion(f32[64,128,256]{2,1,0:T(8,128)} %copy-done.3, f32[2,4,16,128,256]{4,3,2,1,0:T(8,128)} %bitcast.53), kind=kLoop, calls=%fused_computation.11 | loop fusion | flops 1572864 | bytes 18874368 | tf_op jit(solution)/shard_map/add | solution.py:167
  270.0 1.2 collective-permute-start.12
  271.2 0.9 collective-permute-start.10
  272.1 2.3 collective-permute-start.11
  274.3 44.4 %collective-permute-done.12 = f32[16,128,256]{2,1,0:T(8,128)S(1)} collective-permute-done((f32[16,128,256]{2,1,0:T(8,128)}, f32[16,128,256]{2,1,0:T(8,128)S(1)}, u32[]{:S(2)}, u32[]{:S(2)}) %collective-permute-start.12) | collective-permute-done | bytes 2097184 | tf_op jit(solution)/shard_map/ppermute | solution.py:160
  318.7 46.2 %collective-permute-done.10 = f32[16,128,256]{2,1,0:T(8,128)S(1)} collective-permute-done((f32[16,128,256]{2,1,0:T(8,128)}, f32[16,128,256]{2,1,0:T(8,128)S(1)}, u32[]{:S(2)}, u32[]{:S(2)}) %collective-permute-start.10) | collective-permute-done | bytes 2097184 | tf_op jit(solution)/shard_map/ppermute | solution.py:160
  364.9 1.4 copy-done.4
  366.3 6.7 %slice_add_fusion.1 = (f32[16,128,256]{2,1,0:T(8,128)S(1)}, f32[16,128,256]{2,1,0:T(8,128)}, f32[16,128,256]{2,1,0:T(8,128)S(1)}, f32[16,128,256]{2,1,0:T(8,128)S(1)}) fusion(f32[64,128,256]{2,1,0:T(8,128)} %collective-permute-done.17, f32[2,4,16,128,256]{4,3,2,1,0:T(8,128)S(1)} %bitcast.54, f32[16,128,256]{2,1,0:T(8,128)S(1)} %collective-permute-done.12, ...), kind=kLoop, calls=%fused_computation.2 | loop fusion | flops 3670016 | bytes 31457280 | tf_op jit(solution)/shard_map/add | solution.py:169
  373.1 3.1 collective-permute-start.20
  376.2 1.5 collective-permute-start.19
  377.7 1.2 fusion.4
  378.9 1.7 collective-permute-start.15
  380.6 0.9 collective-permute-start.13
  381.5 86.1 %collective-permute-done.20 = f32[16,128,256]{2,1,0:T(8,128)S(1)} collective-permute-done((f32[16,128,256]{2,1,0:T(8,128)}, f32[16,128,256]{2,1,0:T(8,128)S(1)}, u32[]{:S(2)}, u32[]{:S(2)}) %collective-permute-start.20) | collective-permute-done | bytes 2097184 | tf_op jit(solution)/shard_map/ppermute | solution.py:160
  467.5 3.4 collective-permute-done.18
  470.9 2.7 fusion
  474.1 1.7 collective-permute-start.21
  475.8 12.1 %collective-permute-done.15 = f32[4,128,256]{2,1,0:T(8,128)S(1)} collective-permute-done((f32[4,128,256]{2,1,0:T(8,128)}, f32[4,128,256]{2,1,0:T(8,128)S(1)}, u32[]{:S(2)}, u32[]{:S(2)}) %collective-permute-start.15) | collective-permute-done | bytes 524320 | tf_op jit(solution)/shard_map/ppermute | solution.py:160
  487.9 3.1 collective-permute-done.13
  491.4 9.8 %collective-permute-done.22 = f32[4,128,256]{2,1,0:T(8,128)S(1)} collective-permute-done((f32[4,128,256]{2,1,0:T(8,128)S(1)}, f32[4,128,256]{2,1,0:T(8,128)S(1)}, u32[]{:S(2)}, u32[]{:S(2)}) %collective-permute-start.22) | collective-permute-done | bytes 524320 | tf_op jit(solution)/shard_map/ppermute | solution.py:160
  502.3 5.6 %collective-permute-done.24 = f32[2,128,256]{2,1,0:T(8,128)S(1)} collective-permute-done((f32[2,128,256]{2,1,0:T(8,128)S(1)}, f32[2,128,256]{2,1,0:T(8,128)S(1)}, u32[]{:S(2)}, u32[]{:S(2)}) %collective-permute-start.24) | collective-permute-done | bytes 262176 | tf_op jit(solution)/shard_map/ppermute | solution.py:160
  507.9 0.7 pad_maximum_fusion.1
  (47 shorter events, 4.7 us)
Async XLA Ops:
  7.2 157.1 %copy-start = (bf16[256,256]{1,0:T(8,128)(2,1)S(1)}, bf16[256,256]{1,0:T(8,128)(2,1)}, u32[]{:S(2)}) copy-start(bf16[256,256]{1,0:T(8,128)(2,1)} %param.7) | copy-start | bytes 393220
  7.2 128.1 %all-gather.2.cloned.1.call-start = ((), (), s32[]{:S(2)}) async-start(), calls=%async_computation | async-start | bytes 17039360 | tf_op jit(solution)/shard_map/all_gather | solution.py:195
  146.4 17.9 %copy-start.5 = (bf16[512,256]{1,0:T(8,128)(2,1)S(1)}, bf16[512,256]{1,0:T(8,128)(2,1)}, u32[]{:S(2)}) copy-start(bf16[512,256]{1,0:T(8,128)(2,1)} %param.11) | copy-start | bytes 786436
  147.5 15.7 %collective-permute-start = (f32[512,256]{1,0:T(8,128)S(1)}, f32[512,256]{1,0:T(8,128)S(1)}, u32[]{:S(2)}, u32[]{:S(2)}) collective-permute-start(f32[512,256]{1,0:T(8,128)S(1)} %constant_dynamic-slice_fusion), channel_id=1, source_target_pairs={{0,64},{64,0},{1,65},{65,1},{2,66},{66,2},{3,67},{67,3},{4,68},{68... | collective-permute-start | bytes 1572872 | tf_op jit(solution)/shard_map/ppermute | solution.py:152
  165.7 9.2 %collective-permute-start.1 = (f32[256,256]{1,0:T(8,128)S(1)}, f32[256,256]{1,0:T(8,128)S(1)}, u32[]{:S(2)}, u32[]{:S(2)}) collective-permute-start(f32[256,256]{1,0:T(8,128)S(1)} %fusion.6), channel_id=1, source_target_pairs={{0,64},{64,0},{1,65},{65,1},{2,66},{66,2},{3,67},{67,3},{4,68},{68... | collective-permute-start | bytes 786440 | tf_op jit(solution)/shard_map/ppermute | solution.py:183
  174.9 1.6 collective-permute-start.2
  176.6 8.4 %collective-permute-start.3 = (f32[256,256]{1,0:T(8,128)S(1)}, f32[256,256]{1,0:T(8,128)S(1)}, u32[]{:S(2)}, u32[]{:S(2)}) collective-permute-start(f32[256,256]{1,0:T(8,128)S(1)} %add.110), channel_id=1, source_target_pairs={{0,2},{1,3},{2,0},{3,1},{4,6},{5,7},{6,4},{7,5},{8,10},{9,11},{10,... | collective-permute-start | bytes 786440 | tf_op jit(solution)/shard_map/ppermute | solution.py:183
  185.0 9.1 %collective-permute-start.4 = (f32[256,256]{1,0:T(8,128)S(1)}, f32[256,256]{1,0:T(8,128)S(1)}, u32[]{:S(2)}, u32[]{:S(2)}) collective-permute-start(f32[256,256]{1,0:T(8,128)S(1)} %add.111), channel_id=1, source_target_pairs={{0,4},{1,5},{2,6},{3,7},{4,0},{5,1},{6,2},{7,3},{8,12},{9,13},{10,... | collective-permute-start | bytes 786440 | tf_op jit(solution)/shard_map/ppermute | solution.py:183
  194.2 6.7 %collective-permute-start.5 = (f32[256,256]{1,0:T(8,128)S(1)}, f32[256,256]{1,0:T(8,128)S(1)}, u32[]{:S(2)}, u32[]{:S(2)}) collective-permute-start(f32[256,256]{1,0:T(8,128)S(1)} %add.112), channel_id=1, source_target_pairs={{0,8},{1,9},{2,10},{3,11},{4,12},{5,13},{6,14},{7,15},{8,0},{9,1},... | collective-permute-start | bytes 786440 | tf_op jit(solution)/shard_map/ppermute | solution.py:183
  200.9 6.9 %collective-permute-start.6 = (f32[256,256]{1,0:T(8,128)S(1)}, f32[256,256]{1,0:T(8,128)S(1)}, u32[]{:S(2)}, u32[]{:S(2)}) collective-permute-start(f32[256,256]{1,0:T(8,128)S(1)} %add.113), channel_id=1, source_target_pairs={{0,16},{1,17},{2,18},{3,19},{4,20},{5,21},{6,22},{7,23},{8,24},{9,... | collective-permute-start | bytes 786440 | tf_op jit(solution)/shard_map/ppermute | solution.py:183
  202.2 8.3 %collective-permute-start.8 = (bf16[512,256]{1,0:T(8,128)(2,1)S(1)}, bf16[512,256]{1,0:T(8,128)(2,1)S(1)}, u32[]{:S(2)}, u32[]{:S(2)}) collective-permute-start(bf16[512,256]{1,0:T(8,128)(2,1)S(1)} %convolution_convert_fusion), channel_id=1, source_target_pairs={{0,64},{64,0},{1,65},{65,1},{2,66},{66,2},{3,67},{67,3},{4,68},{68... | collective-permute-start | bytes 786440 | tf_op jit(solution)/shard_map/ppermute | solution.py:152
  207.9 8.0 %collective-permute-start.7 = (f32[256,256]{1,0:T(8,128)S(1)}, f32[256,256]{1,0:T(8,128)S(1)}, u32[]{:S(2)}, u32[]{:S(2)}) collective-permute-start(f32[256,256]{1,0:T(8,128)S(1)} %add.114), channel_id=1, source_target_pairs={{0,32},{1,33},{2,34},{3,35},{4,36},{5,37},{6,38},{7,39},{8,40},{9,... | collective-permute-start | bytes 786440 | tf_op jit(solution)/shard_map/ppermute | solution.py:183
  235.8 22.7 %collective-permute-start.9 = (f32[64,128,256]{2,1,0:T(8,128)}, f32[64,128,256]{2,1,0:T(8,128)S(1)}, u32[]{:S(2)}, u32[]{:S(2)}) collective-permute-start(f32[64,128,256]{2,1,0:T(8,128)} %get-tuple-element.15), channel_id=1, source_target_pairs={{0,1},{1,0},{2,3},{3,2},{4,5},{5,4},{6,7},{7,6},{8,9},{9,8},{10,11... | collective-permute-start | bytes 25165832 | tf_op jit(solution)/shard_map/ppermute | solution.py:160
  235.9 38.4 %collective-permute-start.17 = (f32[64,128,256]{2,1,0:T(8,128)}, f32[64,128,256]{2,1,0:T(8,128)}, u32[]{:S(2)}, u32[]{:S(2)}) collective-permute-start(f32[64,128,256]{2,1,0:T(8,128)} %get-tuple-element.16), channel_id=1, source_target_pairs={{0,1},{1,0},{2,3},{3,2},{4,5},{5,4},{6,7},{7,6},{8,9},{9,8},{10,11... | collective-permute-start | bytes 25165832 | tf_op jit(solution)/shard_map/ppermute | solution.py:160
  258.5 3.3 copy-start.3
  261.8 104.5 %copy-start.2 = (f32[128,128,256]{2,1,0:T(8,128)S(1)}, f32[128,128,256]{2,1,0:T(8,128)}, u32[]{:S(2)}) copy-start(f32[128,128,256]{2,1,0:T(8,128)} %get-tuple-element.14) | copy-start | bytes 50331652
  270.0 48.7 %collective-permute-start.12 = (f32[16,128,256]{2,1,0:T(8,128)}, f32[16,128,256]{2,1,0:T(8,128)S(1)}, u32[]{:S(2)}, u32[]{:S(2)}) collective-permute-start(f32[16,128,256]{2,1,0:T(8,128)} %get-tuple-element.18), channel_id=1, source_target_pairs={{0,6},{1,7},{2,0},{3,1},{4,2},{5,3},{6,4},{7,5},{8,14},{9,15},{10,... | collective-permute-start | bytes 6291464 | tf_op jit(solution)/shard_map/ppermute | solution.py:160
  271.2 93.8 %collective-permute-start.10 = (f32[16,128,256]{2,1,0:T(8,128)}, f32[16,128,256]{2,1,0:T(8,128)S(1)}, u32[]{:S(2)}, u32[]{:S(2)}) collective-permute-start(f32[16,128,256]{2,1,0:T(8,128)} %get-tuple-element.19), channel_id=1, source_target_pairs={{0,2},{1,3},{2,4},{3,5},{4,6},{5,7},{6,0},{7,1},{8,10},{9,11},{10,... | collective-permute-start | bytes 6291464 | tf_op jit(solution)/shard_map/ppermute | solution.py:160
  272.1 94.3 %collective-permute-start.11 = (f32[16,128,256]{2,1,0:T(8,128)S(1)}, f32[16,128,256]{2,1,0:T(8,128)}, u32[]{:S(2)}, u32[]{:S(2)}) collective-permute-start(f32[16,128,256]{2,1,0:T(8,128)S(1)} %get-tuple-element.17), channel_id=1, source_target_pairs={{0,4},{1,5},{2,6},{3,7},{4,0},{5,1},{6,2},{7,3},{8,12},{9,13},{10,... | collective-permute-start | bytes 6291464 | tf_op jit(solution)/shard_map/ppermute | solution.py:160
  364.9 1.4 copy-start.4
  373.1 94.5 %collective-permute-start.20 = (f32[16,128,256]{2,1,0:T(8,128)}, f32[16,128,256]{2,1,0:T(8,128)S(1)}, u32[]{:S(2)}, u32[]{:S(2)}) collective-permute-start(f32[16,128,256]{2,1,0:T(8,128)} %get-tuple-element.21), channel_id=1, source_target_pairs={{0,48},{1,49},{2,50},{3,51},{4,52},{5,53},{6,54},{7,55},{8,56},{9,... | collective-permute-start | bytes 6291464 | tf_op jit(solution)/shard_map/ppermute | solution.py:160
  376.2 94.7 %collective-permute-start.18 = (f32[16,128,256]{2,1,0:T(8,128)S(1)}, f32[16,128,256]{2,1,0:T(8,128)S(1)}, u32[]{:S(2)}, u32[]{:S(2)}) collective-permute-start(f32[16,128,256]{2,1,0:T(8,128)S(1)} %get-tuple-element.22), channel_id=1, source_target_pairs={{0,16},{1,17},{2,18},{3,19},{4,20},{5,21},{6,22},{7,23},{8,24},{9,... | collective-permute-start | bytes 6291464 | tf_op jit(solution)/shard_map/ppermute | solution.py:160
  376.2 94.7 %collective-permute-start.19 = (f32[16,128,256]{2,1,0:T(8,128)S(1)}, f32[16,128,256]{2,1,0:T(8,128)S(1)}, u32[]{:S(2)}, u32[]{:S(2)}) collective-permute-start(f32[16,128,256]{2,1,0:T(8,128)S(1)} %get-tuple-element.20), channel_id=1, source_target_pairs={{0,32},{1,33},{2,34},{3,35},{4,36},{5,37},{6,38},{7,39},{8,40},{9,... | collective-permute-start | bytes 6291464 | tf_op jit(solution)/shard_map/ppermute | solution.py:160
  378.9 109.0 %collective-permute-start.15 = (f32[4,128,256]{2,1,0:T(8,128)}, f32[4,128,256]{2,1,0:T(8,128)S(1)}, u32[]{:S(2)}, u32[]{:S(2)}) collective-permute-start(f32[4,128,256]{2,1,0:T(8,128)} %get-tuple-element.25), channel_id=1, source_target_pairs={{0,48},{1,49},{2,50},{3,51},{4,52},{5,53},{6,54},{7,55},{8,56},{9,... | collective-permute-start | bytes 1572872 | tf_op jit(solution)/shard_map/ppermute | solution.py:160
  380.6 110.4 %collective-permute-start.13 = (f32[4,128,256]{2,1,0:T(8,128)}, f32[4,128,256]{2,1,0:T(8,128)S(1)}, u32[]{:S(2)}, u32[]{:S(2)}) collective-permute-start(f32[4,128,256]{2,1,0:T(8,128)} %get-tuple-element.26), channel_id=1, source_target_pairs={{0,16},{1,17},{2,18},{3,19},{4,20},{5,21},{6,22},{7,23},{8,24},{9,... | collective-permute-start | bytes 1572872 | tf_op jit(solution)/shard_map/ppermute | solution.py:160
  467.5 23.5 %collective-permute-start.14 = (f32[4,128,256]{2,1,0:T(8,128)}, f32[4,128,256]{2,1,0:T(8,128)S(1)}, u32[]{:S(2)}, u32[]{:S(2)}) collective-permute-start(f32[4,128,256]{2,1,0:T(8,128)} %get-tuple-element.24), channel_id=1, source_target_pairs={{0,32},{1,33},{2,34},{3,35},{4,36},{5,37},{6,38},{7,39},{8,40},{9,... | collective-permute-start | bytes 1572872 | tf_op jit(solution)/shard_map/ppermute | solution.py:160
  473.7 17.6 %collective-permute-start.23 = (f32[4,128,256]{2,1,0:T(8,128)S(1)}, f32[4,128,256]{2,1,0:T(8,128)S(1)}, u32[]{:S(2)}, u32[]{:S(2)}) collective-permute-start(f32[4,128,256]{2,1,0:T(8,128)S(1)} %get-tuple-element.28), channel_id=1, source_target_pairs={{0,6},{1,7},{2,0},{3,1},{4,2},{5,3},{6,4},{7,5},{8,14},{9,15},{10,... | collective-permute-start | bytes 1572872 | tf_op jit(solution)/shard_map/ppermute | solution.py:160
  474.1 17.3 %collective-permute-start.21 = (f32[4,128,256]{2,1,0:T(8,128)S(1)}, f32[4,128,256]{2,1,0:T(8,128)S(1)}, u32[]{:S(2)}, u32[]{:S(2)}) collective-permute-start(f32[4,128,256]{2,1,0:T(8,128)S(1)} %get-tuple-element.29), channel_id=1, source_target_pairs={{0,2},{1,3},{2,4},{3,5},{4,6},{5,7},{6,0},{7,1},{8,10},{9,11},{10,... | collective-permute-start | bytes 1572872 | tf_op jit(solution)/shard_map/ppermute | solution.py:160
  487.9 13.3 %collective-permute-start.22 = (f32[4,128,256]{2,1,0:T(8,128)S(1)}, f32[4,128,256]{2,1,0:T(8,128)S(1)}, u32[]{:S(2)}, u32[]{:S(2)}) collective-permute-start(f32[4,128,256]{2,1,0:T(8,128)S(1)} %get-tuple-element.27), channel_id=1, source_target_pairs={{0,4},{1,5},{2,6},{3,7},{4,0},{5,1},{6,2},{7,3},{8,12},{9,13},{10,... | collective-permute-start | bytes 1572872 | tf_op jit(solution)/shard_map/ppermute | solution.py:160
  491.3 11.0 %collective-permute-start.16 = (f32[2,128,256]{2,1,0:T(8,128)S(1)}, f32[2,128,256]{2,1,0:T(8,128)S(1)}, u32[]{:S(2)}, u32[]{:S(2)}) collective-permute-start(f32[2,128,256]{2,1,0:T(8,128)S(1)} %slice.145), channel_id=1, source_target_pairs={{0,8},{1,9},{2,10},{3,11},{4,12},{5,13},{6,14},{7,15},{8,0},{9,1},... | collective-permute-start | bytes 786440 | tf_op jit(solution)/shard_map/ppermute | solution.py:160
  501.2 7.4 %copy-start.1 = (bf16[256,256]{1,0:T(8,128)(2,1)S(1)}, bf16[256,256]{1,0:T(8,128)(2,1)}, u32[]{:S(2)}) copy-start(bf16[256,256]{1,0:T(8,128)(2,1)} %param.7) | copy-start | bytes 393220
  501.4 6.5 %collective-permute-start.24 = (f32[2,128,256]{2,1,0:T(8,128)S(1)}, f32[2,128,256]{2,1,0:T(8,128)S(1)}, u32[]{:S(2)}, u32[]{:S(2)}) collective-permute-start(f32[2,128,256]{2,1,0:T(8,128)S(1)} %slice.159), channel_id=1, source_target_pairs={{0,8},{1,9},{2,10},{3,11},{4,12},{5,13},{6,14},{7,15},{8,0},{9,1},... | collective-permute-start | bytes 786440 | tf_op jit(solution)/shard_map/ppermute | solution.py:160
Sparse Core Ops, SparseCore 0:
  9.7 125.4 all-gather.1

commit v14 on v12

--- a/solution.py
+++ b/solution.py
@@ -62,7 +62,7 @@
         total[c] = jnp.zeros(total.shape[1:], total.dtype)
         return carry
 
-    lax.fori_loop(0, col_blocks, clear, 0)
+    lax.fori_loop(0, col_blocks, clear, 0, unroll=8)
     load_vals.wait()
     for t in range(row_blocks):
         live = jnp.clip(count_ref[t], 0, slot_total)

time: 435 us -> 435 us (level)
  no operation moved by 1% of the time
where the time goes in v14:
time: 435 us; the launch traced here: 434 us
  waiting for transfers between devices  310 us (71%)
  starting transfers between devices  38 us (9%)
  Pallas kernels  30.8 us (7%)
  other arithmetic  29.3 us (7%)
  between operations  14.2 us (3%)
  local copies, waits for them, and re-layouts  10.7 us (2%)
    ppermute x15, waiting for transfers between devices, shifted(): return lax.ppermute(value, 'row', [(r, dest(r)) for r in range(64)])  141 us
    all_gather x1, waiting for transfers between devices, body(): gathered = lax.all_gather(features, 'row', axis=0, tiled=True)  121 us
    ppermute x7, waiting for transfers between devices, all_sum(): lax.ppermute(value, axis, [(i, i ^ step) for i in range(size)])  34.6 us
    ppermute x15, starting transfers between devices, shifted(): return lax.ppermute(value, 'row', [(r, dest(r)) for r in range(64)])  21.7 us
    pallas_call x1, Pallas kernels, spread(): pl.pallas_call(spread_kernel, out_shape=[jax.ShapeDtypeStruct((col_blocks...  19.7 us
    add x1, other arithmetic, row_reduce_scatter(): first = [keep[0, s] + came[0, s] for s in range(4)]  15.9 us
    ppermute x2, waiting for transfers between devices, swap(): return lax.ppermute(value, axis, [(i, i ^ 1) for i in range(size)])  12.9 us
    pallas_call x1, Pallas kernels, aggregate(): pl.pallas_call(aggregate_kernel, out_shape=jax.ShapeDtypeStruct((row_bloc...  11.1 us
  transfers between devices with their start and end apart: 25, of which 19 were waited for; matrix products, arithmetic and copies ran while one was open for 2% of the time, Pallas kernels for 0%

profile of v14, /device:TPU:0, one launch (start us, length us, event | category | flops | bytes accessed | tf_op | source)
XLA Modules:
  0.0 434.5 jit_solution(4906119264562796739)
XLA Ops:
  7.9 6.5 %copy.9 = bf16[1,8,16,128,128]{3,4,2,1,0:T(8,128)(2,1)} copy(bf16[1,8,16,128,128]{4,3,2,1,0:T(8,128)(2,1)} %param.8) | data formatting | bytes 8388608 | tf_op args[2]
  14.4 120.9 %all-gather.2.cloned.1.call-done.panel_hbm = bf16[32768,256]{1,0:T(8,128)(2,1)} async-done(((bf16[512,256]{1,0:T(8,128)(2,1)}), bf16[32768,256]{1,0:T(8,128)(2,1)}) %all-gather.2.cloned.1.call-update) | async-done | bytes 16777232 | tf_op jit(solution)/shard_map/all_gather | solution.py:186
  135.3 11.1 %shard_map.85 = f32[8,128,256]{2,1,0:T(8,128)} custom-call(s32[8,16]{1,0:T(8,128)} %bitcast.51, s32[8]{0:T(128)} %bitcast.53, bf16[8,16,128,128]{3,2,1,0:T(8,128)(2,1)} %bitcast.45, bf16[32768,256]{1,0:T(8,128)(2,1)} %all-gather.2.cloned.1.call-done.panel_hbm), custom_call_target="tpu_custom_call" | custom-call | flops 1073741824 | bytes 22020096 | tf_op jit(solution)/shard_map/pallas_call | solution.py:90
  146.4 1.1 constant_dynamic-slice_fusion
  147.5 2.8 collective-permute-start
  150.3 12.9 %collective-permute-done = f32[512,256]{1,0:T(8,128)S(1)} collective-permute-done((f32[512,256]{1,0:T(8,128)S(1)}, f32[512,256]{1,0:T(8,128)S(1)}, u32[]{:S(2)}, u32[]{:S(2)}) %collective-permute-start) | collective-permute-done | bytes 524320 | tf_op jit(solution)/shard_map/ppermute | solution.py:144
  163.1 1.1 add_convert_fusion
  164.3 1.1 multiply_convert_fusion
  165.6 2.8 collective-permute-start.1
  168.4 6.5 %collective-permute-done.1 = f32[256,256]{1,0:T(8,128)S(1)} collective-permute-done((f32[256,256]{1,0:T(8,128)S(1)}, f32[256,256]{1,0:T(8,128)S(1)}, u32[]{:S(2)}, u32[]{:S(2)}) %collective-permute-start.1) | collective-permute-done | bytes 262176 | tf_op jit(solution)/shard_map/ppermute | solution.py:174
  175.0 1.5 collective-permute-done.2
  176.5 1.5 collective-permute-start.3
  178.0 7.0 %collective-permute-done.3 = f32[256,256]{1,0:T(8,128)S(1)} collective-permute-done((f32[256,256]{1,0:T(8,128)S(1)}, f32[256,256]{1,0:T(8,128)S(1)}, u32[]{:S(2)}, u32[]{:S(2)}) %collective-permute-start.3) | collective-permute-done | bytes 262176 | tf_op jit(solution)/shard_map/ppermute | solution.py:174
  185.0 2.2 collective-permute-start.4
  187.2 6.9 %collective-permute-done.4 = f32[256,256]{1,0:T(8,128)S(1)} collective-permute-done((f32[256,256]{1,0:T(8,128)S(1)}, f32[256,256]{1,0:T(8,128)S(1)}, u32[]{:S(2)}, u32[]{:S(2)}) %collective-permute-start.4) | collective-permute-done | bytes 262176 | tf_op jit(solution)/shard_map/ppermute | solution.py:174
  194.1 1.0 collective-permute-start.5
  195.1 5.7 %collective-permute-done.5 = f32[256,256]{1,0:T(8,128)S(1)} collective-permute-done((f32[256,256]{1,0:T(8,128)S(1)}, f32[256,256]{1,0:T(8,128)S(1)}, u32[]{:S(2)}, u32[]{:S(2)}) %collective-permute-start.5) | collective-permute-done | bytes 262176 | tf_op jit(solution)/shard_map/ppermute | solution.py:174
  202.1 3.2 collective-permute-start.8
  205.3 2.5 collective-permute-done.6
  207.8 1.9 collective-permute-start.7
  211.3 4.5 %collective-permute-done.7 = f32[256,256]{1,0:T(8,128)S(1)} collective-permute-done((f32[256,256]{1,0:T(8,128)S(1)}, f32[256,256]{1,0:T(8,128)S(1)}, u32[]{:S(2)}, u32[]{:S(2)}) %collective-permute-start.7) | collective-permute-done | bytes 262176 | tf_op jit(solution)/shard_map/ppermute | solution.py:174
  215.8 19.7 %shard_map.86 = (f32[128,128,256]{2,1,0:T(8,128)}, f32[128,128,256]{2,1,0:T(8,128)}) custom-call(s32[2]{0:T(128)} %pad_add_fusion.side_ref, s32[8,16]{1,0:T(8,128)} %bitcast.52, s32[8]{0:T(128)} %bitcast.54, bf16[8,16,128,128]{3,2,1,0:T(8,128)(2,1)} %bitcast.40, bf16[2,4,128,256]{3,2,1,0:T(8,128)(2,1)} %pad_maximum_fusion.grad_ref), custom_call_target="tpu_custom_call" | custom-call | flops 1073741824 | bytes 38273024 | tf_op jit(solution)/shard_map/pallas_call | solution.py:117
  235.8 25.4 %collective-permute-done.9 = f32[128,128,256]{2,1,0:T(8,128)S(1)} collective-permute-done((f32[128,128,256]{2,1,0:T(8,128)}, f32[128,128,256]{2,1,0:T(8,128)S(1)}, u32[]{:S(2)}, u32[]{:S(2)}) %collective-permute-start.9) | collective-permute-done | bytes 16777248 | tf_op jit(solution)/shard_map/ppermute | solution.py:152
  261.2 15.9 %fusion.6 = (f32[16,128,256]{2,1,0:T(8,128)}, f32[16,128,256]{2,1,0:T(8,128)}, f32[16,128,256]{2,1,0:T(8,128)}, f32[16,128,256]{2,1,0:T(8,128)}, f32[16,128,256]{2,1,0:T(8,128)}, /*index=5*/f32[16,128,256]{2,1,0:T(8,128)}) fusion(f32[2,4,16,128,256]{4,3,2,1,0:T(8,128)S(1)} %bitcast.43, f32[2,4,16,128,256]{4,3,2,1,0:T(8,128)} %bitcast.41), kind=kLoop, calls=%fused_computation.12 | loop fusion | flops 3145728 | bytes 37748736 | tf_op jit(solution)/shard_map/add | solution.py:159
  277.1 2.3 collective-permute-start.11
  279.4 1.1 collective-permute-start.19
  280.5 1.3 collective-permute-start.18
  282.5 1.2 collective-permute-start.12
  283.8 42.8 %collective-permute-done.11 = f32[16,128,256]{2,1,0:T(8,128)S(1)} collective-permute-done((f32[16,128,256]{2,1,0:T(8,128)}, f32[16,128,256]{2,1,0:T(8,128)S(1)}, u32[]{:S(2)}, u32[]{:S(2)}) %collective-permute-start.11) | collective-permute-done | bytes 2097184 | tf_op jit(solution)/shard_map/ppermute | solution.py:152
  326.5 2.5 collective-permute-start.10
  329.0 1.8 collective-permute-done.18
  330.8 43.4 %collective-permute-done.17 = f32[16,128,256]{2,1,0:T(8,128)S(1)} collective-permute-done((f32[16,128,256]{2,1,0:T(8,128)}, f32[16,128,256]{2,1,0:T(8,128)S(1)}, u32[]{:S(2)}, u32[]{:S(2)}) %collective-permute-start.17) | collective-permute-done | bytes 2097184 | tf_op jit(solution)/shard_map/ppermute | solution.py:152
  374.3 1.3 copy-done.5
  375.6 1.4 copy-done.6
  377.0 8.7 %fusion.9 = (f32[16,128,256]{2,1,0:T(8,128)S(1)}, f32[16,128,256]{2,1,0:T(8,128)S(1)}) fusion(f32[2,4,16,128,256]{4,3,2,1,0:T(8,128)} %bitcast.44, f32[2,4,16,128,256]{4,3,2,1,0:T(8,128)} %bitcast.42, f32[16,128,256]{2,1,0:T(8,128)} %copy-done.6, f32[16,128,256]{2,1,0:T(8,128)} %collective-permute-done.10, f32[16,128,256]{2,1,0:T(8,128)S(1)} %collective-permute-done.11, ...), kind=kLoop, calls=%fused_computation.17 | loop fusion | flops 4194304 | bytes 25165824 | tf_op jit(solution)/shard_map/add | solution.py:161
  385.9 1.3 collective-permute-start.14
  387.2 1.2 collective-permute-start.15
  389.4 1.5 collective-permute-start.21
  390.9 2.1 collective-permute-start.22
  393.0 9.3 %collective-permute-done.14 = f32[4,128,256]{2,1,0:T(8,128)S(1)} collective-permute-done((f32[4,128,256]{2,1,0:T(8,128)S(1)}, f32[4,128,256]{2,1,0:T(8,128)S(1)}, u32[]{:S(2)}, u32[]{:S(2)}) %collective-permute-start.14) | collective-permute-done | bytes 524320 | tf_op jit(solution)/shard_map/ppermute | solution.py:152
  402.3 1.6 collective-permute-start.20
  403.8 6.0 %collective-permute-done.15 = f32[4,128,256]{2,1,0:T(8,128)S(1)} collective-permute-done((f32[4,128,256]{2,1,0:T(8,128)S(1)}, f32[4,128,256]{2,1,0:T(8,128)S(1)}, u32[]{:S(2)}, u32[]{:S(2)}) %collective-permute-start.15) | collective-permute-done | bytes 524320 | tf_op jit(solution)/shard_map/ppermute | solution.py:152
  409.8 2.8 collective-permute-done.13
  412.8 1.9 collective-permute-start.16
  414.8 1.0 collective-permute-done.20
  416.0 1.8 collective-permute-start.23
  418.5 3.6 collective-permute-done.16
  422.1 4.8 %collective-permute-done.23 = f32[2,128,256]{2,1,0:T(8,128)S(1)} collective-permute-done((f32[2,128,256]{2,1,0:T(8,128)S(1)}, f32[2,128,256]{2,1,0:T(8,128)S(1)}, u32[]{:S(2)}, u32[]{:S(2)}) %collective-permute-start.23) | collective-permute-done | bytes 262176 | tf_op jit(solution)/shard_map/ppermute | solution.py:152
  (48 shorter events, 8.3 us)
Async XLA Ops:
  7.2 157.1 %copy-start = (bf16[256,256]{1,0:T(8,128)(2,1)S(1)}, bf16[256,256]{1,0:T(8,128)(2,1)}, u32[]{:S(2)}) copy-start(bf16[256,256]{1,0:T(8,128)(2,1)} %param.7) | copy-start | bytes 393220
  7.2 128.1 %all-gather.2.cloned.1.call-start = ((), (), s32[]{:S(2)}) async-start(), calls=%async_computation | async-start | bytes 17039360 | tf_op jit(solution)/shard_map/all_gather | solution.py:186
  146.4 17.9 %copy-start.7 = (bf16[512,256]{1,0:T(8,128)(2,1)S(1)}, bf16[512,256]{1,0:T(8,128)(2,1)}, u32[]{:S(2)}) copy-start(bf16[512,256]{1,0:T(8,128)(2,1)} %param.11) | copy-start | bytes 786436
  147.5 15.7 %collective-permute-start = (f32[512,256]{1,0:T(8,128)S(1)}, f32[512,256]{1,0:T(8,128)S(1)}, u32[]{:S(2)}, u32[]{:S(2)}) collective-permute-start(f32[512,256]{1,0:T(8,128)S(1)} %constant_dynamic-slice_fusion), channel_id=1, source_target_pairs={{0,64},{64,0},{1,65},{65,1},{2,66},{66,2},{3,67},{67,3},{4,68},{68... | collective-permute-start | bytes 1572872 | tf_op jit(solution)/shard_map/ppermute | solution.py:144
  165.6 9.2 %collective-permute-start.1 = (f32[256,256]{1,0:T(8,128)S(1)}, f32[256,256]{1,0:T(8,128)S(1)}, u32[]{:S(2)}, u32[]{:S(2)}) collective-permute-start(f32[256,256]{1,0:T(8,128)S(1)} %fusion.14), channel_id=1, source_target_pairs={{0,64},{64,0},{1,65},{65,1},{2,66},{66,2},{3,67},{67,3},{4,68},{68... | collective-permute-start | bytes 786440 | tf_op jit(solution)/shard_map/ppermute | solution.py:174
  174.9 1.6 collective-permute-start.2
  176.5 8.4 %collective-permute-start.3 = (f32[256,256]{1,0:T(8,128)S(1)}, f32[256,256]{1,0:T(8,128)S(1)}, u32[]{:S(2)}, u32[]{:S(2)}) collective-permute-start(f32[256,256]{1,0:T(8,128)S(1)} %add.134), channel_id=1, source_target_pairs={{0,2},{1,3},{2,0},{3,1},{4,6},{5,7},{6,4},{7,5},{8,10},{9,11},{10,... | collective-permute-start | bytes 786440 | tf_op jit(solution)/shard_map/ppermute | solution.py:174
  185.0 9.1 %collective-permute-start.4 = (f32[256,256]{1,0:T(8,128)S(1)}, f32[256,256]{1,0:T(8,128)S(1)}, u32[]{:S(2)}, u32[]{:S(2)}) collective-permute-start(f32[256,256]{1,0:T(8,128)S(1)} %add.135), channel_id=1, source_target_pairs={{0,4},{1,5},{2,6},{3,7},{4,0},{5,1},{6,2},{7,3},{8,12},{9,13},{10,... | collective-permute-start | bytes 786440 | tf_op jit(solution)/shard_map/ppermute | solution.py:174
  194.1 6.7 %collective-permute-start.5 = (f32[256,256]{1,0:T(8,128)S(1)}, f32[256,256]{1,0:T(8,128)S(1)}, u32[]{:S(2)}, u32[]{:S(2)}) collective-permute-start(f32[256,256]{1,0:T(8,128)S(1)} %add.136), channel_id=1, source_target_pairs={{0,8},{1,9},{2,10},{3,11},{4,12},{5,13},{6,14},{7,15},{8,0},{9,1},... | collective-permute-start | bytes 786440 | tf_op jit(solution)/shard_map/ppermute | solution.py:174
  200.9 6.9 %collective-permute-start.6 = (f32[256,256]{1,0:T(8,128)S(1)}, f32[256,256]{1,0:T(8,128)S(1)}, u32[]{:S(2)}, u32[]{:S(2)}) collective-permute-start(f32[256,256]{1,0:T(8,128)S(1)} %add.137), channel_id=1, source_target_pairs={{0,16},{1,17},{2,18},{3,19},{4,20},{5,21},{6,22},{7,23},{8,24},{9,... | collective-permute-start | bytes 786440 | tf_op jit(solution)/shard_map/ppermute | solution.py:174
  202.1 8.3 %collective-permute-start.8 = (bf16[512,256]{1,0:T(8,128)(2,1)S(1)}, bf16[512,256]{1,0:T(8,128)(2,1)S(1)}, u32[]{:S(2)}, u32[]{:S(2)}) collective-permute-start(bf16[512,256]{1,0:T(8,128)(2,1)S(1)} %convolution_convert_fusion), channel_id=1, source_target_pairs={{0,64},{64,0},{1,65},{65,1},{2,66},{66,2},{3,67},{67,3},{4,68},{68... | collective-permute-start | bytes 786440 | tf_op jit(solution)/shard_map/ppermute | solution.py:144
  207.8 8.0 %collective-permute-start.7 = (f32[256,256]{1,0:T(8,128)S(1)}, f32[256,256]{1,0:T(8,128)S(1)}, u32[]{:S(2)}, u32[]{:S(2)}) collective-permute-start(f32[256,256]{1,0:T(8,128)S(1)} %add.138), channel_id=1, source_target_pairs={{0,32},{1,33},{2,34},{3,35},{4,36},{5,37},{6,38},{7,39},{8,40},{9,... | collective-permute-start | bytes 786440 | tf_op jit(solution)/shard_map/ppermute | solution.py:174
  235.5 25.6 %collective-permute-start.9 = (f32[128,128,256]{2,1,0:T(8,128)}, f32[128,128,256]{2,1,0:T(8,128)S(1)}, u32[]{:S(2)}, u32[]{:S(2)}) collective-permute-start(f32[128,128,256]{2,1,0:T(8,128)} %get-tuple-element.14), channel_id=1, source_target_pairs={{0,1},{1,0},{2,3},{3,2},{4,5},{5,4},{6,7},{7,6},{8,9},{9,8},{10,11... | collective-permute-start | bytes 50331656 | tf_op jit(solution)/shard_map/ppermute | solution.py:152
  261.2 15.9 %copy-start.2 = (f32[128,128,256]{2,1,0:T(8,128)}, f32[128,128,256]{2,1,0:T(8,128)S(1)}, u32[]{:S(2)}) copy-start(f32[128,128,256]{2,1,0:T(8,128)S(1)} %collective-permute-done.9) | copy-start | bytes 50331652
  277.1 49.5 %collective-permute-start.11 = (f32[16,128,256]{2,1,0:T(8,128)}, f32[16,128,256]{2,1,0:T(8,128)S(1)}, u32[]{:S(2)}, u32[]{:S(2)}) collective-permute-start(f32[16,128,256]{2,1,0:T(8,128)} %get-tuple-element.17), channel_id=1, source_target_pairs={{0,4},{1,5},{2,6},{3,7},{4,0},{5,1},{6,2},{7,3},{8,12},{9,13},{10,... | collective-permute-start | bytes 6291464 | tf_op jit(solution)/shard_map/ppermute | solution.py:152
  279.4 49.7 %collective-permute-start.19 = (f32[16,128,256]{2,1,0:T(8,128)}, f32[16,128,256]{2,1,0:T(8,128)S(1)}, u32[]{:S(2)}, u32[]{:S(2)}) collective-permute-start(f32[16,128,256]{2,1,0:T(8,128)} %get-tuple-element.18), channel_id=1, source_target_pairs={{0,48},{1,49},{2,50},{3,51},{4,52},{5,53},{6,54},{7,55},{8,56},{9,... | collective-permute-start | bytes 6291464 | tf_op jit(solution)/shard_map/ppermute | solution.py:152
  280.5 50.3 %collective-permute-start.18 = (f32[16,128,256]{2,1,0:T(8,128)}, f32[16,128,256]{2,1,0:T(8,128)S(1)}, u32[]{:S(2)}, u32[]{:S(2)}) collective-permute-start(f32[16,128,256]{2,1,0:T(8,128)} %get-tuple-element.19), channel_id=1, source_target_pairs={{0,32},{1,33},{2,34},{3,35},{4,36},{5,37},{6,38},{7,39},{8,40},{9,... | collective-permute-start | bytes 6291464 | tf_op jit(solution)/shard_map/ppermute | solution.py:152
  281.7 92.5 %collective-permute-start.17 = (f32[16,128,256]{2,1,0:T(8,128)}, f32[16,128,256]{2,1,0:T(8,128)S(1)}, u32[]{:S(2)}, u32[]{:S(2)}) collective-permute-start(f32[16,128,256]{2,1,0:T(8,128)} %get-tuple-element.20), channel_id=1, source_target_pairs={{0,16},{1,17},{2,18},{3,19},{4,20},{5,21},{6,22},{7,23},{8,24},{9,... | collective-permute-start | bytes 6291464 | tf_op jit(solution)/shard_map/ppermute | solution.py:152
  282.5 91.7 %collective-permute-start.12 = (f32[16,128,256]{2,1,0:T(8,128)}, f32[16,128,256]{2,1,0:T(8,128)S(1)}, u32[]{:S(2)}, u32[]{:S(2)}) collective-permute-start(f32[16,128,256]{2,1,0:T(8,128)} %get-tuple-element.21), channel_id=1, source_target_pairs={{0,6},{1,7},{2,0},{3,1},{4,2},{5,3},{6,4},{7,5},{8,14},{9,15},{10,... | collective-permute-start | bytes 6291464 | tf_op jit(solution)/shard_map/ppermute | solution.py:152
  326.5 50.5 %collective-permute-start.10 = (f32[16,128,256]{2,1,0:T(8,128)}, f32[16,128,256]{2,1,0:T(8,128)}, u32[]{:S(2)}, u32[]{:S(2)}) collective-permute-start(f32[16,128,256]{2,1,0:T(8,128)} %get-tuple-element.22), channel_id=1, source_target_pairs={{0,2},{1,3},{2,4},{3,5},{4,6},{5,7},{6,0},{7,1},{8,10},{9,11},{10,... | collective-permute-start | bytes 6291464 | tf_op jit(solution)/shard_map/ppermute | solution.py:152
  329.0 45.2 %copy-start.3 = (f32[16,128,256]{2,1,0:T(8,128)}, f32[16,128,256]{2,1,0:T(8,128)S(1)}, u32[]{:S(2)}) copy-start(f32[16,128,256]{2,1,0:T(8,128)S(1)} %collective-permute-done.19) | copy-start | bytes 6291460
  330.8 43.5 %copy-start.4 = (f32[16,128,256]{2,1,0:T(8,128)}, f32[16,128,256]{2,1,0:T(8,128)S(1)}, u32[]{:S(2)}) copy-start(f32[16,128,256]{2,1,0:T(8,128)S(1)} %collective-permute-done.18) | copy-start | bytes 6291460
  374.2 1.4 copy-start.5
  375.6 1.4 copy-start.6
  385.9 16.4 %collective-permute-start.14 = (f32[4,128,256]{2,1,0:T(8,128)S(1)}, f32[4,128,256]{2,1,0:T(8,128)S(1)}, u32[]{:S(2)}, u32[]{:S(2)}) collective-permute-start(f32[4,128,256]{2,1,0:T(8,128)S(1)} %get-tuple-element.23), channel_id=1, source_target_pairs={{0,32},{1,33},{2,34},{3,35},{4,36},{5,37},{6,38},{7,39},{8,40},{9,... | collective-permute-start | bytes 1572872 | tf_op jit(solution)/shard_map/ppermute | solution.py:152
  387.2 22.6 %collective-permute-start.15 = (f32[4,128,256]{2,1,0:T(8,128)S(1)}, f32[4,128,256]{2,1,0:T(8,128)S(1)}, u32[]{:S(2)}, u32[]{:S(2)}) collective-permute-start(f32[4,128,256]{2,1,0:T(8,128)S(1)} %get-tuple-element.24), channel_id=1, source_target_pairs={{0,48},{1,49},{2,50},{3,51},{4,52},{5,53},{6,54},{7,55},{8,56},{9,... | collective-permute-start | bytes 1572872 | tf_op jit(solution)/shard_map/ppermute | solution.py:152
  388.4 24.2 %collective-permute-start.13 = (f32[4,128,256]{2,1,0:T(8,128)S(1)}, f32[4,128,256]{2,1,0:T(8,128)S(1)}, u32[]{:S(2)}, u32[]{:S(2)}) collective-permute-start(f32[4,128,256]{2,1,0:T(8,128)S(1)} %get-tuple-element.25), channel_id=1, source_target_pairs={{0,16},{1,17},{2,18},{3,19},{4,20},{5,21},{6,22},{7,23},{8,24},{9,... | collective-permute-start | bytes 1572872 | tf_op jit(solution)/shard_map/ppermute | solution.py:152
  389.4 25.4 %collective-permute-start.21 = (f32[4,128,256]{2,1,0:T(8,128)S(1)}, f32[4,128,256]{2,1,0:T(8,128)S(1)}, u32[]{:S(2)}, u32[]{:S(2)}) collective-permute-start(f32[4,128,256]{2,1,0:T(8,128)S(1)} %get-tuple-element.26), channel_id=1, source_target_pairs={{0,4},{1,5},{2,6},{3,7},{4,0},{5,1},{6,2},{7,3},{8,12},{9,13},{10,... | collective-permute-start | bytes 1572872 | tf_op jit(solution)/shard_map/ppermute | solution.py:152
  390.9 23.9 %collective-permute-start.22 = (f32[4,128,256]{2,1,0:T(8,128)S(1)}, f32[4,128,256]{2,1,0:T(8,128)S(1)}, u32[]{:S(2)}, u32[]{:S(2)}) collective-permute-start(f32[4,128,256]{2,1,0:T(8,128)S(1)} %get-tuple-element.27), channel_id=1, source_target_pairs={{0,6},{1,7},{2,0},{3,1},{4,2},{5,3},{6,4},{7,5},{8,14},{9,15},{10,... | collective-permute-start | bytes 1572872 | tf_op jit(solution)/shard_map/ppermute | solution.py:152
  402.3 13.5 %collective-permute-start.20 = (f32[4,128,256]{2,1,0:T(8,128)S(1)}, f32[4,128,256]{2,1,0:T(8,128)S(1)}, u32[]{:S(2)}, u32[]{:S(2)}) collective-permute-start(f32[4,128,256]{2,1,0:T(8,128)S(1)} %get-tuple-element.28), channel_id=1, source_target_pairs={{0,2},{1,3},{2,4},{3,5},{4,6},{5,7},{6,0},{7,1},{8,10},{9,11},{10,... | collective-permute-start | bytes 1572872 | tf_op jit(solution)/shard_map/ppermute | solution.py:152
  412.8 9.2 %collective-permute-start.16 = (f32[2,128,256]{2,1,0:T(8,128)S(1)}, f32[2,128,256]{2,1,0:T(8,128)S(1)}, u32[]{:S(2)}, u32[]{:S(2)}) collective-permute-start(f32[2,128,256]{2,1,0:T(8,128)S(1)} %slice.137), channel_id=1, source_target_pairs={{0,8},{1,9},{2,10},{3,11},{4,12},{5,13},{6,14},{7,15},{8,0},{9,1},... | collective-permute-start | bytes 786440 | tf_op jit(solution)/shard_map/ppermute | solution.py:152
  415.8 11.9 %copy-start.1 = (bf16[256,256]{1,0:T(8,128)(2,1)S(1)}, bf16[256,256]{1,0:T(8,128)(2,1)}, u32[]{:S(2)}) copy-start(bf16[256,256]{1,0:T(8,128)(2,1)} %param.7) | copy-start | bytes 393220
  416.0 10.9 %collective-permute-start.23 = (f32[2,128,256]{2,1,0:T(8,128)S(1)}, f32[2,128,256]{2,1,0:T(8,128)S(1)}, u32[]{:S(2)}, u32[]{:S(2)}) collective-permute-start(f32[2,128,256]{2,1,0:T(8,128)S(1)} %slice.151), channel_id=1, source_target_pairs={{0,8},{1,9},{2,10},{3,11},{4,12},{5,13},{6,14},{7,15},{8,0},{9,1},... | collective-permute-start | bytes 786440 | tf_op jit(solution)/shard_map/ppermute | solution.py:152
Sparse Core Ops, SparseCore 0:
  9.7 125.4 all-gather.1

commit v15 on v12

--- a/solution.py
+++ b/solution.py
@@ -201,9 +201,9 @@
     local_grad = jnp.dot(aggregated.T, pre_grad, preferred_element_type=jnp.float32)
     own_grad = jnp.dot(pre_grad, weight.T, preferred_element_type=jnp.float32).astype(jnp.bfloat16)
     both_grad = jnp.stack([own_grad, swap(own_grad, "grp")]).reshape(2, -1, block, width)
-    weight_grad = all_sum(all_sum(local_grad, "grp"), "row")
+    weight_grad = all_sum(local_grad, "row")
     weight_grad, both_grad = lax.optimization_barrier((weight_grad, both_grad))
-    weight_grad = weight_grad * (1.0 / math.sqrt(verts))
+    weight_grad = (weight_grad + swap(weight_grad, "grp")) * (1.0 / math.sqrt(verts))
 
     where = jnp.stack([side, lax.axis_index("row")]).astype(jnp.int32)
     keep, send = spread(where, cols, count, flipped, both_grad, col_blocks)

time: 435 us -> 429 us (0.986)
  waiting for transfers between devices: 310 us -> 304 us
    ppermute x7 -> x6, waiting for transfers between devices: 34.6 us -> 28.4 us  [all_sum(): lax.ppermute(value, axis, [(i, i ^ step) for i in range(size)])]
    ppermute x2 -> x3, starting transfers between devices: 5.95 us -> 9.19 us  [swap(): return lax.ppermute(value, axis, [(i, i ^ 1) for i in range(size)])]
    ppermute x7 -> x6, starting transfers between devices: 10.3 us -> 7.31 us  [all_sum(): lax.ppermute(value, axis, [(i, i ^ step) for i in range(size)])]
    ppermute x2 -> x3, waiting for transfers between devices: 12.9 us -> 15 us  [swap(): return lax.ppermute(value, axis, [(i, i ^ 1) for i in range(size)])]
  transfers between devices with their start and end apart: 25 -> 25, of which waited for: 19 -> 18; matrix products, arithmetic and copies ran while one was open for 2% -> 2% of each run, Pallas kernels for 0% -> 0%
where the time goes in v15:
time: 429 us; the launch traced here: 428 us
  waiting for transfers between devices  304 us (71%)
  starting transfers between devices  37.2 us (9%)
  Pallas kernels  31 us (7%)
  other arithmetic  29.3 us (7%)
  between operations  14.2 us (3%)
  local copies, waits for them, and re-layouts  10.7 us (2%)
    ppermute x15, waiting for transfers between devices, shifted(): return lax.ppermute(value, 'row', [(r, dest(r)) for r in range(64)])  139 us
    all_gather x1, waiting for transfers between devices, body(): gathered = lax.all_gather(features, 'row', axis=0, tiled=True)  121 us
    ppermute x6, waiting for transfers between devices, all_sum(): lax.ppermute(value, axis, [(i, i ^ step) for i in range(size)])  28.4 us
    ppermute x15, starting transfers between devices, shifted(): return lax.ppermute(value, 'row', [(r, dest(r)) for r in range(64)])  20.7 us
    pallas_call x1, Pallas kernels, spread(): pl.pallas_call(spread_kernel, out_shape=[jax.ShapeDtypeStruct((col_blocks...  19.9 us
    add x1, other arithmetic, row_reduce_scatter(): first = [keep[0, s] + came[0, s] for s in range(4)]  15.9 us
    ppermute x3, waiting for transfers between devices, swap(): return lax.ppermute(value, axis, [(i, i ^ 1) for i in range(size)])  15 us
    pallas_call x1, Pallas kernels, aggregate(): pl.pallas_call(aggregate_kernel, out_shape=jax.ShapeDtypeStruct((row_bloc...  11.1 us
  transfers between devices with their start and end apart: 25, of which 18 were waited for; matrix products, arithmetic and copies ran while one was open for 2% of the time, Pallas kernels for 0%

profile of v15, /device:TPU:0, one launch (start us, length us, event | category | flops | bytes accessed | tf_op | source)
XLA Modules:
  0.0 428.3 jit_solution(11469383440016982820)
XLA Ops:
  7.9 6.5 %copy.9 = bf16[1,8,16,128,128]{3,4,2,1,0:T(8,128)(2,1)} copy(bf16[1,8,16,128,128]{4,3,2,1,0:T(8,128)(2,1)} %param.8) | data formatting | bytes 8388608 | tf_op args[2]
  14.4 120.9 %all-gather.2.cloned.1.call-done.panel_hbm = bf16[32768,256]{1,0:T(8,128)(2,1)} async-done(((bf16[512,256]{1,0:T(8,128)(2,1)}), bf16[32768,256]{1,0:T(8,128)(2,1)}) %all-gather.2.cloned.1.call-update) | async-done | bytes 16777232 | tf_op jit(solution)/shard_map/all_gather | solution.py:186
  135.3 11.1 %shard_map.85 = f32[8,128,256]{2,1,0:T(8,128)} custom-call(s32[8,16]{1,0:T(8,128)} %bitcast.51, s32[8]{0:T(128)} %bitcast.53, bf16[8,16,128,128]{3,2,1,0:T(8,128)(2,1)} %bitcast.45, bf16[32768,256]{1,0:T(8,128)(2,1)} %all-gather.2.cloned.1.call-done.panel_hbm), custom_call_target="tpu_custom_call" | custom-call | flops 1073741824 | bytes 22020096 | tf_op jit(solution)/shard_map/pallas_call | solution.py:90
  146.4 1.1 constant_dynamic-slice_fusion
  147.5 2.8 collective-permute-start
  150.3 12.9 %collective-permute-done = f32[512,256]{1,0:T(8,128)S(1)} collective-permute-done((f32[512,256]{1,0:T(8,128)S(1)}, f32[512,256]{1,0:T(8,128)S(1)}, u32[]{:S(2)}, u32[]{:S(2)}) %collective-permute-start) | collective-permute-done | bytes 524320 | tf_op jit(solution)/shard_map/ppermute | solution.py:144
  163.1 1.1 add_convert_fusion
  164.3 1.1 multiply_convert_fusion
  165.7 1.5 collective-permute-done.1
  167.3 1.2 collective-permute-start.2
  168.4 7.3 %collective-permute-done.2 = f32[256,256]{1,0:T(8,128)S(1)} collective-permute-done((f32[256,256]{1,0:T(8,128)S(1)}, f32[256,256]{1,0:T(8,128)S(1)}, u32[]{:S(2)}, u32[]{:S(2)}) %collective-permute-start.2) | collective-permute-done | bytes 262176 | tf_op jit(solution)/shard_map/ppermute | solution.py:174
  175.8 2.2 collective-permute-start.3
  177.9 6.9 %collective-permute-done.3 = f32[256,256]{1,0:T(8,128)S(1)} collective-permute-done((f32[256,256]{1,0:T(8,128)S(1)}, f32[256,256]{1,0:T(8,128)S(1)}, u32[]{:S(2)}, u32[]{:S(2)}) %collective-permute-start.3) | collective-permute-done | bytes 262176 | tf_op jit(solution)/shard_map/ppermute | solution.py:174
  184.9 1.0 collective-permute-start.4
  185.9 5.7 %collective-permute-done.4 = f32[256,256]{1,0:T(8,128)S(1)} collective-permute-done((f32[256,256]{1,0:T(8,128)S(1)}, f32[256,256]{1,0:T(8,128)S(1)}, u32[]{:S(2)}, u32[]{:S(2)}) %collective-permute-start.4) | collective-permute-done | bytes 262176 | tf_op jit(solution)/shard_map/ppermute | solution.py:174
  191.6 1.0 collective-permute-start.5
  192.9 3.2 collective-permute-start.7
  196.0 2.5 collective-permute-done.5
  198.6 1.9 collective-permute-start.6
  202.0 4.5 %collective-permute-done.6 = f32[256,256]{1,0:T(8,128)S(1)} collective-permute-done((f32[256,256]{1,0:T(8,128)S(1)}, f32[256,256]{1,0:T(8,128)S(1)}, u32[]{:S(2)}, u32[]{:S(2)}) %collective-permute-start.6) | collective-permute-done | bytes 262176 | tf_op jit(solution)/shard_map/ppermute | solution.py:174
  206.6 19.9 %shard_map.86 = (f32[128,128,256]{2,1,0:T(8,128)}, f32[128,128,256]{2,1,0:T(8,128)}) custom-call(s32[2]{0:T(128)} %pad_add_fusion.side_ref, s32[8,16]{1,0:T(8,128)} %bitcast.52, s32[8]{0:T(128)} %bitcast.54, bf16[8,16,128,128]{3,2,1,0:T(8,128)(2,1)} %bitcast.40, bf16[2,4,128,256]{3,2,1,0:T(8,128)(2,1)} %pad_maximum_fusion.grad_ref), custom_call_target="tpu_custom_call" | custom-call | flops 1073741824 | bytes 38273024 | tf_op jit(solution)/shard_map/pallas_call | solution.py:117
  226.8 25.4 %collective-permute-done.9 = f32[128,128,256]{2,1,0:T(8,128)S(1)} collective-permute-done((f32[128,128,256]{2,1,0:T(8,128)}, f32[128,128,256]{2,1,0:T(8,128)S(1)}, u32[]{:S(2)}, u32[]{:S(2)}) %collective-permute-start.9) | collective-permute-done | bytes 16777248 | tf_op jit(solution)/shard_map/ppermute | solution.py:152
  252.1 15.9 %fusion.6 = (f32[16,128,256]{2,1,0:T(8,128)}, f32[16,128,256]{2,1,0:T(8,128)}, f32[16,128,256]{2,1,0:T(8,128)}, f32[16,128,256]{2,1,0:T(8,128)}, f32[16,128,256]{2,1,0:T(8,128)}, /*index=5*/f32[16,128,256]{2,1,0:T(8,128)}) fusion(f32[2,4,16,128,256]{4,3,2,1,0:T(8,128)S(1)} %bitcast.43, f32[2,4,16,128,256]{4,3,2,1,0:T(8,128)} %bitcast.41), kind=kLoop, calls=%fused_computation.12 | loop fusion | flops 3145728 | bytes 37748736 | tf_op jit(solution)/shard_map/add | solution.py:159
  268.0 2.3 collective-permute-start.11
  270.4 1.0 collective-permute-start.19
  271.4 1.3 collective-permute-start.18
  273.5 1.2 collective-permute-start.12
  274.7 42.8 %collective-permute-done.11 = f32[16,128,256]{2,1,0:T(8,128)S(1)} collective-permute-done((f32[16,128,256]{2,1,0:T(8,128)}, f32[16,128,256]{2,1,0:T(8,128)S(1)}, u32[]{:S(2)}, u32[]{:S(2)}) %collective-permute-start.11) | collective-permute-done | bytes 2097184 | tf_op jit(solution)/shard_map/ppermute | solution.py:152
  317.5 1.9 collective-permute-start.10
  319.4 2.4 collective-permute-done.18
  321.7 43.4 %collective-permute-done.17 = f32[16,128,256]{2,1,0:T(8,128)S(1)} collective-permute-done((f32[16,128,256]{2,1,0:T(8,128)}, f32[16,128,256]{2,1,0:T(8,128)S(1)}, u32[]{:S(2)}, u32[]{:S(2)}) %collective-permute-start.17) | collective-permute-done | bytes 2097184 | tf_op jit(solution)/shard_map/ppermute | solution.py:152
  365.2 1.3 copy-done.5
  366.6 1.4 copy-done.6
  367.9 8.7 %fusion.9 = (f32[16,128,256]{2,1,0:T(8,128)S(1)}, f32[16,128,256]{2,1,0:T(8,128)S(1)}) fusion(f32[2,4,16,128,256]{4,3,2,1,0:T(8,128)} %bitcast.44, f32[2,4,16,128,256]{4,3,2,1,0:T(8,128)} %bitcast.42, f32[16,128,256]{2,1,0:T(8,128)} %copy-done.6, f32[16,128,256]{2,1,0:T(8,128)} %collective-permute-done.10, f32[16,128,256]{2,1,0:T(8,128)S(1)} %collective-permute-done.11, ...), kind=kLoop, calls=%fused_computation.17 | loop fusion | flops 4194304 | bytes 25165824 | tf_op jit(solution)/shard_map/add | solution.py:161
  376.8 1.4 collective-permute-start.14
  378.2 1.2 collective-permute-start.15
  380.4 1.5 collective-permute-start.21
  381.9 2.1 collective-permute-start.22
  384.0 9.3 %collective-permute-done.14 = f32[4,128,256]{2,1,0:T(8,128)S(1)} collective-permute-done((f32[4,128,256]{2,1,0:T(8,128)S(1)}, f32[4,128,256]{2,1,0:T(8,128)S(1)}, u32[]{:S(2)}, u32[]{:S(2)}) %collective-permute-start.14) | collective-permute-done | bytes 524320 | tf_op jit(solution)/shard_map/ppermute | solution.py:152
  393.2 1.6 collective-permute-start.20
  394.8 6.0 %collective-permute-done.15 = f32[4,128,256]{2,1,0:T(8,128)S(1)} collective-permute-done((f32[4,128,256]{2,1,0:T(8,128)S(1)}, f32[4,128,256]{2,1,0:T(8,128)S(1)}, u32[]{:S(2)}, u32[]{:S(2)}) %collective-permute-start.15) | collective-permute-done | bytes 524320 | tf_op jit(solution)/shard_map/ppermute | solution.py:152
  400.9 3.3 collective-permute-start.8
  404.3 1.4 collective-permute-start.16
  405.7 1.0 collective-permute-done.20
  406.9 1.8 collective-permute-start.23
  408.8 2.1 collective-permute-done.8
  411.6 5.5 %collective-permute-done.16 = f32[2,128,256]{2,1,0:T(8,128)S(1)} collective-permute-done((f32[2,128,256]{2,1,0:T(8,128)S(1)}, f32[2,128,256]{2,1,0:T(8,128)S(1)}, u32[]{:S(2)}, u32[]{:S(2)}) %collective-permute-start.16) | collective-permute-done | bytes 262176 | tf_op jit(solution)/shard_map/ppermute | solution.py:152
  417.2 3.5 collective-permute-done.23
  (47 shorter events, 7.3 us)
Async XLA Ops:
  7.2 157.1 %copy-start = (bf16[256,256]{1,0:T(8,128)(2,1)S(1)}, bf16[256,256]{1,0:T(8,128)(2,1)}, u32[]{:S(2)}) copy-start(bf16[256,256]{1,0:T(8,128)(2,1)} %param.7) | copy-start | bytes 393220
  7.2 128.1 %all-gather.2.cloned.1.call-start = ((), (), s32[]{:S(2)}) async-start(), calls=%async_computation | async-start | bytes 17039360 | tf_op jit(solution)/shard_map/all_gather | solution.py:186
  146.4 17.9 %copy-start.7 = (bf16[512,256]{1,0:T(8,128)(2,1)S(1)}, bf16[512,256]{1,0:T(8,128)(2,1)}, u32[]{:S(2)}) copy-start(bf16[512,256]{1,0:T(8,128)(2,1)} %param.11) | copy-start | bytes 786436
  147.5 15.7 %collective-permute-start = (f32[512,256]{1,0:T(8,128)S(1)}, f32[512,256]{1,0:T(8,128)S(1)}, u32[]{:S(2)}, u32[]{:S(2)}) collective-permute-start(f32[512,256]{1,0:T(8,128)S(1)} %constant_dynamic-slice_fusion), channel_id=1, source_target_pairs={{0,64},{64,0},{1,65},{65,1},{2,66},{66,2},{3,67},{67,3},{4,68},{68... | collective-permute-start | bytes 1572872 | tf_op jit(solution)/shard_map/ppermute | solution.py:144
  165.6 1.6 collective-permute-start.1
  167.3 8.4 %collective-permute-start.2 = (f32[256,256]{1,0:T(8,128)S(1)}, f32[256,256]{1,0:T(8,128)S(1)}, u32[]{:S(2)}, u32[]{:S(2)}) collective-permute-start(f32[256,256]{1,0:T(8,128)S(1)} %add.133), channel_id=1, source_target_pairs={{0,2},{1,3},{2,0},{3,1},{4,6},{5,7},{6,4},{7,5},{8,10},{9,11},{10,... | collective-permute-start | bytes 786440 | tf_op jit(solution)/shard_map/ppermute | solution.py:174
  175.8 9.1 %collective-permute-start.3 = (f32[256,256]{1,0:T(8,128)S(1)}, f32[256,256]{1,0:T(8,128)S(1)}, u32[]{:S(2)}, u32[]{:S(2)}) collective-permute-start(f32[256,256]{1,0:T(8,128)S(1)} %add.134), channel_id=1, source_target_pairs={{0,4},{1,5},{2,6},{3,7},{4,0},{5,1},{6,2},{7,3},{8,12},{9,13},{10,... | collective-permute-start | bytes 786440 | tf_op jit(solution)/shard_map/ppermute | solution.py:174
  184.9 6.7 %collective-permute-start.4 = (f32[256,256]{1,0:T(8,128)S(1)}, f32[256,256]{1,0:T(8,128)S(1)}, u32[]{:S(2)}, u32[]{:S(2)}) collective-permute-start(f32[256,256]{1,0:T(8,128)S(1)} %add.135), channel_id=1, source_target_pairs={{0,8},{1,9},{2,10},{3,11},{4,12},{5,13},{6,14},{7,15},{8,0},{9,1},... | collective-permute-start | bytes 786440 | tf_op jit(solution)/shard_map/ppermute | solution.py:174
  191.6 6.9 %collective-permute-start.5 = (f32[256,256]{1,0:T(8,128)S(1)}, f32[256,256]{1,0:T(8,128)S(1)}, u32[]{:S(2)}, u32[]{:S(2)}) collective-permute-start(f32[256,256]{1,0:T(8,128)S(1)} %add.136), channel_id=1, source_target_pairs={{0,16},{1,17},{2,18},{3,19},{4,20},{5,21},{6,22},{7,23},{8,24},{9,... | collective-permute-start | bytes 786440 | tf_op jit(solution)/shard_map/ppermute | solution.py:174
  192.9 8.3 %collective-permute-start.7 = (bf16[512,256]{1,0:T(8,128)(2,1)S(1)}, bf16[512,256]{1,0:T(8,128)(2,1)S(1)}, u32[]{:S(2)}, u32[]{:S(2)}) collective-permute-start(bf16[512,256]{1,0:T(8,128)(2,1)S(1)} %convolution_convert_fusion), channel_id=1, source_target_pairs={{0,64},{64,0},{1,65},{65,1},{2,66},{66,2},{3,67},{67,3},{4,68},{68... | collective-permute-start | bytes 786440 | tf_op jit(solution)/shard_map/ppermute | solution.py:144
  198.6 8.0 %collective-permute-start.6 = (f32[256,256]{1,0:T(8,128)S(1)}, f32[256,256]{1,0:T(8,128)S(1)}, u32[]{:S(2)}, u32[]{:S(2)}) collective-permute-start(f32[256,256]{1,0:T(8,128)S(1)} %add.137), channel_id=1, source_target_pairs={{0,32},{1,33},{2,34},{3,35},{4,36},{5,37},{6,38},{7,39},{8,40},{9,... | collective-permute-start | bytes 786440 | tf_op jit(solution)/shard_map/ppermute | solution.py:174
  226.5 25.6 %collective-permute-start.9 = (f32[128,128,256]{2,1,0:T(8,128)}, f32[128,128,256]{2,1,0:T(8,128)S(1)}, u32[]{:S(2)}, u32[]{:S(2)}) collective-permute-start(f32[128,128,256]{2,1,0:T(8,128)} %get-tuple-element.14), channel_id=1, source_target_pairs={{0,1},{1,0},{2,3},{3,2},{4,5},{5,4},{6,7},{7,6},{8,9},{9,8},{10,11... | collective-permute-start | bytes 50331656 | tf_op jit(solution)/shard_map/ppermute | solution.py:152
  252.1 15.9 %copy-start.2 = (f32[128,128,256]{2,1,0:T(8,128)}, f32[128,128,256]{2,1,0:T(8,128)S(1)}, u32[]{:S(2)}) copy-start(f32[128,128,256]{2,1,0:T(8,128)S(1)} %collective-permute-done.9) | copy-start | bytes 50331652
  268.0 49.5 %collective-permute-start.11 = (f32[16,128,256]{2,1,0:T(8,128)}, f32[16,128,256]{2,1,0:T(8,128)S(1)}, u32[]{:S(2)}, u32[]{:S(2)}) collective-permute-start(f32[16,128,256]{2,1,0:T(8,128)} %get-tuple-element.17), channel_id=1, source_target_pairs={{0,4},{1,5},{2,6},{3,7},{4,0},{5,1},{6,2},{7,3},{8,12},{9,13},{10,... | collective-permute-start | bytes 6291464 | tf_op jit(solution)/shard_map/ppermute | solution.py:152
  270.4 49.0 %collective-permute-start.19 = (f32[16,128,256]{2,1,0:T(8,128)}, f32[16,128,256]{2,1,0:T(8,128)S(1)}, u32[]{:S(2)}, u32[]{:S(2)}) collective-permute-start(f32[16,128,256]{2,1,0:T(8,128)} %get-tuple-element.18), channel_id=1, source_target_pairs={{0,48},{1,49},{2,50},{3,51},{4,52},{5,53},{6,54},{7,55},{8,56},{9,... | collective-permute-start | bytes 6291464 | tf_op jit(solution)/shard_map/ppermute | solution.py:152
  271.4 50.3 %collective-permute-start.18 = (f32[16,128,256]{2,1,0:T(8,128)}, f32[16,128,256]{2,1,0:T(8,128)S(1)}, u32[]{:S(2)}, u32[]{:S(2)}) collective-permute-start(f32[16,128,256]{2,1,0:T(8,128)} %get-tuple-element.19), channel_id=1, source_target_pairs={{0,32},{1,33},{2,34},{3,35},{4,36},{5,37},{6,38},{7,39},{8,40},{9,... | collective-permute-start | bytes 6291464 | tf_op jit(solution)/shard_map/ppermute | solution.py:152
  272.7 92.5 %collective-permute-start.17 = (f32[16,128,256]{2,1,0:T(8,128)}, f32[16,128,256]{2,1,0:T(8,128)S(1)}, u32[]{:S(2)}, u32[]{:S(2)}) collective-permute-start(f32[16,128,256]{2,1,0:T(8,128)} %get-tuple-element.20), channel_id=1, source_target_pairs={{0,16},{1,17},{2,18},{3,19},{4,20},{5,21},{6,22},{7,23},{8,24},{9,... | collective-permute-start | bytes 6291464 | tf_op jit(solution)/shard_map/ppermute | solution.py:152
  273.5 91.7 %collective-permute-start.12 = (f32[16,128,256]{2,1,0:T(8,128)}, f32[16,128,256]{2,1,0:T(8,128)S(1)}, u32[]{:S(2)}, u32[]{:S(2)}) collective-permute-start(f32[16,128,256]{2,1,0:T(8,128)} %get-tuple-element.21), channel_id=1, source_target_pairs={{0,6},{1,7},{2,0},{3,1},{4,2},{5,3},{6,4},{7,5},{8,14},{9,15},{10,... | collective-permute-start | bytes 6291464 | tf_op jit(solution)/shard_map/ppermute | solution.py:152
  317.5 50.4 %collective-permute-start.10 = (f32[16,128,256]{2,1,0:T(8,128)}, f32[16,128,256]{2,1,0:T(8,128)}, u32[]{:S(2)}, u32[]{:S(2)}) collective-permute-start(f32[16,128,256]{2,1,0:T(8,128)} %get-tuple-element.22), channel_id=1, source_target_pairs={{0,2},{1,3},{2,4},{3,5},{4,6},{5,7},{6,0},{7,1},{8,10},{9,11},{10,... | collective-permute-start | bytes 6291464 | tf_op jit(solution)/shard_map/ppermute | solution.py:152
  319.4 45.8 %copy-start.3 = (f32[16,128,256]{2,1,0:T(8,128)}, f32[16,128,256]{2,1,0:T(8,128)S(1)}, u32[]{:S(2)}) copy-start(f32[16,128,256]{2,1,0:T(8,128)S(1)} %collective-permute-done.19) | copy-start | bytes 6291460
  321.7 43.5 %copy-start.4 = (f32[16,128,256]{2,1,0:T(8,128)}, f32[16,128,256]{2,1,0:T(8,128)S(1)}, u32[]{:S(2)}) copy-start(f32[16,128,256]{2,1,0:T(8,128)S(1)} %collective-permute-done.18) | copy-start | bytes 6291460
  365.2 1.4 copy-start.5
  366.6 1.4 copy-start.6
  376.8 16.4 %collective-permute-start.14 = (f32[4,128,256]{2,1,0:T(8,128)S(1)}, f32[4,128,256]{2,1,0:T(8,128)S(1)}, u32[]{:S(2)}, u32[]{:S(2)}) collective-permute-start(f32[4,128,256]{2,1,0:T(8,128)S(1)} %get-tuple-element.23), channel_id=1, source_target_pairs={{0,32},{1,33},{2,34},{3,35},{4,36},{5,37},{6,38},{7,39},{8,40},{9,... | collective-permute-start | bytes 1572872 | tf_op jit(solution)/shard_map/ppermute | solution.py:152
  378.2 22.7 %collective-permute-start.15 = (f32[4,128,256]{2,1,0:T(8,128)S(1)}, f32[4,128,256]{2,1,0:T(8,128)S(1)}, u32[]{:S(2)}, u32[]{:S(2)}) collective-permute-start(f32[4,128,256]{2,1,0:T(8,128)S(1)} %get-tuple-element.24), channel_id=1, source_target_pairs={{0,48},{1,49},{2,50},{3,51},{4,52},{5,53},{6,54},{7,55},{8,56},{9,... | collective-permute-start | bytes 1572872 | tf_op jit(solution)/shard_map/ppermute | solution.py:152
  379.4 24.7 %collective-permute-start.13 = (f32[4,128,256]{2,1,0:T(8,128)S(1)}, f32[4,128,256]{2,1,0:T(8,128)S(1)}, u32[]{:S(2)}, u32[]{:S(2)}) collective-permute-start(f32[4,128,256]{2,1,0:T(8,128)S(1)} %get-tuple-element.25), channel_id=1, source_target_pairs={{0,16},{1,17},{2,18},{3,19},{4,20},{5,21},{6,22},{7,23},{8,24},{9,... | collective-permute-start | bytes 1572872 | tf_op jit(solution)/shard_map/ppermute | solution.py:152
  380.4 25.3 %collective-permute-start.21 = (f32[4,128,256]{2,1,0:T(8,128)S(1)}, f32[4,128,256]{2,1,0:T(8,128)S(1)}, u32[]{:S(2)}, u32[]{:S(2)}) collective-permute-start(f32[4,128,256]{2,1,0:T(8,128)S(1)} %get-tuple-element.26), channel_id=1, source_target_pairs={{0,4},{1,5},{2,6},{3,7},{4,0},{5,1},{6,2},{7,3},{8,12},{9,13},{10,... | collective-permute-start | bytes 1572872 | tf_op jit(solution)/shard_map/ppermute | solution.py:152
  381.9 23.8 %collective-permute-start.22 = (f32[4,128,256]{2,1,0:T(8,128)S(1)}, f32[4,128,256]{2,1,0:T(8,128)S(1)}, u32[]{:S(2)}, u32[]{:S(2)}) collective-permute-start(f32[4,128,256]{2,1,0:T(8,128)S(1)} %get-tuple-element.27), channel_id=1, source_target_pairs={{0,6},{1,7},{2,0},{3,1},{4,2},{5,3},{6,4},{7,5},{8,14},{9,15},{10,... | collective-permute-start | bytes 1572872 | tf_op jit(solution)/shard_map/ppermute | solution.py:152
  393.2 13.5 %collective-permute-start.20 = (f32[4,128,256]{2,1,0:T(8,128)S(1)}, f32[4,128,256]{2,1,0:T(8,128)S(1)}, u32[]{:S(2)}, u32[]{:S(2)}) collective-permute-start(f32[4,128,256]{2,1,0:T(8,128)S(1)} %get-tuple-element.28), channel_id=1, source_target_pairs={{0,2},{1,3},{2,4},{3,5},{4,6},{5,7},{6,0},{7,1},{8,10},{9,11},{10,... | collective-permute-start | bytes 1572872 | tf_op jit(solution)/shard_map/ppermute | solution.py:152
  400.9 10.0 %collective-permute-start.8 = (f32[256,256]{1,0:T(8,128)S(1)}, f32[256,256]{1,0:T(8,128)S(1)}, u32[]{:S(2)}, u32[]{:S(2)}) collective-permute-start(f32[256,256]{1,0:T(8,128)S(1)} %add.138), channel_id=1, source_target_pairs={{0,64},{64,0},{1,65},{65,1},{2,66},{66,2},{3,67},{67,3},{4,68},{68... | collective-permute-start | bytes 786440 | tf_op jit(solution)/shard_map/ppermute | solution.py:144
  404.3 12.8 %collective-permute-start.16 = (f32[2,128,256]{2,1,0:T(8,128)S(1)}, f32[2,128,256]{2,1,0:T(8,128)S(1)}, u32[]{:S(2)}, u32[]{:S(2)}) collective-permute-start(f32[2,128,256]{2,1,0:T(8,128)S(1)} %slice.137), channel_id=1, source_target_pairs={{0,8},{1,9},{2,10},{3,11},{4,12},{5,13},{6,14},{7,15},{8,0},{9,1},... | collective-permute-start | bytes 786440 | tf_op jit(solution)/shard_map/ppermute | solution.py:152
  406.7 14.7 %copy-start.1 = (bf16[256,256]{1,0:T(8,128)(2,1)S(1)}, bf16[256,256]{1,0:T(8,128)(2,1)}, u32[]{:S(2)}) copy-start(bf16[256,256]{1,0:T(8,128)(2,1)} %param.7) | copy-start | bytes 393220
  406.9 13.7 %collective-permute-start.23 = (f32[2,128,256]{2,1,0:T(8,128)S(1)}, f32[2,128,256]{2,1,0:T(8,128)S(1)}, u32[]{:S(2)}, u32[]{:S(2)}) collective-permute-start(f32[2,128,256]{2,1,0:T(8,128)S(1)} %slice.151), channel_id=1, source_target_pairs={{0,8},{1,9},{2,10},{3,11},{4,12},{5,13},{6,14},{7,15},{8,0},{9,1},... | collective-permute-start | bytes 786440 | tf_op jit(solution)/shard_map/ppermute | solution.py:152
Sparse Core Ops, SparseCore 0:
  9.7 125.4 all-gather.1
